TPU v7x, 128 devices: a whole 4x4x4 slice. The times are simulated.
128 devices in a mesh: gy: 8 (over x, y_hi), gz: 16 (over z, y_lo, core).
Axes of the slice: x: 4, y: 4 (y_hi: 2, y_lo: 2; y = y_hi * 2 + y_lo), z: 4, core: 2. Of those that a mesh axis runs over, the one named last changes fastest.
Arguments:
- fixed_features: bfloat16 [1024, 131072], P('gy', 'gz'), may hold values from -14 to 14
- moving_features: bfloat16 [1024, 131072], P('gy', 'gz'), may hold values from -14 to 14
- cand_offsets: int32 [256, 16, 16], P('gy', 'gz'), may hold values from -32 to 32, as said below
- cand_lengths: int32 [256, 16], P('gy', 'gz'), may hold values from 6 to 16, as said below
- smooth_radii: int32 [3], replicated, may hold values from 1 to 4, as said below
Outputs:
- disp_init: float32 [1024, 8192], P('gy', 'gz')
- disp_final: float32 [1024, 8192], P('gy', 'gz')
Inputs may be any that keep to these rules, and one draw needn't show every extreme that they name: Each offset is a multiple of 4 and moves its block inside the grid: 0 <= 4 b + cand_offsets[b, s, k] <= 1020 for every slot. `cand_lengths`: some list is full in every draw. `smooth_radii`: the radii of the iterations differ from one another; 1 and 4 both occur in every draw.
All inputs are finite; a program needn't handle non-finite values.
Results may differ from a plain program's by a relative error of at most 0.0003.
Values may be sent and summed in bfloat16 or wider, within the bound.
No kernel may reach another device: no remote copies, remote signals or barrier semaphores. Data moves between devices by JAX's collectives and lax.ppermute only.
A program may use at most 128 MiB of HBM per device.

v0:
```python
import jax
import jax.numpy as jnp
from jax import lax
from jax.sharding import PartitionSpec as P

CH = 16
XS = 8
REACH = 32
RMAX = 4
ITERS = 3


softmin_temp = 2.0
smooth_weight = 2.0
adam_rate = 0.2
beta_first = 0.9
beta_second = 0.999
adam_floor = 0.05


def with_halo(cells, sides, width):
    for axis, dim in sides:
        count = lax.axis_size(axis)
        ends = count - 1
        head = lax.slice_in_dim(cells, 0, width, axis=dim)
        tail = lax.slice_in_dim(cells, cells.shape[dim] - width, cells.shape[dim], axis=dim)
        cells = jnp.concatenate(
            [
                lax.ppermute(tail, axis, [(i, (i + 1) % count) for i in range(ends)]),
                cells,
                lax.ppermute(head, axis, [((i + 1) % count, i) for i in range(ends)]),
            ],
            axis=dim,
        )
    return cells


def box_weights(radius):
    spread = jnp.arange(-RMAX, RMAX + 1)
    inside = jnp.abs(spread) <= radius
    return jnp.where(inside, 1.0, 0.0).astype(jnp.float32) / (2 * radius + 1).astype(jnp.float32)


def smooth_inner(padded, radius, margin):
    weights = box_weights(radius)
    height = padded.shape[0] - 2 * margin
    layers = padded.shape[1] - 2 * margin
    depth_cells = padded.shape[2]
    along_y = jnp.zeros((height, padded.shape[1], depth_cells), jnp.float32)
    for offset in range(-RMAX, RMAX + 1):
        along_y = (
            along_y + weights[RMAX + offset] * padded[margin + offset : margin + offset + height]
        )
    along_z = jnp.zeros((height, layers, depth_cells), jnp.float32)
    for offset in range(-RMAX, RMAX + 1):
        along_z = (
            along_z
            + weights[RMAX + offset] * along_y[:, margin + offset : margin + offset + layers]
        )
    x_padded = jnp.pad(along_z, ((0, 0), (0, 0), (RMAX, RMAX)))
    along_x = jnp.zeros((height, layers, depth_cells), jnp.float32)
    for offset in range(-RMAX, RMAX + 1):
        along_x = (
            along_x
            + weights[RMAX + offset] * x_padded[:, :, RMAX + offset : RMAX + offset + depth_cells]
        )
    return along_x


def adam_update(field, target_field, smoothed, first_moment, second_moment, iteration):
    gradient = field - target_field + smooth_weight * (field - smoothed)
    first_moment = beta_first * first_moment + (1.0 - beta_first) * gradient
    second_moment = beta_second * second_moment + (1.0 - beta_second) * gradient * gradient
    first_hat = first_moment / (1.0 - beta_first ** (iteration + 1))
    second_hat = second_moment / (1.0 - beta_second ** (iteration + 1))
    field = field - adam_rate * first_hat / (jnp.sqrt(second_hat) + adam_floor)
    return (field, first_moment, second_moment)


def per_device(fixed_features, moving_features, cand_offsets, cand_lengths, smooth_radii):
    height = fixed_features.shape[0]
    columns_dev = fixed_features.shape[1] // CH
    blocks = height // 4
    total_y = height * lax.axis_size("gy")
    block_ids = lax.axis_index("gy") * blocks + jnp.arange(blocks, dtype=jnp.int32)
    shifts = cand_offsets[:, 0, :]
    targets = 4 * block_ids[:, None] + shifts
    counts = cand_lengths[:, 0]
    quad_rows = jnp.arange(4, dtype=jnp.int32)
    fixed_rows = fixed_features.reshape(blocks, 4, columns_dev, CH)
    longest = jnp.max(counts)
    start_state = (
        jnp.full((blocks, 4, columns_dev), -1e30, jnp.float32),
        jnp.zeros((blocks, 4, columns_dev), jnp.float32),
        jnp.zeros((blocks, 4, columns_dev), jnp.float32),
    )
    source = with_halo(moving_features, (("gy", 0),), REACH)
    row_base = lax.axis_index("gy") * height - REACH
    source_rows = source.shape[0]

    def absorb(candidate, softmin_state):
        peak_score, total_weight, weighted = softmin_state
        wanted = lax.dynamic_index_in_dim(targets, candidate, 1, keepdims=False)
        live = candidate < counts
        local_rows = jnp.clip(wanted - row_base, 0, source_rows - 4)
        row_ids = (local_rows[:, None] + quad_rows).reshape(-1)
        moved_rows = jnp.take(source, row_ids, axis=0).reshape(blocks, 4, columns_dev, CH)
        differences = fixed_rows.astype(jnp.float32) - moved_rows.astype(jnp.float32)
        cost_sum = jnp.sum(differences * differences, axis=-1)
        scores = -cost_sum / softmin_temp
        live_mask = live[:, None, None]
        new_peak = jnp.where(live_mask, jnp.maximum(peak_score, scores), peak_score)
        rescale = jnp.exp(peak_score - new_peak)
        fresh_term = jnp.where(
            live_mask, jnp.exp(jnp.where(live_mask, scores, new_peak) - new_peak), 0.0
        )
        chosen_shift = lax.dynamic_index_in_dim(shifts, candidate, 1, keepdims=False)
        shift_norm = (2.0 * chosen_shift.astype(jnp.float32) / total_y)[:, None, None]
        return (
            new_peak,
            total_weight * rescale + fresh_term,
            weighted * rescale + fresh_term * shift_norm,
        )

    final_state = lax.fori_loop(0, longest, absorb, start_state)
    disp_init = (final_state[2] / final_state[1]).reshape(height, columns_dev)
    target_field = disp_init.reshape(height, -1, XS)
    field = target_field
    first_moment = jnp.zeros_like(target_field)
    second_moment = jnp.zeros_like(target_field)
    for iteration in range(ITERS):
        padded = with_halo(field, (("gy", 0), ("gz", 1)), RMAX)
        smoothed = smooth_inner(padded, smooth_radii[iteration], RMAX)
        field, first_moment, second_moment = adam_update(
            field, target_field, smoothed, first_moment, second_moment, iteration
        )
    return (disp_init, field.reshape(height, columns_dev))


def solution(mesh):
    in_specs = (P("gy", "gz"), P("gy", "gz"), P("gy", "gz", None), P("gy", "gz"), P())
    out_specs = (P("gy", "gz"), P("gy", "gz"))
    return jax.shard_map(
        per_device, mesh=mesh, in_specs=in_specs, out_specs=out_specs, check_vma=False
    )
```

profile of v0, /device:TPU:11, one launch (start us, length us, event | category | flops | bytes accessed | tf_op | source)
XLA Modules:
  0.0 786.4 jit_solution(12559759159196684666)
XLA Ops:
  1.9 3.9 collective-permute-start
  5.8 3.8 collective-permute-start.1
  9.6 16.7 %reshape.94 = bf16[32,4,512,16]{3,2,1,0:T(8,128)(2,1)} reshape(bf16[128,8192]{1,0:T(8,128)(2,1)} %param.7) | data formatting | bytes 4194304 | tf_op jit(solution)/shard_map/reshape | solution.py:90
  29.1 2.2 collective-permute-done.1
  34.9 459.2 %while.17 = (s32[]{:T(128)}, f32[32,4,512]{2,1,0:T(4,128)S(1)}, f32[32,4,512]{2,1,0:T(4,128)}, f32[32,4,512]{2,1,0:T(4,128)}, s32[]{:T(128)}, /*index=5*/s32[32]...) while((s32[]{:T(128)}, f32[32,4,512]{2,1,0:T(4,128)S(1)}, ...), condition=%wide.region_3.4_spmd.clone, body=%wide.region_1.3_spmd.clone.sunk | while | flops 7473701 | bytes 20195720 | solution.py:125
  35.8 3.2 gather_fusion
  39.0 16.8 %gather.16 = bf16[32,4,512,16]{3,2,1,0:T(8,128)(2,1)} reshape(bf16[128,8192]{1,0:T(8,128)(2,1)} %gather_fusion) | data formatting | bytes 4194304 | tf_op jit(solution)/shard_map/while/body/jit(_take)/gather | solution.py:107
  55.9 15.7 %multiply_reduce_fusion.2 = f32[32,4,512]{2,1,0:T(4,128)S(1)} fusion(bf16[32,4,512,16]{3,2,1,0:T(8,128)(2,1)} %get-tuple-element.370, bf16[32,4,512,16]{3,2,1,0:T(8,128)(2,1)} %gather.16, pred[32,4]{1,0:T(8,128)(4,1)S(1)} %copy.210), kind=kLoop, calls=%fused_computation.2.clone.1 | loop fusion | flops 6225920 | bytes 4456576 | tf_op jit(solution)/shard_map/while/body/reduce_sum | solution.py:109
  74.0 3.2 gather_fusion
  77.2 16.8 %gather.16 = bf16[32,4,512,16]{3,2,1,0:T(8,128)(2,1)} reshape(bf16[128,8192]{1,0:T(8,128)(2,1)} %gather_fusion) | data formatting | bytes 4194304 | tf_op jit(solution)/shard_map/while/body/jit(_take)/gather | solution.py:107
  94.1 15.7 %multiply_reduce_fusion.2 = f32[32,4,512]{2,1,0:T(4,128)S(1)} fusion(bf16[32,4,512,16]{3,2,1,0:T(8,128)(2,1)} %get-tuple-element.370, bf16[32,4,512,16]{3,2,1,0:T(8,128)(2,1)} %gather.16, pred[32,4]{1,0:T(8,128)(4,1)S(1)} %copy.210), kind=kLoop, calls=%fused_computation.2.clone.1 | loop fusion | flops 6225920 | bytes 4456576 | tf_op jit(solution)/shard_map/while/body/reduce_sum | solution.py:109
  112.2 3.2 gather_fusion
  115.4 16.8 %gather.16 = bf16[32,4,512,16]{3,2,1,0:T(8,128)(2,1)} reshape(bf16[128,8192]{1,0:T(8,128)(2,1)} %gather_fusion) | data formatting | bytes 4194304 | tf_op jit(solution)/shard_map/while/body/jit(_take)/gather | solution.py:107
  132.3 15.7 %multiply_reduce_fusion.2 = f32[32,4,512]{2,1,0:T(4,128)S(1)} fusion(bf16[32,4,512,16]{3,2,1,0:T(8,128)(2,1)} %get-tuple-element.370, bf16[32,4,512,16]{3,2,1,0:T(8,128)(2,1)} %gather.16, pred[32,4]{1,0:T(8,128)(4,1)S(1)} %copy.210), kind=kLoop, calls=%fused_computation.2.clone.1 | loop fusion | flops 6225920 | bytes 4456576 | tf_op jit(solution)/shard_map/while/body/reduce_sum | solution.py:109
  150.4 3.2 gather_fusion
  153.6 16.8 %gather.16 = bf16[32,4,512,16]{3,2,1,0:T(8,128)(2,1)} reshape(bf16[128,8192]{1,0:T(8,128)(2,1)} %gather_fusion) | data formatting | bytes 4194304 | tf_op jit(solution)/shard_map/while/body/jit(_take)/gather | solution.py:107
  170.5 15.7 %multiply_reduce_fusion.2 = f32[32,4,512]{2,1,0:T(4,128)S(1)} fusion(bf16[32,4,512,16]{3,2,1,0:T(8,128)(2,1)} %get-tuple-element.370, bf16[32,4,512,16]{3,2,1,0:T(8,128)(2,1)} %gather.16, pred[32,4]{1,0:T(8,128)(4,1)S(1)} %copy.210), kind=kLoop, calls=%fused_computation.2.clone.1 | loop fusion | flops 6225920 | bytes 4456576 | tf_op jit(solution)/shard_map/while/body/reduce_sum | solution.py:109
  188.7 3.2 gather_fusion
  191.8 16.8 %gather.16 = bf16[32,4,512,16]{3,2,1,0:T(8,128)(2,1)} reshape(bf16[128,8192]{1,0:T(8,128)(2,1)} %gather_fusion) | data formatting | bytes 4194304 | tf_op jit(solution)/shard_map/while/body/jit(_take)/gather | solution.py:107
  208.7 15.7 %multiply_reduce_fusion.2 = f32[32,4,512]{2,1,0:T(4,128)S(1)} fusion(bf16[32,4,512,16]{3,2,1,0:T(8,128)(2,1)} %get-tuple-element.370, bf16[32,4,512,16]{3,2,1,0:T(8,128)(2,1)} %gather.16, pred[32,4]{1,0:T(8,128)(4,1)S(1)} %copy.210), kind=kLoop, calls=%fused_computation.2.clone.1 | loop fusion | flops 6225920 | bytes 4456576 | tf_op jit(solution)/shard_map/while/body/reduce_sum | solution.py:109
  226.9 3.2 gather_fusion
  230.0 16.8 %gather.16 = bf16[32,4,512,16]{3,2,1,0:T(8,128)(2,1)} reshape(bf16[128,8192]{1,0:T(8,128)(2,1)} %gather_fusion) | data formatting | bytes 4194304 | tf_op jit(solution)/shard_map/while/body/jit(_take)/gather | solution.py:107
  246.9 15.7 %multiply_reduce_fusion.2 = f32[32,4,512]{2,1,0:T(4,128)S(1)} fusion(bf16[32,4,512,16]{3,2,1,0:T(8,128)(2,1)} %get-tuple-element.370, bf16[32,4,512,16]{3,2,1,0:T(8,128)(2,1)} %gather.16, pred[32,4]{1,0:T(8,128)(4,1)S(1)} %copy.210), kind=kLoop, calls=%fused_computation.2.clone.1 | loop fusion | flops 6225920 | bytes 4456576 | tf_op jit(solution)/shard_map/while/body/reduce_sum | solution.py:109
  265.1 3.2 gather_fusion
  268.2 16.8 %gather.16 = bf16[32,4,512,16]{3,2,1,0:T(8,128)(2,1)} reshape(bf16[128,8192]{1,0:T(8,128)(2,1)} %gather_fusion) | data formatting | bytes 4194304 | tf_op jit(solution)/shard_map/while/body/jit(_take)/gather | solution.py:107
  285.2 15.7 %multiply_reduce_fusion.2 = f32[32,4,512]{2,1,0:T(4,128)S(1)} fusion(bf16[32,4,512,16]{3,2,1,0:T(8,128)(2,1)} %get-tuple-element.370, bf16[32,4,512,16]{3,2,1,0:T(8,128)(2,1)} %gather.16, pred[32,4]{1,0:T(8,128)(4,1)S(1)} %copy.210), kind=kLoop, calls=%fused_computation.2.clone.1 | loop fusion | flops 6225920 | bytes 4456576 | tf_op jit(solution)/shard_map/while/body/reduce_sum | solution.py:109
  303.3 3.2 gather_fusion
  306.5 16.8 %gather.16 = bf16[32,4,512,16]{3,2,1,0:T(8,128)(2,1)} reshape(bf16[128,8192]{1,0:T(8,128)(2,1)} %gather_fusion) | data formatting | bytes 4194304 | tf_op jit(solution)/shard_map/while/body/jit(_take)/gather | solution.py:107
  323.4 15.7 %multiply_reduce_fusion.2 = f32[32,4,512]{2,1,0:T(4,128)S(1)} fusion(bf16[32,4,512,16]{3,2,1,0:T(8,128)(2,1)} %get-tuple-element.370, bf16[32,4,512,16]{3,2,1,0:T(8,128)(2,1)} %gather.16, pred[32,4]{1,0:T(8,128)(4,1)S(1)} %copy.210), kind=kLoop, calls=%fused_computation.2.clone.1 | loop fusion | flops 6225920 | bytes 4456576 | tf_op jit(solution)/shard_map/while/body/reduce_sum | solution.py:109
  341.5 3.2 gather_fusion
  344.7 16.8 %gather.16 = bf16[32,4,512,16]{3,2,1,0:T(8,128)(2,1)} reshape(bf16[128,8192]{1,0:T(8,128)(2,1)} %gather_fusion) | data formatting | bytes 4194304 | tf_op jit(solution)/shard_map/while/body/jit(_take)/gather | solution.py:107
  361.6 15.7 %multiply_reduce_fusion.2 = f32[32,4,512]{2,1,0:T(4,128)S(1)} fusion(bf16[32,4,512,16]{3,2,1,0:T(8,128)(2,1)} %get-tuple-element.370, bf16[32,4,512,16]{3,2,1,0:T(8,128)(2,1)} %gather.16, pred[32,4]{1,0:T(8,128)(4,1)S(1)} %copy.210), kind=kLoop, calls=%fused_computation.2.clone.1 | loop fusion | flops 6225920 | bytes 4456576 | tf_op jit(solution)/shard_map/while/body/reduce_sum | solution.py:109
  379.7 3.2 gather_fusion
  382.9 16.8 %gather.16 = bf16[32,4,512,16]{3,2,1,0:T(8,128)(2,1)} reshape(bf16[128,8192]{1,0:T(8,128)(2,1)} %gather_fusion) | data formatting | bytes 4194304 | tf_op jit(solution)/shard_map/while/body/jit(_take)/gather | solution.py:107
  399.8 15.7 %multiply_reduce_fusion.2 = f32[32,4,512]{2,1,0:T(4,128)S(1)} fusion(bf16[32,4,512,16]{3,2,1,0:T(8,128)(2,1)} %get-tuple-element.370, bf16[32,4,512,16]{3,2,1,0:T(8,128)(2,1)} %gather.16, pred[32,4]{1,0:T(8,128)(4,1)S(1)} %copy.210), kind=kLoop, calls=%fused_computation.2.clone.1 | loop fusion | flops 6225920 | bytes 4456576 | tf_op jit(solution)/shard_map/while/body/reduce_sum | solution.py:109
  417.9 3.2 gather_fusion
  421.1 16.8 %gather.16 = bf16[32,4,512,16]{3,2,1,0:T(8,128)(2,1)} reshape(bf16[128,8192]{1,0:T(8,128)(2,1)} %gather_fusion) | data formatting | bytes 4194304 | tf_op jit(solution)/shard_map/while/body/jit(_take)/gather | solution.py:107
  438.0 15.7 %multiply_reduce_fusion.2 = f32[32,4,512]{2,1,0:T(4,128)S(1)} fusion(bf16[32,4,512,16]{3,2,1,0:T(8,128)(2,1)} %get-tuple-element.370, bf16[32,4,512,16]{3,2,1,0:T(8,128)(2,1)} %gather.16, pred[32,4]{1,0:T(8,128)(4,1)S(1)} %copy.210), kind=kLoop, calls=%fused_computation.2.clone.1 | loop fusion | flops 6225920 | bytes 4456576 | tf_op jit(solution)/shard_map/while/body/reduce_sum | solution.py:109
  456.1 3.2 gather_fusion
  459.3 16.8 %gather.16 = bf16[32,4,512,16]{3,2,1,0:T(8,128)(2,1)} reshape(bf16[128,8192]{1,0:T(8,128)(2,1)} %gather_fusion) | data formatting | bytes 4194304 | tf_op jit(solution)/shard_map/while/body/jit(_take)/gather | solution.py:107
  476.2 15.7 %multiply_reduce_fusion.2 = f32[32,4,512]{2,1,0:T(4,128)S(1)} fusion(bf16[32,4,512,16]{3,2,1,0:T(8,128)(2,1)} %get-tuple-element.370, bf16[32,4,512,16]{3,2,1,0:T(8,128)(2,1)} %gather.16, pred[32,4]{1,0:T(8,128)(4,1)S(1)} %copy.210), kind=kLoop, calls=%fused_computation.2.clone.1 | loop fusion | flops 6225920 | bytes 4456576 | tf_op jit(solution)/shard_map/while/body/reduce_sum | solution.py:109
  495.4 155.5 %collective-permute-start.2 = (f32[4,64,8]{0,2,1:T(8,128)S(1)}, f32[4,64,8]{0,2,1:T(8,128)S(1)}, u32[]{:S(2)}, u32[]{:S(2)}) collective-permute-start(f32[4,64,8]{0,2,1:T(8,128)S(1)} %bitcast.49), channel_id=1, source_target_pairs={{0,16},{16,32},{32,48},{48,64},{64,80},{80,96},{96,112},{1,17},{17... | collective-permute-start | bytes 24584 | tf_op jit(solution)/shard_map/ppermute | solution.py:29
  653.6 3.6 reshape_reshape.3
  657.2 3.7 copy.201
  661.0 7.4 collective-permute-start.4
  671.7 2.9 collective-permute-done.5
  674.9 6.4 fusion.21
  681.2 5.8 fusion.109
  687.1 6.2 divide_subtract_fusion.1
  693.4 3.1 collective-permute-start.6
  696.5 4.5 collective-permute-start.7
  701.7 5.1 collective-permute-done.6
  709.1 5.4 collective-permute-start.8
  718.0 2.6 collective-permute-done.9
  720.9 6.4 fusion.13
  727.3 5.8 fusion.101
  733.1 6.3 divide_subtract_fusion
  741.6 5.6 collective-permute-start.11
  749.5 5.7 collective-permute-done.11
  755.3 5.4 collective-permute-start.12
  764.1 2.7 collective-permute-done.13
  767.1 6.3 fusion.5
  773.4 5.8 fusion.93
  779.2 6.4 fusion.117
  (302 shorter events, 50.4 us)
Async XLA Ops:
  1.9 26.4 %collective-permute-start = (bf16[32,8192]{1,0:T(8,128)(2,1)S(1)}, bf16[32,8192]{1,0:T(8,128)(2,1)S(1)}, u32[]{:S(2)}, u32[]{:S(2)}) collective-permute-start(bf16[32,8192]{1,0:T(8,128)(2,1)S(1)} %get-tuple-element.220), channel_id=1, source_target_pairs={{0,16},{16,32},{32,48},{48,64},{64,80},{80,96},{96,112},{1,17},{17... | collective-permute-start | bytes 1572872 | tf_op jit(solution)/shard_map/ppermute | solution.py:29
  5.8 25.6 %collective-permute-start.1 = (bf16[32,8192]{1,0:T(8,128)(2,1)S(1)}, bf16[32,8192]{1,0:T(8,128)(2,1)}, u32[]{:S(2)}, u32[]{:S(2)}) collective-permute-start(bf16[32,8192]{1,0:T(8,128)(2,1)S(1)} %get-tuple-element.221), channel_id=1, source_target_pairs={{16,0},{32,16},{48,32},{64,48},{80,64},{96,80},{112,96},{17,1},{33... | collective-permute-start | bytes 1572872 | tf_op jit(solution)/shard_map/ppermute | solution.py:31
  9.6 16.8 %copy-start.6 = (s32[3]{0:T(128)S(1)}, s32[3]{0:T(128)}, u32[]{:S(2)}) copy-start(s32[3]{0:T(128)} %param.11) | copy-start | bytes 40
  9.6 18.0 %copy-start.7 = (s32[32,1]{0,1:T(1,128)S(1)}, s32[32,1]{0,1:T(1,128)}, u32[]{:S(2)}) copy-start(s32[32,1]{0,1:T(1,128)} %param.10) | copy-start | bytes 388
  9.6 18.7 %copy-start.5 = (s32[32,1,16]{0,2,1:T(8,128)S(1)}, s32[32,1,16]{0,2,1:T(8,128)}, u32[]{:S(2)}) copy-start(s32[32,1,16]{0,2,1:T(8,128)} %param.9) | copy-start | bytes 6148
  28.3 0.8 copy-start.4
  55.9 15.8 %copy-start.2 = (f32[32,4,512]{2,1,0:T(4,128)S(1)}, f32[32,4,512]{2,1,0:T(4,128)}, u32[]{:S(2)}) copy-start(f32[32,4,512]{2,1,0:T(4,128)} %get-tuple-element.353) | copy-start | bytes 786436 | tf_op jit(solution)/shard_map/while
  55.9 16.2 %copy-start = (f32[32,4,512]{2,1,0:T(4,128)S(1)}, f32[32,4,512]{2,1,0:T(4,128)}, u32[]{:S(2)}) copy-start(f32[32,4,512]{2,1,0:T(4,128)} %get-tuple-element.352) | copy-start | bytes 786436 | tf_op jit(solution)/shard_map/while
  72.1 0.7 copy-start.3
  72.4 0.7 copy-start.1
  94.1 15.8 %copy-start.2 = (f32[32,4,512]{2,1,0:T(4,128)S(1)}, f32[32,4,512]{2,1,0:T(4,128)}, u32[]{:S(2)}) copy-start(f32[32,4,512]{2,1,0:T(4,128)} %get-tuple-element.353) | copy-start | bytes 786436 | tf_op jit(solution)/shard_map/while
  94.1 16.2 %copy-start = (f32[32,4,512]{2,1,0:T(4,128)S(1)}, f32[32,4,512]{2,1,0:T(4,128)}, u32[]{:S(2)}) copy-start(f32[32,4,512]{2,1,0:T(4,128)} %get-tuple-element.352) | copy-start | bytes 786436 | tf_op jit(solution)/shard_map/while
  110.3 0.7 copy-start.3
  110.6 0.7 copy-start.1
  132.3 15.8 %copy-start.2 = (f32[32,4,512]{2,1,0:T(4,128)S(1)}, f32[32,4,512]{2,1,0:T(4,128)}, u32[]{:S(2)}) copy-start(f32[32,4,512]{2,1,0:T(4,128)} %get-tuple-element.353) | copy-start | bytes 786436 | tf_op jit(solution)/shard_map/while
  132.3 16.2 %copy-start = (f32[32,4,512]{2,1,0:T(4,128)S(1)}, f32[32,4,512]{2,1,0:T(4,128)}, u32[]{:S(2)}) copy-start(f32[32,4,512]{2,1,0:T(4,128)} %get-tuple-element.352) | copy-start | bytes 786436 | tf_op jit(solution)/shard_map/while
  148.5 0.7 copy-start.3
  148.8 0.7 copy-start.1
  170.5 15.8 %copy-start.2 = (f32[32,4,512]{2,1,0:T(4,128)S(1)}, f32[32,4,512]{2,1,0:T(4,128)}, u32[]{:S(2)}) copy-start(f32[32,4,512]{2,1,0:T(4,128)} %get-tuple-element.353) | copy-start | bytes 786436 | tf_op jit(solution)/shard_map/while
  170.5 16.2 %copy-start = (f32[32,4,512]{2,1,0:T(4,128)S(1)}, f32[32,4,512]{2,1,0:T(4,128)}, u32[]{:S(2)}) copy-start(f32[32,4,512]{2,1,0:T(4,128)} %get-tuple-element.352) | copy-start | bytes 786436 | tf_op jit(solution)/shard_map/while
  186.7 0.7 copy-start.3
  187.0 0.7 copy-start.1
  208.7 15.8 %copy-start.2 = (f32[32,4,512]{2,1,0:T(4,128)S(1)}, f32[32,4,512]{2,1,0:T(4,128)}, u32[]{:S(2)}) copy-start(f32[32,4,512]{2,1,0:T(4,128)} %get-tuple-element.353) | copy-start | bytes 786436 | tf_op jit(solution)/shard_map/while
  208.7 16.2 %copy-start = (f32[32,4,512]{2,1,0:T(4,128)S(1)}, f32[32,4,512]{2,1,0:T(4,128)}, u32[]{:S(2)}) copy-start(f32[32,4,512]{2,1,0:T(4,128)} %get-tuple-element.352) | copy-start | bytes 786436 | tf_op jit(solution)/shard_map/while
  224.9 0.7 copy-start.3
  225.3 0.7 copy-start.1
  246.9 15.8 %copy-start.2 = (f32[32,4,512]{2,1,0:T(4,128)S(1)}, f32[32,4,512]{2,1,0:T(4,128)}, u32[]{:S(2)}) copy-start(f32[32,4,512]{2,1,0:T(4,128)} %get-tuple-element.353) | copy-start | bytes 786436 | tf_op jit(solution)/shard_map/while
  246.9 16.2 %copy-start = (f32[32,4,512]{2,1,0:T(4,128)S(1)}, f32[32,4,512]{2,1,0:T(4,128)}, u32[]{:S(2)}) copy-start(f32[32,4,512]{2,1,0:T(4,128)} %get-tuple-element.352) | copy-start | bytes 786436 | tf_op jit(solution)/shard_map/while
  263.1 0.7 copy-start.3
  263.5 0.7 copy-start.1
  285.1 15.8 %copy-start.2 = (f32[32,4,512]{2,1,0:T(4,128)S(1)}, f32[32,4,512]{2,1,0:T(4,128)}, u32[]{:S(2)}) copy-start(f32[32,4,512]{2,1,0:T(4,128)} %get-tuple-element.353) | copy-start | bytes 786436 | tf_op jit(solution)/shard_map/while
  285.2 16.2 %copy-start = (f32[32,4,512]{2,1,0:T(4,128)S(1)}, f32[32,4,512]{2,1,0:T(4,128)}, u32[]{:S(2)}) copy-start(f32[32,4,512]{2,1,0:T(4,128)} %get-tuple-element.352) | copy-start | bytes 786436 | tf_op jit(solution)/shard_map/while
  301.3 0.7 copy-start.3
  301.7 0.7 copy-start.1
  323.4 15.8 %copy-start.2 = (f32[32,4,512]{2,1,0:T(4,128)S(1)}, f32[32,4,512]{2,1,0:T(4,128)}, u32[]{:S(2)}) copy-start(f32[32,4,512]{2,1,0:T(4,128)} %get-tuple-element.353) | copy-start | bytes 786436 | tf_op jit(solution)/shard_map/while
  323.4 16.2 %copy-start = (f32[32,4,512]{2,1,0:T(4,128)S(1)}, f32[32,4,512]{2,1,0:T(4,128)}, u32[]{:S(2)}) copy-start(f32[32,4,512]{2,1,0:T(4,128)} %get-tuple-element.352) | copy-start | bytes 786436 | tf_op jit(solution)/shard_map/while
  339.6 0.7 copy-start.3
  339.9 0.7 copy-start.1
  361.6 15.8 %copy-start.2 = (f32[32,4,512]{2,1,0:T(4,128)S(1)}, f32[32,4,512]{2,1,0:T(4,128)}, u32[]{:S(2)}) copy-start(f32[32,4,512]{2,1,0:T(4,128)} %get-tuple-element.353) | copy-start | bytes 786436 | tf_op jit(solution)/shard_map/while
  361.6 16.2 %copy-start = (f32[32,4,512]{2,1,0:T(4,128)S(1)}, f32[32,4,512]{2,1,0:T(4,128)}, u32[]{:S(2)}) copy-start(f32[32,4,512]{2,1,0:T(4,128)} %get-tuple-element.352) | copy-start | bytes 786436 | tf_op jit(solution)/shard_map/while
  377.8 0.7 copy-start.3
  378.1 0.7 copy-start.1
  399.8 15.8 %copy-start.2 = (f32[32,4,512]{2,1,0:T(4,128)S(1)}, f32[32,4,512]{2,1,0:T(4,128)}, u32[]{:S(2)}) copy-start(f32[32,4,512]{2,1,0:T(4,128)} %get-tuple-element.353) | copy-start | bytes 786436 | tf_op jit(solution)/shard_map/while
  399.8 16.2 %copy-start = (f32[32,4,512]{2,1,0:T(4,128)S(1)}, f32[32,4,512]{2,1,0:T(4,128)}, u32[]{:S(2)}) copy-start(f32[32,4,512]{2,1,0:T(4,128)} %get-tuple-element.352) | copy-start | bytes 786436 | tf_op jit(solution)/shard_map/while
  416.0 0.7 copy-start.3
  416.3 0.7 copy-start.1
  438.0 15.8 %copy-start.2 = (f32[32,4,512]{2,1,0:T(4,128)S(1)}, f32[32,4,512]{2,1,0:T(4,128)}, u32[]{:S(2)}) copy-start(f32[32,4,512]{2,1,0:T(4,128)} %get-tuple-element.353) | copy-start | bytes 786436 | tf_op jit(solution)/shard_map/while
  438.0 16.2 %copy-start = (f32[32,4,512]{2,1,0:T(4,128)S(1)}, f32[32,4,512]{2,1,0:T(4,128)}, u32[]{:S(2)}) copy-start(f32[32,4,512]{2,1,0:T(4,128)} %get-tuple-element.352) | copy-start | bytes 786436 | tf_op jit(solution)/shard_map/while
  454.2 0.7 copy-start.3
  454.5 0.7 copy-start.1
  476.2 15.8 %copy-start.2 = (f32[32,4,512]{2,1,0:T(4,128)S(1)}, f32[32,4,512]{2,1,0:T(4,128)}, u32[]{:S(2)}) copy-start(f32[32,4,512]{2,1,0:T(4,128)} %get-tuple-element.353) | copy-start | bytes 786436 | tf_op jit(solution)/shard_map/while
  476.2 16.2 %copy-start = (f32[32,4,512]{2,1,0:T(4,128)S(1)}, f32[32,4,512]{2,1,0:T(4,128)}, u32[]{:S(2)}) copy-start(f32[32,4,512]{2,1,0:T(4,128)} %get-tuple-element.352) | copy-start | bytes 786436 | tf_op jit(solution)/shard_map/while
  495.4 165.5 %collective-permute-start.2 = (f32[4,64,8]{0,2,1:T(8,128)S(1)}, f32[4,64,8]{0,2,1:T(8,128)S(1)}, u32[]{:S(2)}, u32[]{:S(2)}) collective-permute-start(f32[4,64,8]{0,2,1:T(8,128)S(1)} %bitcast.49), channel_id=1, source_target_pairs={{0,16},{16,32},{32,48},{48,64},{64,80},{80,96},{96,112},{1,17},{17... | collective-permute-start | bytes 24584 | tf_op jit(solution)/shard_map/ppermute | solution.py:29
  651.1 9.8 %collective-permute-start.3 = (f32[4,64,8]{0,2,1:T(8,128)S(1)}, f32[4,64,8]{0,2,1:T(8,128)S(1)}, u32[]{:S(2)}, u32[]{:S(2)}) collective-permute-start(f32[4,64,8]{0,2,1:T(8,128)S(1)} %bitcast.50), channel_id=1, source_target_pairs={{16,0},{32,16},{48,32},{64,48},{80,64},{96,80},{112,96},{17,1},{33... | collective-permute-start | bytes 24584 | tf_op jit(solution)/shard_map/ppermute | solution.py:31
  661.0 10.7 %collective-permute-start.4 = (f32[136,4,8]{0,2,1:T(8,128)S(1)}, f32[136,4,8]{0,2,1:T(8,128)S(1)}, u32[]{:S(2)}, u32[]{:S(2)}) collective-permute-start(f32[136,4,8]{0,2,1:T(8,128)S(1)} %get-tuple-element.226), channel_id=1, source_target_pairs={{0,1},{1,2},{2,3},{3,4},{4,5},{5,6},{6,7},{7,8},{8,9},{9,10},{10,1... | collective-permute-start | bytes 52232 | tf_op jit(solution)/shard_map/ppermute | solution.py:29
  668.5 6.1 collective-permute-start.5
  693.4 13.5 %collective-permute-start.6 = (f32[4,64,8]{0,2,1:T(8,128)S(1)}, f32[4,64,8]{0,2,1:T(8,128)S(1)}, u32[]{:S(2)}, u32[]{:S(2)}) collective-permute-start(f32[4,64,8]{0,2,1:T(8,128)S(1)} %get-tuple-element.230), channel_id=1, source_target_pairs={{0,16},{16,32},{32,48},{48,64},{64,80},{80,96},{96,112},{1,17},{17... | collective-permute-start | bytes 24584 | tf_op jit(solution)/shard_map/ppermute | solution.py:29
  696.5 12.4 %collective-permute-start.7 = (f32[4,64,8]{0,2,1:T(8,128)S(1)}, f32[4,64,8]{0,2,1:T(8,128)S(1)}, u32[]{:S(2)}, u32[]{:S(2)}) collective-permute-start(f32[4,64,8]{0,2,1:T(8,128)S(1)} %get-tuple-element.231), channel_id=1, source_target_pairs={{16,0},{32,16},{48,32},{64,48},{80,64},{96,80},{112,96},{17,1},{33... | collective-permute-start | bytes 24584 | tf_op jit(solution)/shard_map/ppermute | solution.py:31
  709.1 8.9 %collective-permute-start.8 = (f32[136,4,8]{0,2,1:T(8,128)S(1)}, f32[136,4,8]{0,2,1:T(8,128)S(1)}, u32[]{:S(2)}, u32[]{:S(2)}) collective-permute-start(f32[136,4,8]{0,2,1:T(8,128)S(1)} %get-tuple-element.224), channel_id=1, source_target_pairs={{0,1},{1,2},{2,3},{3,4},{4,5},{5,6},{6,7},{7,8},{8,9},{9,10},{10,1... | collective-permute-start | bytes 52232 | tf_op jit(solution)/shard_map/ppermute | solution.py:29
  714.5 6.1 collective-permute-start.9
  739.6 9.9 %collective-permute-start.10 = (f32[4,64,8]{0,2,1:T(8,128)S(1)}, f32[4,64,8]{0,2,1:T(8,128)S(1)}, u32[]{:S(2)}, u32[]{:S(2)}) collective-permute-start(f32[4,64,8]{0,2,1:T(8,128)S(1)} %get-tuple-element.228), channel_id=1, source_target_pairs={{0,16},{16,32},{32,48},{48,64},{64,80},{80,96},{96,112},{1,17},{17... | collective-permute-start | bytes 24584 | tf_op jit(solution)/shard_map/ppermute | solution.py:29
  741.6 13.5 %collective-permute-start.11 = (f32[4,64,8]{0,2,1:T(8,128)S(1)}, f32[4,64,8]{0,2,1:T(8,128)S(1)}, u32[]{:S(2)}, u32[]{:S(2)}) collective-permute-start(f32[4,64,8]{0,2,1:T(8,128)S(1)} %get-tuple-element.229), channel_id=1, source_target_pairs={{16,0},{32,16},{48,32},{64,48},{80,64},{96,80},{112,96},{17,1},{33... | collective-permute-start | bytes 24584 | tf_op jit(solution)/shard_map/ppermute | solution.py:31
  755.3 8.8 %collective-permute-start.12 = (f32[136,4,8]{0,2,1:T(8,128)S(1)}, f32[136,4,8]{0,2,1:T(8,128)S(1)}, u32[]{:S(2)}, u32[]{:S(2)}) collective-permute-start(f32[136,4,8]{0,2,1:T(8,128)S(1)} %get-tuple-element.222), channel_id=1, source_target_pairs={{0,1},{1,2},{2,3},{3,4},{4,5},{5,6},{6,7},{7,8},{8,9},{9,10},{10,1... | collective-permute-start | bytes 52232 | tf_op jit(solution)/shard_map/ppermute | solution.py:29
  760.7 6.1 collective-permute-start.13
  (2 other events, 1.4 us)
where the time goes:
time: 795 us; the launch traced here: 786 us
  local copies, waits for them, and re-layouts  284 us (36%)
  other arithmetic  260 us (33%)
  starting transfers between devices  205 us (26%)
  waiting for transfers between devices  24.9 us (3%)
  loops' own time  9.78 us (1%)
    gather x24, local copies, waits for them, and re-layouts, absorb(): jnp.take(source, row_ids, axis=0).reshape(blocks, 4, columns_dev, CH)  239 us
    reduce_sum x12, other arithmetic, absorb(): cost_sum = jnp.sum(differences * differences, axis=-1)  188 us
    ppermute x7, starting transfers between devices, with_halo(): lax.ppermute(tail, axis, [(i, (i + 1) % count) for i in range(ends)])  183 us
    ppermute x7, starting transfers between devices, with_halo(): lax.ppermute(head, axis, [((i + 1) % count, i) for i in range(ends)])  21.8 us
    add x3, other arithmetic, smooth_inner(): along_y + weights[RMAX + offset] * padded[margin + offset:margin + offset...  19 us
    ppermute x7, waiting for transfers between devices, with_halo(): lax.ppermute(head, axis, [((i + 1) % count, i) for i in range(ends)])  18.3 us
    add x3, other arithmetic, smooth_inner(): along_z + weights[RMAX + offset] * along_y[:, margin + offset:margin + of...  17.5 us
    reshape x1, local copies, waits for them, and re-layouts, per_device(): fixed_rows = fixed_features.reshape(blocks, 4, columns_dev, CH)  16.7 us
  transfers between devices with their start and end apart: 14, of which 8 were waited for; matrix products, arithmetic and copies ran while one was open for 4% of the time, Pallas kernels for 0%

commit v1 on v0

--- a/solution.py
+++ b/solution.py
@@ -1,6 +1,8 @@
 import jax
 import jax.numpy as jnp
 from jax import lax
+from jax.experimental import pallas as pl
+from jax.experimental.pallas import tpu as pltpu
 from jax.sharding import PartitionSpec as P
 
 CH = 16
@@ -8,6 +10,7 @@
 REACH = 32
 RMAX = 4
 ITERS = 3
+NOFF = 2 * (REACH // 4) + 1
 
 
 softmin_temp = 2.0
@@ -77,53 +80,73 @@
     return (field, first_moment, second_moment)
 
 
+def softmin_kernel(total_y, f_ref, m0_ref, m4_ref, n_ref, o_ref):
+    height = f_ref.shape[1]
+    lanes_total = f_ref.shape[2]
+
+    def body(t, carry):
+        r0 = pl.multiple_of(t * 8, 8)
+        for j in range(lanes_total // 128):
+            lanes = pl.ds(128 * j, 128)
+            fixed = [f_ref[c, pl.ds(r0, 8), lanes] for c in range(CH)]
+            scores = []
+            counts = []
+            for o in range(NOFF):
+                shift = 4 * o
+                if shift % 8 == 0:
+                    src, base = m0_ref, shift
+                else:
+                    src, base = m4_ref, shift - 4
+                acc = None
+                for c in range(CH):
+                    d = fixed[c] - src[c, pl.ds(r0 + base, 8), lanes]
+                    acc = d * d if acc is None else acc + d * d
+                n_o = n_ref[o, pl.ds(r0, 8), :]
+                counts.append(n_o)
+                scores.append(jnp.where(n_o > 0.0, -acc / softmin_temp, -jnp.inf))
+            peak = scores[0]
+            for s in scores[1:]:
+                peak = jnp.maximum(peak, s)
+            den = None
+            num = None
+            for o in range(NOFF):
+                w = counts[o] * jnp.exp(scores[o] - peak)
+                shift_norm = 2.0 * float(4 * o - REACH) / total_y
+                den = w if den is None else den + w
+                num = w * shift_norm if num is None else num + w * shift_norm
+            o_ref[pl.ds(r0, 8), lanes] = num / den
+        return carry
+
+    lax.fori_loop(0, height // 8, body, 0)
+
+
 def per_device(fixed_features, moving_features, cand_offsets, cand_lengths, smooth_radii):
     height = fixed_features.shape[0]
     columns_dev = fixed_features.shape[1] // CH
     blocks = height // 4
     total_y = height * lax.axis_size("gy")
-    block_ids = lax.axis_index("gy") * blocks + jnp.arange(blocks, dtype=jnp.int32)
     shifts = cand_offsets[:, 0, :]
-    targets = 4 * block_ids[:, None] + shifts
     counts = cand_lengths[:, 0]
-    quad_rows = jnp.arange(4, dtype=jnp.int32)
-    fixed_rows = fixed_features.reshape(blocks, 4, columns_dev, CH)
-    longest = jnp.max(counts)
-    start_state = (
-        jnp.full((blocks, 4, columns_dev), -1e30, jnp.float32),
-        jnp.zeros((blocks, 4, columns_dev), jnp.float32),
-        jnp.zeros((blocks, 4, columns_dev), jnp.float32),
-    )
-    source = with_halo(moving_features, (("gy", 0),), REACH)
-    row_base = lax.axis_index("gy") * height - REACH
-    source_rows = source.shape[0]
+    live = jnp.arange(shifts.shape[1], dtype=jnp.int32)[None, :] < counts[:, None]
+    offset_values = 4 * jnp.arange(NOFF, dtype=jnp.int32) - REACH
+    hits = (shifts[:, :, None] == offset_values[None, None, :]) & live[:, :, None]
+    mult = jnp.sum(hits.astype(jnp.float32), axis=1)
+    mult_rows = jnp.repeat(mult.T, 4, axis=1)
+    mult_rows = jnp.broadcast_to(mult_rows[:, :, None], (NOFF, height, 128))
 
-    def absorb(candidate, softmin_state):
-        peak_score, total_weight, weighted = softmin_state
-        wanted = lax.dynamic_index_in_dim(targets, candidate, 1, keepdims=False)
-        live = candidate < counts
-        local_rows = jnp.clip(wanted - row_base, 0, source_rows - 4)
-        row_ids = (local_rows[:, None] + quad_rows).reshape(-1)
-        moved_rows = jnp.take(source, row_ids, axis=0).reshape(blocks, 4, columns_dev, CH)
-        differences = fixed_rows.astype(jnp.float32) - moved_rows.astype(jnp.float32)
-        cost_sum = jnp.sum(differences * differences, axis=-1)
-        scores = -cost_sum / softmin_temp
-        live_mask = live[:, None, None]
-        new_peak = jnp.where(live_mask, jnp.maximum(peak_score, scores), peak_score)
-        rescale = jnp.exp(peak_score - new_peak)
-        fresh_term = jnp.where(
-            live_mask, jnp.exp(jnp.where(live_mask, scores, new_peak) - new_peak), 0.0
-        )
-        chosen_shift = lax.dynamic_index_in_dim(shifts, candidate, 1, keepdims=False)
-        shift_norm = (2.0 * chosen_shift.astype(jnp.float32) / total_y)[:, None, None]
-        return (
-            new_peak,
-            total_weight * rescale + fresh_term,
-            weighted * rescale + fresh_term * shift_norm,
-        )
+    fixed_t = fixed_features.reshape(height, columns_dev, CH).transpose(2, 0, 1)
+    moving_t = moving_features.reshape(height, columns_dev, CH).transpose(2, 0, 1)
+    moving_h = with_halo(moving_t, (("gy", 1),), REACH).astype(jnp.float32)
+    moving_h = jnp.pad(moving_h, ((0, 0), (0, 4), (0, 0)))
+    rows = height + 2 * REACH
+    m0 = moving_h[:, :rows]
+    m4 = moving_h[:, 4 : rows + 4]
+    disp_init = pl.pallas_call(
+        lambda *refs: softmin_kernel(total_y, *refs),
+        out_shape=jax.ShapeDtypeStruct((height, columns_dev), jnp.float32),
+        compiler_params=pltpu.CompilerParams(vmem_limit_bytes=60 * 1024 * 1024),
+    )(fixed_t.astype(jnp.float32), m0, m4, mult_rows)
 
-    final_state = lax.fori_loop(0, longest, absorb, start_state)
-    disp_init = (final_state[2] / final_state[1]).reshape(height, columns_dev)
     target_field = disp_init.reshape(height, -1, XS)
     field = target_field
     first_moment = jnp.zeros_like(target_field)

time: 795 us -> 202 us (0.25)
  the two profiles are of different devices: /device:TPU:11 before, /device:TPU:112 now
where the time goes in v1:
time: 202 us; the launch traced here: 201 us
  other arithmetic  59.1 us (29%)
  starting transfers between devices  49.5 us (25%)
  waiting for transfers between devices  41.6 us (21%)
  local copies, waits for them, and re-layouts  29.1 us (14%)
  Pallas kernels  18.4 us (9%)
  between operations  2.86 us (1%)
    ppermute x7, waiting for transfers between devices, with_halo(): lax.ppermute(tail, axis, [(i, (i + 1) % count) for i in range(ends)])  35.4 us
    ppermute x7, starting transfers between devices, with_halo(): lax.ppermute(tail, axis, [(i, (i + 1) % count) for i in range(ends)])  30.7 us
    add x3, other arithmetic, smooth_inner(): along_y + weights[RMAX + offset] * padded[margin + offset:margin + offset...  18.9 us
    ppermute x7, starting transfers between devices, with_halo(): lax.ppermute(head, axis, [((i + 1) % count, i) for i in range(ends)])  18.8 us
    pallas_call x1, Pallas kernels, per_device(): pl.pallas_call(lambda *refs: softmin_kernel(total_y, *refs), out_shape=ja...  18.4 us
    add x3, other arithmetic, smooth_inner(): along_z + weights[RMAX + offset] * along_y[:, margin + offset:margin + of...  17.4 us
    sub x2, other arithmetic, adam_update(): field = field - adam_rate * first_hat / (jnp.sqrt(second_hat) + adam_floor)  12.4 us
    unnamed x11, local copies, waits for them, and re-layouts  9.64 us
  transfers between devices with their start and end apart: 14, of which 10 were waited for; matrix products, arithmetic and copies ran while one was open for 8% of the time, Pallas kernels for 0%

profile of v1, /device:TPU:112, one launch (start us, length us, event | category | flops | bytes accessed | tf_op | source)
XLA Modules:
  0.0 200.6 jit_solution(10560593891984889488)
XLA Ops:
  0.6 4.1 %copy.20 = bf16[128,8192]{0,1:T(8,128)(2,1)} copy(bf16[128,8192]{1,0:T(8,128)(2,1)} %param.6) | data formatting | bytes 4194304 | tf_op args[1]
  4.7 3.0 %copy.21 = bf16[128,512,16]{1,0,2:T(8,128)(2,1)S(1)} copy(bf16[128,512,16]{0,2,1:T(8,128)(2,1)} %bitcast.62) | data formatting | bytes 4194304 | tf_op jit(solution)/shard_map/reshape | solution.py:138
  7.7 1.1 fusion.118
  8.8 2.2 %collective-permute-start.1 = (bf16[16,32,512]{2,1,0:T(8,128)(2,1)}, bf16[16,32,512]{2,1,0:T(8,128)(2,1)S(1)}, u32[]{:S(2)}, u32[]{:S(2)}) collective-permute-start(bf16[16,32,512]{2,1,0:T(8,128)(2,1)} %get-tuple-element.11), channel_id=1, source_target_pairs={{16,0},{32,16},{48,32},{64,48},{80,64},{96,80},{112,96},{17,1},{33... | collective-permute-start | bytes 1572872 | tf_op jit(solution)/shard_map/ppermute | solution.py:34
  11.0 6.0 %collective-permute-start = (bf16[16,32,512]{2,1,0:T(8,128)(2,1)}, bf16[16,32,512]{2,1,0:T(8,128)(2,1)S(1)}, u32[]{:S(2)}, u32[]{:S(2)}) collective-permute-start(bf16[16,32,512]{2,1,0:T(8,128)(2,1)} %get-tuple-element.10), channel_id=1, source_target_pairs={{0,16},{16,32},{32,48},{48,64},{64,80},{80,96},{96,112},{1,17},{17... | collective-permute-start | bytes 1572872 | tf_op jit(solution)/shard_map/ppermute | solution.py:32
  17.0 4.1 %copy.18 = bf16[128,8192]{0,1:T(8,128)(2,1)} copy(bf16[128,8192]{1,0:T(8,128)(2,1)} %param.5) | data formatting | bytes 4194304 | tf_op args[0]
  21.1 5.0 %copy.19 = f32[128,512,16]{1,0,2:T(8,128)} copy(bf16[128,512,16]{0,2,1:T(8,128)(2,1)} %bitcast.61) | data formatting | bytes 6291456 | tf_op jit(solution)/shard_map/convert_element_type | solution.py:148
  26.1 0.1 convert_reduce_fusion
  26.4 0.6 fusion.123
  27.7 10.5 %collective-permute-done = bf16[16,32,512]{2,1,0:T(8,128)(2,1)S(1)} collective-permute-done((bf16[16,32,512]{2,1,0:T(8,128)(2,1)}, bf16[16,32,512]{2,1,0:T(8,128)(2,1)S(1)}, u32[]{:S(2)}, u32[]{:S(2)}) %collective-permute-start) | collective-permute-done | bytes 524320 | tf_op jit(solution)/shard_map/ppermute | solution.py:32
  38.2 0.8 maximum_convert_fusion.refs_1_
  39.0 3.9 %pad_slice_fusion.refs_2_ = f32[16,192,512]{2,1,0:T(8,128)} fusion(f32[16,192,512]{2,1,0:T(8,128)S(1)} %maximum_convert_fusion.refs_1_), kind=kLoop, calls=%fused_computation | loop fusion | bytes 12582912 | tf_op jit(solution)/shard_map/slice | solution.py:143
  42.9 0.7 copy-done
  43.6 1.4 broadcast_in_dim.27.refs_3_
  44.9 18.4 %shard_map.71 = f32[128,512]{1,0:T(8,128)} custom-call(f32[16,128,512]{2,1,0:T(8,128)} %bitcast.56, f32[16,192,512]{2,1,0:T(8,128)} %copy-done, f32[16,192,512]{2,1,0:T(8,128)} %pad_slice_fusion.refs_2_, f32[17,128,128]{2,1,0:T(8,128)} %broadcast_in_dim.27.refs_3_), custom_call_target="tpu_custom_call" | custom-call | tf_op jit(solution)/shard_map/pallas_call | solution.py:144
  63.4 0.7 fusion.121
  64.1 0.1 copy.29
  64.2 1.9 collective-permute-start.3
  66.2 0.1 copy.28
  66.3 6.3 %collective-permute-start.2 = (f32[4,64,8]{0,2,1:T(8,128)S(1)}, f32[4,64,8]{0,2,1:T(8,128)S(1)}, u32[]{:S(2)}, u32[]{:S(2)}) collective-permute-start(f32[4,64,8]{0,2,1:T(8,128)S(1)} %bitcast.65), channel_id=1, source_target_pairs={{0,16},{16,32},{32,48},{48,64},{64,80},{80,96},{96,112},{1,17},{17... | collective-permute-start | bytes 24584 | tf_op jit(solution)/shard_map/ppermute | solution.py:32
  72.7 0.6 fusion.113
  73.3 1.1 copy.24
  74.4 2.5 %collective-permute-done.3 = f32[4,64,8]{0,2,1:T(8,128)S(1)} collective-permute-done((f32[4,64,8]{0,2,1:T(8,128)S(1)}, f32[4,64,8]{0,2,1:T(8,128)S(1)}, u32[]{:S(2)}, u32[]{:S(2)}) %collective-permute-start.3) | collective-permute-done | bytes 8224 | tf_op jit(solution)/shard_map/ppermute | solution.py:34
  76.9 5.5 %collective-permute-done.2 = f32[4,64,8]{0,2,1:T(8,128)S(1)} collective-permute-done((f32[4,64,8]{0,2,1:T(8,128)S(1)}, f32[4,64,8]{0,2,1:T(8,128)S(1)}, u32[]{:S(2)}, u32[]{:S(2)}) %collective-permute-start.2) | collective-permute-done | bytes 8224 | tf_op jit(solution)/shard_map/ppermute | solution.py:32
  82.4 0.1 pad_maximum_fusion.11
  82.5 2.7 %collective-permute-start.5 = (f32[136,4,8]{0,2,1:T(8,128)S(1)}, f32[136,4,8]{0,2,1:T(8,128)S(1)}, u32[]{:S(2)}, u32[]{:S(2)}) collective-permute-start(f32[136,4,8]{0,2,1:T(8,128)S(1)} %get-tuple-element.17), channel_id=1, source_target_pairs={{1,0},{2,1},{3,2},{4,3},{5,4},{6,5},{7,6},{8,7},{9,8},{10,9},{11,1... | collective-permute-start | bytes 52232 | tf_op jit(solution)/shard_map/ppermute | solution.py:34
  85.2 1.9 collective-permute-start.4
  87.1 0.7 fusion.125
  88.4 2.9 %collective-permute-done.4 = f32[136,4,8]{0,2,1:T(8,128)S(1)} collective-permute-done((f32[136,4,8]{0,2,1:T(8,128)S(1)}, f32[136,4,8]{0,2,1:T(8,128)S(1)}, u32[]{:S(2)}, u32[]{:S(2)}) %collective-permute-start.4) | collective-permute-done | bytes 17440 | tf_op jit(solution)/shard_map/ppermute | solution.py:32
  91.3 0.3 pad_maximum_fusion
  91.6 6.3 %fusion.16 = f32[128,72,8]{0,2,1:T(8,128)S(1)} fusion(f32[136,72,8]{0,2,1:T(8,128)S(1)} %pad_maximum_fusion, f32[]{:T(128)} %bitcast.20, f32[]{:T(128)} %bitcast.19, f32[]{:T(128)} %bitcast.18, f32[]{:T(128)} %bitcast.17, f32[]{:T(128)} %bitcast.16, f32[]{:T(128)} %bitcast.15, f32[]{:T(128)} %bitcast.14, f32[]{:T(128)} %bitcast.13, f32[]{:T(128)} %bitcast.10), kind=kLoop, calls=%fused_computation.67 | loop fusion | flops 1253376 | bytes 2949156 | tf_op jit(solution)/shard_map/add | solution.py:55
  97.9 5.8 %fusion.104 = f32[128,64,8]{0,2,1:T(8,128)S(1)} fusion(f32[128,72,8]{0,2,1:T(8,128)S(1)} %fusion.16, f32[]{:T(128)} %bitcast.20, f32[]{:T(128)} %bitcast.19, f32[]{:T(128)} %bitcast.18, f32[]{:T(128)} %bitcast.17, f32[]{:T(128)} %bitcast.16, f32[]{:T(128)} %bitcast.15, f32[]{:T(128)} %bitcast.14, f32[]{:T(128)} %bitcast.13, f32[]{:T(128)} %bitcast.10), kind=kLoop, calls=%fused_computation.182 | loop fusion | flops 1114112 | bytes 2621476 | tf_op jit(solution)/shard_map/add | solution.py:60
  103.7 6.1 %divide_subtract_fusion.1 = (f32[128,64,8]{0,2,1:T(8,128)S(1)}, f32[128,64,8]{0,2,1:T(8,128)S(1)}) fusion(f32[128,512]{0,1:T(8,128)S(1)} %copy.24, f32[]{:T(128)} %bitcast.20, f32[]{:T(128)} %bitcast.19, f32[]{:T(128)} %bitcast.18, f32[]{:T(128)} %bitcast.17, f32[128,64,8]{0,2,1:T(8,128)S(1)} %fusion.104, f32[]{:T(128)} %bitcast.16, f32[]{:T(128)} %bitcast.15, ...), kind=kLoop, calls=%fused_computation.200 | loop fusion | flops 1835008 | bytes 1048612 | tf_op jit(solution)/shard_map/sub | solution.py:79
  109.8 0.1 fusion.120
  109.9 1.9 collective-permute-start.7
  111.9 6.3 %collective-permute-start.6 = (f32[4,64,8]{0,2,1:T(8,128)S(1)}, f32[4,64,8]{0,2,1:T(8,128)S(1)}, u32[]{:S(2)}, u32[]{:S(2)}) collective-permute-start(f32[4,64,8]{0,2,1:T(8,128)S(1)} %get-tuple-element.20), channel_id=1, source_target_pairs={{0,16},{16,32},{32,48},{48,64},{64,80},{80,96},{96,112},{1,17},{17... | collective-permute-start | bytes 24584 | tf_op jit(solution)/shard_map/ppermute | solution.py:32
  118.2 0.6 fusion.114
  118.8 1.8 collective-permute-done.7
  120.7 5.5 %collective-permute-done.6 = f32[4,64,8]{0,2,1:T(8,128)S(1)} collective-permute-done((f32[4,64,8]{0,2,1:T(8,128)S(1)}, f32[4,64,8]{0,2,1:T(8,128)S(1)}, u32[]{:S(2)}, u32[]{:S(2)}) %collective-permute-start.6) | collective-permute-done | bytes 8224 | tf_op jit(solution)/shard_map/ppermute | solution.py:32
  126.2 0.1 pad_maximum_fusion.8
  126.3 3.6 %collective-permute-start.9 = (f32[136,4,8]{0,2,1:T(8,128)S(1)}, f32[136,4,8]{0,2,1:T(8,128)S(1)}, u32[]{:S(2)}, u32[]{:S(2)}) collective-permute-start(f32[136,4,8]{0,2,1:T(8,128)S(1)} %get-tuple-element.15), channel_id=1, source_target_pairs={{1,0},{2,1},{3,2},{4,3},{5,4},{6,5},{7,6},{8,7},{9,8},{10,9},{11,1... | collective-permute-start | bytes 52232 | tf_op jit(solution)/shard_map/ppermute | solution.py:34
  129.9 1.9 collective-permute-start.8
  131.8 0.7 fusion.124
  133.1 2.9 %collective-permute-done.8 = f32[136,4,8]{0,2,1:T(8,128)S(1)} collective-permute-done((f32[136,4,8]{0,2,1:T(8,128)S(1)}, f32[136,4,8]{0,2,1:T(8,128)S(1)}, u32[]{:S(2)}, u32[]{:S(2)}) %collective-permute-start.8) | collective-permute-done | bytes 17440 | tf_op jit(solution)/shard_map/ppermute | solution.py:32
  136.0 0.3 pad_maximum_fusion.1
  136.3 6.3 %fusion.8 = f32[128,72,8]{0,2,1:T(8,128)S(1)} fusion(f32[136,72,8]{0,2,1:T(8,128)S(1)} %pad_maximum_fusion.1, f32[]{:T(128)} %bitcast.30, f32[]{:T(128)} %bitcast.29, f32[]{:T(128)} %bitcast.28, f32[]{:T(128)} %bitcast.27, f32[]{:T(128)} %bitcast.26, f32[]{:T(128)} %bitcast.25, f32[]{:T(128)} %bitcast.24, f32[]{:T(128)} %bitcast.23, f32[]{:T(128)} %bitcast.22), kind=kLoop, calls=%fused_computation.50 | loop fusion | flops 1253376 | bytes 2949156 | tf_op jit(solution)/shard_map/add | solution.py:55
  142.6 5.8 %fusion.96 = f32[128,64,8]{0,2,1:T(8,128)S(1)} fusion(f32[128,72,8]{0,2,1:T(8,128)S(1)} %fusion.8, f32[]{:T(128)} %bitcast.30, f32[]{:T(128)} %bitcast.29, f32[]{:T(128)} %bitcast.28, f32[]{:T(128)} %bitcast.27, f32[]{:T(128)} %bitcast.26, f32[]{:T(128)} %bitcast.25, f32[]{:T(128)} %bitcast.24, f32[]{:T(128)} %bitcast.23, f32[]{:T(128)} %bitcast.22), kind=kLoop, calls=%fused_computation.165 | loop fusion | flops 1114112 | bytes 2621476 | tf_op jit(solution)/shard_map/add | solution.py:60
  148.4 6.3 %divide_subtract_fusion = (f32[128,64,8]{0,2,1:T(8,128)S(1)}, f32[128,64,8]{0,2,1:T(8,128)S(1)}) fusion(f32[128,64,8]{0,2,1:T(8,128)S(1)} %get-tuple-element.9, f32[128,512]{0,1:T(8,128)S(1)} %copy.24, f32[]{:T(128)} %bitcast.30, f32[]{:T(128)} %bitcast.29, f32[]{:T(128)} %bitcast.28, f32[]{:T(128)} %bitcast.27, f32[128,64,8]{0,2,1:T(8,128)S(1)} %fusion.96, ...), kind=kLoop, calls=%fused_computation.198 | loop fusion | flops 2621440 | bytes 1310756 | tf_op jit(solution)/shard_map/sub | solution.py:79
  154.7 0.1 fusion.119
  154.8 1.9 collective-permute-start.11
  156.8 6.3 %collective-permute-start.10 = (f32[4,64,8]{0,2,1:T(8,128)S(1)}, f32[4,64,8]{0,2,1:T(8,128)S(1)}, u32[]{:S(2)}, u32[]{:S(2)}) collective-permute-start(f32[4,64,8]{0,2,1:T(8,128)S(1)} %get-tuple-element.18), channel_id=1, source_target_pairs={{0,16},{16,32},{32,48},{48,64},{64,80},{80,96},{96,112},{1,17},{17... | collective-permute-start | bytes 24584 | tf_op jit(solution)/shard_map/ppermute | solution.py:32
  163.1 0.7 fusion.115
  163.7 1.8 collective-permute-done.11
  165.6 4.6 %collective-permute-done.10 = f32[4,64,8]{0,2,1:T(8,128)S(1)} collective-permute-done((f32[4,64,8]{0,2,1:T(8,128)S(1)}, f32[4,64,8]{0,2,1:T(8,128)S(1)}, u32[]{:S(2)}, u32[]{:S(2)}) %collective-permute-start.10) | collective-permute-done | bytes 8224 | tf_op jit(solution)/shard_map/ppermute | solution.py:32
  170.2 0.1 pad_maximum_fusion.5
  170.3 4.5 %collective-permute-start.13 = (f32[136,4,8]{0,2,1:T(8,128)S(1)}, f32[136,4,8]{0,2,1:T(8,128)S(1)}, u32[]{:S(2)}, u32[]{:S(2)}) collective-permute-start(f32[136,4,8]{0,2,1:T(8,128)S(1)} %get-tuple-element.13), channel_id=1, source_target_pairs={{1,0},{2,1},{3,2},{4,3},{5,4},{6,5},{7,6},{8,7},{9,8},{10,9},{11,1... | collective-permute-start | bytes 52232 | tf_op jit(solution)/shard_map/ppermute | solution.py:34
  174.8 1.9 collective-permute-start.12
  176.8 0.7 fusion.122
  177.5 3.5 %collective-permute-done.12 = f32[136,4,8]{0,2,1:T(8,128)S(1)} collective-permute-done((f32[136,4,8]{0,2,1:T(8,128)S(1)}, f32[136,4,8]{0,2,1:T(8,128)S(1)}, u32[]{:S(2)}, u32[]{:S(2)}) %collective-permute-start.12) | collective-permute-done | bytes 17440 | tf_op jit(solution)/shard_map/ppermute | solution.py:32
  181.0 0.3 pad_maximum_fusion.2
  181.2 6.3 %fusion = f32[128,72,8]{0,2,1:T(8,128)S(1)} fusion(f32[136,72,8]{0,2,1:T(8,128)S(1)} %pad_maximum_fusion.2, f32[]{:T(128)} %bitcast.40, f32[]{:T(128)} %bitcast.39, f32[]{:T(128)} %bitcast.38, f32[]{:T(128)} %bitcast.37, f32[]{:T(128)} %bitcast.36, f32[]{:T(128)} %bitcast.35, f32[]{:T(128)} %bitcast.34, f32[]{:T(128)} %bitcast.33, f32[]{:T(128)} %bitcast.32), kind=kLoop, calls=%fused_computation.33 | loop fusion | flops 1253376 | bytes 2949156 | tf_op jit(solution)/shard_map/add | solution.py:55
  187.6 5.8 %fusion.88 = f32[128,64,8]{0,2,1:T(8,128)S(1)} fusion(f32[128,72,8]{0,2,1:T(8,128)S(1)} %fusion, f32[]{:T(128)} %bitcast.40, f32[]{:T(128)} %bitcast.39, f32[]{:T(128)} %bitcast.38, f32[]{:T(128)} %bitcast.37, f32[]{:T(128)} %bitcast.36, f32[]{:T(128)} %bitcast.35, f32[]{:T(128)} %bitcast.34, f32[]{:T(128)} %bitcast.33, f32[]{:T(128)} %bitcast.32), kind=kLoop, calls=%fused_computation.148 | loop fusion | flops 1114112 | bytes 2621476 | tf_op jit(solution)/shard_map/add | solution.py:60
  193.3 6.4 %fusion.112 = f32[128,512]{0,1:T(8,128)S(1)} fusion(f32[128,64,8]{0,2,1:T(8,128)S(1)} %fusion.88, f32[]{:T(128)} %bitcast.40, f32[]{:T(128)} %bitcast.39, f32[]{:T(128)} %bitcast.38, f32[]{:T(128)} %bitcast.37, f32[]{:T(128)} %bitcast.36, f32[]{:T(128)} %bitcast.35, f32[]{:T(128)} %bitcast.34, f32[]{:T(128)} %bitcast.33, f32[]{:T(128)} %bitcast.32, ...), kind=kLoop, calls=%fused_computation.201 | loop fusion | flops 3407872 | bytes 1310756 | tf_op jit(solution)/shard_map/reshape | solution.py:160
  199.8 0.8 copy.27
  (16 shorter events, 0.2 us)
Async XLA Ops:
  8.8 18.9 %collective-permute-start.1 = (bf16[16,32,512]{2,1,0:T(8,128)(2,1)}, bf16[16,32,512]{2,1,0:T(8,128)(2,1)S(1)}, u32[]{:S(2)}, u32[]{:S(2)}) collective-permute-start(bf16[16,32,512]{2,1,0:T(8,128)(2,1)} %get-tuple-element.11), channel_id=1, source_target_pairs={{16,0},{32,16},{48,32},{64,48},{80,64},{96,80},{112,96},{17,1},{33... | collective-permute-start | bytes 1572872 | tf_op jit(solution)/shard_map/ppermute | solution.py:34
  11.0 27.2 %collective-permute-start = (bf16[16,32,512]{2,1,0:T(8,128)(2,1)}, bf16[16,32,512]{2,1,0:T(8,128)(2,1)S(1)}, u32[]{:S(2)}, u32[]{:S(2)}) collective-permute-start(bf16[16,32,512]{2,1,0:T(8,128)(2,1)} %get-tuple-element.10), channel_id=1, source_target_pairs={{0,16},{16,32},{32,48},{48,64},{64,80},{80,96},{96,112},{1,17},{17... | collective-permute-start | bytes 1572872 | tf_op jit(solution)/shard_map/ppermute | solution.py:32
  21.1 5.0 %copy-start.3 = (s32[32,1]{0,1:T(1,128)S(1)}, s32[32,1]{0,1:T(1,128)}, u32[]{:S(2)}) copy-start(s32[32,1]{0,1:T(1,128)} %param.8) | copy-start | bytes 388
  21.1 5.0 %copy-start.1 = (s32[32,1,16]{0,2,1:T(8,128)S(1)}, s32[32,1,16]{0,2,1:T(8,128)}, u32[]{:S(2)}) copy-start(s32[32,1,16]{0,2,1:T(8,128)} %param.7) | copy-start | bytes 6148
  21.1 5.3 %copy-start.2 = (s32[3]{0:T(128)S(1)}, s32[3]{0:T(128)}, u32[]{:S(2)}) copy-start(s32[3]{0:T(128)} %param.9) | copy-start | bytes 40
  39.0 4.5 %copy-start = (f32[16,192,512]{2,1,0:T(8,128)}, f32[16,192,512]{2,1,0:T(8,128)S(1)}, u32[]{:S(2)}) copy-start(f32[16,192,512]{2,1,0:T(8,128)S(1)} %maximum_convert_fusion.refs_1_) | copy-start | bytes 18874372
  64.2 12.6 %collective-permute-start.3 = (f32[4,64,8]{0,2,1:T(8,128)S(1)}, f32[4,64,8]{0,2,1:T(8,128)S(1)}, u32[]{:S(2)}, u32[]{:S(2)}) collective-permute-start(f32[4,64,8]{0,2,1:T(8,128)S(1)} %bitcast.64), channel_id=1, source_target_pairs={{16,0},{32,16},{48,32},{64,48},{80,64},{96,80},{112,96},{17,1},{33... | collective-permute-start | bytes 24584 | tf_op jit(solution)/shard_map/ppermute | solution.py:34
  66.3 16.1 %collective-permute-start.2 = (f32[4,64,8]{0,2,1:T(8,128)S(1)}, f32[4,64,8]{0,2,1:T(8,128)S(1)}, u32[]{:S(2)}, u32[]{:S(2)}) collective-permute-start(f32[4,64,8]{0,2,1:T(8,128)S(1)} %bitcast.65), channel_id=1, source_target_pairs={{0,16},{16,32},{32,48},{48,64},{64,80},{80,96},{96,112},{1,17},{17... | collective-permute-start | bytes 24584 | tf_op jit(solution)/shard_map/ppermute | solution.py:32
  82.5 5.9 %collective-permute-start.5 = (f32[136,4,8]{0,2,1:T(8,128)S(1)}, f32[136,4,8]{0,2,1:T(8,128)S(1)}, u32[]{:S(2)}, u32[]{:S(2)}) collective-permute-start(f32[136,4,8]{0,2,1:T(8,128)S(1)} %get-tuple-element.17), channel_id=1, source_target_pairs={{1,0},{2,1},{3,2},{4,3},{5,4},{6,5},{7,6},{8,7},{9,8},{10,9},{11,1... | collective-permute-start | bytes 52232 | tf_op jit(solution)/shard_map/ppermute | solution.py:34
  85.2 6.1 %collective-permute-start.4 = (f32[136,4,8]{0,2,1:T(8,128)S(1)}, f32[136,4,8]{0,2,1:T(8,128)S(1)}, u32[]{:S(2)}, u32[]{:S(2)}) collective-permute-start(f32[136,4,8]{0,2,1:T(8,128)S(1)} %get-tuple-element.16), channel_id=1, source_target_pairs={{0,1},{1,2},{2,3},{3,4},{4,5},{5,6},{6,7},{7,8},{8,9},{9,10},{10,1... | collective-permute-start | bytes 52232 | tf_op jit(solution)/shard_map/ppermute | solution.py:32
  109.9 10.7 %collective-permute-start.7 = (f32[4,64,8]{0,2,1:T(8,128)S(1)}, f32[4,64,8]{0,2,1:T(8,128)S(1)}, u32[]{:S(2)}, u32[]{:S(2)}) collective-permute-start(f32[4,64,8]{0,2,1:T(8,128)S(1)} %get-tuple-element.21), channel_id=1, source_target_pairs={{16,0},{32,16},{48,32},{64,48},{80,64},{96,80},{112,96},{17,1},{33... | collective-permute-start | bytes 24584 | tf_op jit(solution)/shard_map/ppermute | solution.py:34
  111.9 14.3 %collective-permute-start.6 = (f32[4,64,8]{0,2,1:T(8,128)S(1)}, f32[4,64,8]{0,2,1:T(8,128)S(1)}, u32[]{:S(2)}, u32[]{:S(2)}) collective-permute-start(f32[4,64,8]{0,2,1:T(8,128)S(1)} %get-tuple-element.20), channel_id=1, source_target_pairs={{0,16},{16,32},{32,48},{48,64},{64,80},{80,96},{96,112},{1,17},{17... | collective-permute-start | bytes 24584 | tf_op jit(solution)/shard_map/ppermute | solution.py:32
  126.3 6.8 %collective-permute-start.9 = (f32[136,4,8]{0,2,1:T(8,128)S(1)}, f32[136,4,8]{0,2,1:T(8,128)S(1)}, u32[]{:S(2)}, u32[]{:S(2)}) collective-permute-start(f32[136,4,8]{0,2,1:T(8,128)S(1)} %get-tuple-element.15), channel_id=1, source_target_pairs={{1,0},{2,1},{3,2},{4,3},{5,4},{6,5},{7,6},{8,7},{9,8},{10,9},{11,1... | collective-permute-start | bytes 52232 | tf_op jit(solution)/shard_map/ppermute | solution.py:34
  129.9 6.1 %collective-permute-start.8 = (f32[136,4,8]{0,2,1:T(8,128)S(1)}, f32[136,4,8]{0,2,1:T(8,128)S(1)}, u32[]{:S(2)}, u32[]{:S(2)}) collective-permute-start(f32[136,4,8]{0,2,1:T(8,128)S(1)} %get-tuple-element.14), channel_id=1, source_target_pairs={{0,1},{1,2},{2,3},{3,4},{4,5},{5,6},{6,7},{7,8},{8,9},{9,10},{10,1... | collective-permute-start | bytes 52232 | tf_op jit(solution)/shard_map/ppermute | solution.py:32
  154.8 10.8 %collective-permute-start.11 = (f32[4,64,8]{0,2,1:T(8,128)S(1)}, f32[4,64,8]{0,2,1:T(8,128)S(1)}, u32[]{:S(2)}, u32[]{:S(2)}) collective-permute-start(f32[4,64,8]{0,2,1:T(8,128)S(1)} %get-tuple-element.19), channel_id=1, source_target_pairs={{16,0},{32,16},{48,32},{64,48},{80,64},{96,80},{112,96},{17,1},{33... | collective-permute-start | bytes 24584 | tf_op jit(solution)/shard_map/ppermute | solution.py:34
  156.8 13.4 %collective-permute-start.10 = (f32[4,64,8]{0,2,1:T(8,128)S(1)}, f32[4,64,8]{0,2,1:T(8,128)S(1)}, u32[]{:S(2)}, u32[]{:S(2)}) collective-permute-start(f32[4,64,8]{0,2,1:T(8,128)S(1)} %get-tuple-element.18), channel_id=1, source_target_pairs={{0,16},{16,32},{32,48},{48,64},{64,80},{80,96},{96,112},{1,17},{17... | collective-permute-start | bytes 24584 | tf_op jit(solution)/shard_map/ppermute | solution.py:32
  170.3 7.2 %collective-permute-start.13 = (f32[136,4,8]{0,2,1:T(8,128)S(1)}, f32[136,4,8]{0,2,1:T(8,128)S(1)}, u32[]{:S(2)}, u32[]{:S(2)}) collective-permute-start(f32[136,4,8]{0,2,1:T(8,128)S(1)} %get-tuple-element.13), channel_id=1, source_target_pairs={{1,0},{2,1},{3,2},{4,3},{5,4},{6,5},{7,6},{8,7},{9,8},{10,9},{11,1... | collective-permute-start | bytes 52232 | tf_op jit(solution)/shard_map/ppermute | solution.py:34
  174.8 6.1 %collective-permute-start.12 = (f32[136,4,8]{0,2,1:T(8,128)S(1)}, f32[136,4,8]{0,2,1:T(8,128)S(1)}, u32[]{:S(2)}, u32[]{:S(2)}) collective-permute-start(f32[136,4,8]{0,2,1:T(8,128)S(1)} %get-tuple-element.12), channel_id=1, source_target_pairs={{0,1},{1,2},{2,3},{3,4},{4,5},{5,6},{6,7},{7,8},{8,9},{9,10},{10,1... | collective-permute-start | bytes 52232 | tf_op jit(solution)/shard_map/ppermute | solution.py:32

commit v2 on v1

--- a/solution.py
+++ b/solution.py
@@ -78,6 +78,91 @@
     second_hat = second_moment / (1.0 - beta_second ** (iteration + 1))
     field = field - adam_rate * first_hat / (jnp.sqrt(second_hat) + adam_floor)
     return (field, first_moment, second_moment)
+
+
+HALO_Y = 16
+HALO_Z = 128
+
+
+def exchange_halo(cells, wy, wz):
+    ny = lax.axis_size("gy")
+    nz = lax.axis_size("gz")
+
+    def send(piece, dy, dz):
+        pairs = []
+        for a in range(ny):
+            for b in range(nz):
+                if 0 <= a + dy < ny and 0 <= b + dz < nz:
+                    pairs.append((a * nz + b, (a + dy) * nz + b + dz))
+        return lax.ppermute(piece, ("gy", "gz"), pairs)
+
+    top_rows = cells[-wy:]
+    bottom_rows = cells[:wy]
+    top = send(top_rows, 1, 0)
+    bottom = send(bottom_rows, -1, 0)
+    left = send(cells[:, -wz:], 0, 1)
+    right = send(cells[:, :wz], 0, -1)
+    top_left = send(top_rows[:, -wz:], 1, 1)
+    top_right = send(top_rows[:, :wz], 1, -1)
+    bottom_left = send(bottom_rows[:, -wz:], -1, 1)
+    bottom_right = send(bottom_rows[:, :wz], -1, -1)
+    return jnp.concatenate(
+        [
+            jnp.concatenate([top_left, top, top_right], axis=1),
+            jnp.concatenate([left, cells, right], axis=1),
+            jnp.concatenate([bottom_left, bottom, bottom_right], axis=1),
+        ],
+        axis=0,
+    )
+
+
+def shifted(a, offset, axis):
+    if offset == 0:
+        return a
+    return pltpu.roll(a, (-offset) % a.shape[axis], axis)
+
+
+def box_smooth(u, radius, lane_x):
+    scale = 1.0 / float(2 * radius + 1)
+    along_y = u
+    for o in range(1, radius + 1):
+        along_y = along_y + shifted(u, -o, 0) + shifted(u, o, 0)
+    along_y = along_y * scale
+    along_z = along_y
+    for o in range(1, radius + 1):
+        along_z = along_z + shifted(along_y, -XS * o, 1) + shifted(along_y, XS * o, 1)
+    along_z = along_z * scale
+    along_x = along_z
+    for o in range(1, radius + 1):
+        along_x = (
+            along_x
+            + jnp.where(lane_x >= o, shifted(along_z, -o, 1), 0.0)
+            + jnp.where(lane_x < XS - o, shifted(along_z, o, 1), 0.0)
+        )
+    return along_x * scale
+
+
+def adam_kernel(radii_ref, d_ref, mask_ref, o_ref):
+    target = d_ref[...]
+    inside = mask_ref[...] > 0.0
+    lane_x = lax.broadcasted_iota(jnp.int32, target.shape, 1) % XS
+    field = jnp.where(inside, target, 0.0)
+    first_moment = jnp.zeros_like(target)
+    second_moment = jnp.zeros_like(target)
+    for iteration in range(ITERS):
+        radius = radii_ref[iteration]
+        smoothed = lax.switch(
+            jnp.clip(radius - 1, 0, RMAX - 1),
+            [lambda u, r=r: box_smooth(u, r, lane_x) for r in range(1, RMAX + 1)],
+            field,
+        )
+        field, first_moment, second_moment = adam_update(
+            field, target, smoothed, first_moment, second_moment, iteration
+        )
+        field = jnp.where(inside, field, 0.0)
+    height = o_ref.shape[0]
+    width = o_ref.shape[1]
+    o_ref[...] = field[HALO_Y : HALO_Y + height, HALO_Z : HALO_Z + width]
 
 
 def softmin_kernel(total_y, f_ref, m0_ref, m4_ref, n_ref, o_ref):
@@ -147,17 +232,32 @@
         compiler_params=pltpu.CompilerParams(vmem_limit_bytes=60 * 1024 * 1024),
     )(fixed_t.astype(jnp.float32), m0, m4, mult_rows)
 
-    target_field = disp_init.reshape(height, -1, XS)
-    field = target_field
-    first_moment = jnp.zeros_like(target_field)
-    second_moment = jnp.zeros_like(target_field)
-    for iteration in range(ITERS):
-        padded = with_halo(field, (("gy", 0), ("gz", 1)), RMAX)
-        smoothed = smooth_inner(padded, smooth_radii[iteration], RMAX)
-        field, first_moment, second_moment = adam_update(
-            field, target_field, smoothed, first_moment, second_moment, iteration
-        )
-    return (disp_init, field.reshape(height, columns_dev))
+    ext = exchange_halo(disp_init, HALO_Y, HALO_Z)
+    rows_ext, lanes_ext = ext.shape
+    row_global = lax.axis_index("gy") * height - HALO_Y + lax.broadcasted_iota(
+        jnp.int32, (rows_ext, lanes_ext), 0
+    )
+    lane_global = lax.axis_index("gz") * columns_dev - HALO_Z + lax.broadcasted_iota(
+        jnp.int32, (rows_ext, lanes_ext), 1
+    )
+    inside = (
+        (row_global >= 0)
+        & (row_global < total_y)
+        & (lane_global >= 0)
+        & (lane_global < columns_dev * lax.axis_size("gz"))
+    )
+    grid_mask = inside.astype(jnp.float32)
+    final_ext = pl.pallas_call(
+        adam_kernel,
+        out_shape=jax.ShapeDtypeStruct((height, columns_dev), jnp.float32),
+        in_specs=[
+            pl.BlockSpec(memory_space=pltpu.SMEM),
+            pl.BlockSpec(memory_space=pltpu.VMEM),
+            pl.BlockSpec(memory_space=pltpu.VMEM),
+        ],
+        compiler_params=pltpu.CompilerParams(vmem_limit_bytes=32 * 1024 * 1024),
+    )(smooth_radii.astype(jnp.int32), ext, grid_mask)
+    return (disp_init, final_ext)
 
 
 def solution(mesh):

time: 202 us -> 108 us (0.53)
  the two profiles are of different devices: /device:TPU:112 before, /device:TPU:11 now
where the time goes in v2:
time: 108 us; the launch traced here: 107 us
  starting transfers between devices  35.2 us (33%)
  Pallas kernels  26.3 us (24%)
  local copies, waits for them, and re-layouts  25.7 us (24%)
  waiting for transfers between devices  16.7 us (15%)
  other arithmetic  2.11 us (2%)
    ppermute x8, starting transfers between devices, send(): return lax.ppermute(piece, ('gy', 'gz'), pairs)  28.5 us
    pallas_call x1, Pallas kernels, per_device(): pl.pallas_call(lambda *refs: softmin_kernel(total_y, *refs), out_shape=ja...  18.5 us
    ppermute x1, waiting for transfers between devices, with_halo(): lax.ppermute(head, axis, [((i + 1) % count, i) for i in range(ends)])  11.4 us
    unnamed x10, local copies, waits for them, and re-layouts  8.84 us
    pallas_call x1, Pallas kernels, per_device(): pl.pallas_call(adam_kernel, out_shape=jax.ShapeDtypeStruct((height, colum...  7.86 us
    convert_element_type x1, local copies, waits for them, and re-layouts, per_device(): fixed_t.astype(jnp.float32)  5.02 us
    ppermute x8, waiting for transfers between devices, send(): return lax.ppermute(piece, ('gy', 'gz'), pairs)  4.95 us
    slice x1, local copies, waits for them, and re-layouts, per_device(): m4 = moving_h[:, 4:rows + 4]  3.91 us
  transfers between devices with their start and end apart: 10, of which 3 were waited for; matrix products, arithmetic and copies ran while one was open for 10% of the time, Pallas kernels for 0%

profile of v2, /device:TPU:11, one launch (start us, length us, event | category | flops | bytes accessed | tf_op | source)
XLA Modules:
  0.0 106.9 jit_solution(8902531478846873194)
XLA Ops:
  0.6 4.1 %copy.16 = bf16[128,8192]{0,1:T(8,128)(2,1)} copy(bf16[128,8192]{1,0:T(8,128)(2,1)} %param.6) | data formatting | bytes 4194304 | tf_op args[1]
  4.7 3.0 %copy.17 = bf16[128,512,16]{1,0,2:T(8,128)(2,1)S(1)} copy(bf16[128,512,16]{0,2,1:T(8,128)(2,1)} %bitcast.13) | data formatting | bytes 4194304 | tf_op jit(solution)/shard_map/reshape | solution.py:223
  7.7 1.0 fusion.2
  8.8 3.9 %collective-permute-start.1 = (bf16[16,32,512]{2,1,0:T(8,128)(2,1)}, bf16[16,32,512]{2,1,0:T(8,128)(2,1)S(1)}, u32[]{:S(2)}, u32[]{:S(2)}) collective-permute-start(bf16[16,32,512]{2,1,0:T(8,128)(2,1)} %get-tuple-element.3), channel_id=1, source_target_pairs={{16,0},{32,16},{48,32},{64,48},{80,64},{96,80},{112,96},{17,1},{33... | collective-permute-start | bytes 1572872 | tf_op jit(solution)/shard_map/ppermute | solution.py:34
  12.7 2.9 %collective-permute-start = (bf16[16,32,512]{2,1,0:T(8,128)(2,1)}, bf16[16,32,512]{2,1,0:T(8,128)(2,1)S(1)}, u32[]{:S(2)}, u32[]{:S(2)}) collective-permute-start(bf16[16,32,512]{2,1,0:T(8,128)(2,1)} %get-tuple-element.2), channel_id=1, source_target_pairs={{0,16},{16,32},{32,48},{48,64},{64,80},{80,96},{96,112},{1,17},{17... | collective-permute-start | bytes 1572872 | tf_op jit(solution)/shard_map/ppermute | solution.py:32
  15.6 4.1 %copy.14 = bf16[128,8192]{0,1:T(8,128)(2,1)} copy(bf16[128,8192]{1,0:T(8,128)(2,1)} %param.5) | data formatting | bytes 4194304 | tf_op args[0]
  19.7 0.0 copy-start.3
  19.7 0.0 copy-start.2
  19.7 5.0 %copy.15 = f32[128,512,16]{1,0,2:T(8,128)} copy(bf16[128,512,16]{0,2,1:T(8,128)(2,1)} %bitcast.12) | data formatting | bytes 6291456 | tf_op jit(solution)/shard_map/convert_element_type | solution.py:233
  24.7 0.0 copy-done.3
  24.7 0.0 copy-done.2
  24.7 0.1 convert_reduce_fusion
  24.8 0.1 copy.18
  24.9 0.1 copy.19
  25.0 11.4 %collective-permute-done.1 = bf16[16,32,512]{2,1,0:T(8,128)(2,1)S(1)} collective-permute-done((bf16[16,32,512]{2,1,0:T(8,128)(2,1)}, bf16[16,32,512]{2,1,0:T(8,128)(2,1)S(1)}, u32[]{:S(2)}, u32[]{:S(2)}) %collective-permute-start.1) | collective-permute-done | bytes 524320 | tf_op jit(solution)/shard_map/ppermute | solution.py:34
  36.4 0.4 collective-permute-done
  36.8 0.8 maximum_convert_fusion.refs_1_
  37.6 0.0 copy-start.1
  37.6 3.9 %pad_slice_fusion.refs_2_ = f32[16,192,512]{2,1,0:T(8,128)} fusion(f32[16,192,512]{2,1,0:T(8,128)S(1)} %maximum_convert_fusion.refs_1_), kind=kLoop, calls=%fused_computation | loop fusion | bytes 12582912 | tf_op jit(solution)/shard_map/slice | solution.py:228
  41.5 0.6 copy-done.1
  42.2 1.4 %broadcast_in_dim.15.refs_3_ = f32[17,128,128]{2,1,0:T(8,128)} broadcast(f32[17,128]{1,0:T(8,128)S(1)} %copy.19), dimensions={0,1} | broadcast | bytes 1122816 | tf_op jit(solution)/shard_map/broadcast_in_dim | solution.py:220
  43.5 0.0 copy-start
  43.5 18.5 %shard_map.71 = f32[128,512]{1,0:T(8,128)} custom-call(f32[16,128,512]{2,1,0:T(8,128)} %bitcast.9, f32[16,192,512]{2,1,0:T(8,128)} %copy-done.1, f32[16,192,512]{2,1,0:T(8,128)} %pad_slice_fusion.refs_2_, f32[17,128,128]{2,1,0:T(8,128)} %broadcast_in_dim.15.refs_3_), custom_call_target="tpu_custom_call" | custom-call | tf_op jit(solution)/shard_map/pallas_call | solution.py:229
  62.0 0.7 fusion.3
  62.7 0.9 fusion.5
  63.6 5.9 %collective-permute-start.9 = (f32[16,128]{1,0:T(8,128)S(1)}, f32[16,128]{1,0:T(8,128)S(1)}, u32[]{:S(2)}, u32[]{:S(2)}) collective-permute-start(f32[16,128]{1,0:T(8,128)S(1)} %get-tuple-element.5), channel_id=1, source_target_pairs={{17,0},{18,1},{19,2},{20,3},{21,4},{22,5},{23,6},{24,7},{25,8},{26... | collective-permute-start | bytes 24584 | tf_op jit(solution)/shard_map/ppermute | solution.py:97
  69.5 2.6 %collective-permute-start.7 = (f32[16,128]{1,0:T(8,128)S(1)}, f32[16,128]{1,0:T(8,128)S(1)}, u32[]{:S(2)}, u32[]{:S(2)}) collective-permute-start(f32[16,128]{1,0:T(8,128)S(1)} %get-tuple-element.6), channel_id=1, source_target_pairs={{16,1},{17,2},{18,3},{19,4},{20,5},{21,6},{22,7},{23,8},{24,9},{25... | collective-permute-start | bytes 24584 | tf_op jit(solution)/shard_map/ppermute | solution.py:97
  72.1 4.5 %collective-permute-start.4 = (f32[16,128]{1,0:T(8,128)S(1)}, f32[16,128]{1,0:T(8,128)S(1)}, u32[]{:S(2)}, u32[]{:S(2)}) collective-permute-start(f32[16,128]{1,0:T(8,128)S(1)} %get-tuple-element.7), channel_id=1, source_target_pairs={{1,16},{2,17},{3,18},{4,19},{5,20},{6,21},{7,22},{8,23},{9,24},{10... | collective-permute-start | bytes 24584 | tf_op jit(solution)/shard_map/ppermute | solution.py:97
  76.6 0.8 fusion.4
  77.4 2.4 %collective-permute-start.8 = (f32[16,512]{1,0:T(8,128)S(1)}, f32[16,512]{1,0:T(8,128)S(1)}, u32[]{:S(2)}, u32[]{:S(2)}) collective-permute-start(f32[16,512]{1,0:T(8,128)S(1)} %get-tuple-element.9), channel_id=1, source_target_pairs={{16,0},{17,1},{18,2},{19,3},{20,4},{21,5},{22,6},{23,7},{24,8},{25... | collective-permute-start | bytes 98312 | tf_op jit(solution)/shard_map/ppermute | solution.py:97
  79.8 2.6 %collective-permute-start.6 = (f32[128,128]{1,0:T(8,128)S(1)}, f32[128,128]{1,0:T(8,128)S(1)}, u32[]{:S(2)}, u32[]{:S(2)}) collective-permute-start(f32[128,128]{1,0:T(8,128)S(1)} %get-tuple-element.11), channel_id=1, source_target_pairs={{1,0},{2,1},{3,2},{4,3},{5,4},{6,5},{7,6},{8,7},{9,8},{10,9},{11,1... | collective-permute-start | bytes 196616 | tf_op jit(solution)/shard_map/ppermute | solution.py:97
  82.4 0.0 collective-permute-done.9
  82.4 3.9 %collective-permute-start.5 = (f32[128,128]{1,0:T(8,128)S(1)}, f32[128,128]{1,0:T(8,128)S(1)}, u32[]{:S(2)}, u32[]{:S(2)}) collective-permute-start(f32[128,128]{1,0:T(8,128)S(1)} %get-tuple-element.10), channel_id=1, source_target_pairs={{0,1},{1,2},{2,3},{3,4},{4,5},{5,6},{6,7},{7,8},{8,9},{9,10},{10,1... | collective-permute-start | bytes 196616 | tf_op jit(solution)/shard_map/ppermute | solution.py:97
  86.3 0.0 collective-permute-done.7
  86.3 4.3 %collective-permute-start.3 = (f32[16,512]{1,0:T(8,128)S(1)}, f32[16,512]{1,0:T(8,128)S(1)}, u32[]{:S(2)}, u32[]{:S(2)}) collective-permute-start(f32[16,512]{1,0:T(8,128)S(1)} %get-tuple-element.8), channel_id=1, source_target_pairs={{0,16},{1,17},{2,18},{3,19},{4,20},{5,21},{6,22},{7,23},{8,24},{9,... | collective-permute-start | bytes 98312 | tf_op jit(solution)/shard_map/ppermute | solution.py:97
  90.7 0.0 collective-permute-done.4
  90.7 2.3 %collective-permute-start.2 = (f32[16,128]{1,0:T(8,128)S(1)}, f32[16,128]{1,0:T(8,128)S(1)}, u32[]{:S(2)}, u32[]{:S(2)}) collective-permute-start(f32[16,128]{1,0:T(8,128)S(1)} %get-tuple-element.4), channel_id=1, source_target_pairs={{0,17},{1,18},{2,19},{3,20},{4,21},{5,22},{6,23},{7,24},{8,25},{9,... | collective-permute-start | bytes 24584 | tf_op jit(solution)/shard_map/ppermute | solution.py:97
  93.0 0.1 and_convert_fusion.mask_ref
  93.1 4.9 %collective-permute-done.2 = f32[16,128]{1,0:T(8,128)S(1)} collective-permute-done((f32[16,128]{1,0:T(8,128)S(1)}, f32[16,128]{1,0:T(8,128)S(1)}, u32[]{:S(2)}, u32[]{:S(2)}) %collective-permute-start.2) | collective-permute-done | bytes 8224 | tf_op jit(solution)/shard_map/ppermute | solution.py:97
  98.0 0.0 collective-permute-done.8
  98.0 0.0 collective-permute-done.3
  98.0 0.0 collective-permute-done.6
  98.0 0.0 collective-permute-done.5
  98.1 1.0 maximum_maximum_fusion.d_ref
  99.1 0.0 copy-done
  99.1 7.9 %shard_map.72 = f32[128,512]{1,0:T(8,128)} custom-call(s32[3]{0:T(128)S(1)} %copy-done, f32[160,768]{1,0:T(8,128)S(1)} %maximum_maximum_fusion.d_ref, f32[160,768]{1,0:T(8,128)S(1)} %and_convert_fusion.mask_ref), custom_call_target="tpu_custom_call" | custom-call | tf_op jit(solution)/shard_map/pallas_call | solution.py:250
  (5 shorter events, 0.0 us)
Async XLA Ops:
  8.8 27.6 %collective-permute-start.1 = (bf16[16,32,512]{2,1,0:T(8,128)(2,1)}, bf16[16,32,512]{2,1,0:T(8,128)(2,1)S(1)}, u32[]{:S(2)}, u32[]{:S(2)}) collective-permute-start(bf16[16,32,512]{2,1,0:T(8,128)(2,1)} %get-tuple-element.3), channel_id=1, source_target_pairs={{16,0},{32,16},{48,32},{64,48},{80,64},{96,80},{112,96},{17,1},{33... | collective-permute-start | bytes 1572872 | tf_op jit(solution)/shard_map/ppermute | solution.py:34
  12.7 24.1 %collective-permute-start = (bf16[16,32,512]{2,1,0:T(8,128)(2,1)}, bf16[16,32,512]{2,1,0:T(8,128)(2,1)S(1)}, u32[]{:S(2)}, u32[]{:S(2)}) collective-permute-start(bf16[16,32,512]{2,1,0:T(8,128)(2,1)} %get-tuple-element.2), channel_id=1, source_target_pairs={{0,16},{16,32},{32,48},{48,64},{64,80},{80,96},{96,112},{1,17},{17... | collective-permute-start | bytes 1572872 | tf_op jit(solution)/shard_map/ppermute | solution.py:32
  19.7 5.0 %copy-start.3 = (s32[32,1]{0,1:T(1,128)S(1)}, s32[32,1]{0,1:T(1,128)}, u32[]{:S(2)}) copy-start(s32[32,1]{0,1:T(1,128)} %param.8) | copy-start | bytes 388
  19.7 5.0 %copy-start.2 = (s32[32,1,16]{0,2,1:T(8,128)S(1)}, s32[32,1,16]{0,2,1:T(8,128)}, u32[]{:S(2)}) copy-start(s32[32,1,16]{0,2,1:T(8,128)} %param.7) | copy-start | bytes 6148
  37.6 4.5 %copy-start.1 = (f32[16,192,512]{2,1,0:T(8,128)}, f32[16,192,512]{2,1,0:T(8,128)S(1)}, u32[]{:S(2)}) copy-start(f32[16,192,512]{2,1,0:T(8,128)S(1)} %maximum_convert_fusion.refs_1_) | copy-start | bytes 18874372
  43.5 55.5 %copy-start = (s32[3]{0:T(128)S(1)}, s32[3]{0:T(128)}, u32[]{:S(2)}) copy-start(s32[3]{0:T(128)} %radii_ref.1) | copy-start | bytes 40
  63.6 18.7 %collective-permute-start.9 = (f32[16,128]{1,0:T(8,128)S(1)}, f32[16,128]{1,0:T(8,128)S(1)}, u32[]{:S(2)}, u32[]{:S(2)}) collective-permute-start(f32[16,128]{1,0:T(8,128)S(1)} %get-tuple-element.5), channel_id=1, source_target_pairs={{17,0},{18,1},{19,2},{20,3},{21,4},{22,5},{23,6},{24,7},{25,8},{26... | collective-permute-start | bytes 24584 | tf_op jit(solution)/shard_map/ppermute | solution.py:97
  69.5 16.8 %collective-permute-start.7 = (f32[16,128]{1,0:T(8,128)S(1)}, f32[16,128]{1,0:T(8,128)S(1)}, u32[]{:S(2)}, u32[]{:S(2)}) collective-permute-start(f32[16,128]{1,0:T(8,128)S(1)} %get-tuple-element.6), channel_id=1, source_target_pairs={{16,1},{17,2},{18,3},{19,4},{20,5},{21,6},{22,7},{23,8},{24,9},{25... | collective-permute-start | bytes 24584 | tf_op jit(solution)/shard_map/ppermute | solution.py:97
  72.1 18.6 %collective-permute-start.4 = (f32[16,128]{1,0:T(8,128)S(1)}, f32[16,128]{1,0:T(8,128)S(1)}, u32[]{:S(2)}, u32[]{:S(2)}) collective-permute-start(f32[16,128]{1,0:T(8,128)S(1)} %get-tuple-element.7), channel_id=1, source_target_pairs={{1,16},{2,17},{3,18},{4,19},{5,20},{6,21},{7,22},{8,23},{9,24},{10... | collective-permute-start | bytes 24584 | tf_op jit(solution)/shard_map/ppermute | solution.py:97
  77.4 20.7 %collective-permute-start.8 = (f32[16,512]{1,0:T(8,128)S(1)}, f32[16,512]{1,0:T(8,128)S(1)}, u32[]{:S(2)}, u32[]{:S(2)}) collective-permute-start(f32[16,512]{1,0:T(8,128)S(1)} %get-tuple-element.9), channel_id=1, source_target_pairs={{16,0},{17,1},{18,2},{19,3},{20,4},{21,5},{22,6},{23,7},{24,8},{25... | collective-permute-start | bytes 98312 | tf_op jit(solution)/shard_map/ppermute | solution.py:97
  79.8 18.2 %collective-permute-start.6 = (f32[128,128]{1,0:T(8,128)S(1)}, f32[128,128]{1,0:T(8,128)S(1)}, u32[]{:S(2)}, u32[]{:S(2)}) collective-permute-start(f32[128,128]{1,0:T(8,128)S(1)} %get-tuple-element.11), channel_id=1, source_target_pairs={{1,0},{2,1},{3,2},{4,3},{5,4},{6,5},{7,6},{8,7},{9,8},{10,9},{11,1... | collective-permute-start | bytes 196616 | tf_op jit(solution)/shard_map/ppermute | solution.py:97
  82.4 15.7 %collective-permute-start.5 = (f32[128,128]{1,0:T(8,128)S(1)}, f32[128,128]{1,0:T(8,128)S(1)}, u32[]{:S(2)}, u32[]{:S(2)}) collective-permute-start(f32[128,128]{1,0:T(8,128)S(1)} %get-tuple-element.10), channel_id=1, source_target_pairs={{0,1},{1,2},{2,3},{3,4},{4,5},{5,6},{6,7},{7,8},{8,9},{9,10},{10,1... | collective-permute-start | bytes 196616 | tf_op jit(solution)/shard_map/ppermute | solution.py:97
  86.3 11.7 %collective-permute-start.3 = (f32[16,512]{1,0:T(8,128)S(1)}, f32[16,512]{1,0:T(8,128)S(1)}, u32[]{:S(2)}, u32[]{:S(2)}) collective-permute-start(f32[16,512]{1,0:T(8,128)S(1)} %get-tuple-element.8), channel_id=1, source_target_pairs={{0,16},{1,17},{2,18},{3,19},{4,20},{5,21},{6,22},{7,23},{8,24},{9,... | collective-permute-start | bytes 98312 | tf_op jit(solution)/shard_map/ppermute | solution.py:97
  90.7 7.4 %collective-permute-start.2 = (f32[16,128]{1,0:T(8,128)S(1)}, f32[16,128]{1,0:T(8,128)S(1)}, u32[]{:S(2)}, u32[]{:S(2)}) collective-permute-start(f32[16,128]{1,0:T(8,128)S(1)} %get-tuple-element.4), channel_id=1, source_target_pairs={{0,17},{1,18},{2,19},{3,20},{4,21},{5,22},{6,23},{7,24},{8,25},{9,... | collective-permute-start | bytes 24584 | tf_op jit(solution)/shard_map/ppermute | solution.py:97

commit v3 on v2

--- a/solution.py
+++ b/solution.py
@@ -82,38 +82,20 @@
 
 HALO_Y = 16
 HALO_Z = 128
-
-
-def exchange_halo(cells, wy, wz):
+SEND_Y = 8
+SEND_Z = 8 * XS
+
+
+def exchange_halo(cells, wy, wz, send_y, send_z):
     ny = lax.axis_size("gy")
     nz = lax.axis_size("gz")
-
-    def send(piece, dy, dz):
-        pairs = []
-        for a in range(ny):
-            for b in range(nz):
-                if 0 <= a + dy < ny and 0 <= b + dz < nz:
-                    pairs.append((a * nz + b, (a + dy) * nz + b + dz))
-        return lax.ppermute(piece, ("gy", "gz"), pairs)
-
-    top_rows = cells[-wy:]
-    bottom_rows = cells[:wy]
-    top = send(top_rows, 1, 0)
-    bottom = send(bottom_rows, -1, 0)
-    left = send(cells[:, -wz:], 0, 1)
-    right = send(cells[:, :wz], 0, -1)
-    top_left = send(top_rows[:, -wz:], 1, 1)
-    top_right = send(top_rows[:, :wz], 1, -1)
-    bottom_left = send(bottom_rows[:, -wz:], -1, 1)
-    bottom_right = send(bottom_rows[:, :wz], -1, -1)
-    return jnp.concatenate(
-        [
-            jnp.concatenate([top_left, top, top_right], axis=1),
-            jnp.concatenate([left, cells, right], axis=1),
-            jnp.concatenate([bottom_left, bottom, bottom_right], axis=1),
-        ],
-        axis=0,
-    )
+    top = lax.ppermute(cells[-send_y:], "gy", [(i, i + 1) for i in range(ny - 1)])
+    bottom = lax.ppermute(cells[:send_y], "gy", [(i + 1, i) for i in range(ny - 1)])
+    cells = jnp.concatenate([top, cells, bottom], axis=0)
+    left = lax.ppermute(cells[:, -send_z:], "gz", [(i, i + 1) for i in range(nz - 1)])
+    right = lax.ppermute(cells[:, :send_z], "gz", [(i + 1, i) for i in range(nz - 1)])
+    cells = jnp.concatenate([left, cells, right], axis=1)
+    return jnp.pad(cells, ((wy - send_y, wy - send_y), (wz - send_z, wz - send_z)))
 
 
 def shifted(a, offset, axis):
@@ -165,9 +147,26 @@
     o_ref[...] = field[HALO_Y : HALO_Y + height, HALO_Z : HALO_Z + width]
 
 
-def softmin_kernel(total_y, f_ref, m0_ref, m4_ref, n_ref, o_ref):
-    height = f_ref.shape[1]
-    lanes_total = f_ref.shape[2]
+def softmin_kernel(total_y, ft_ref, mt_ref, top_ref, bot_ref, n_ref, o_ref, f_ref, m0_ref, m4_ref):
+    height = ft_ref.shape[1]
+    lanes_total = ft_ref.shape[2]
+    rows = height + 2 * REACH
+
+    def build(c, carry):
+        f_ref[c] = ft_ref[c].astype(jnp.float32)
+        m0_ref[c, pl.ds(0, REACH), :] = top_ref[c].astype(jnp.float32)
+        m0_ref[c, pl.ds(REACH, height), :] = mt_ref[c].astype(jnp.float32)
+        m0_ref[c, pl.ds(REACH + height, REACH), :] = bot_ref[c].astype(jnp.float32)
+        return carry
+
+    lax.fori_loop(0, CH, build, 0)
+
+    def build_shifted(c, carry):
+        m4_ref[c, pl.ds(0, rows - 8), :] = m0_ref[c, pl.ds(4, rows - 8), :]
+        m4_ref[c, pl.ds(rows - 8, 8), :] = jnp.zeros((8, lanes_total), jnp.float32)
+        return carry
+
+    lax.fori_loop(0, CH, build_shifted, 0)
 
     def body(t, carry):
         r0 = pl.multiple_of(t * 8, 8)
@@ -219,20 +218,36 @@
     mult_rows = jnp.repeat(mult.T, 4, axis=1)
     mult_rows = jnp.broadcast_to(mult_rows[:, :, None], (NOFF, height, 128))
 
-    fixed_t = fixed_features.reshape(height, columns_dev, CH).transpose(2, 0, 1)
-    moving_t = moving_features.reshape(height, columns_dev, CH).transpose(2, 0, 1)
-    moving_h = with_halo(moving_t, (("gy", 1),), REACH).astype(jnp.float32)
-    moving_h = jnp.pad(moving_h, ((0, 0), (0, 4), (0, 0)))
+    gy_count = lax.axis_size("gy")
+    top_rows = lax.ppermute(
+        moving_features[height - REACH :], "gy", [(i, i + 1) for i in range(gy_count - 1)]
+    )
+    bottom_rows = lax.ppermute(
+        moving_features[:REACH], "gy", [(i + 1, i) for i in range(gy_count - 1)]
+    )
+
+    def channel_major(a):
+        return a.reshape(a.shape[0], columns_dev, CH).transpose(2, 0, 1)
+
     rows = height + 2 * REACH
-    m0 = moving_h[:, :rows]
-    m4 = moving_h[:, 4 : rows + 4]
     disp_init = pl.pallas_call(
         lambda *refs: softmin_kernel(total_y, *refs),
         out_shape=jax.ShapeDtypeStruct((height, columns_dev), jnp.float32),
+        scratch_shapes=[
+            pltpu.VMEM((CH, height, columns_dev), jnp.float32),
+            pltpu.VMEM((CH, rows, columns_dev), jnp.float32),
+            pltpu.VMEM((CH, rows, columns_dev), jnp.float32),
+        ],
         compiler_params=pltpu.CompilerParams(vmem_limit_bytes=60 * 1024 * 1024),
-    )(fixed_t.astype(jnp.float32), m0, m4, mult_rows)
-
-    ext = exchange_halo(disp_init, HALO_Y, HALO_Z)
+    )(
+        channel_major(fixed_features),
+        channel_major(moving_features),
+        channel_major(top_rows),
+        channel_major(bottom_rows),
+        mult_rows,
+    )
+
+    ext = exchange_halo(disp_init, HALO_Y, HALO_Z, SEND_Y, SEND_Z)
     rows_ext, lanes_ext = ext.shape
     row_global = lax.axis_index("gy") * height - HALO_Y + lax.broadcasted_iota(
         jnp.int32, (rows_ext, lanes_ext), 0

time: 108 us -> 89.7 us (0.83)
  starting transfers between devices: 35.2 us -> 24.5 us
  waiting for transfers between devices: 16.7 us -> 11.9 us
  Pallas kernels: 26.3 us -> 24.3 us
    ppermute x10 -> x6, starting transfers between devices: 35.2 us -> 24.5 us  [the longest x1 7.19 us: exchange_halo(): lax.ppermute(cells[:, -send_z:], 'gz', [(i, i + 1) for i in range(nz - 1)])]
    reshape x1 -> x4, local copies, waits for them, and re-layouts: 2.99 us -> 11.8 us  [channel_major(): return a.reshape(a.shape[0], columns_dev, CH).transpose(2, 0, 1)]
    convert_element_type x1 -> x0, local copies, waits for them, and re-layouts: 5.02 us -> none  [per_device(): fixed_t.astype(jnp.float32)]
    ppermute x10 -> x6, waiting for transfers between devices: 16.7 us -> 11.9 us  [the longest x1 4.5 us: exchange_halo(): lax.ppermute(cells[:, :send_z], 'gz', [(i + 1, i) for i in range(nz - 1)])]
    slice x5 -> x2, local copies, waits for them, and re-layouts: 7.37 us -> 2.97 us  [the longest x1 2.23 us: per_device(): moving_features[:REACH]]
    ppermute x0 -> x2, local copies, waits for them, and re-layouts: none -> 2.06 us  [the longest x1 1.03 us: per_device(): lax.ppermute(moving_features[:REACH], 'gy', [(i + 1, i) for i in range(gy...]
    pallas_call x1, Pallas kernels: 18.5 us -> 16.5 us  [per_device(): pl.pallas_call(lambda *refs: softmin_kernel(total_y, *refs), out_shape=ja...]
    unnamed x10 -> x8, local copies, waits for them, and re-layouts: 8.84 us -> 7.31 us
  transfers between devices with their start and end apart: 10 -> 6, of which waited for: 3 -> 4; matrix products, arithmetic and copies ran while one was open for 10% -> 20% of each run, Pallas kernels for 0% -> 0%
where the time goes in v3:
time: 89.7 us; the launch traced here: 89.4 us
  local copies, waits for them, and re-layouts  25.7 us (29%)
  starting transfers between devices  24.5 us (27%)
  Pallas kernels  24.3 us (27%)
  waiting for transfers between devices  11.9 us (13%)
  other arithmetic  2.28 us (3%)
    pallas_call x1, Pallas kernels, per_device(): pl.pallas_call(lambda *refs: softmin_kernel(total_y, *refs), out_shape=ja...  16.5 us
    reshape x4, local copies, waits for them, and re-layouts, channel_major(): return a.reshape(a.shape[0], columns_dev, CH).transpose(2, 0, 1)  11.8 us
    pallas_call x1, Pallas kernels, per_device(): pl.pallas_call(adam_kernel, out_shape=jax.ShapeDtypeStruct((height, colum...  7.86 us
    unnamed x8, local copies, waits for them, and re-layouts  7.31 us
    ppermute x1, starting transfers between devices, exchange_halo(): lax.ppermute(cells[:, -send_z:], 'gz', [(i, i + 1) for i in range(nz - 1)])  7.19 us
    ppermute x1, starting transfers between devices, exchange_halo(): lax.ppermute(cells[-send_y:], 'gy', [(i, i + 1) for i in range(ny - 1)])  5.36 us
    ppermute x1, waiting for transfers between devices, exchange_halo(): lax.ppermute(cells[:, :send_z], 'gz', [(i + 1, i) for i in range(nz - 1)])  4.5 us
    ppermute x1, starting transfers between devices, per_device(): lax.ppermute(moving_features[height - REACH:], 'gy', [(i, i + 1) for i in...  3.91 us
  transfers between devices with their start and end apart: 6, of which 4 were waited for; matrix products, arithmetic and copies ran while one was open for 20% of the time, Pallas kernels for 0%

profile of v3, /device:TPU:11, one launch (start us, length us, event | category | flops | bytes accessed | tf_op | source)
XLA Modules:
  0.0 89.4 jit_solution(17602642000747499601)
XLA Ops:
  0.6 2.2 %fusion.5 = (bf16[32,8192]{1,0:T(8,128)(2,1)}, bf16[32,8192]{1,0:T(8,128)(2,1)}) fusion(bf16[128,8192]{1,0:T(8,128)(2,1)} %param.6), kind=kLoop, calls=%fused_computation.22 | loop fusion | bytes 2097152 | tf_op jit(solution)/shard_map/slice | solution.py:226
  2.9 3.9 %collective-permute-start = (bf16[32,8192]{1,0:T(8,128)(2,1)}, bf16[32,8192]{1,0:T(8,128)(2,1)S(1)}, u32[]{:S(2)}, u32[]{:S(2)}) collective-permute-start(bf16[32,8192]{1,0:T(8,128)(2,1)} %get-tuple-element.3), channel_id=1, source_target_pairs={{0,16},{16,32},{32,48},{48,64},{64,80},{80,96},{96,112},{1,17},{17... | collective-permute-start | bytes 1572872 | tf_op jit(solution)/shard_map/ppermute | solution.py:222
  6.8 3.8 %collective-permute-start.1 = (bf16[32,8192]{1,0:T(8,128)(2,1)}, bf16[32,8192]{1,0:T(8,128)(2,1)S(1)}, u32[]{:S(2)}, u32[]{:S(2)}) collective-permute-start(bf16[32,8192]{1,0:T(8,128)(2,1)} %get-tuple-element.2), channel_id=1, source_target_pairs={{16,0},{32,16},{48,32},{64,48},{80,64},{96,80},{112,96},{17,1},{33... | collective-permute-start | bytes 1572872 | tf_op jit(solution)/shard_map/ppermute | solution.py:225
  10.5 3.2 %copy.20 = bf16[128,8192]{0,1:T(8,128)(2,1)S(1)} copy(bf16[128,8192]{1,0:T(8,128)(2,1)} %param.6) | data formatting | bytes 4194304 | tf_op args[1]
  13.8 4.1 %copy.18 = bf16[128,8192]{0,1:T(8,128)(2,1)} copy(bf16[128,8192]{1,0:T(8,128)(2,1)} %param.5) | data formatting | bytes 4194304 | tf_op args[0]
  17.9 4.3 %copy.19 = bf16[128,512,16]{1,0,2:T(8,128)(2,1)} copy(bf16[128,512,16]{0,2,1:T(8,128)(2,1)} %bitcast.17) | data formatting | bytes 4194304 | tf_op jit(solution)/shard_map/reshape | solution.py:230
  22.2 0.0 copy-start.2
  22.2 0.0 copy-start.1
  22.2 2.8 %copy.21 = bf16[128,512,16]{1,0,2:T(8,128)(2,1)} copy(bf16[128,512,16]{0,2,1:T(8,128)(2,1)S(1)} %bitcast.16) | data formatting | bytes 4194304 | tf_op jit(solution)/shard_map/reshape | solution.py:230
  25.0 0.0 copy-done.2
  25.0 0.0 copy-done.1
  25.0 0.1 convert_reduce_fusion
  25.1 0.1 copy.26
  25.2 0.1 copy.27
  25.3 3.6 %collective-permute-done = bf16[32,8192]{1,0:T(8,128)(2,1)S(1)} collective-permute-done((bf16[32,8192]{1,0:T(8,128)(2,1)}, bf16[32,8192]{1,0:T(8,128)(2,1)S(1)}, u32[]{:S(2)}, u32[]{:S(2)}) %collective-permute-start) | collective-permute-done | bytes 524320 | tf_op jit(solution)/shard_map/ppermute | solution.py:222
  28.9 1.0 %copy.22 = bf16[32,8192]{0,1:T(8,128)(2,1)S(1)} copy(bf16[32,8192]{1,0:T(8,128)(2,1)S(1)} %collective-permute-done) | data formatting | bytes 1048576 | tf_op jit(solution)/shard_map/ppermute | solution.py:222
  29.9 2.4 %copy.23 = bf16[32,512,16]{1,0,2:T(8,128)(2,1)} copy(bf16[32,512,16]{0,2,1:T(8,128)(2,1)S(1)} %bitcast.14) | data formatting | bytes 1048576 | tf_op jit(solution)/shard_map/reshape | solution.py:230
  32.3 0.1 collective-permute-done.1
  32.4 1.0 %copy.24 = bf16[32,8192]{0,1:T(8,128)(2,1)S(1)} copy(bf16[32,8192]{1,0:T(8,128)(2,1)S(1)} %collective-permute-done.1) | data formatting | bytes 1048576 | tf_op jit(solution)/shard_map/ppermute | solution.py:225
  33.5 2.4 %copy.25 = bf16[32,512,16]{1,0,2:T(8,128)(2,1)} copy(bf16[32,512,16]{0,2,1:T(8,128)(2,1)S(1)} %bitcast.15) | data formatting | bytes 1048576 | tf_op jit(solution)/shard_map/reshape | solution.py:230
  35.8 1.3 %broadcast_in_dim.15.refs_4_ = f32[17,128,128]{2,1,0:T(8,128)} broadcast(f32[17,128]{1,0:T(8,128)S(1)} %copy.27), dimensions={0,1} | broadcast | bytes 1122816 | tf_op jit(solution)/shard_map/broadcast_in_dim | solution.py:219
  37.2 0.0 copy-start
  37.2 16.5 %shard_map.71 = f32[128,512]{1,0:T(8,128)} custom-call(bf16[16,128,512]{2,1,0:T(8,128)(2,1)} %bitcast.12, bf16[16,128,512]{2,1,0:T(8,128)(2,1)} %bitcast.13, bf16[16,32,512]{2,1,0:T(8,128)(2,1)} %bitcast.18, bf16[16,32,512]{2,1,0:T(8,128)(2,1)} %bitcast.19, f32[17,128,128]{2,1,0:T(8,128)} %broadcast_in_dim.15.refs_4_), custom_call_target="tpu_custom_call" | custom-call | tf_op jit(solution)/shard_map/pallas_call | solution.py:233
  53.6 0.7 fusion.6
  54.4 5.4 %collective-permute-start.2 = (f32[8,512]{1,0:T(8,128)S(1)}, f32[8,512]{1,0:T(8,128)S(1)}, u32[]{:S(2)}, u32[]{:S(2)}) collective-permute-start(f32[8,512]{1,0:T(8,128)S(1)} %get-tuple-element.6), channel_id=1, source_target_pairs={{0,16},{16,32},{32,48},{48,64},{64,80},{80,96},{96,112},{1,17},{17... | collective-permute-start | bytes 49160 | tf_op jit(solution)/shard_map/ppermute | solution.py:92
  59.7 2.3 %collective-permute-start.3 = (f32[8,512]{1,0:T(8,128)S(1)}, f32[8,512]{1,0:T(8,128)S(1)}, u32[]{:S(2)}, u32[]{:S(2)}) collective-permute-start(f32[8,512]{1,0:T(8,128)S(1)} %get-tuple-element.7), channel_id=1, source_target_pairs={{16,0},{32,16},{48,32},{64,48},{80,64},{96,80},{112,96},{17,1},{33... | collective-permute-start | bytes 49160 | tf_op jit(solution)/shard_map/ppermute | solution.py:93
  62.1 0.0 collective-permute-done.2
  62.1 3.6 %collective-permute-done.3 = f32[8,512]{1,0:T(8,128)S(1)} collective-permute-done((f32[8,512]{1,0:T(8,128)S(1)}, f32[8,512]{1,0:T(8,128)S(1)}, u32[]{:S(2)}, u32[]{:S(2)}) %collective-permute-start.3) | collective-permute-done | bytes 16416 | tf_op jit(solution)/shard_map/ppermute | solution.py:93
  65.7 1.0 %pad_maximum_fusion.2 = (f32[144,64]{1,0:T(8,128)S(1)}, f32[144,64]{1,0:T(8,128)S(1)}) fusion(f32[8,512]{1,0:T(8,128)S(1)} %collective-permute-done.3, f32[128,512]{1,0:T(8,128)} %shard_map.71, f32[8,512]{1,0:T(8,128)S(1)} %collective-permute-done.2), kind=kLoop, calls=%fused_computation.15 | loop fusion | flops 36864 | bytes 368640 | tf_op jit(solution)/shard_map/slice | solution.py:95
  66.7 7.2 %collective-permute-start.4 = (f32[144,64]{1,0:T(8,128)S(1)}, f32[144,64]{1,0:T(8,128)S(1)}, u32[]{:S(2)}, u32[]{:S(2)}) collective-permute-start(f32[144,64]{1,0:T(8,128)S(1)} %get-tuple-element.4), channel_id=1, source_target_pairs={{0,1},{1,2},{2,3},{3,4},{4,5},{5,6},{6,7},{7,8},{8,9},{9,10},{10,1... | collective-permute-start | bytes 110600 | tf_op jit(solution)/shard_map/ppermute | solution.py:95
  73.9 1.9 %collective-permute-start.5 = (f32[144,64]{1,0:T(8,128)S(1)}, f32[144,64]{1,0:T(8,128)S(1)}, u32[]{:S(2)}, u32[]{:S(2)}) collective-permute-start(f32[144,64]{1,0:T(8,128)S(1)} %get-tuple-element.5), channel_id=1, source_target_pairs={{1,0},{2,1},{3,2},{4,3},{5,4},{6,5},{7,6},{8,7},{9,8},{10,9},{11,1... | collective-permute-start | bytes 110600 | tf_op jit(solution)/shard_map/ppermute | solution.py:96
  75.8 0.1 and_convert_fusion.mask_ref
  76.0 0.0 collective-permute-done.4
  76.0 4.5 %collective-permute-done.5 = f32[144,64]{1,0:T(8,128)S(1)} collective-permute-done((f32[144,64]{1,0:T(8,128)S(1)}, f32[144,64]{1,0:T(8,128)S(1)}, u32[]{:S(2)}, u32[]{:S(2)}) %collective-permute-start.5) | collective-permute-done | bytes 36896 | tf_op jit(solution)/shard_map/ppermute | solution.py:96
  80.5 1.1 %select_maximum_fusion.d_ref = f32[160,768]{1,0:T(8,128)S(1)} fusion(f32[144,64]{1,0:T(8,128)S(1)} %collective-permute-done.5, f32[144,64]{1,0:T(8,128)S(1)} %collective-permute-done.4, f32[8,512]{1,0:T(8,128)S(1)} %collective-permute-done.3, f32[128,512]{1,0:T(8,128)} %shard_map.71, f32[8,512]{1,0:T(8,128)S(1)} %collective-permute-done.2), kind=kLoop, calls=%fused_computation.4 | loop fusion | flops 2580480 | bytes 860160 | tf_op jit(solution)/shard_map/concatenate | solution.py:97
  81.5 0.0 copy-done
  81.5 7.9 %shard_map.72 = f32[128,512]{1,0:T(8,128)} custom-call(s32[3]{0:T(128)S(1)} %copy-done, f32[160,768]{1,0:T(8,128)S(1)} %select_maximum_fusion.d_ref, f32[160,768]{1,0:T(8,128)S(1)} %and_convert_fusion.mask_ref), custom_call_target="tpu_custom_call" | custom-call | tf_op jit(solution)/shard_map/pallas_call | solution.py:265
  (5 shorter events, 0.0 us)
Async XLA Ops:
  2.9 26.0 %collective-permute-start = (bf16[32,8192]{1,0:T(8,128)(2,1)}, bf16[32,8192]{1,0:T(8,128)(2,1)S(1)}, u32[]{:S(2)}, u32[]{:S(2)}) collective-permute-start(bf16[32,8192]{1,0:T(8,128)(2,1)} %get-tuple-element.3), channel_id=1, source_target_pairs={{0,16},{16,32},{32,48},{48,64},{64,80},{80,96},{96,112},{1,17},{17... | collective-permute-start | bytes 1572872 | tf_op jit(solution)/shard_map/ppermute | solution.py:222
  6.8 25.7 %collective-permute-start.1 = (bf16[32,8192]{1,0:T(8,128)(2,1)}, bf16[32,8192]{1,0:T(8,128)(2,1)S(1)}, u32[]{:S(2)}, u32[]{:S(2)}) collective-permute-start(bf16[32,8192]{1,0:T(8,128)(2,1)} %get-tuple-element.2), channel_id=1, source_target_pairs={{16,0},{32,16},{48,32},{64,48},{80,64},{96,80},{112,96},{17,1},{33... | collective-permute-start | bytes 1572872 | tf_op jit(solution)/shard_map/ppermute | solution.py:225
  22.2 2.8 %copy-start.2 = (s32[32,1]{0,1:T(1,128)S(1)}, s32[32,1]{0,1:T(1,128)}, u32[]{:S(2)}) copy-start(s32[32,1]{0,1:T(1,128)} %param.8) | copy-start | bytes 388
  22.2 2.8 %copy-start.1 = (s32[32,1,16]{0,2,1:T(8,128)S(1)}, s32[32,1,16]{0,2,1:T(8,128)}, u32[]{:S(2)}) copy-start(s32[32,1,16]{0,2,1:T(8,128)} %param.7) | copy-start | bytes 6148
  37.2 44.4 %copy-start = (s32[3]{0:T(128)S(1)}, s32[3]{0:T(128)}, u32[]{:S(2)}) copy-start(s32[3]{0:T(128)} %radii_ref.1) | copy-start | bytes 40
  54.4 7.7 %collective-permute-start.2 = (f32[8,512]{1,0:T(8,128)S(1)}, f32[8,512]{1,0:T(8,128)S(1)}, u32[]{:S(2)}, u32[]{:S(2)}) collective-permute-start(f32[8,512]{1,0:T(8,128)S(1)} %get-tuple-element.6), channel_id=1, source_target_pairs={{0,16},{16,32},{32,48},{48,64},{64,80},{80,96},{96,112},{1,17},{17... | collective-permute-start | bytes 49160 | tf_op jit(solution)/shard_map/ppermute | solution.py:92
  59.7 6.0 %collective-permute-start.3 = (f32[8,512]{1,0:T(8,128)S(1)}, f32[8,512]{1,0:T(8,128)S(1)}, u32[]{:S(2)}, u32[]{:S(2)}) collective-permute-start(f32[8,512]{1,0:T(8,128)S(1)} %get-tuple-element.7), channel_id=1, source_target_pairs={{16,0},{32,16},{48,32},{64,48},{80,64},{96,80},{112,96},{17,1},{33... | collective-permute-start | bytes 49160 | tf_op jit(solution)/shard_map/ppermute | solution.py:93
  66.7 9.3 %collective-permute-start.4 = (f32[144,64]{1,0:T(8,128)S(1)}, f32[144,64]{1,0:T(8,128)S(1)}, u32[]{:S(2)}, u32[]{:S(2)}) collective-permute-start(f32[144,64]{1,0:T(8,128)S(1)} %get-tuple-element.4), channel_id=1, source_target_pairs={{0,1},{1,2},{2,3},{3,4},{4,5},{5,6},{6,7},{7,8},{8,9},{9,10},{10,1... | collective-permute-start | bytes 110600 | tf_op jit(solution)/shard_map/ppermute | solution.py:95
  73.9 6.6 %collective-permute-start.5 = (f32[144,64]{1,0:T(8,128)S(1)}, f32[144,64]{1,0:T(8,128)S(1)}, u32[]{:S(2)}, u32[]{:S(2)}) collective-permute-start(f32[144,64]{1,0:T(8,128)S(1)} %get-tuple-element.5), channel_id=1, source_target_pairs={{1,0},{2,1},{3,2},{4,3},{5,4},{6,5},{7,6},{8,7},{9,8},{10,9},{11,1... | collective-permute-start | bytes 110600 | tf_op jit(solution)/shard_map/ppermute | solution.py:96

commit v4 on v3

--- a/solution.py
+++ b/solution.py
@@ -80,8 +80,8 @@
     return (field, first_moment, second_moment)
 
 
-HALO_Y = 16
-HALO_Z = 128
+HALO_Y = 8
+HALO_Z = 8 * XS
 SEND_Y = 8
 SEND_Z = 8 * XS
 
@@ -147,16 +147,24 @@
     o_ref[...] = field[HALO_Y : HALO_Y + height, HALO_Z : HALO_Z + width]
 
 
-def softmin_kernel(total_y, ft_ref, mt_ref, top_ref, bot_ref, n_ref, o_ref, f_ref, m0_ref, m4_ref):
+def softmin_kernel(total_y, tile_ranges, with_rows_beyond, *refs):
+    if with_rows_beyond:
+        ft_ref, mt_ref, top_ref, bot_ref, n_ref, done_ref, o_ref, f_ref, m0_ref, m4_ref = refs
+    else:
+        ft_ref, mt_ref, n_ref, o_ref, f_ref, m0_ref, m4_ref = refs
     height = ft_ref.shape[1]
     lanes_total = ft_ref.shape[2]
     rows = height + 2 * REACH
 
     def build(c, carry):
         f_ref[c] = ft_ref[c].astype(jnp.float32)
-        m0_ref[c, pl.ds(0, REACH), :] = top_ref[c].astype(jnp.float32)
         m0_ref[c, pl.ds(REACH, height), :] = mt_ref[c].astype(jnp.float32)
-        m0_ref[c, pl.ds(REACH + height, REACH), :] = bot_ref[c].astype(jnp.float32)
+        if with_rows_beyond:
+            m0_ref[c, pl.ds(0, REACH), :] = top_ref[c].astype(jnp.float32)
+            m0_ref[c, pl.ds(REACH + height, REACH), :] = bot_ref[c].astype(jnp.float32)
+        else:
+            m0_ref[c, pl.ds(0, REACH), :] = jnp.zeros((REACH, lanes_total), jnp.float32)
+            m0_ref[c, pl.ds(REACH + height, REACH), :] = jnp.zeros((REACH, lanes_total), jnp.float32)
         return carry
 
     lax.fori_loop(0, CH, build, 0)
@@ -168,7 +176,11 @@
 
     lax.fori_loop(0, CH, build_shifted, 0)
 
-    def body(t, carry):
+    def body(i, carry):
+        t = i
+        for lo, hi in tile_ranges[1:]:
+            t = jnp.where(t >= tile_ranges[0][1], t - tile_ranges[0][1] + lo, t)
+        t = t + tile_ranges[0][0]
         r0 = pl.multiple_of(t * 8, 8)
         for j in range(lanes_total // 128):
             lanes = pl.ds(128 * j, 128)
@@ -201,7 +213,11 @@
             o_ref[pl.ds(r0, 8), lanes] = num / den
         return carry
 
-    lax.fori_loop(0, height // 8, body, 0)
+    lax.fori_loop(0, sum(hi - lo for lo, hi in tile_ranges), body, 0)
+    if with_rows_beyond:
+        lo = tile_ranges[0][1] * 8
+        hi = tile_ranges[1][0] * 8
+        o_ref[pl.ds(lo, hi - lo), :] = done_ref[pl.ds(lo, hi - lo), :]
 
 
 def per_device(fixed_features, moving_features, cand_offsets, cand_lengths, smooth_radii):
@@ -230,21 +246,37 @@
         return a.reshape(a.shape[0], columns_dev, CH).transpose(2, 0, 1)
 
     rows = height + 2 * REACH
+    tiles = height // 8
+    reach_tiles = REACH // 8
+    scratch = [
+        pltpu.VMEM((CH, height, columns_dev), jnp.float32),
+        pltpu.VMEM((CH, rows, columns_dev), jnp.float32),
+        pltpu.VMEM((CH, rows, columns_dev), jnp.float32),
+    ]
+    params = pltpu.CompilerParams(vmem_limit_bytes=60 * 1024 * 1024)
+    out_shape = jax.ShapeDtypeStruct((height, columns_dev), jnp.float32)
+    fixed_c = channel_major(fixed_features)
+    moving_c = channel_major(moving_features)
+    middle = pl.pallas_call(
+        lambda *refs: softmin_kernel(total_y, [(reach_tiles, tiles - reach_tiles)], False, *refs),
+        out_shape=out_shape,
+        scratch_shapes=scratch,
+        compiler_params=params,
+    )(fixed_c, moving_c, mult_rows)
     disp_init = pl.pallas_call(
-        lambda *refs: softmin_kernel(total_y, *refs),
-        out_shape=jax.ShapeDtypeStruct((height, columns_dev), jnp.float32),
-        scratch_shapes=[
-            pltpu.VMEM((CH, height, columns_dev), jnp.float32),
-            pltpu.VMEM((CH, rows, columns_dev), jnp.float32),
-            pltpu.VMEM((CH, rows, columns_dev), jnp.float32),
-        ],
-        compiler_params=pltpu.CompilerParams(vmem_limit_bytes=60 * 1024 * 1024),
+        lambda *refs: softmin_kernel(
+            total_y, [(0, reach_tiles), (tiles - reach_tiles, tiles)], True, *refs
+        ),
+        out_shape=out_shape,
+        scratch_shapes=scratch,
+        compiler_params=params,
     )(
-        channel_major(fixed_features),
-        channel_major(moving_features),
+        fixed_c,
+        moving_c,
         channel_major(top_rows),
         channel_major(bottom_rows),
         mult_rows,
+        middle,
     )
 
     ext = exchange_halo(disp_init, HALO_Y, HALO_Z, SEND_Y, SEND_Z)

time: 89.7 us -> 86.3 us (0.962)
  the two profiles are of different devices: /device:TPU:11 before, /device:TPU:38 now
where the time goes in v4:
time: 86.3 us; the launch traced here: 86 us
  Pallas kernels  28.1 us (33%)
  local copies, waits for them, and re-layouts  25.7 us (30%)
  starting transfers between devices  19.9 us (23%)
  waiting for transfers between devices  9.17 us (11%)
  other arithmetic  2.33 us (3%)
    reshape x4, local copies, waits for them, and re-layouts, channel_major(): return a.reshape(a.shape[0], columns_dev, CH).transpose(2, 0, 1)  11.8 us
    pallas_call x1, Pallas kernels, per_device(): pl.pallas_call(lambda *refs: softmin_kernel(total_y, [(0, reach_tiles), (...  10.6 us
    pallas_call x1, Pallas kernels, per_device(): pl.pallas_call(lambda *refs: softmin_kernel(total_y, [(reach_tiles, tiles...  10.3 us
    unnamed x8, local copies, waits for them, and re-layouts  7.31 us
    pallas_call x1, Pallas kernels, per_device(): pl.pallas_call(adam_kernel, out_shape=jax.ShapeDtypeStruct((height, colum...  7.15 us
    ppermute x1, waiting for transfers between devices, exchange_halo(): lax.ppermute(cells[-send_y:], 'gy', [(i, i + 1) for i in range(ny - 1)])  5.13 us
    ppermute x1, starting transfers between devices, per_device(): lax.ppermute(moving_features[height - REACH:], 'gy', [(i, i + 1) for i in...  5.09 us
    ppermute x1, starting transfers between devices, exchange_halo(): lax.ppermute(cells[:send_y], 'gy', [(i + 1, i) for i in range(ny - 1)])  4.46 us
  transfers between devices with their start and end apart: 6, of which 2 were waited for; matrix products, arithmetic and copies ran while one was open for 23% of the time, Pallas kernels for 12%

profile of v4, /device:TPU:38, one launch (start us, length us, event | category | flops | bytes accessed | tf_op | source)
XLA Modules:
  0.0 86.0 jit_solution(14369252218705393198)
XLA Ops:
  0.6 2.3 %fusion.2 = (bf16[32,8192]{1,0:T(8,128)(2,1)}, bf16[32,8192]{1,0:T(8,128)(2,1)}) fusion(bf16[128,8192]{1,0:T(8,128)(2,1)} %param.6), kind=kLoop, calls=%fused_computation.12 | loop fusion | bytes 2097152 | tf_op jit(solution)/shard_map/slice | solution.py:242
  2.9 5.1 %collective-permute-start = (bf16[32,8192]{1,0:T(8,128)(2,1)}, bf16[32,8192]{1,0:T(8,128)(2,1)S(1)}, u32[]{:S(2)}, u32[]{:S(2)}) collective-permute-start(bf16[32,8192]{1,0:T(8,128)(2,1)} %get-tuple-element.3), channel_id=1, source_target_pairs={{0,16},{16,32},{32,48},{48,64},{64,80},{80,96},{96,112},{1,17},{17... | collective-permute-start | bytes 1572872 | tf_op jit(solution)/shard_map/ppermute | solution.py:238
  8.0 3.1 %collective-permute-start.1 = (bf16[32,8192]{1,0:T(8,128)(2,1)}, bf16[32,8192]{1,0:T(8,128)(2,1)S(1)}, u32[]{:S(2)}, u32[]{:S(2)}) collective-permute-start(bf16[32,8192]{1,0:T(8,128)(2,1)} %get-tuple-element.2), channel_id=1, source_target_pairs={{16,0},{32,16},{48,32},{64,48},{80,64},{96,80},{112,96},{17,1},{33... | collective-permute-start | bytes 1572872 | tf_op jit(solution)/shard_map/ppermute | solution.py:241
  11.2 3.2 %copy.20 = bf16[128,8192]{0,1:T(8,128)(2,1)S(1)} copy(bf16[128,8192]{1,0:T(8,128)(2,1)} %param.6) | data formatting | bytes 4194304 | tf_op args[1]
  14.4 4.1 %copy.18 = bf16[128,8192]{0,1:T(8,128)(2,1)} copy(bf16[128,8192]{1,0:T(8,128)(2,1)} %param.5) | data formatting | bytes 4194304 | tf_op args[0]
  18.5 4.3 %copy.19 = bf16[128,512,16]{1,0,2:T(8,128)(2,1)} copy(bf16[128,512,16]{0,2,1:T(8,128)(2,1)} %bitcast.19) | data formatting | bytes 4194304 | tf_op jit(solution)/shard_map/reshape | solution.py:246
  22.8 0.0 copy-start.2
  22.8 0.0 copy-start.1
  22.8 2.8 %copy.21 = bf16[128,512,16]{1,0,2:T(8,128)(2,1)} copy(bf16[128,512,16]{0,2,1:T(8,128)(2,1)S(1)} %bitcast.18) | data formatting | bytes 4194304 | tf_op jit(solution)/shard_map/reshape | solution.py:246
  25.6 0.0 copy-done.2
  25.6 0.0 copy-done.1
  25.6 0.1 convert_reduce_fusion
  25.7 0.1 copy.26
  25.8 0.1 copy.27
  25.9 1.4 %broadcast_in_dim.15.refs_2_.refs_4_ = f32[17,128,128]{2,1,0:T(8,128)} broadcast(f32[17,128]{1,0:T(8,128)S(1)} %copy.27), dimensions={0,1} | broadcast | bytes 1122816 | tf_op jit(solution)/shard_map/broadcast_in_dim | solution.py:235
  27.2 10.3 %shard_map.71.refs_5_ = f32[128,512]{1,0:T(8,128)} custom-call(bf16[16,128,512]{2,1,0:T(8,128)(2,1)} %bitcast.12, bf16[16,128,512]{2,1,0:T(8,128)(2,1)} %bitcast.14, f32[17,128,128]{2,1,0:T(8,128)} %broadcast_in_dim.15.refs_2_.refs_4_), custom_call_target="tpu_custom_call" | custom-call | tf_op jit(solution)/shard_map/pallas_call | solution.py:260
  37.5 0.0 collective-permute-done
  37.5 1.0 %copy.22 = bf16[32,8192]{0,1:T(8,128)(2,1)S(1)} copy(bf16[32,8192]{1,0:T(8,128)(2,1)S(1)} %collective-permute-done) | data formatting | bytes 1048576 | tf_op jit(solution)/shard_map/ppermute | solution.py:238
  38.6 2.4 %copy.23 = bf16[32,512,16]{1,0,2:T(8,128)(2,1)} copy(bf16[32,512,16]{0,2,1:T(8,128)(2,1)S(1)} %bitcast.16) | data formatting | bytes 1048576 | tf_op jit(solution)/shard_map/reshape | solution.py:246
  40.9 0.0 collective-permute-done.1
  41.0 1.0 %copy.24 = bf16[32,8192]{0,1:T(8,128)(2,1)S(1)} copy(bf16[32,8192]{1,0:T(8,128)(2,1)S(1)} %collective-permute-done.1) | data formatting | bytes 1048576 | tf_op jit(solution)/shard_map/ppermute | solution.py:241
  42.0 2.4 %copy.25 = bf16[32,512,16]{1,0,2:T(8,128)(2,1)} copy(bf16[32,512,16]{0,2,1:T(8,128)(2,1)S(1)} %bitcast.17) | data formatting | bytes 1048576 | tf_op jit(solution)/shard_map/reshape | solution.py:246
  44.3 0.0 copy-start
  44.4 10.6 %shard_map.72 = f32[128,512]{1,0:T(8,128)} custom-call(bf16[16,128,512]{2,1,0:T(8,128)(2,1)} %bitcast.13, bf16[16,128,512]{2,1,0:T(8,128)(2,1)} %bitcast.15, bf16[16,32,512]{2,1,0:T(8,128)(2,1)} %bitcast.20, bf16[16,32,512]{2,1,0:T(8,128)(2,1)} %bitcast.21, f32[17,128,128]{2,1,0:T(8,128)} %broadcast_in_dim.15.refs_2_.refs_4_, f32[128,512]{1,0:T(8,128)} %shard_map.71.refs_5_), custom_call_target="tpu_custom_call" | custom-call | tf_op jit(solution)/shard_map/pallas_call | solution.py:266
  55.0 0.7 fusion.3
  55.7 4.5 %collective-permute-start.3 = (f32[8,512]{1,0:T(8,128)S(1)}, f32[8,512]{1,0:T(8,128)S(1)}, u32[]{:S(2)}, u32[]{:S(2)}) collective-permute-start(f32[8,512]{1,0:T(8,128)S(1)} %get-tuple-element.7), channel_id=1, source_target_pairs={{16,0},{32,16},{48,32},{64,48},{80,64},{96,80},{112,96},{17,1},{33... | collective-permute-start | bytes 49160 | tf_op jit(solution)/shard_map/ppermute | solution.py:93
  60.2 2.9 %collective-permute-start.2 = (f32[8,512]{1,0:T(8,128)S(1)}, f32[8,512]{1,0:T(8,128)S(1)}, u32[]{:S(2)}, u32[]{:S(2)}) collective-permute-start(f32[8,512]{1,0:T(8,128)S(1)} %get-tuple-element.6), channel_id=1, source_target_pairs={{0,16},{16,32},{32,48},{48,64},{64,80},{80,96},{96,112},{1,17},{17... | collective-permute-start | bytes 49160 | tf_op jit(solution)/shard_map/ppermute | solution.py:92
  63.1 0.0 collective-permute-done.3
  63.1 5.1 %collective-permute-done.2 = f32[8,512]{1,0:T(8,128)S(1)} collective-permute-done((f32[8,512]{1,0:T(8,128)S(1)}, f32[8,512]{1,0:T(8,128)S(1)}, u32[]{:S(2)}, u32[]{:S(2)}) %collective-permute-start.2) | collective-permute-done | bytes 16416 | tf_op jit(solution)/shard_map/ppermute | solution.py:92
  68.2 1.0 %pad_maximum_fusion.3 = (f32[144,64]{1,0:T(8,128)S(1)}, f32[144,64]{1,0:T(8,128)S(1)}) fusion(f32[8,512]{1,0:T(8,128)S(1)} %collective-permute-done.3, f32[128,512]{1,0:T(8,128)} %shard_map.72, f32[8,512]{1,0:T(8,128)S(1)} %collective-permute-done.2), kind=kLoop, calls=%fused_computation.5 | loop fusion | flops 36864 | bytes 368640 | tf_op jit(solution)/shard_map/slice | solution.py:95
  69.2 1.9 %collective-permute-start.5 = (f32[144,64]{1,0:T(8,128)S(1)}, f32[144,64]{1,0:T(8,128)S(1)}, u32[]{:S(2)}, u32[]{:S(2)}) collective-permute-start(f32[144,64]{1,0:T(8,128)S(1)} %get-tuple-element.5), channel_id=1, source_target_pairs={{1,0},{2,1},{3,2},{4,3},{5,4},{6,5},{7,6},{8,7},{9,8},{10,9},{11,1... | collective-permute-start | bytes 110600 | tf_op jit(solution)/shard_map/ppermute | solution.py:96
  71.1 2.4 %collective-permute-start.4 = (f32[144,64]{1,0:T(8,128)S(1)}, f32[144,64]{1,0:T(8,128)S(1)}, u32[]{:S(2)}, u32[]{:S(2)}) collective-permute-start(f32[144,64]{1,0:T(8,128)S(1)} %get-tuple-element.4), channel_id=1, source_target_pairs={{0,1},{1,2},{2,3},{3,4},{4,5},{5,6},{6,7},{7,8},{8,9},{9,10},{10,1... | collective-permute-start | bytes 110600 | tf_op jit(solution)/shard_map/ppermute | solution.py:95
  73.5 0.1 and_convert_fusion.mask_ref
  73.7 0.0 collective-permute-done.5
  73.7 4.0 %collective-permute-done.4 = f32[144,64]{1,0:T(8,128)S(1)} collective-permute-done((f32[144,64]{1,0:T(8,128)S(1)}, f32[144,64]{1,0:T(8,128)S(1)}, u32[]{:S(2)}, u32[]{:S(2)}) %collective-permute-start.4) | collective-permute-done | bytes 36896 | tf_op jit(solution)/shard_map/ppermute | solution.py:95
  77.7 1.1 %pad_maximum_fusion.d_ref = f32[144,640]{1,0:T(8,128)S(1)} fusion(f32[144,64]{1,0:T(8,128)S(1)} %collective-permute-done.5, f32[8,512]{1,0:T(8,128)S(1)} %collective-permute-done.3, f32[128,512]{1,0:T(8,128)} %shard_map.72, f32[8,512]{1,0:T(8,128)S(1)} %collective-permute-done.2, f32[144,64]{1,0:T(8,128)S(1)} %collective-permute-done.4), kind=kLoop, calls=%fused_computation | loop fusion | flops 368640 | bytes 737280 | tf_op jit(solution)/shard_map/concatenate | solution.py:97
  78.8 0.0 copy-done
  78.8 7.2 %shard_map.73 = f32[128,512]{1,0:T(8,128)} custom-call(s32[3]{0:T(128)S(1)} %copy-done, f32[144,640]{1,0:T(8,128)S(1)} %pad_maximum_fusion.d_ref, f32[144,640]{1,0:T(8,128)S(1)} %and_convert_fusion.mask_ref), custom_call_target="tpu_custom_call" | custom-call | tf_op jit(solution)/shard_map/pallas_call | solution.py:297
  (5 shorter events, 0.0 us)
Async XLA Ops:
  2.9 34.6 %collective-permute-start = (bf16[32,8192]{1,0:T(8,128)(2,1)}, bf16[32,8192]{1,0:T(8,128)(2,1)S(1)}, u32[]{:S(2)}, u32[]{:S(2)}) collective-permute-start(bf16[32,8192]{1,0:T(8,128)(2,1)} %get-tuple-element.3), channel_id=1, source_target_pairs={{0,16},{16,32},{32,48},{48,64},{64,80},{80,96},{96,112},{1,17},{17... | collective-permute-start | bytes 1572872 | tf_op jit(solution)/shard_map/ppermute | solution.py:238
  8.0 32.9 %collective-permute-start.1 = (bf16[32,8192]{1,0:T(8,128)(2,1)}, bf16[32,8192]{1,0:T(8,128)(2,1)S(1)}, u32[]{:S(2)}, u32[]{:S(2)}) collective-permute-start(bf16[32,8192]{1,0:T(8,128)(2,1)} %get-tuple-element.2), channel_id=1, source_target_pairs={{16,0},{32,16},{48,32},{64,48},{80,64},{96,80},{112,96},{17,1},{33... | collective-permute-start | bytes 1572872 | tf_op jit(solution)/shard_map/ppermute | solution.py:241
  22.8 2.8 %copy-start.2 = (s32[32,1]{0,1:T(1,128)S(1)}, s32[32,1]{0,1:T(1,128)}, u32[]{:S(2)}) copy-start(s32[32,1]{0,1:T(1,128)} %param.8) | copy-start | bytes 388
  22.8 2.8 %copy-start.1 = (s32[32,1,16]{0,2,1:T(8,128)S(1)}, s32[32,1,16]{0,2,1:T(8,128)}, u32[]{:S(2)}) copy-start(s32[32,1,16]{0,2,1:T(8,128)} %param.7) | copy-start | bytes 6148
  44.3 34.5 %copy-start = (s32[3]{0:T(128)S(1)}, s32[3]{0:T(128)}, u32[]{:S(2)}) copy-start(s32[3]{0:T(128)} %radii_ref.1) | copy-start | bytes 40
  55.7 7.4 %collective-permute-start.3 = (f32[8,512]{1,0:T(8,128)S(1)}, f32[8,512]{1,0:T(8,128)S(1)}, u32[]{:S(2)}, u32[]{:S(2)}) collective-permute-start(f32[8,512]{1,0:T(8,128)S(1)} %get-tuple-element.7), channel_id=1, source_target_pairs={{16,0},{32,16},{48,32},{64,48},{80,64},{96,80},{112,96},{17,1},{33... | collective-permute-start | bytes 49160 | tf_op jit(solution)/shard_map/ppermute | solution.py:93
  60.2 8.0 %collective-permute-start.2 = (f32[8,512]{1,0:T(8,128)S(1)}, f32[8,512]{1,0:T(8,128)S(1)}, u32[]{:S(2)}, u32[]{:S(2)}) collective-permute-start(f32[8,512]{1,0:T(8,128)S(1)} %get-tuple-element.6), channel_id=1, source_target_pairs={{0,16},{16,32},{32,48},{48,64},{64,80},{80,96},{96,112},{1,17},{17... | collective-permute-start | bytes 49160 | tf_op jit(solution)/shard_map/ppermute | solution.py:92
  69.2 4.5 %collective-permute-start.5 = (f32[144,64]{1,0:T(8,128)S(1)}, f32[144,64]{1,0:T(8,128)S(1)}, u32[]{:S(2)}, u32[]{:S(2)}) collective-permute-start(f32[144,64]{1,0:T(8,128)S(1)} %get-tuple-element.5), channel_id=1, source_target_pairs={{1,0},{2,1},{3,2},{4,3},{5,4},{6,5},{7,6},{8,7},{9,8},{10,9},{11,1... | collective-permute-start | bytes 110600 | tf_op jit(solution)/shard_map/ppermute | solution.py:96
  71.1 6.6 %collective-permute-start.4 = (f32[144,64]{1,0:T(8,128)S(1)}, f32[144,64]{1,0:T(8,128)S(1)}, u32[]{:S(2)}, u32[]{:S(2)}) collective-permute-start(f32[144,64]{1,0:T(8,128)S(1)} %get-tuple-element.4), channel_id=1, source_target_pairs={{0,1},{1,2},{2,3},{3,4},{4,5},{5,6},{6,7},{7,8},{8,9},{9,10},{10,1... | collective-permute-start | bytes 110600 | tf_op jit(solution)/shard_map/ppermute | solution.py:95

commit v5 on v4

--- a/solution.py
+++ b/solution.py
@@ -145,6 +145,24 @@
     height = o_ref.shape[0]
     width = o_ref.shape[1]
     o_ref[...] = field[HALO_Y : HALO_Y + height, HALO_Z : HALO_Z + width]
+
+
+def transpose_kernel(x_ref, o_ref, s_ref):
+    chunk = 128 * CH
+    for j in range(x_ref.shape[1] // chunk):
+        s_ref[...] = x_ref[:, pl.ds(chunk * j, chunk)].astype(jnp.float32).T
+        for c in range(CH):
+            cols = s_ref[pl.ds(c, 128, stride=CH), :]
+            o_ref[c, :, pl.ds(128 * j, 128)] = cols.T.astype(o_ref.dtype)
+
+
+def channel_major(x):
+    rows, lanes = x.shape
+    return pl.pallas_call(
+        transpose_kernel,
+        out_shape=jax.ShapeDtypeStruct((CH, rows, lanes // CH), x.dtype),
+        scratch_shapes=[pltpu.VMEM((128 * CH, rows), jnp.float32)],
+    )(x)
 
 
 def softmin_kernel(total_y, tile_ranges, with_rows_beyond, *refs):
@@ -235,15 +253,14 @@
     mult_rows = jnp.broadcast_to(mult_rows[:, :, None], (NOFF, height, 128))
 
     gy_count = lax.axis_size("gy")
+    fixed_c = channel_major(fixed_features)
+    moving_c = channel_major(moving_features)
     top_rows = lax.ppermute(
-        moving_features[height - REACH :], "gy", [(i, i + 1) for i in range(gy_count - 1)]
+        moving_c[:, height - REACH :], "gy", [(i, i + 1) for i in range(gy_count - 1)]
     )
     bottom_rows = lax.ppermute(
-        moving_features[:REACH], "gy", [(i + 1, i) for i in range(gy_count - 1)]
-    )
-
-    def channel_major(a):
-        return a.reshape(a.shape[0], columns_dev, CH).transpose(2, 0, 1)
+        moving_c[:, :REACH], "gy", [(i + 1, i) for i in range(gy_count - 1)]
+    )
 
     rows = height + 2 * REACH
     tiles = height // 8
@@ -255,8 +272,6 @@
     ]
     params = pltpu.CompilerParams(vmem_limit_bytes=60 * 1024 * 1024)
     out_shape = jax.ShapeDtypeStruct((height, columns_dev), jnp.float32)
-    fixed_c = channel_major(fixed_features)
-    moving_c = channel_major(moving_features)
     middle = pl.pallas_call(
         lambda *refs: softmin_kernel(total_y, [(reach_tiles, tiles - reach_tiles)], False, *refs),
         out_shape=out_shape,
@@ -273,8 +288,8 @@
     )(
         fixed_c,
         moving_c,
-        channel_major(top_rows),
-        channel_major(bottom_rows),
+        top_rows,
+        bottom_rows,
         mult_rows,
         middle,
     )

time: 86.3 us -> 79.4 us (0.920)
  the two profiles are of different devices: /device:TPU:38 before, /device:TPU:11 now
where the time goes in v5:
time: 79.4 us; the launch traced here: 77.8 us
  Pallas kernels  37.9 us (48%)
  starting transfers between devices  23.6 us (30%)
  waiting for transfers between devices  8.89 us (11%)
  local copies, waits for them, and re-layouts  4.39 us (6%)
  other arithmetic  2.33 us (3%)
    pallas_call x1, Pallas kernels, per_device(): pl.pallas_call(lambda *refs: softmin_kernel(total_y, [(0, reach_tiles), (...  10.6 us
    pallas_call x1, Pallas kernels, per_device(): pl.pallas_call(lambda *refs: softmin_kernel(total_y, [(reach_tiles, tiles...  10.3 us
    pallas_call x2, Pallas kernels, channel_major(): pl.pallas_call(transpose_kernel, out_shape=jax.ShapeDtypeStruct((CH, rows...  9.72 us
    pallas_call x1, Pallas kernels, per_device(): pl.pallas_call(adam_kernel, out_shape=jax.ShapeDtypeStruct((height, colum...  7.22 us
    ppermute x1, starting transfers between devices, exchange_halo(): lax.ppermute(cells[:, :send_z], 'gz', [(i + 1, i) for i in range(nz - 1)])  4.88 us
    ppermute x1, starting transfers between devices, exchange_halo(): lax.ppermute(cells[:, -send_z:], 'gz', [(i, i + 1) for i in range(nz - 1)])  4.23 us
    ppermute x1, starting transfers between devices, exchange_halo(): lax.ppermute(cells[-send_y:], 'gy', [(i, i + 1) for i in range(ny - 1)])  4.02 us
    ppermute x1, starting transfers between devices, per_device(): lax.ppermute(moving_c[:, height - REACH:], 'gy', [(i, i + 1) for i in ran...  3.92 us
  transfers between devices with their start and end apart: 6, of which 4 were waited for; matrix products, arithmetic and copies ran while one was open for 2% of the time, Pallas kernels for 19%

profile of v5, /device:TPU:11, one launch (start us, length us, event | category | flops | bytes accessed | tf_op | source)
XLA Modules:
  0.0 77.8 jit_solution(15858617242048617405)
XLA Ops:
  0.6 4.8 %shard_map.72.refs_1_ = bf16[16,128,512]{2,1,0:T(8,128)(2,1)} custom-call(bf16[128,8192]{1,0:T(8,128)(2,1)} %x_ref.3), custom_call_target="tpu_custom_call" | custom-call | tf_op jit(solution)/shard_map/pallas_call | solution.py:161
  5.5 1.3 %fusion.2 = (bf16[16,32,512]{2,1,0:T(8,128)(2,1)S(1)}, bf16[16,32,512]{2,1,0:T(8,128)(2,1)S(1)}) fusion(bf16[16,128,512]{2,1,0:T(8,128)(2,1)} %shard_map.72.refs_1_), kind=kLoop, calls=%fused_computation.12 | loop fusion | bytes 2097152 | tf_op jit(solution)/shard_map/slice | solution.py:262
  6.8 3.9 %collective-permute-start = (bf16[16,32,512]{2,1,0:T(8,128)(2,1)S(1)}, bf16[16,32,512]{2,1,0:T(8,128)(2,1)S(1)}, u32[]{:S(2)}, u32[]{:S(2)}) collective-permute-start(bf16[16,32,512]{2,1,0:T(8,128)(2,1)S(1)} %get-tuple-element.3), channel_id=1, source_target_pairs={{0,16},{16,32},{32,48},{48,64},{64,80},{80,96},{96,112},{1,17},{17... | collective-permute-start | bytes 1572872 | tf_op jit(solution)/shard_map/ppermute | solution.py:258
  10.7 3.8 %collective-permute-start.1 = (bf16[16,32,512]{2,1,0:T(8,128)(2,1)S(1)}, bf16[16,32,512]{2,1,0:T(8,128)(2,1)S(1)}, u32[]{:S(2)}, u32[]{:S(2)}) collective-permute-start(bf16[16,32,512]{2,1,0:T(8,128)(2,1)S(1)} %get-tuple-element.2), channel_id=1, source_target_pairs={{16,0},{32,16},{48,32},{64,48},{80,64},{96,80},{112,96},{17,1},{33... | collective-permute-start | bytes 1572872 | tf_op jit(solution)/shard_map/ppermute | solution.py:261
  14.5 0.0 copy-start.4
  14.5 0.0 copy-start.3
  14.5 4.9 %shard_map.71.refs_0_ = bf16[16,128,512]{2,1,0:T(8,128)(2,1)} custom-call(bf16[128,8192]{1,0:T(8,128)(2,1)} %x_ref.2), custom_call_target="tpu_custom_call" | custom-call | tf_op jit(solution)/shard_map/pallas_call | solution.py:161
  19.4 0.0 copy-done.4
  19.4 0.0 copy-done.3
  19.4 0.1 convert_reduce_fusion
  19.5 0.1 copy.10
  19.6 0.1 copy.11
  19.7 1.4 %broadcast_in_dim.15.refs_2_.refs_4_ = f32[17,128,128]{2,1,0:T(8,128)} broadcast(f32[17,128]{1,0:T(8,128)S(1)} %copy.11), dimensions={0,1} | broadcast | bytes 1122816 | tf_op jit(solution)/shard_map/broadcast_in_dim | solution.py:253
  21.0 10.3 %shard_map.73.refs_5_ = f32[128,512]{1,0:T(8,128)} custom-call(bf16[16,128,512]{2,1,0:T(8,128)(2,1)} %shard_map.71.refs_0_, bf16[16,128,512]{2,1,0:T(8,128)(2,1)} %shard_map.72.refs_1_, f32[17,128,128]{2,1,0:T(8,128)} %broadcast_in_dim.15.refs_2_.refs_4_), custom_call_target="tpu_custom_call" | custom-call | tf_op jit(solution)/shard_map/pallas_call | solution.py:275
  31.3 0.0 copy-start
  31.3 1.2 %collective-permute-done.refs_2_ = bf16[16,32,512]{2,1,0:T(8,128)(2,1)S(1)} collective-permute-done((bf16[16,32,512]{2,1,0:T(8,128)(2,1)S(1)}, bf16[16,32,512]{2,1,0:T(8,128)(2,1)S(1)}, u32[]{:S(2)}, u32[]{:S(2)}) %collective-permute-start) | collective-permute-done | bytes 524320 | tf_op jit(solution)/shard_map/ppermute | solution.py:258
  32.5 0.0 copy-start.1
  32.5 3.6 %collective-permute-done.1.refs_3_ = bf16[16,32,512]{2,1,0:T(8,128)(2,1)S(1)} collective-permute-done((bf16[16,32,512]{2,1,0:T(8,128)(2,1)S(1)}, bf16[16,32,512]{2,1,0:T(8,128)(2,1)S(1)}, u32[]{:S(2)}, u32[]{:S(2)}) %collective-permute-start.1) | collective-permute-done | bytes 524320 | tf_op jit(solution)/shard_map/ppermute | solution.py:261
  36.1 0.0 copy-done.1
  36.1 0.0 copy-start.2
  36.1 0.8 %copy-done.2 = bf16[16,32,512]{2,1,0:T(8,128)(2,1)} copy-done((bf16[16,32,512]{2,1,0:T(8,128)(2,1)}, bf16[16,32,512]{2,1,0:T(8,128)(2,1)S(1)}, u32[]{:S(2)}) %copy-start.2) | copy-done | bytes 524312
  37.0 10.6 %shard_map.74 = f32[128,512]{1,0:T(8,128)} custom-call(bf16[16,128,512]{2,1,0:T(8,128)(2,1)} %shard_map.71.refs_0_, bf16[16,128,512]{2,1,0:T(8,128)(2,1)} %shard_map.72.refs_1_, bf16[16,32,512]{2,1,0:T(8,128)(2,1)} %copy-done.1, bf16[16,32,512]{2,1,0:T(8,128)(2,1)} %copy-done.2, f32[17,128,128]{2,1,0:T(8,128)} %broadcast_in_dim.15.refs_2_.refs_4_, ...), custom_call_target="tpu_custom_call" | custom-call | tf_op jit(solution)/shard_map/pallas_call | solution.py:281
  47.6 0.7 fusion.3
  48.3 2.8 %collective-permute-start.3 = (f32[8,512]{1,0:T(8,128)S(1)}, f32[8,512]{1,0:T(8,128)S(1)}, u32[]{:S(2)}, u32[]{:S(2)}) collective-permute-start(f32[8,512]{1,0:T(8,128)S(1)} %get-tuple-element.7), channel_id=1, source_target_pairs={{16,0},{32,16},{48,32},{64,48},{80,64},{96,80},{112,96},{17,1},{33... | collective-permute-start | bytes 49160 | tf_op jit(solution)/shard_map/ppermute | solution.py:93
  51.1 4.0 %collective-permute-start.2 = (f32[8,512]{1,0:T(8,128)S(1)}, f32[8,512]{1,0:T(8,128)S(1)}, u32[]{:S(2)}, u32[]{:S(2)}) collective-permute-start(f32[8,512]{1,0:T(8,128)S(1)} %get-tuple-element.6), channel_id=1, source_target_pairs={{0,16},{16,32},{32,48},{48,64},{64,80},{80,96},{96,112},{1,17},{17... | collective-permute-start | bytes 49160 | tf_op jit(solution)/shard_map/ppermute | solution.py:92
  55.1 0.0 collective-permute-done.3
  55.1 2.8 %collective-permute-done.2 = f32[8,512]{1,0:T(8,128)S(1)} collective-permute-done((f32[8,512]{1,0:T(8,128)S(1)}, f32[8,512]{1,0:T(8,128)S(1)}, u32[]{:S(2)}, u32[]{:S(2)}) %collective-permute-start.2) | collective-permute-done | bytes 16416 | tf_op jit(solution)/shard_map/ppermute | solution.py:92
  58.0 1.0 %pad_maximum_fusion.3 = (f32[144,64]{1,0:T(8,128)S(1)}, f32[144,64]{1,0:T(8,128)S(1)}) fusion(f32[8,512]{1,0:T(8,128)S(1)} %collective-permute-done.3, f32[128,512]{1,0:T(8,128)} %shard_map.74, f32[8,512]{1,0:T(8,128)S(1)} %collective-permute-done.2), kind=kLoop, calls=%fused_computation.5 | loop fusion | flops 36864 | bytes 368640 | tf_op jit(solution)/shard_map/slice | solution.py:95
  58.9 4.9 %collective-permute-start.5 = (f32[144,64]{1,0:T(8,128)S(1)}, f32[144,64]{1,0:T(8,128)S(1)}, u32[]{:S(2)}, u32[]{:S(2)}) collective-permute-start(f32[144,64]{1,0:T(8,128)S(1)} %get-tuple-element.5), channel_id=1, source_target_pairs={{1,0},{2,1},{3,2},{4,3},{5,4},{6,5},{7,6},{8,7},{9,8},{10,9},{11,1... | collective-permute-start | bytes 110600 | tf_op jit(solution)/shard_map/ppermute | solution.py:96
  63.8 4.2 %collective-permute-start.4 = (f32[144,64]{1,0:T(8,128)S(1)}, f32[144,64]{1,0:T(8,128)S(1)}, u32[]{:S(2)}, u32[]{:S(2)}) collective-permute-start(f32[144,64]{1,0:T(8,128)S(1)} %get-tuple-element.4), channel_id=1, source_target_pairs={{0,1},{1,2},{2,3},{3,4},{4,5},{5,6},{6,7},{7,8},{8,9},{9,10},{10,1... | collective-permute-start | bytes 110600 | tf_op jit(solution)/shard_map/ppermute | solution.py:95
  68.1 0.1 and_convert_fusion.mask_ref
  68.2 0.0 collective-permute-done.5
  68.2 1.3 %collective-permute-done.4 = f32[144,64]{1,0:T(8,128)S(1)} collective-permute-done((f32[144,64]{1,0:T(8,128)S(1)}, f32[144,64]{1,0:T(8,128)S(1)}, u32[]{:S(2)}, u32[]{:S(2)}) %collective-permute-start.4) | collective-permute-done | bytes 36896 | tf_op jit(solution)/shard_map/ppermute | solution.py:95
  69.5 1.1 %pad_maximum_fusion.d_ref = f32[144,640]{1,0:T(8,128)S(1)} fusion(f32[144,64]{1,0:T(8,128)S(1)} %collective-permute-done.5, f32[8,512]{1,0:T(8,128)S(1)} %collective-permute-done.3, f32[128,512]{1,0:T(8,128)} %shard_map.74, f32[8,512]{1,0:T(8,128)S(1)} %collective-permute-done.2, f32[144,64]{1,0:T(8,128)S(1)} %collective-permute-done.4), kind=kLoop, calls=%fused_computation | loop fusion | flops 368640 | bytes 737280 | tf_op jit(solution)/shard_map/concatenate | solution.py:97
  70.6 0.0 copy-done
  70.6 7.2 %shard_map.75 = f32[128,512]{1,0:T(8,128)} custom-call(s32[3]{0:T(128)S(1)} %copy-done, f32[144,640]{1,0:T(8,128)S(1)} %pad_maximum_fusion.d_ref, f32[144,640]{1,0:T(8,128)S(1)} %and_convert_fusion.mask_ref), custom_call_target="tpu_custom_call" | custom-call | tf_op jit(solution)/shard_map/pallas_call | solution.py:312
  (5 shorter events, 0.0 us)
Async XLA Ops:
  6.8 25.7 %collective-permute-start = (bf16[16,32,512]{2,1,0:T(8,128)(2,1)S(1)}, bf16[16,32,512]{2,1,0:T(8,128)(2,1)S(1)}, u32[]{:S(2)}, u32[]{:S(2)}) collective-permute-start(bf16[16,32,512]{2,1,0:T(8,128)(2,1)S(1)} %get-tuple-element.3), channel_id=1, source_target_pairs={{0,16},{16,32},{32,48},{48,64},{64,80},{80,96},{96,112},{1,17},{17... | collective-permute-start | bytes 1572872 | tf_op jit(solution)/shard_map/ppermute | solution.py:258
  10.7 25.4 %collective-permute-start.1 = (bf16[16,32,512]{2,1,0:T(8,128)(2,1)S(1)}, bf16[16,32,512]{2,1,0:T(8,128)(2,1)S(1)}, u32[]{:S(2)}, u32[]{:S(2)}) collective-permute-start(bf16[16,32,512]{2,1,0:T(8,128)(2,1)S(1)} %get-tuple-element.2), channel_id=1, source_target_pairs={{16,0},{32,16},{48,32},{64,48},{80,64},{96,80},{112,96},{17,1},{33... | collective-permute-start | bytes 1572872 | tf_op jit(solution)/shard_map/ppermute | solution.py:261
  14.5 4.9 %copy-start.4 = (s32[32,1]{0,1:T(1,128)S(1)}, s32[32,1]{0,1:T(1,128)}, u32[]{:S(2)}) copy-start(s32[32,1]{0,1:T(1,128)} %param.8) | copy-start | bytes 388
  14.5 4.9 %copy-start.3 = (s32[32,1,16]{0,2,1:T(8,128)S(1)}, s32[32,1,16]{0,2,1:T(8,128)}, u32[]{:S(2)}) copy-start(s32[32,1,16]{0,2,1:T(8,128)} %param.7) | copy-start | bytes 6148
  31.3 39.3 %copy-start = (s32[3]{0:T(128)S(1)}, s32[3]{0:T(128)}, u32[]{:S(2)}) copy-start(s32[3]{0:T(128)} %radii_ref.1) | copy-start | bytes 40
  32.5 3.6 %copy-start.1 = (bf16[16,32,512]{2,1,0:T(8,128)(2,1)}, bf16[16,32,512]{2,1,0:T(8,128)(2,1)S(1)}, u32[]{:S(2)}) copy-start(bf16[16,32,512]{2,1,0:T(8,128)(2,1)S(1)} %collective-permute-done.refs_2_) | copy-start | bytes 1572868
  36.1 0.8 %copy-start.2 = (bf16[16,32,512]{2,1,0:T(8,128)(2,1)}, bf16[16,32,512]{2,1,0:T(8,128)(2,1)S(1)}, u32[]{:S(2)}) copy-start(bf16[16,32,512]{2,1,0:T(8,128)(2,1)S(1)} %collective-permute-done.1.refs_3_) | copy-start | bytes 1572868
  48.3 6.8 %collective-permute-start.3 = (f32[8,512]{1,0:T(8,128)S(1)}, f32[8,512]{1,0:T(8,128)S(1)}, u32[]{:S(2)}, u32[]{:S(2)}) collective-permute-start(f32[8,512]{1,0:T(8,128)S(1)} %get-tuple-element.7), channel_id=1, source_target_pairs={{16,0},{32,16},{48,32},{64,48},{80,64},{96,80},{112,96},{17,1},{33... | collective-permute-start | bytes 49160 | tf_op jit(solution)/shard_map/ppermute | solution.py:93
  51.1 6.9 %collective-permute-start.2 = (f32[8,512]{1,0:T(8,128)S(1)}, f32[8,512]{1,0:T(8,128)S(1)}, u32[]{:S(2)}, u32[]{:S(2)}) collective-permute-start(f32[8,512]{1,0:T(8,128)S(1)} %get-tuple-element.6), channel_id=1, source_target_pairs={{0,16},{16,32},{32,48},{48,64},{64,80},{80,96},{96,112},{1,17},{17... | collective-permute-start | bytes 49160 | tf_op jit(solution)/shard_map/ppermute | solution.py:92
  58.9 9.2 %collective-permute-start.5 = (f32[144,64]{1,0:T(8,128)S(1)}, f32[144,64]{1,0:T(8,128)S(1)}, u32[]{:S(2)}, u32[]{:S(2)}) collective-permute-start(f32[144,64]{1,0:T(8,128)S(1)} %get-tuple-element.5), channel_id=1, source_target_pairs={{1,0},{2,1},{3,2},{4,3},{5,4},{6,5},{7,6},{8,7},{9,8},{10,9},{11,1... | collective-permute-start | bytes 110600 | tf_op jit(solution)/shard_map/ppermute | solution.py:96
  63.8 5.6 %collective-permute-start.4 = (f32[144,64]{1,0:T(8,128)S(1)}, f32[144,64]{1,0:T(8,128)S(1)}, u32[]{:S(2)}, u32[]{:S(2)}) collective-permute-start(f32[144,64]{1,0:T(8,128)S(1)} %get-tuple-element.4), channel_id=1, source_target_pairs={{0,1},{1,2},{2,3},{3,4},{4,5},{5,6},{6,7},{7,8},{8,9},{9,10},{10,1... | collective-permute-start | bytes 110600 | tf_op jit(solution)/shard_map/ppermute | solution.py:95

commit v6 on v5

--- a/solution.py
+++ b/solution.py
@@ -82,6 +82,7 @@
 
 HALO_Y = 8
 HALO_Z = 8 * XS
+EXT_ROWS = HALO_Y
 SEND_Y = 8
 SEND_Z = 8 * XS
 
@@ -165,34 +166,8 @@
     )(x)
 
 
-def softmin_kernel(total_y, tile_ranges, with_rows_beyond, *refs):
-    if with_rows_beyond:
-        ft_ref, mt_ref, top_ref, bot_ref, n_ref, done_ref, o_ref, f_ref, m0_ref, m4_ref = refs
-    else:
-        ft_ref, mt_ref, n_ref, o_ref, f_ref, m0_ref, m4_ref = refs
-    height = ft_ref.shape[1]
-    lanes_total = ft_ref.shape[2]
-    rows = height + 2 * REACH
-
-    def build(c, carry):
-        f_ref[c] = ft_ref[c].astype(jnp.float32)
-        m0_ref[c, pl.ds(REACH, height), :] = mt_ref[c].astype(jnp.float32)
-        if with_rows_beyond:
-            m0_ref[c, pl.ds(0, REACH), :] = top_ref[c].astype(jnp.float32)
-            m0_ref[c, pl.ds(REACH + height, REACH), :] = bot_ref[c].astype(jnp.float32)
-        else:
-            m0_ref[c, pl.ds(0, REACH), :] = jnp.zeros((REACH, lanes_total), jnp.float32)
-            m0_ref[c, pl.ds(REACH + height, REACH), :] = jnp.zeros((REACH, lanes_total), jnp.float32)
-        return carry
-
-    lax.fori_loop(0, CH, build, 0)
-
-    def build_shifted(c, carry):
-        m4_ref[c, pl.ds(0, rows - 8), :] = m0_ref[c, pl.ds(4, rows - 8), :]
-        m4_ref[c, pl.ds(rows - 8, 8), :] = jnp.zeros((8, lanes_total), jnp.float32)
-        return carry
-
-    lax.fori_loop(0, CH, build_shifted, 0)
+def softmin_tiles(total_y, f_ref, m0_ref, m4_ref, n_ref, o_ref, tile_ranges):
+    lanes_total = f_ref.shape[2]
 
     def body(i, carry):
         t = i
@@ -228,14 +203,66 @@
                 shift_norm = 2.0 * float(4 * o - REACH) / total_y
                 den = w if den is None else den + w
                 num = w * shift_norm if num is None else num + w * shift_norm
-            o_ref[pl.ds(r0, 8), lanes] = num / den
+            o_ref[pl.ds(r0, 8), lanes] = jnp.where(den > 0.0, num / den, 0.0)
         return carry
 
     lax.fori_loop(0, sum(hi - lo for lo, hi in tile_ranges), body, 0)
-    if with_rows_beyond:
-        lo = tile_ranges[0][1] * 8
-        hi = tile_ranges[1][0] * 8
-        o_ref[pl.ds(lo, hi - lo), :] = done_ref[pl.ds(lo, hi - lo), :]
+
+
+def build_shifted(m0_ref, m4_ref):
+    rows = m0_ref.shape[1]
+
+    def step(c, carry):
+        m4_ref[c, pl.ds(0, rows - 8), :] = m0_ref[c, pl.ds(4, rows - 8), :]
+        m4_ref[c, pl.ds(rows - 8, 8), :] = jnp.zeros((8, m0_ref.shape[2]), jnp.float32)
+        return carry
+
+    lax.fori_loop(0, CH, step, 0)
+
+
+def softmin_middle_kernel(total_y, ft_ref, mt_ref, n_ref, o_ref, f_ref, m0_ref, m4_ref):
+    height = ft_ref.shape[1]
+    lanes_total = ft_ref.shape[2]
+
+    def build(c, carry):
+        f_ref[c] = ft_ref[c].astype(jnp.float32)
+        m0_ref[c, pl.ds(REACH, height), :] = mt_ref[c].astype(jnp.float32)
+        m0_ref[c, pl.ds(0, REACH), :] = jnp.zeros((REACH, lanes_total), jnp.float32)
+        m0_ref[c, pl.ds(REACH + height, REACH), :] = jnp.zeros((REACH, lanes_total), jnp.float32)
+        return carry
+
+    lax.fori_loop(0, CH, build, 0)
+    build_shifted(m0_ref, m4_ref)
+    tiles = height // 8
+    softmin_tiles(
+        total_y, f_ref, m0_ref, m4_ref, n_ref, o_ref, [(REACH // 8, tiles - REACH // 8)]
+    )
+
+
+def softmin_edge_kernel(
+    total_y, ft_ref, mt_ref, top_ref, bot_ref, n_ref, done_ref, ext_ref, o_ref, f_ref, m0_ref, m4_ref
+):
+    height = ft_ref.shape[1]
+    reach_rows = REACH + EXT_ROWS
+
+    def build(c, carry):
+        top = top_ref[c].astype(jnp.float32)
+        bot = bot_ref[c].astype(jnp.float32)
+        f_ref[c, pl.ds(0, EXT_ROWS), :] = top[reach_rows : reach_rows + EXT_ROWS]
+        f_ref[c, pl.ds(EXT_ROWS, height), :] = ft_ref[c].astype(jnp.float32)
+        f_ref[c, pl.ds(EXT_ROWS + height, EXT_ROWS), :] = bot[reach_rows : reach_rows + EXT_ROWS]
+        m0_ref[c, pl.ds(0, reach_rows), :] = top[:reach_rows]
+        m0_ref[c, pl.ds(reach_rows, height), :] = mt_ref[c].astype(jnp.float32)
+        m0_ref[c, pl.ds(reach_rows + height, reach_rows), :] = bot[:reach_rows]
+        return carry
+
+    lax.fori_loop(0, CH, build, 0)
+    build_shifted(m0_ref, m4_ref)
+    tiles = (height + 2 * EXT_ROWS) // 8
+    edge = reach_rows // 8
+    softmin_tiles(total_y, f_ref, m0_ref, m4_ref, n_ref, ext_ref, [(0, edge), (tiles - edge, tiles)])
+    ext_ref[pl.ds(reach_rows, height - 2 * REACH), :] = done_ref[pl.ds(REACH, height - 2 * REACH), :]
+    o_ref[...] = ext_ref[pl.ds(EXT_ROWS, height), :]
 
 
 def per_device(fixed_features, moving_features, cand_offsets, cand_lengths, smooth_radii):
@@ -250,21 +277,30 @@
     hits = (shifts[:, :, None] == offset_values[None, None, :]) & live[:, :, None]
     mult = jnp.sum(hits.astype(jnp.float32), axis=1)
     mult_rows = jnp.repeat(mult.T, 4, axis=1)
-    mult_rows = jnp.broadcast_to(mult_rows[:, :, None], (NOFF, height, 128))
+    lanes_n = 128
 
     gy_count = lax.axis_size("gy")
     fixed_c = channel_major(fixed_features)
     moving_c = channel_major(moving_features)
-    top_rows = lax.ppermute(
-        moving_c[:, height - REACH :], "gy", [(i, i + 1) for i in range(gy_count - 1)]
-    )
-    bottom_rows = lax.ppermute(
-        moving_c[:, :REACH], "gy", [(i + 1, i) for i in range(gy_count - 1)]
-    )
+    reach_rows = REACH + EXT_ROWS
+
+    def payload(moving_part, fixed_part, mult_part):
+        counts_part = jnp.pad(mult_part.T, ((0, 0), (0, columns_dev - NOFF)))
+        counts_part = jnp.zeros((CH, EXT_ROWS, columns_dev), jnp.float32).at[0].set(counts_part)
+        return jnp.concatenate(
+            [moving_part, fixed_part, counts_part.astype(moving_part.dtype)], axis=1
+        )
+
+    down = payload(
+        moving_c[:, height - reach_rows :],
+        fixed_c[:, height - EXT_ROWS :],
+        mult_rows[:, height - EXT_ROWS :],
+    )
+    up = payload(moving_c[:, :reach_rows], fixed_c[:, :EXT_ROWS], mult_rows[:, :EXT_ROWS])
+    top = lax.ppermute(down, "gy", [(i, i + 1) for i in range(gy_count - 1)])
+    bottom = lax.ppermute(up, "gy", [(i + 1, i) for i in range(gy_count - 1)])
 
     rows = height + 2 * REACH
-    tiles = height // 8
-    reach_tiles = REACH // 8
     scratch = [
         pltpu.VMEM((CH, height, columns_dev), jnp.float32),
         pltpu.VMEM((CH, rows, columns_dev), jnp.float32),
@@ -273,28 +309,40 @@
     params = pltpu.CompilerParams(vmem_limit_bytes=60 * 1024 * 1024)
     out_shape = jax.ShapeDtypeStruct((height, columns_dev), jnp.float32)
     middle = pl.pallas_call(
-        lambda *refs: softmin_kernel(total_y, [(reach_tiles, tiles - reach_tiles)], False, *refs),
+        lambda *refs: softmin_middle_kernel(total_y, *refs),
         out_shape=out_shape,
         scratch_shapes=scratch,
         compiler_params=params,
-    )(fixed_c, moving_c, mult_rows)
-    disp_init = pl.pallas_call(
-        lambda *refs: softmin_kernel(
-            total_y, [(0, reach_tiles), (tiles - reach_tiles, tiles)], True, *refs
-        ),
-        out_shape=out_shape,
-        scratch_shapes=scratch,
+    )(fixed_c, moving_c, jnp.broadcast_to(mult_rows[:, :, None], (NOFF, height, lanes_n)))
+
+    def counts_of(part):
+        return part[0, reach_rows + EXT_ROWS :, :NOFF].astype(jnp.float32).T
+
+    mult_ext = jnp.concatenate([counts_of(top), mult_rows, counts_of(bottom)], axis=1)
+    frame = height + 2 * EXT_ROWS
+    edge_scratch = [
+        pltpu.VMEM((CH, frame, columns_dev), jnp.float32),
+        pltpu.VMEM((CH, frame + 2 * REACH, columns_dev), jnp.float32),
+        pltpu.VMEM((CH, frame + 2 * REACH, columns_dev), jnp.float32),
+    ]
+    ext_y, disp_init = pl.pallas_call(
+        lambda *refs: softmin_edge_kernel(total_y, *refs),
+        out_shape=(jax.ShapeDtypeStruct((frame, columns_dev), jnp.float32), out_shape),
+        scratch_shapes=edge_scratch,
         compiler_params=params,
     )(
         fixed_c,
         moving_c,
-        top_rows,
-        bottom_rows,
-        mult_rows,
+        top,
+        bottom,
+        jnp.broadcast_to(mult_ext[:, :, None], (NOFF, frame, lanes_n)),
         middle,
     )
 
-    ext = exchange_halo(disp_init, HALO_Y, HALO_Z, SEND_Y, SEND_Z)
+    gz_count = lax.axis_size("gz")
+    left = lax.ppermute(ext_y[:, -HALO_Z:], "gz", [(i, i + 1) for i in range(gz_count - 1)])
+    right = lax.ppermute(ext_y[:, :HALO_Z], "gz", [(i + 1, i) for i in range(gz_count - 1)])
+    ext = jnp.concatenate([left, ext_y, right], axis=1)
     rows_ext, lanes_ext = ext.shape
     row_global = lax.axis_index("gy") * height - HALO_Y + lax.broadcasted_iota(
         jnp.int32, (rows_ext, lanes_ext), 0

time: 79.4 us -> 95 us (1.20); the launches traced: 77.8 us -> 94.6 us
  waiting for transfers between devices: 8.89 us -> 30.2 us
  starting transfers between devices: 23.6 us -> 13.4 us
  local copies, waits for them, and re-layouts: 4.39 us -> 6.53 us
  Pallas kernels: 37.9 us -> 39.8 us
  other arithmetic: 2.33 us -> 3.91 us
    ppermute x6 -> x4, waiting for transfers between devices: 8.89 us -> 30.2 us  [the longest x1 22.1 us: per_device(): top = lax.ppermute(down, 'gy', [(i, i + 1) for i in range(gy_count - 1)])]
    ppermute x6 -> x4, starting transfers between devices: 23.6 us -> 13.4 us  [the longest x1 3.92 us: per_device(): top = lax.ppermute(down, 'gy', [(i, i + 1) for i in range(gy_count - 1)])]
    pallas_call x2, Pallas kernels: 20.9 us -> 22.8 us  [the longest x1 12.5 us: per_device(): pl.pallas_call(lambda *refs: softmin_edge_kernel(total_y, *refs), out_sha...]
    broadcast_in_dim x2, local copies, waits for them, and re-layouts: 1.44 us -> 2.81 us  [the longest x1 1.44 us: per_device(): jnp.broadcast_to(mult_ext[:, :, None], (NOFF, frame, lanes_n))]
    slice x2 -> x3, local copies, waits for them, and re-layouts: 2.01 us -> 3.36 us  [the longest x1 1.37 us: per_device(): moving_c[:, :reach_rows]]
    concatenate x1 -> x4, other arithmetic: 1.13 us -> 2.3 us  [the longest x1 1.14 us: per_device(): ext = jnp.concatenate([left, ext_y, right], axis=1)]
    slice x1 -> x0, other arithmetic: 0.95 us -> none  [exchange_halo(): cells[:, -send_z:]]
  transfers between devices with their start and end apart: 6 -> 4, of which waited for: 4 -> 3; matrix products, arithmetic and copies ran while one was open for 2% -> 3% of each run, Pallas kernels for 19% -> 11%
where the time goes in v6:
time: 95 us; the launch traced here: 94.6 us
  Pallas kernels  39.8 us (42%)
  waiting for transfers between devices  30.2 us (32%)
  starting transfers between devices  13.4 us (14%)
  local copies, waits for them, and re-layouts  6.53 us (7%)
  other arithmetic  3.91 us (4%)
    ppermute x1, waiting for transfers between devices, per_device(): top = lax.ppermute(down, 'gy', [(i, i + 1) for i in range(gy_count - 1)])  22.1 us
    pallas_call x1, Pallas kernels, per_device(): pl.pallas_call(lambda *refs: softmin_edge_kernel(total_y, *refs), out_sha...  12.5 us
    pallas_call x1, Pallas kernels, per_device(): pl.pallas_call(lambda *refs: softmin_middle_kernel(total_y, *refs), out_s...  10.3 us
    pallas_call x2, Pallas kernels, channel_major(): pl.pallas_call(transpose_kernel, out_shape=jax.ShapeDtypeStruct((CH, rows...  9.72 us
    pallas_call x1, Pallas kernels, per_device(): pl.pallas_call(adam_kernel, out_shape=jax.ShapeDtypeStruct((height, colum...  7.22 us
    ppermute x1, waiting for transfers between devices, per_device(): lax.ppermute(ext_y[:, :HALO_Z], 'gz', [(i + 1, i) for i in range(gz_count...  4.51 us
    ppermute x1, starting transfers between devices, per_device(): top = lax.ppermute(down, 'gy', [(i, i + 1) for i in range(gy_count - 1)])  3.92 us
    ppermute x1, starting transfers between devices, per_device(): lax.ppermute(ext_y[:, -HALO_Z:], 'gz', [(i, i + 1) for i in range(gz_coun...  3.81 us
  transfers between devices with their start and end apart: 4, of which 3 were waited for; matrix products, arithmetic and copies ran while one was open for 3% of the time, Pallas kernels for 11%

profile of v6, /device:TPU:11, one launch (start us, length us, event | category | flops | bytes accessed | tf_op | source)
XLA Modules:
  0.0 94.6 jit_solution(10896048345622549207)
XLA Ops:
  0.6 0.7 iota_compare_fusion.1
  1.3 0.8 convert_reduce_fusion
  2.1 0.1 copy.15
  2.3 4.9 %shard_map.71.refs_0_ = bf16[16,128,512]{2,1,0:T(8,128)(2,1)} custom-call(bf16[128,8192]{1,0:T(8,128)(2,1)} %x_ref.2), custom_call_target="tpu_custom_call" | custom-call | tf_op jit(solution)/shard_map/pallas_call | solution.py:162
  7.1 1.0 %fusion.7 = (bf16[16,8,512]{2,1,0:T(8,128)(2,1)S(1)}, bf16[16,8,512]{2,1,0:T(8,128)(2,1)S(1)}) fusion(bf16[16,128,512]{2,1,0:T(8,128)(2,1)} %shard_map.71.refs_0_), kind=kLoop, calls=%fused_computation.24 | loop fusion | bytes 524288 | tf_op jit(solution)/shard_map/slice | solution.py:299
  8.1 4.9 %shard_map.72.refs_1_ = bf16[16,128,512]{2,1,0:T(8,128)(2,1)} custom-call(bf16[128,8192]{1,0:T(8,128)(2,1)} %x_ref.3), custom_call_target="tpu_custom_call" | custom-call | tf_op jit(solution)/shard_map/pallas_call | solution.py:162
  13.0 1.4 %fusion.6 = (bf16[16,40,512]{2,1,0:T(8,128)(2,1)S(1)}, bf16[16,40,512]{2,1,0:T(8,128)(2,1)S(1)}) fusion(bf16[16,128,512]{2,1,0:T(8,128)(2,1)} %shard_map.72.refs_1_), kind=kLoop, calls=%fused_computation.23 | loop fusion | bytes 2621440 | tf_op jit(solution)/shard_map/slice | solution.py:299
  14.3 0.1 fusion.2
  14.4 3.9 %collective-permute-start = (bf16[16,56,512]{2,1,0:T(8,128)(2,1)S(1)}, bf16[16,56,512]{2,1,0:T(8,128)(2,1)S(1)}, u32[]{:S(2)}, u32[]{:S(2)}) collective-permute-start(bf16[16,56,512]{2,1,0:T(8,128)(2,1)S(1)} %fusion.2), channel_id=1, source_target_pairs={{0,16},{16,32},{32,48},{48,64},{64,80},{80,96},{96,112},{1,17},{17... | collective-permute-start | bytes 2752520 | tf_op jit(solution)/shard_map/ppermute | solution.py:300
  18.4 1.0 %fusion.3 = bf16[16,56,512]{2,1,0:T(8,128)(2,1)} fusion(bf16[1,8,512]{2,1,0:T(8,128)(2,1)S(1)} %pad_bitcast_fusion, bf16[16,8,512]{2,1,0:T(8,128)(2,1)S(1)} %get-tuple-element.32, bf16[16,40,512]{2,1,0:T(8,128)(2,1)S(1)} %get-tuple-element.30), kind=kLoop, calls=%fused_computation.4 | loop fusion | flops 3670016 | bytes 1712128 | tf_op jit(solution)/shard_map/concatenate | solution.py:290
  19.4 3.7 %collective-permute-start.1 = (bf16[16,56,512]{2,1,0:T(8,128)(2,1)}, bf16[16,56,512]{2,1,0:T(8,128)(2,1)S(1)}, u32[]{:S(2)}, u32[]{:S(2)}) collective-permute-start(bf16[16,56,512]{2,1,0:T(8,128)(2,1)} %fusion.3), channel_id=1, source_target_pairs={{16,0},{32,16},{48,32},{64,48},{80,64},{96,80},{112,96},{17,1},{33... | collective-permute-start | bytes 2752520 | tf_op jit(solution)/shard_map/ppermute | solution.py:301
  23.1 0.1 copy.17
  23.2 1.4 %broadcast_in_dim.8.refs_2_ = f32[17,128,128]{2,1,0:T(8,128)} broadcast(f32[17,128]{1,0:T(8,128)S(1)} %copy.17), dimensions={0,1} | broadcast | bytes 1122816 | tf_op jit(solution)/shard_map/broadcast_in_dim | solution.py:316
  24.6 10.3 %shard_map.73.refs_5_ = f32[128,512]{1,0:T(8,128)} custom-call(bf16[16,128,512]{2,1,0:T(8,128)(2,1)} %shard_map.71.refs_0_, bf16[16,128,512]{2,1,0:T(8,128)(2,1)} %shard_map.72.refs_1_, f32[17,128,128]{2,1,0:T(8,128)} %broadcast_in_dim.8.refs_2_), custom_call_target="tpu_custom_call" | custom-call | tf_op jit(solution)/shard_map/pallas_call | solution.py:311
  34.9 22.1 %collective-permute-done.refs_2_ = bf16[16,56,512]{2,1,0:T(8,128)(2,1)S(1)} collective-permute-done((bf16[16,56,512]{2,1,0:T(8,128)(2,1)S(1)}, bf16[16,56,512]{2,1,0:T(8,128)(2,1)S(1)}, u32[]{:S(2)}, u32[]{:S(2)}) %collective-permute-start) | collective-permute-done | bytes 917536 | tf_op jit(solution)/shard_map/ppermute | solution.py:300
  57.0 0.0 copy-start.1
  57.0 0.1 copy.16
  57.1 3.5 %collective-permute-done.1.refs_3_ = bf16[16,56,512]{2,1,0:T(8,128)(2,1)S(1)} collective-permute-done((bf16[16,56,512]{2,1,0:T(8,128)(2,1)}, bf16[16,56,512]{2,1,0:T(8,128)(2,1)S(1)}, u32[]{:S(2)}, u32[]{:S(2)}) %collective-permute-start.1) | collective-permute-done | bytes 917536 | tf_op jit(solution)/shard_map/ppermute | solution.py:301
  60.6 0.0 copy-start.2
  60.7 0.1 copy.18
  60.7 0.1 pad_maximum_fusion.1
  60.8 1.4 %broadcast_in_dim.7.refs_4_ = f32[17,144,128]{2,1,0:T(8,128)} broadcast(f32[17,144]{1,0:T(8,128)S(1)} %pad_maximum_fusion.1), dimensions={0,1} | broadcast | bytes 1263168 | tf_op jit(solution)/shard_map/broadcast_in_dim | solution.py:338
  62.3 0.0 copy-done.1
  62.3 0.0 copy-done.2
  62.3 0.0 copy-start
  62.3 12.5 %shard_map.74 = (f32[144,512]{1,0:T(8,128)}, f32[128,512]{1,0:T(8,128)}) custom-call(bf16[16,128,512]{2,1,0:T(8,128)(2,1)} %shard_map.71.refs_0_, bf16[16,128,512]{2,1,0:T(8,128)(2,1)} %shard_map.72.refs_1_, bf16[16,56,512]{2,1,0:T(8,128)(2,1)} %copy-done.1, bf16[16,56,512]{2,1,0:T(8,128)(2,1)} %copy-done.2, f32[17,144,128]{2,1,0:T(8,128)} %broadcast_in_dim.7.refs_4_, ...), custom_call_target="tpu_custom_call" | custom-call | tf_op jit(solution)/shard_map/pallas_call | solution.py:328
  74.8 1.0 %fusion.8 = (f32[144,64]{1,0:T(8,128)S(1)}, f32[144,64]{1,0:T(8,128)S(1)}) fusion(f32[144,512]{1,0:T(8,128)} %get-tuple-element.29), kind=kLoop, calls=%fused_computation.25 | loop fusion | bytes 147456 | tf_op jit(solution)/shard_map/slice | solution.py:343
  75.8 3.8 %collective-permute-start.2 = (f32[144,64]{1,0:T(8,128)S(1)}, f32[144,64]{1,0:T(8,128)S(1)}, u32[]{:S(2)}, u32[]{:S(2)}) collective-permute-start(f32[144,64]{1,0:T(8,128)S(1)} %get-tuple-element.34), channel_id=1, source_target_pairs={{0,1},{1,2},{2,3},{3,4},{4,5},{5,6},{6,7},{7,8},{8,9},{9,10},{10,1... | collective-permute-start | bytes 110600 | tf_op jit(solution)/shard_map/ppermute | solution.py:343
  79.6 1.9 %collective-permute-start.3 = (f32[144,64]{1,0:T(8,128)S(1)}, f32[144,64]{1,0:T(8,128)S(1)}, u32[]{:S(2)}, u32[]{:S(2)}) collective-permute-start(f32[144,64]{1,0:T(8,128)S(1)} %get-tuple-element.35), channel_id=1, source_target_pairs={{1,0},{2,1},{3,2},{4,3},{5,4},{6,5},{7,6},{8,7},{9,8},{10,9},{11,1... | collective-permute-start | bytes 110600 | tf_op jit(solution)/shard_map/ppermute | solution.py:344
  81.6 0.1 and_convert_fusion.mask_ref
  81.7 0.0 collective-permute-done.2
  81.7 4.5 %collective-permute-done.3 = f32[144,64]{1,0:T(8,128)S(1)} collective-permute-done((f32[144,64]{1,0:T(8,128)S(1)}, f32[144,64]{1,0:T(8,128)S(1)}, u32[]{:S(2)}, u32[]{:S(2)}) %collective-permute-start.3) | collective-permute-done | bytes 36896 | tf_op jit(solution)/shard_map/ppermute | solution.py:344
  86.2 1.1 %pad_maximum_fusion.d_ref = f32[144,640]{1,0:T(8,128)S(1)} fusion(f32[144,64]{1,0:T(8,128)S(1)} %collective-permute-done.3, f32[144,512]{1,0:T(8,128)} %get-tuple-element.29, f32[144,64]{1,0:T(8,128)S(1)} %collective-permute-done.2), kind=kLoop, calls=%fused_computation.5 | loop fusion | flops 184320 | bytes 737280 | tf_op jit(solution)/shard_map/concatenate | solution.py:345
  87.4 0.0 copy-done
  87.4 7.2 %shard_map.75 = f32[128,512]{1,0:T(8,128)} custom-call(s32[3]{0:T(128)S(1)} %copy-done, f32[144,640]{1,0:T(8,128)S(1)} %pad_maximum_fusion.d_ref, f32[144,640]{1,0:T(8,128)S(1)} %and_convert_fusion.mask_ref), custom_call_target="tpu_custom_call" | custom-call | tf_op jit(solution)/shard_map/pallas_call | solution.py:360
  (10 shorter events, 0.1 us)
Async XLA Ops:
  14.4 42.6 %collective-permute-start = (bf16[16,56,512]{2,1,0:T(8,128)(2,1)S(1)}, bf16[16,56,512]{2,1,0:T(8,128)(2,1)S(1)}, u32[]{:S(2)}, u32[]{:S(2)}) collective-permute-start(bf16[16,56,512]{2,1,0:T(8,128)(2,1)S(1)} %fusion.2), channel_id=1, source_target_pairs={{0,16},{16,32},{32,48},{48,64},{64,80},{80,96},{96,112},{1,17},{17... | collective-permute-start | bytes 2752520 | tf_op jit(solution)/shard_map/ppermute | solution.py:300
  19.4 41.3 %collective-permute-start.1 = (bf16[16,56,512]{2,1,0:T(8,128)(2,1)}, bf16[16,56,512]{2,1,0:T(8,128)(2,1)S(1)}, u32[]{:S(2)}, u32[]{:S(2)}) collective-permute-start(bf16[16,56,512]{2,1,0:T(8,128)(2,1)} %fusion.3), channel_id=1, source_target_pairs={{16,0},{32,16},{48,32},{64,48},{80,64},{96,80},{112,96},{17,1},{33... | collective-permute-start | bytes 2752520 | tf_op jit(solution)/shard_map/ppermute | solution.py:301
  57.0 5.3 %copy-start.1 = (bf16[16,56,512]{2,1,0:T(8,128)(2,1)}, bf16[16,56,512]{2,1,0:T(8,128)(2,1)S(1)}, u32[]{:S(2)}) copy-start(bf16[16,56,512]{2,1,0:T(8,128)(2,1)S(1)} %collective-permute-done.refs_2_) | copy-start | bytes 2752516
  60.6 1.6 %copy-start.2 = (bf16[16,56,512]{2,1,0:T(8,128)(2,1)}, bf16[16,56,512]{2,1,0:T(8,128)(2,1)S(1)}, u32[]{:S(2)}) copy-start(bf16[16,56,512]{2,1,0:T(8,128)(2,1)S(1)} %collective-permute-done.1.refs_3_) | copy-start | bytes 2752516
  62.3 25.1 %copy-start = (s32[3]{0:T(128)S(1)}, s32[3]{0:T(128)}, u32[]{:S(2)}) copy-start(s32[3]{0:T(128)} %radii_ref.1) | copy-start | bytes 40
  75.8 5.9 %collective-permute-start.2 = (f32[144,64]{1,0:T(8,128)S(1)}, f32[144,64]{1,0:T(8,128)S(1)}, u32[]{:S(2)}, u32[]{:S(2)}) collective-permute-start(f32[144,64]{1,0:T(8,128)S(1)} %get-tuple-element.34), channel_id=1, source_target_pairs={{0,1},{1,2},{2,3},{3,4},{4,5},{5,6},{6,7},{7,8},{8,9},{9,10},{10,1... | collective-permute-start | bytes 110600 | tf_op jit(solution)/shard_map/ppermute | solution.py:343
  79.6 6.6 %collective-permute-start.3 = (f32[144,64]{1,0:T(8,128)S(1)}, f32[144,64]{1,0:T(8,128)S(1)}, u32[]{:S(2)}, u32[]{:S(2)}) collective-permute-start(f32[144,64]{1,0:T(8,128)S(1)} %get-tuple-element.35), channel_id=1, source_target_pairs={{1,0},{2,1},{3,2},{4,3},{5,4},{6,5},{7,6},{8,7},{9,8},{10,9},{11,1... | collective-permute-start | bytes 110600 | tf_op jit(solution)/shard_map/ppermute | solution.py:344

commit v7 on v5

--- a/solution.py
+++ b/solution.py
@@ -165,11 +165,62 @@
     )(x)
 
 
-def softmin_kernel(total_y, tile_ranges, with_rows_beyond, *refs):
-    if with_rows_beyond:
-        ft_ref, mt_ref, top_ref, bot_ref, n_ref, done_ref, o_ref, f_ref, m0_ref, m4_ref = refs
-    else:
-        ft_ref, mt_ref, n_ref, o_ref, f_ref, m0_ref, m4_ref = refs
+def softmin_tiles(total_y, f_ref, m0_ref, m4_ref, n_ref, o_ref, first, last):
+    lanes_total = f_ref.shape[2]
+
+    def body(t, carry):
+        r0 = pl.multiple_of(t * 8, 8)
+        for j in range(lanes_total // 128):
+            peak, den, num = offset_partial(
+                total_y, f_ref, m0_ref, m4_ref, n_ref, r0, range(NOFF), pl.ds(128 * j, 128)
+            )
+            o_ref[pl.ds(r0, 8), pl.ds(128 * j, 128)] = num / den
+        return carry
+
+    lax.fori_loop(first, last, body, 0)
+
+
+def offset_partial(total_y, f_ref, m0_ref, m4_ref, n_ref, r0, offsets, lanes):
+    fixed = [f_ref[c, pl.ds(r0, 8), lanes] for c in range(CH)]
+    scores = []
+    counts = []
+    for o in offsets:
+        shift = 4 * o
+        if shift % 8 == 0:
+            src, base = m0_ref, shift
+        else:
+            src, base = m4_ref, shift - 4
+        acc = None
+        for c in range(CH):
+            d = fixed[c] - src[c, pl.ds(r0 + base, 8), lanes]
+            acc = d * d if acc is None else acc + d * d
+        n_o = n_ref[o, pl.ds(r0, 8), :]
+        counts.append(n_o)
+        scores.append(jnp.where(n_o > 0.0, -acc / softmin_temp, -jnp.inf))
+    peak = scores[0]
+    for s in scores[1:]:
+        peak = jnp.maximum(peak, s)
+    base_score = jnp.where(peak == -jnp.inf, 0.0, peak)
+    den = None
+    num = None
+    for o, s, n_o in zip(offsets, scores, counts):
+        w = n_o * jnp.exp(s - base_score)
+        shift_norm = 2.0 * float(4 * o - REACH) / total_y
+        den = w if den is None else den + w
+        num = w * shift_norm if num is None else num + w * shift_norm
+    return peak, den, num
+
+
+def edge_tiles(height):
+    reach_tiles = REACH // 8
+    return list(range(reach_tiles)) + list(range(height // 8 - reach_tiles, height // 8))
+
+
+def halo_offsets(t, height):
+    return [o for o in range(NOFF) if 8 * t + 4 * o < REACH or 8 * t + 4 * o + 8 > height + REACH]
+
+
+def softmin_middle_kernel(total_y, ft_ref, mt_ref, n_ref, o_ref, pk_ref, dn_ref, nm_ref, f_ref, m0_ref, m4_ref):
     height = ft_ref.shape[1]
     lanes_total = ft_ref.shape[2]
     rows = height + 2 * REACH
@@ -177,65 +228,77 @@
     def build(c, carry):
         f_ref[c] = ft_ref[c].astype(jnp.float32)
         m0_ref[c, pl.ds(REACH, height), :] = mt_ref[c].astype(jnp.float32)
-        if with_rows_beyond:
-            m0_ref[c, pl.ds(0, REACH), :] = top_ref[c].astype(jnp.float32)
-            m0_ref[c, pl.ds(REACH + height, REACH), :] = bot_ref[c].astype(jnp.float32)
-        else:
-            m0_ref[c, pl.ds(0, REACH), :] = jnp.zeros((REACH, lanes_total), jnp.float32)
-            m0_ref[c, pl.ds(REACH + height, REACH), :] = jnp.zeros((REACH, lanes_total), jnp.float32)
-        return carry
-
-    lax.fori_loop(0, CH, build, 0)
-
-    def build_shifted(c, carry):
+        m0_ref[c, pl.ds(0, REACH), :] = jnp.zeros((REACH, lanes_total), jnp.float32)
+        m0_ref[c, pl.ds(REACH + height, REACH), :] = jnp.zeros((REACH, lanes_total), jnp.float32)
         m4_ref[c, pl.ds(0, rows - 8), :] = m0_ref[c, pl.ds(4, rows - 8), :]
         m4_ref[c, pl.ds(rows - 8, 8), :] = jnp.zeros((8, lanes_total), jnp.float32)
         return carry
 
-    lax.fori_loop(0, CH, build_shifted, 0)
-
-    def body(i, carry):
-        t = i
-        for lo, hi in tile_ranges[1:]:
-            t = jnp.where(t >= tile_ranges[0][1], t - tile_ranges[0][1] + lo, t)
-        t = t + tile_ranges[0][0]
-        r0 = pl.multiple_of(t * 8, 8)
-        for j in range(lanes_total // 128):
-            lanes = pl.ds(128 * j, 128)
-            fixed = [f_ref[c, pl.ds(r0, 8), lanes] for c in range(CH)]
-            scores = []
-            counts = []
-            for o in range(NOFF):
-                shift = 4 * o
-                if shift % 8 == 0:
-                    src, base = m0_ref, shift
-                else:
-                    src, base = m4_ref, shift - 4
-                acc = None
-                for c in range(CH):
-                    d = fixed[c] - src[c, pl.ds(r0 + base, 8), lanes]
-                    acc = d * d if acc is None else acc + d * d
-                n_o = n_ref[o, pl.ds(r0, 8), :]
-                counts.append(n_o)
-                scores.append(jnp.where(n_o > 0.0, -acc / softmin_temp, -jnp.inf))
-            peak = scores[0]
-            for s in scores[1:]:
-                peak = jnp.maximum(peak, s)
-            den = None
-            num = None
-            for o in range(NOFF):
-                w = counts[o] * jnp.exp(scores[o] - peak)
-                shift_norm = 2.0 * float(4 * o - REACH) / total_y
-                den = w if den is None else den + w
-                num = w * shift_norm if num is None else num + w * shift_norm
-            o_ref[pl.ds(r0, 8), lanes] = num / den
+    lax.fori_loop(0, CH, build, 0)
+    tiles = height // 8
+    softmin_tiles(total_y, f_ref, m0_ref, m4_ref, n_ref, o_ref, REACH // 8, tiles - REACH // 8)
+    for t in edge_tiles(height):
+        beyond = halo_offsets(t, height)
+        inner = [o for o in range(NOFF) if o not in beyond]
+
+        def part(j, carry, t=t, inner=inner):
+            lanes = pl.ds(pl.multiple_of(j * 128, 128), 128)
+            peak, den, num = offset_partial(
+                total_y, f_ref, m0_ref, m4_ref, n_ref, 8 * t, inner, lanes
+            )
+            pk_ref[pl.ds(8 * t, 8), lanes] = peak
+            dn_ref[pl.ds(8 * t, 8), lanes] = den
+            nm_ref[pl.ds(8 * t, 8), lanes] = num
+            return carry
+
+        lax.fori_loop(0, lanes_total // 128, part, 0)
+
+
+def softmin_edge_kernel(
+    total_y, ft_ref, mt_ref, top_ref, bot_ref, n_ref, done_ref, pk_ref, dn_ref, nm_ref,
+    o_ref, f_ref, m0_ref, m4_ref,
+):
+    height = ft_ref.shape[1]
+    lanes_total = ft_ref.shape[2]
+    rows = height + 2 * REACH
+    span = REACH + 16
+
+    def build(c, carry):
+        f_ref[c, pl.ds(0, REACH), :] = ft_ref[c, pl.ds(0, REACH), :].astype(jnp.float32)
+        f_ref[c, pl.ds(height - REACH, REACH), :] = ft_ref[c, pl.ds(height - REACH, REACH), :].astype(
+            jnp.float32
+        )
+        m0_ref[c, pl.ds(0, REACH), :] = top_ref[c].astype(jnp.float32)
+        m0_ref[c, pl.ds(REACH, 16), :] = mt_ref[c, pl.ds(0, 16), :].astype(jnp.float32)
+        m0_ref[c, pl.ds(rows - span, 16), :] = mt_ref[c, pl.ds(height - 16, 16), :].astype(jnp.float32)
+        m0_ref[c, pl.ds(rows - REACH, REACH), :] = bot_ref[c].astype(jnp.float32)
+        m4_ref[c, pl.ds(0, span - 8), :] = m0_ref[c, pl.ds(4, span - 8), :]
+        m4_ref[c, pl.ds(rows - span, span - 8), :] = m0_ref[c, pl.ds(rows - span + 4, span - 8), :]
+        m4_ref[c, pl.ds(rows - 8, 8), :] = jnp.zeros((8, lanes_total), jnp.float32)
         return carry
 
-    lax.fori_loop(0, sum(hi - lo for lo, hi in tile_ranges), body, 0)
-    if with_rows_beyond:
-        lo = tile_ranges[0][1] * 8
-        hi = tile_ranges[1][0] * 8
-        o_ref[pl.ds(lo, hi - lo), :] = done_ref[pl.ds(lo, hi - lo), :]
+    lax.fori_loop(0, CH, build, 0)
+    for t in edge_tiles(height):
+        beyond = halo_offsets(t, height)
+
+        def part(j, carry, t=t, beyond=beyond):
+            lanes = pl.ds(pl.multiple_of(j * 128, 128), 128)
+            rows_t = pl.ds(8 * t, 8)
+            peak, den, num = offset_partial(
+                total_y, f_ref, m0_ref, m4_ref, n_ref, 8 * t, beyond, lanes
+            )
+            peak_in = pk_ref[rows_t, lanes]
+            top_score = jnp.maximum(peak, peak_in)
+            scale = jnp.exp(peak - top_score)
+            scale_in = jnp.exp(peak_in - top_score)
+            den = den * scale + dn_ref[rows_t, lanes] * scale_in
+            num = num * scale + nm_ref[rows_t, lanes] * scale_in
+            o_ref[rows_t, lanes] = num / den
+            return carry
+
+        lax.fori_loop(0, lanes_total // 128, part, 0)
+    middle_rows = pl.ds(REACH, height - 2 * REACH)
+    o_ref[middle_rows, :] = done_ref[middle_rows, :]
 
 
 def per_device(fixed_features, moving_features, cand_offsets, cand_lengths, smooth_radii):
@@ -250,7 +313,6 @@
     hits = (shifts[:, :, None] == offset_values[None, None, :]) & live[:, :, None]
     mult = jnp.sum(hits.astype(jnp.float32), axis=1)
     mult_rows = jnp.repeat(mult.T, 4, axis=1)
-    mult_rows = jnp.broadcast_to(mult_rows[:, :, None], (NOFF, height, 128))
 
     gy_count = lax.axis_size("gy")
     fixed_c = channel_major(fixed_features)
@@ -272,16 +334,15 @@
     ]
     params = pltpu.CompilerParams(vmem_limit_bytes=60 * 1024 * 1024)
     out_shape = jax.ShapeDtypeStruct((height, columns_dev), jnp.float32)
-    middle = pl.pallas_call(
-        lambda *refs: softmin_kernel(total_y, [(reach_tiles, tiles - reach_tiles)], False, *refs),
-        out_shape=out_shape,
+    n_lanes = jnp.broadcast_to(mult_rows[:, :, None], (NOFF, height, 128))
+    middle, peak_part, den_part, num_part = pl.pallas_call(
+        lambda *refs: softmin_middle_kernel(total_y, *refs),
+        out_shape=(out_shape, out_shape, out_shape, out_shape),
         scratch_shapes=scratch,
         compiler_params=params,
-    )(fixed_c, moving_c, mult_rows)
+    )(fixed_c, moving_c, n_lanes)
     disp_init = pl.pallas_call(
-        lambda *refs: softmin_kernel(
-            total_y, [(0, reach_tiles), (tiles - reach_tiles, tiles)], True, *refs
-        ),
+        lambda *refs: softmin_edge_kernel(total_y, *refs),
         out_shape=out_shape,
         scratch_shapes=scratch,
         compiler_params=params,
@@ -290,8 +351,11 @@
         moving_c,
         top_rows,
         bottom_rows,
-        mult_rows,
+        n_lanes,
         middle,
+        peak_part,
+        den_part,
+        num_part,
     )
 
     ext = exchange_halo(disp_init, HALO_Y, HALO_Z, SEND_Y, SEND_Z)

time: 79.4 us -> 76.3 us (0.961)
  the two profiles are of different devices: /device:TPU:11 before, /device:TPU:38 now
where the time goes in v7:
time: 76.3 us; the launch traced here: 76.1 us
  Pallas kernels  39.3 us (52%)
  starting transfers between devices  19.9 us (26%)
  waiting for transfers between devices  9.17 us (12%)
  local copies, waits for them, and re-layouts  4.55 us (6%)
  other arithmetic  2.33 us (3%)
  between operations  0.8 us (1%)
    pallas_call x1, Pallas kernels, per_device(): pl.pallas_call(lambda *refs: softmin_middle_kernel(total_y, *refs), out_s...  15.4 us
    pallas_call x2, Pallas kernels, channel_major(): pl.pallas_call(transpose_kernel, out_shape=jax.ShapeDtypeStruct((CH, rows...  9.71 us
    pallas_call x1, Pallas kernels, per_device(): pl.pallas_call(lambda *refs: softmin_edge_kernel(total_y, *refs), out_sha...  7.16 us
    pallas_call x1, Pallas kernels, per_device(): pl.pallas_call(adam_kernel, out_shape=jax.ShapeDtypeStruct((height, colum...  7.02 us
    ppermute x1, waiting for transfers between devices, exchange_halo(): lax.ppermute(cells[-send_y:], 'gy', [(i, i + 1) for i in range(ny - 1)])  5.13 us
    ppermute x1, starting transfers between devices, per_device(): lax.ppermute(moving_c[:, height - REACH:], 'gy', [(i, i + 1) for i in ran...  5.1 us
    ppermute x1, starting transfers between devices, exchange_halo(): lax.ppermute(cells[:send_y], 'gy', [(i + 1, i) for i in range(ny - 1)])  4.46 us
    ppermute x1, waiting for transfers between devices, exchange_halo(): lax.ppermute(cells[:, -send_z:], 'gz', [(i, i + 1) for i in range(nz - 1)])  4.03 us
  transfers between devices with their start and end apart: 6, of which 2 were waited for; matrix products, arithmetic and copies ran while one was open for 2% of the time, Pallas kernels for 27%

profile of v7, /device:TPU:38, one launch (start us, length us, event | category | flops | bytes accessed | tf_op | source)
XLA Modules:
  0.0 76.1 jit_solution(13307048054157060332)
XLA Ops:
  0.6 4.8 %shard_map.72.refs_1_ = bf16[16,128,512]{2,1,0:T(8,128)(2,1)} custom-call(bf16[128,8192]{1,0:T(8,128)(2,1)} %x_ref.3), custom_call_target="tpu_custom_call" | custom-call | tf_op jit(solution)/shard_map/pallas_call | solution.py:161
  5.5 1.3 %fusion.2 = (bf16[16,32,512]{2,1,0:T(8,128)(2,1)S(1)}, bf16[16,32,512]{2,1,0:T(8,128)(2,1)S(1)}) fusion(bf16[16,128,512]{2,1,0:T(8,128)(2,1)} %shard_map.72.refs_1_), kind=kLoop, calls=%fused_computation.12 | loop fusion | bytes 2097152 | tf_op jit(solution)/shard_map/slice | solution.py:324
  6.8 5.1 %collective-permute-start = (bf16[16,32,512]{2,1,0:T(8,128)(2,1)S(1)}, bf16[16,32,512]{2,1,0:T(8,128)(2,1)S(1)}, u32[]{:S(2)}, u32[]{:S(2)}) collective-permute-start(bf16[16,32,512]{2,1,0:T(8,128)(2,1)S(1)} %get-tuple-element.11), channel_id=1, source_target_pairs={{0,16},{16,32},{32,48},{48,64},{64,80},{80,96},{96,112},{1,17},{17... | collective-permute-start | bytes 1572872 | tf_op jit(solution)/shard_map/ppermute | solution.py:320
  11.9 3.1 %collective-permute-start.1 = (bf16[16,32,512]{2,1,0:T(8,128)(2,1)S(1)}, bf16[16,32,512]{2,1,0:T(8,128)(2,1)S(1)}, u32[]{:S(2)}, u32[]{:S(2)}) collective-permute-start(bf16[16,32,512]{2,1,0:T(8,128)(2,1)S(1)} %get-tuple-element.10), channel_id=1, source_target_pairs={{16,0},{32,16},{48,32},{64,48},{80,64},{96,80},{112,96},{17,1},{33... | collective-permute-start | bytes 1572872 | tf_op jit(solution)/shard_map/ppermute | solution.py:323
  15.0 0.0 copy-start.4
  15.0 0.0 copy-start.3
  15.0 4.9 %shard_map.71.refs_0_ = bf16[16,128,512]{2,1,0:T(8,128)(2,1)} custom-call(bf16[128,8192]{1,0:T(8,128)(2,1)} %x_ref.2), custom_call_target="tpu_custom_call" | custom-call | tf_op jit(solution)/shard_map/pallas_call | solution.py:161
  19.9 0.0 copy-done.4
  19.9 0.0 copy-done.3
  19.9 0.1 convert_reduce_fusion
  20.1 0.1 copy.10
  20.2 0.1 copy.11
  20.2 1.4 %broadcast_in_dim.15.refs_2_.refs_4_ = f32[17,128,128]{2,1,0:T(8,128)} broadcast(f32[17,128]{1,0:T(8,128)S(1)} %copy.11), dimensions={0,1} | broadcast | bytes 1122816 | tf_op jit(solution)/shard_map/broadcast_in_dim | solution.py:337
  21.6 15.4 %shard_map.73 = (f32[128,512]{1,0:T(8,128)}, f32[128,512]{1,0:T(8,128)}, f32[128,512]{1,0:T(8,128)}, f32[128,512]{1,0:T(8,128)}) custom-call(bf16[16,128,512]{2,1,0:T(8,128)(2,1)} %shard_map.71.refs_0_, bf16[16,128,512]{2,1,0:T(8,128)(2,1)} %shard_map.72.refs_1_, f32[17,128,128]{2,1,0:T(8,128)} %broadcast_in_dim.15.refs_2_.refs_4_), custom_call_target="tpu_custom_call" | custom-call | tf_op jit(solution)/shard_map/pallas_call | solution.py:338
  37.0 0.0 collective-permute-done.refs_2_
  37.0 0.0 copy-start.1
  37.0 0.0 collective-permute-done.1.refs_3_
  37.0 0.0 copy-start.2
  37.1 0.8 %copy-done.1 = bf16[16,32,512]{2,1,0:T(8,128)(2,1)} copy-done((bf16[16,32,512]{2,1,0:T(8,128)(2,1)}, bf16[16,32,512]{2,1,0:T(8,128)(2,1)S(1)}, u32[]{:S(2)}) %copy-start.1) | copy-done | bytes 524312
  37.9 0.2 copy-done.2
  38.0 0.0 copy-start
  38.0 7.2 %shard_map.74 = f32[128,512]{1,0:T(8,128)} custom-call(bf16[16,128,512]{2,1,0:T(8,128)(2,1)} %shard_map.71.refs_0_, bf16[16,128,512]{2,1,0:T(8,128)(2,1)} %shard_map.72.refs_1_, bf16[16,32,512]{2,1,0:T(8,128)(2,1)} %copy-done.1, bf16[16,32,512]{2,1,0:T(8,128)(2,1)} %copy-done.2, f32[17,128,128]{2,1,0:T(8,128)} %broadcast_in_dim.15.refs_2_.refs_4_, ...), custom_call_target="tpu_custom_call" | custom-call | tf_op jit(solution)/shard_map/pallas_call | solution.py:344
  45.2 0.7 fusion.3
  45.9 4.5 %collective-permute-start.3 = (f32[8,512]{1,0:T(8,128)S(1)}, f32[8,512]{1,0:T(8,128)S(1)}, u32[]{:S(2)}, u32[]{:S(2)}) collective-permute-start(f32[8,512]{1,0:T(8,128)S(1)} %get-tuple-element.15), channel_id=1, source_target_pairs={{16,0},{32,16},{48,32},{64,48},{80,64},{96,80},{112,96},{17,1},{33... | collective-permute-start | bytes 49160 | tf_op jit(solution)/shard_map/ppermute | solution.py:93
  50.4 2.9 %collective-permute-start.2 = (f32[8,512]{1,0:T(8,128)S(1)}, f32[8,512]{1,0:T(8,128)S(1)}, u32[]{:S(2)}, u32[]{:S(2)}) collective-permute-start(f32[8,512]{1,0:T(8,128)S(1)} %get-tuple-element.14), channel_id=1, source_target_pairs={{0,16},{16,32},{32,48},{48,64},{64,80},{80,96},{96,112},{1,17},{17... | collective-permute-start | bytes 49160 | tf_op jit(solution)/shard_map/ppermute | solution.py:92
  53.3 0.0 collective-permute-done.3
  53.3 5.1 %collective-permute-done.2 = f32[8,512]{1,0:T(8,128)S(1)} collective-permute-done((f32[8,512]{1,0:T(8,128)S(1)}, f32[8,512]{1,0:T(8,128)S(1)}, u32[]{:S(2)}, u32[]{:S(2)}) %collective-permute-start.2) | collective-permute-done | bytes 16416 | tf_op jit(solution)/shard_map/ppermute | solution.py:92
  58.4 1.0 %pad_maximum_fusion.3 = (f32[144,64]{1,0:T(8,128)S(1)}, f32[144,64]{1,0:T(8,128)S(1)}) fusion(f32[8,512]{1,0:T(8,128)S(1)} %collective-permute-done.3, f32[128,512]{1,0:T(8,128)} %shard_map.74, f32[8,512]{1,0:T(8,128)S(1)} %collective-permute-done.2), kind=kLoop, calls=%fused_computation.5 | loop fusion | flops 36864 | bytes 368640 | tf_op jit(solution)/shard_map/slice | solution.py:95
  59.4 1.9 %collective-permute-start.5 = (f32[144,64]{1,0:T(8,128)S(1)}, f32[144,64]{1,0:T(8,128)S(1)}, u32[]{:S(2)}, u32[]{:S(2)}) collective-permute-start(f32[144,64]{1,0:T(8,128)S(1)} %get-tuple-element.13), channel_id=1, source_target_pairs={{1,0},{2,1},{3,2},{4,3},{5,4},{6,5},{7,6},{8,7},{9,8},{10,9},{11,1... | collective-permute-start | bytes 110600 | tf_op jit(solution)/shard_map/ppermute | solution.py:96
  61.3 2.4 %collective-permute-start.4 = (f32[144,64]{1,0:T(8,128)S(1)}, f32[144,64]{1,0:T(8,128)S(1)}, u32[]{:S(2)}, u32[]{:S(2)}) collective-permute-start(f32[144,64]{1,0:T(8,128)S(1)} %get-tuple-element.12), channel_id=1, source_target_pairs={{0,1},{1,2},{2,3},{3,4},{4,5},{5,6},{6,7},{7,8},{8,9},{9,10},{10,1... | collective-permute-start | bytes 110600 | tf_op jit(solution)/shard_map/ppermute | solution.py:95
  63.7 0.1 and_convert_fusion.mask_ref
  63.9 0.0 collective-permute-done.5
  63.9 4.0 %collective-permute-done.4 = f32[144,64]{1,0:T(8,128)S(1)} collective-permute-done((f32[144,64]{1,0:T(8,128)S(1)}, f32[144,64]{1,0:T(8,128)S(1)}, u32[]{:S(2)}, u32[]{:S(2)}) %collective-permute-start.4) | collective-permute-done | bytes 36896 | tf_op jit(solution)/shard_map/ppermute | solution.py:95
  67.9 1.1 %pad_maximum_fusion.d_ref = f32[144,640]{1,0:T(8,128)S(1)} fusion(f32[144,64]{1,0:T(8,128)S(1)} %collective-permute-done.5, f32[8,512]{1,0:T(8,128)S(1)} %collective-permute-done.3, f32[128,512]{1,0:T(8,128)} %shard_map.74, f32[8,512]{1,0:T(8,128)S(1)} %collective-permute-done.2, f32[144,64]{1,0:T(8,128)S(1)} %collective-permute-done.4), kind=kLoop, calls=%fused_computation | loop fusion | flops 368640 | bytes 737280 | tf_op jit(solution)/shard_map/concatenate | solution.py:97
  69.0 0.0 copy-done
  69.0 7.0 %shard_map.75 = f32[128,512]{1,0:T(8,128)} custom-call(s32[3]{0:T(128)S(1)} %copy-done, f32[144,640]{1,0:T(8,128)S(1)} %pad_maximum_fusion.d_ref, f32[144,640]{1,0:T(8,128)S(1)} %and_convert_fusion.mask_ref), custom_call_target="tpu_custom_call" | custom-call | tf_op jit(solution)/shard_map/pallas_call | solution.py:376
  (5 shorter events, 0.0 us)
Async XLA Ops:
  6.8 30.3 %collective-permute-start = (bf16[16,32,512]{2,1,0:T(8,128)(2,1)S(1)}, bf16[16,32,512]{2,1,0:T(8,128)(2,1)S(1)}, u32[]{:S(2)}, u32[]{:S(2)}) collective-permute-start(bf16[16,32,512]{2,1,0:T(8,128)(2,1)S(1)} %get-tuple-element.11), channel_id=1, source_target_pairs={{0,16},{16,32},{32,48},{48,64},{64,80},{80,96},{96,112},{1,17},{17... | collective-permute-start | bytes 1572872 | tf_op jit(solution)/shard_map/ppermute | solution.py:320
  11.9 25.2 %collective-permute-start.1 = (bf16[16,32,512]{2,1,0:T(8,128)(2,1)S(1)}, bf16[16,32,512]{2,1,0:T(8,128)(2,1)S(1)}, u32[]{:S(2)}, u32[]{:S(2)}) collective-permute-start(bf16[16,32,512]{2,1,0:T(8,128)(2,1)S(1)} %get-tuple-element.10), channel_id=1, source_target_pairs={{16,0},{32,16},{48,32},{64,48},{80,64},{96,80},{112,96},{17,1},{33... | collective-permute-start | bytes 1572872 | tf_op jit(solution)/shard_map/ppermute | solution.py:323
  15.0 4.9 %copy-start.4 = (s32[32,1]{0,1:T(1,128)S(1)}, s32[32,1]{0,1:T(1,128)}, u32[]{:S(2)}) copy-start(s32[32,1]{0,1:T(1,128)} %param.8) | copy-start | bytes 388
  15.0 4.9 %copy-start.3 = (s32[32,1,16]{0,2,1:T(8,128)S(1)}, s32[32,1,16]{0,2,1:T(8,128)}, u32[]{:S(2)}) copy-start(s32[32,1,16]{0,2,1:T(8,128)} %param.7) | copy-start | bytes 6148
  37.0 0.8 %copy-start.1 = (bf16[16,32,512]{2,1,0:T(8,128)(2,1)}, bf16[16,32,512]{2,1,0:T(8,128)(2,1)S(1)}, u32[]{:S(2)}) copy-start(bf16[16,32,512]{2,1,0:T(8,128)(2,1)S(1)} %collective-permute-done.refs_2_) | copy-start | bytes 1572868
  37.0 1.0 %copy-start.2 = (bf16[16,32,512]{2,1,0:T(8,128)(2,1)}, bf16[16,32,512]{2,1,0:T(8,128)(2,1)S(1)}, u32[]{:S(2)}) copy-start(bf16[16,32,512]{2,1,0:T(8,128)(2,1)S(1)} %collective-permute-done.1.refs_3_) | copy-start | bytes 1572868
  38.0 31.0 %copy-start = (s32[3]{0:T(128)S(1)}, s32[3]{0:T(128)}, u32[]{:S(2)}) copy-start(s32[3]{0:T(128)} %radii_ref.1) | copy-start | bytes 40
  45.9 7.4 %collective-permute-start.3 = (f32[8,512]{1,0:T(8,128)S(1)}, f32[8,512]{1,0:T(8,128)S(1)}, u32[]{:S(2)}, u32[]{:S(2)}) collective-permute-start(f32[8,512]{1,0:T(8,128)S(1)} %get-tuple-element.15), channel_id=1, source_target_pairs={{16,0},{32,16},{48,32},{64,48},{80,64},{96,80},{112,96},{17,1},{33... | collective-permute-start | bytes 49160 | tf_op jit(solution)/shard_map/ppermute | solution.py:93
  50.4 8.0 %collective-permute-start.2 = (f32[8,512]{1,0:T(8,128)S(1)}, f32[8,512]{1,0:T(8,128)S(1)}, u32[]{:S(2)}, u32[]{:S(2)}) collective-permute-start(f32[8,512]{1,0:T(8,128)S(1)} %get-tuple-element.14), channel_id=1, source_target_pairs={{0,16},{16,32},{32,48},{48,64},{64,80},{80,96},{96,112},{1,17},{17... | collective-permute-start | bytes 49160 | tf_op jit(solution)/shard_map/ppermute | solution.py:92
  59.4 4.5 %collective-permute-start.5 = (f32[144,64]{1,0:T(8,128)S(1)}, f32[144,64]{1,0:T(8,128)S(1)}, u32[]{:S(2)}, u32[]{:S(2)}) collective-permute-start(f32[144,64]{1,0:T(8,128)S(1)} %get-tuple-element.13), channel_id=1, source_target_pairs={{1,0},{2,1},{3,2},{4,3},{5,4},{6,5},{7,6},{8,7},{9,8},{10,9},{11,1... | collective-permute-start | bytes 110600 | tf_op jit(solution)/shard_map/ppermute | solution.py:96
  61.3 6.6 %collective-permute-start.4 = (f32[144,64]{1,0:T(8,128)S(1)}, f32[144,64]{1,0:T(8,128)S(1)}, u32[]{:S(2)}, u32[]{:S(2)}) collective-permute-start(f32[144,64]{1,0:T(8,128)S(1)} %get-tuple-element.12), channel_id=1, source_target_pairs={{0,1},{1,2},{2,3},{3,4},{4,5},{5,6},{6,7},{7,8},{8,9},{9,10},{10,1... | collective-permute-start | bytes 110600 | tf_op jit(solution)/shard_map/ppermute | solution.py:95

commit v8 on v7

--- a/solution.py
+++ b/solution.py
@@ -165,14 +165,20 @@
     )(x)
 
 
+def block_counts(n_ref, t, offsets):
+    upper = lax.broadcasted_iota(jnp.int32, (8, 128), 0) < 4
+    return [jnp.where(upper, n_ref[2 * t, o], n_ref[2 * t + 1, o]) for o in offsets]
+
+
 def softmin_tiles(total_y, f_ref, m0_ref, m4_ref, n_ref, o_ref, first, last):
     lanes_total = f_ref.shape[2]
 
     def body(t, carry):
         r0 = pl.multiple_of(t * 8, 8)
+        counts = block_counts(n_ref, t, range(NOFF))
         for j in range(lanes_total // 128):
             peak, den, num = offset_partial(
-                total_y, f_ref, m0_ref, m4_ref, n_ref, r0, range(NOFF), pl.ds(128 * j, 128)
+                total_y, f_ref, m0_ref, m4_ref, counts, r0, range(NOFF), pl.ds(128 * j, 128)
             )
             o_ref[pl.ds(r0, 8), pl.ds(128 * j, 128)] = num / den
         return carry
@@ -180,11 +186,10 @@
     lax.fori_loop(first, last, body, 0)
 
 
-def offset_partial(total_y, f_ref, m0_ref, m4_ref, n_ref, r0, offsets, lanes):
+def offset_partial(total_y, f_ref, m0_ref, m4_ref, counts, r0, offsets, lanes):
     fixed = [f_ref[c, pl.ds(r0, 8), lanes] for c in range(CH)]
     scores = []
-    counts = []
-    for o in offsets:
+    for o, n_o in zip(offsets, counts):
         shift = 4 * o
         if shift % 8 == 0:
             src, base = m0_ref, shift
@@ -194,8 +199,6 @@
         for c in range(CH):
             d = fixed[c] - src[c, pl.ds(r0 + base, 8), lanes]
             acc = d * d if acc is None else acc + d * d
-        n_o = n_ref[o, pl.ds(r0, 8), :]
-        counts.append(n_o)
         scores.append(jnp.where(n_o > 0.0, -acc / softmin_temp, -jnp.inf))
     peak = scores[0]
     for s in scores[1:]:
@@ -216,11 +219,15 @@
     return list(range(reach_tiles)) + list(range(height // 8 - reach_tiles, height // 8))
 
 
+def edge_row(t, height):
+    return 8 * t if 8 * t < REACH else 8 * t - (height - 2 * REACH)
+
+
 def halo_offsets(t, height):
     return [o for o in range(NOFF) if 8 * t + 4 * o < REACH or 8 * t + 4 * o + 8 > height + REACH]
 
 
-def softmin_middle_kernel(total_y, ft_ref, mt_ref, n_ref, o_ref, pk_ref, dn_ref, nm_ref, f_ref, m0_ref, m4_ref):
+def softmin_middle_kernel(total_y, n_ref, ft_ref, mt_ref, o_ref, pk_ref, dn_ref, nm_ref, f_ref, m0_ref, m4_ref):
     height = ft_ref.shape[1]
     lanes_total = ft_ref.shape[2]
     rows = height + 2 * REACH
@@ -240,37 +247,39 @@
     for t in edge_tiles(height):
         beyond = halo_offsets(t, height)
         inner = [o for o in range(NOFF) if o not in beyond]
-
-        def part(j, carry, t=t, inner=inner):
+        row = edge_row(t, height)
+
+        def part(j, carry, t=t, inner=inner, row=row):
             lanes = pl.ds(pl.multiple_of(j * 128, 128), 128)
+            counts = block_counts(n_ref, t, inner)
             peak, den, num = offset_partial(
-                total_y, f_ref, m0_ref, m4_ref, n_ref, 8 * t, inner, lanes
+                total_y, f_ref, m0_ref, m4_ref, counts, 8 * t, inner, lanes
             )
-            pk_ref[pl.ds(8 * t, 8), lanes] = peak
-            dn_ref[pl.ds(8 * t, 8), lanes] = den
-            nm_ref[pl.ds(8 * t, 8), lanes] = num
+            pk_ref[pl.ds(row, 8), lanes] = peak
+            dn_ref[pl.ds(row, 8), lanes] = den
+            nm_ref[pl.ds(row, 8), lanes] = num
             return carry
 
         lax.fori_loop(0, lanes_total // 128, part, 0)
 
 
 def softmin_edge_kernel(
-    total_y, ft_ref, mt_ref, top_ref, bot_ref, n_ref, done_ref, pk_ref, dn_ref, nm_ref,
-    o_ref, f_ref, m0_ref, m4_ref,
+    total_y, n_ref, fe_ref, me_ref, top_ref, bot_ref, pk_ref, dn_ref, nm_ref, _,
+    o_hbm, f_ref, m0_ref, m4_ref, res_ref, sem,
 ):
-    height = ft_ref.shape[1]
-    lanes_total = ft_ref.shape[2]
+    height = o_hbm.shape[0]
+    lanes_total = fe_ref.shape[2]
     rows = height + 2 * REACH
     span = REACH + 16
 
     def build(c, carry):
-        f_ref[c, pl.ds(0, REACH), :] = ft_ref[c, pl.ds(0, REACH), :].astype(jnp.float32)
-        f_ref[c, pl.ds(height - REACH, REACH), :] = ft_ref[c, pl.ds(height - REACH, REACH), :].astype(
+        f_ref[c, pl.ds(0, REACH), :] = fe_ref[c, pl.ds(0, REACH), :].astype(jnp.float32)
+        f_ref[c, pl.ds(height - REACH, REACH), :] = fe_ref[c, pl.ds(REACH, REACH), :].astype(
             jnp.float32
         )
         m0_ref[c, pl.ds(0, REACH), :] = top_ref[c].astype(jnp.float32)
-        m0_ref[c, pl.ds(REACH, 16), :] = mt_ref[c, pl.ds(0, 16), :].astype(jnp.float32)
-        m0_ref[c, pl.ds(rows - span, 16), :] = mt_ref[c, pl.ds(height - 16, 16), :].astype(jnp.float32)
+        m0_ref[c, pl.ds(REACH, 16), :] = me_ref[c, pl.ds(0, 16), :].astype(jnp.float32)
+        m0_ref[c, pl.ds(rows - span, 16), :] = me_ref[c, pl.ds(16, 16), :].astype(jnp.float32)
         m0_ref[c, pl.ds(rows - REACH, REACH), :] = bot_ref[c].astype(jnp.float32)
         m4_ref[c, pl.ds(0, span - 8), :] = m0_ref[c, pl.ds(4, span - 8), :]
         m4_ref[c, pl.ds(rows - span, span - 8), :] = m0_ref[c, pl.ds(rows - span + 4, span - 8), :]
@@ -280,12 +289,14 @@
     lax.fori_loop(0, CH, build, 0)
     for t in edge_tiles(height):
         beyond = halo_offsets(t, height)
-
-        def part(j, carry, t=t, beyond=beyond):
+        row = edge_row(t, height)
+
+        def part(j, carry, t=t, beyond=beyond, row=row):
             lanes = pl.ds(pl.multiple_of(j * 128, 128), 128)
-            rows_t = pl.ds(8 * t, 8)
+            rows_t = pl.ds(row, 8)
+            counts = block_counts(n_ref, t, beyond)
             peak, den, num = offset_partial(
-                total_y, f_ref, m0_ref, m4_ref, n_ref, 8 * t, beyond, lanes
+                total_y, f_ref, m0_ref, m4_ref, counts, 8 * t, beyond, lanes
             )
             peak_in = pk_ref[rows_t, lanes]
             top_score = jnp.maximum(peak, peak_in)
@@ -293,12 +304,20 @@
             scale_in = jnp.exp(peak_in - top_score)
             den = den * scale + dn_ref[rows_t, lanes] * scale_in
             num = num * scale + nm_ref[rows_t, lanes] * scale_in
-            o_ref[rows_t, lanes] = num / den
+            res_ref[rows_t, lanes] = num / den
             return carry
 
         lax.fori_loop(0, lanes_total // 128, part, 0)
-    middle_rows = pl.ds(REACH, height - 2 * REACH)
-    o_ref[middle_rows, :] = done_ref[middle_rows, :]
+    head = pltpu.make_async_copy(
+        res_ref.at[pl.ds(0, REACH)], o_hbm.at[pl.ds(0, REACH)], sem.at[0]
+    )
+    tail = pltpu.make_async_copy(
+        res_ref.at[pl.ds(REACH, REACH)], o_hbm.at[pl.ds(height - REACH, REACH)], sem.at[1]
+    )
+    head.start()
+    tail.start()
+    head.wait()
+    tail.wait()
 
 
 def per_device(fixed_features, moving_features, cand_offsets, cand_lengths, smooth_radii):
@@ -312,7 +331,6 @@
     offset_values = 4 * jnp.arange(NOFF, dtype=jnp.int32) - REACH
     hits = (shifts[:, :, None] == offset_values[None, None, :]) & live[:, :, None]
     mult = jnp.sum(hits.astype(jnp.float32), axis=1)
-    mult_rows = jnp.repeat(mult.T, 4, axis=1)
 
     gy_count = lax.axis_size("gy")
     fixed_c = channel_major(fixed_features)
@@ -334,29 +352,28 @@
     ]
     params = pltpu.CompilerParams(vmem_limit_bytes=60 * 1024 * 1024)
     out_shape = jax.ShapeDtypeStruct((height, columns_dev), jnp.float32)
-    n_lanes = jnp.broadcast_to(mult_rows[:, :, None], (NOFF, height, 128))
+    smem = pl.BlockSpec(memory_space=pltpu.SMEM)
+    vmem = pl.BlockSpec(memory_space=pltpu.VMEM)
+    edge_shape = jax.ShapeDtypeStruct((2 * REACH, columns_dev), jnp.float32)
     middle, peak_part, den_part, num_part = pl.pallas_call(
         lambda *refs: softmin_middle_kernel(total_y, *refs),
-        out_shape=(out_shape, out_shape, out_shape, out_shape),
+        out_shape=(out_shape, edge_shape, edge_shape, edge_shape),
+        in_specs=[smem, vmem, vmem],
         scratch_shapes=scratch,
         compiler_params=params,
-    )(fixed_c, moving_c, n_lanes)
+    )(mult, fixed_c, moving_c)
+    fixed_edge = jnp.concatenate([fixed_c[:, :REACH], fixed_c[:, height - REACH :]], axis=1)
+    moving_edge = jnp.concatenate([moving_c[:, :16], moving_c[:, height - 16 :]], axis=1)
     disp_init = pl.pallas_call(
         lambda *refs: softmin_edge_kernel(total_y, *refs),
         out_shape=out_shape,
-        scratch_shapes=scratch,
+        in_specs=[smem] + [vmem] * 7 + [pl.BlockSpec(memory_space=pl.ANY)],
+        out_specs=pl.BlockSpec(memory_space=pl.ANY),
+        scratch_shapes=scratch
+        + [pltpu.VMEM((2 * REACH, columns_dev), jnp.float32), pltpu.SemaphoreType.DMA((2,))],
         compiler_params=params,
-    )(
-        fixed_c,
-        moving_c,
-        top_rows,
-        bottom_rows,
-        n_lanes,
-        middle,
-        peak_part,
-        den_part,
-        num_part,
-    )
+        input_output_aliases={8: 0},
+    )(mult, fixed_edge, moving_edge, top_rows, bottom_rows, peak_part, den_part, num_part, middle)
 
     ext = exchange_halo(disp_init, HALO_Y, HALO_Z, SEND_Y, SEND_Z)
     rows_ext, lanes_ext = ext.shape

time: 76.3 us -> 79.9 us (1.047)
  the two profiles are of different devices: /device:TPU:38 before, /device:TPU:11 now
where the time goes in v8:
time: 79.9 us; the launch traced here: 78.5 us
  Pallas kernels  37.8 us (47%)
  starting transfers between devices  24.1 us (30%)
  waiting for transfers between devices  5.82 us (7%)
  local copies, waits for them, and re-layouts  5.7 us (7%)
  other arithmetic  4.25 us (5%)
    pallas_call x1, Pallas kernels, per_device(): pl.pallas_call(lambda *refs: softmin_middle_kernel(total_y, *refs), out_s...  15.2 us
    pallas_call x2, Pallas kernels, channel_major(): pl.pallas_call(transpose_kernel, out_shape=jax.ShapeDtypeStruct((CH, rows...  9.72 us
    pallas_call x1, Pallas kernels, per_device(): pl.pallas_call(adam_kernel, out_shape=jax.ShapeDtypeStruct((height, colum...  7.07 us
    ppermute x1, starting transfers between devices, exchange_halo(): lax.ppermute(cells[:, -send_z:], 'gz', [(i, i + 1) for i in range(nz - 1)])  6.88 us
    pallas_call x1, Pallas kernels, per_device(): pl.pallas_call(lambda *refs: softmin_edge_kernel(total_y, *refs), out_sha...  5.82 us
    ppermute x1, starting transfers between devices, exchange_halo(): lax.ppermute(cells[:send_y], 'gy', [(i + 1, i) for i in range(ny - 1)])  4.66 us
    ppermute x1, waiting for transfers between devices, exchange_halo(): lax.ppermute(cells[:, :send_z], 'gz', [(i + 1, i) for i in range(nz - 1)])  4.51 us
    ppermute x1, starting transfers between devices, per_device(): lax.ppermute(moving_c[:, height - REACH:], 'gy', [(i, i + 1) for i in ran...  3.91 us
  transfers between devices with their start and end apart: 6, of which 2 were waited for; matrix products, arithmetic and copies ran while one was open for 5% of the time, Pallas kernels for 26%

profile of v8, /device:TPU:11, one launch (start us, length us, event | category | flops | bytes accessed | tf_op | source)
XLA Modules:
  0.0 78.5 jit_solution(1032408294453065901)
XLA Ops:
  0.6 4.9 %shard_map.72.refs_2_ = bf16[16,128,512]{2,1,0:T(8,128)(2,1)} custom-call(bf16[128,8192]{1,0:T(8,128)(2,1)} %x_ref.3), custom_call_target="tpu_custom_call" | custom-call | tf_op jit(solution)/shard_map/pallas_call | solution.py:161
  5.5 2.3 %fusion.2 = (bf16[16,32,512]{2,1,0:T(8,128)(2,1)}, bf16[16,32,512]{2,1,0:T(8,128)(2,1)}) fusion(bf16[16,128,512]{2,1,0:T(8,128)(2,1)} %shard_map.72.refs_2_), kind=kLoop, calls=%fused_computation.14 | loop fusion | bytes 2097152 | tf_op jit(solution)/shard_map/slice | solution.py:342
  7.8 3.9 %collective-permute-start = (bf16[16,32,512]{2,1,0:T(8,128)(2,1)}, bf16[16,32,512]{2,1,0:T(8,128)(2,1)S(1)}, u32[]{:S(2)}, u32[]{:S(2)}) collective-permute-start(bf16[16,32,512]{2,1,0:T(8,128)(2,1)} %get-tuple-element.11), channel_id=1, source_target_pairs={{0,16},{16,32},{32,48},{48,64},{64,80},{80,96},{96,112},{1,17},{17... | collective-permute-start | bytes 1572872 | tf_op jit(solution)/shard_map/ppermute | solution.py:338
  11.7 3.8 %collective-permute-start.1 = (bf16[16,32,512]{2,1,0:T(8,128)(2,1)}, bf16[16,32,512]{2,1,0:T(8,128)(2,1)}, u32[]{:S(2)}, u32[]{:S(2)}) collective-permute-start(bf16[16,32,512]{2,1,0:T(8,128)(2,1)} %get-tuple-element.10), channel_id=1, source_target_pairs={{16,0},{32,16},{48,32},{64,48},{80,64},{96,80},{112,96},{17,1},{33... | collective-permute-start | bytes 1572872 | tf_op jit(solution)/shard_map/ppermute | solution.py:341
  15.5 1.1 %fusion.3 = (bf16[16,16,512]{2,1,0:T(8,128)(2,1)S(1)}, bf16[16,16,512]{2,1,0:T(8,128)(2,1)S(1)}) fusion(bf16[16,128,512]{2,1,0:T(8,128)(2,1)} %shard_map.72.refs_2_), kind=kLoop, calls=%fused_computation.15 | loop fusion | bytes 1048576 | tf_op jit(solution)/shard_map/slice | solution.py:366
  16.6 0.0 copy-start.4
  16.6 0.0 copy-start.3
  16.6 4.9 %shard_map.71.refs_1_ = bf16[16,128,512]{2,1,0:T(8,128)(2,1)} custom-call(bf16[128,8192]{1,0:T(8,128)(2,1)} %x_ref.2), custom_call_target="tpu_custom_call" | custom-call | tf_op jit(solution)/shard_map/pallas_call | solution.py:161
  21.5 0.0 copy-done.4
  21.5 0.0 copy-done.3
  21.5 0.1 convert_reduce_fusion
  21.6 0.7 copy.10.refs_0_
  22.3 0.0 copy-start.1
  22.3 15.2 %shard_map.73 = (f32[128,512]{1,0:T(8,128)}, f32[64,512]{1,0:T(8,128)}, f32[64,512]{1,0:T(8,128)}, f32[64,512]{1,0:T(8,128)}) custom-call(f32[32,17]{1,0:T(8,128)} %copy.10.refs_0_, bf16[16,128,512]{2,1,0:T(8,128)(2,1)} %shard_map.71.refs_1_, bf16[16,128,512]{2,1,0:T(8,128)(2,1)} %shard_map.72.refs_2_), custom_call_target="tpu_custom_call" | custom-call | tf_op jit(solution)/shard_map/pallas_call | solution.py:358
  37.5 0.9 %pad_maximum_fusion.1.refs_2_ = bf16[16,32,512]{2,1,0:T(8,128)(2,1)} fusion(bf16[16,16,512]{2,1,0:T(8,128)(2,1)S(1)} %get-tuple-element.13, bf16[16,16,512]{2,1,0:T(8,128)(2,1)S(1)} %get-tuple-element.12), kind=kLoop, calls=%fused_computation.1 | loop fusion | flops 1048576 | bytes 1048576 | tf_op jit(solution)/shard_map/concatenate | solution.py:366
  38.4 0.0 copy-done.1
  38.4 0.1 fusion.4
  38.5 1.0 %pad_maximum_fusion.refs_1_ = bf16[16,64,512]{2,1,0:T(8,128)(2,1)} fusion(bf16[16,32,512]{2,1,0:T(8,128)(2,1)S(1)} %get-tuple-element.15, bf16[16,32,512]{2,1,0:T(8,128)(2,1)S(1)} %get-tuple-element.14), kind=kLoop, calls=%fused_computation | loop fusion | flops 2097152 | bytes 2097152 | tf_op jit(solution)/shard_map/concatenate | solution.py:365
  39.5 0.0 collective-permute-done.refs_3_
  39.5 0.0 copy-start.2
  39.5 0.0 collective-permute-done.1.refs_4_
  39.5 0.8 %copy-done.2 = bf16[16,32,512]{2,1,0:T(8,128)(2,1)} copy-done((bf16[16,32,512]{2,1,0:T(8,128)(2,1)}, bf16[16,32,512]{2,1,0:T(8,128)(2,1)S(1)}, u32[]{:S(2)}) %copy-start.2) | copy-done | bytes 524312
  40.3 0.0 copy-start
  40.3 5.8 %shard_map.74 = f32[128,512]{1,0:T(8,128)} custom-call(f32[32,17]{1,0:T(8,128)} %copy.10.refs_0_, bf16[16,64,512]{2,1,0:T(8,128)(2,1)} %pad_maximum_fusion.refs_1_, bf16[16,32,512]{2,1,0:T(8,128)(2,1)} %pad_maximum_fusion.1.refs_2_, bf16[16,32,512]{2,1,0:T(8,128)(2,1)} %copy-done.2, ...), custom_call_target="tpu_custom_call", output_to_operand_aliasing={{}: (8, {})} | custom-call | tf_op jit(solution)/shard_map/pallas_call | solution.py:367
  46.2 0.7 fusion.5
  46.9 3.0 %collective-permute-start.2 = (f32[8,512]{1,0:T(8,128)S(1)}, f32[8,512]{1,0:T(8,128)S(1)}, u32[]{:S(2)}, u32[]{:S(2)}) collective-permute-start(f32[8,512]{1,0:T(8,128)S(1)} %get-tuple-element.18), channel_id=1, source_target_pairs={{0,16},{16,32},{32,48},{48,64},{64,80},{80,96},{96,112},{1,17},{17... | collective-permute-start | bytes 49160 | tf_op jit(solution)/shard_map/ppermute | solution.py:92
  49.9 4.7 %collective-permute-start.3 = (f32[8,512]{1,0:T(8,128)S(1)}, f32[8,512]{1,0:T(8,128)S(1)}, u32[]{:S(2)}, u32[]{:S(2)}) collective-permute-start(f32[8,512]{1,0:T(8,128)S(1)} %get-tuple-element.19), channel_id=1, source_target_pairs={{16,0},{32,16},{48,32},{64,48},{80,64},{96,80},{112,96},{17,1},{33... | collective-permute-start | bytes 49160 | tf_op jit(solution)/shard_map/ppermute | solution.py:93
  54.6 0.0 collective-permute-done.2
  54.6 1.3 %collective-permute-done.3 = f32[8,512]{1,0:T(8,128)S(1)} collective-permute-done((f32[8,512]{1,0:T(8,128)S(1)}, f32[8,512]{1,0:T(8,128)S(1)}, u32[]{:S(2)}, u32[]{:S(2)}) %collective-permute-start.3) | collective-permute-done | bytes 16416 | tf_op jit(solution)/shard_map/ppermute | solution.py:93
  55.9 1.0 %pad_maximum_fusion.5 = (f32[144,64]{1,0:T(8,128)S(1)}, f32[144,64]{1,0:T(8,128)S(1)}) fusion(f32[8,512]{1,0:T(8,128)S(1)} %collective-permute-done.3, f32[128,512]{1,0:T(8,128)} %shard_map.74, f32[8,512]{1,0:T(8,128)S(1)} %collective-permute-done.2), kind=kLoop, calls=%fused_computation.7 | loop fusion | flops 36864 | bytes 368640 | tf_op jit(solution)/shard_map/slice | solution.py:95
  56.9 6.9 %collective-permute-start.4 = (f32[144,64]{1,0:T(8,128)S(1)}, f32[144,64]{1,0:T(8,128)S(1)}, u32[]{:S(2)}, u32[]{:S(2)}) collective-permute-start(f32[144,64]{1,0:T(8,128)S(1)} %get-tuple-element.16), channel_id=1, source_target_pairs={{0,1},{1,2},{2,3},{3,4},{4,5},{5,6},{6,7},{7,8},{8,9},{9,10},{10,1... | collective-permute-start | bytes 110600 | tf_op jit(solution)/shard_map/ppermute | solution.py:95
  63.7 1.9 %collective-permute-start.5 = (f32[144,64]{1,0:T(8,128)S(1)}, f32[144,64]{1,0:T(8,128)S(1)}, u32[]{:S(2)}, u32[]{:S(2)}) collective-permute-start(f32[144,64]{1,0:T(8,128)S(1)} %get-tuple-element.17), channel_id=1, source_target_pairs={{1,0},{2,1},{3,2},{4,3},{5,4},{6,5},{7,6},{8,7},{9,8},{10,9},{11,1... | collective-permute-start | bytes 110600 | tf_op jit(solution)/shard_map/ppermute | solution.py:96
  65.7 0.1 and_convert_fusion.mask_ref
  65.8 0.0 collective-permute-done.4
  65.8 4.5 %collective-permute-done.5 = f32[144,64]{1,0:T(8,128)S(1)} collective-permute-done((f32[144,64]{1,0:T(8,128)S(1)}, f32[144,64]{1,0:T(8,128)S(1)}, u32[]{:S(2)}, u32[]{:S(2)}) %collective-permute-start.5) | collective-permute-done | bytes 36896 | tf_op jit(solution)/shard_map/ppermute | solution.py:96
  70.3 1.1 %pad_maximum_fusion.2.d_ref = f32[144,640]{1,0:T(8,128)S(1)} fusion(f32[144,64]{1,0:T(8,128)S(1)} %collective-permute-done.5, f32[8,512]{1,0:T(8,128)S(1)} %collective-permute-done.3, f32[128,512]{1,0:T(8,128)} %shard_map.74, f32[8,512]{1,0:T(8,128)S(1)} %collective-permute-done.2, f32[144,64]{1,0:T(8,128)S(1)} %collective-permute-done.4), kind=kLoop, calls=%fused_computation.2 | loop fusion | flops 368640 | bytes 737280 | tf_op jit(solution)/shard_map/concatenate | solution.py:97
  71.5 0.0 copy-done
  71.5 7.1 %shard_map.75 = f32[128,512]{1,0:T(8,128)} custom-call(s32[3]{0:T(128)S(1)} %copy-done, f32[144,640]{1,0:T(8,128)S(1)} %pad_maximum_fusion.2.d_ref, f32[144,640]{1,0:T(8,128)S(1)} %and_convert_fusion.mask_ref), custom_call_target="tpu_custom_call" | custom-call | tf_op jit(solution)/shard_map/pallas_call | solution.py:393
  (4 shorter events, 0.0 us)
Async XLA Ops:
  7.8 31.7 %collective-permute-start = (bf16[16,32,512]{2,1,0:T(8,128)(2,1)}, bf16[16,32,512]{2,1,0:T(8,128)(2,1)S(1)}, u32[]{:S(2)}, u32[]{:S(2)}) collective-permute-start(bf16[16,32,512]{2,1,0:T(8,128)(2,1)} %get-tuple-element.11), channel_id=1, source_target_pairs={{0,16},{16,32},{32,48},{48,64},{64,80},{80,96},{96,112},{1,17},{17... | collective-permute-start | bytes 1572872 | tf_op jit(solution)/shard_map/ppermute | solution.py:338
  11.7 27.8 %collective-permute-start.1 = (bf16[16,32,512]{2,1,0:T(8,128)(2,1)}, bf16[16,32,512]{2,1,0:T(8,128)(2,1)}, u32[]{:S(2)}, u32[]{:S(2)}) collective-permute-start(bf16[16,32,512]{2,1,0:T(8,128)(2,1)} %get-tuple-element.10), channel_id=1, source_target_pairs={{16,0},{32,16},{48,32},{64,48},{80,64},{96,80},{112,96},{17,1},{33... | collective-permute-start | bytes 1572872 | tf_op jit(solution)/shard_map/ppermute | solution.py:341
  16.6 4.9 %copy-start.4 = (s32[32,1]{0,1:T(1,128)S(1)}, s32[32,1]{0,1:T(1,128)}, u32[]{:S(2)}) copy-start(s32[32,1]{0,1:T(1,128)} %param.8) | copy-start | bytes 388
  16.6 4.9 %copy-start.3 = (s32[32,1,16]{0,2,1:T(8,128)S(1)}, s32[32,1,16]{0,2,1:T(8,128)}, u32[]{:S(2)}) copy-start(s32[32,1,16]{0,2,1:T(8,128)} %param.7) | copy-start | bytes 6148
  22.3 16.1 %copy-start.1 = (bf16[16,128,512]{2,1,0:T(8,128)(2,1)S(1)}, bf16[16,128,512]{2,1,0:T(8,128)(2,1)}, u32[]{:S(2)}) copy-start(bf16[16,128,512]{2,1,0:T(8,128)(2,1)} %shard_map.71.refs_1_) | copy-start | bytes 6291460
  39.5 0.8 %copy-start.2 = (bf16[16,32,512]{2,1,0:T(8,128)(2,1)}, bf16[16,32,512]{2,1,0:T(8,128)(2,1)S(1)}, u32[]{:S(2)}) copy-start(bf16[16,32,512]{2,1,0:T(8,128)(2,1)S(1)} %collective-permute-done.refs_3_) | copy-start | bytes 1572868
  40.3 31.1 %copy-start = (s32[3]{0:T(128)S(1)}, s32[3]{0:T(128)}, u32[]{:S(2)}) copy-start(s32[3]{0:T(128)} %radii_ref.1) | copy-start | bytes 40
  46.9 7.7 %collective-permute-start.2 = (f32[8,512]{1,0:T(8,128)S(1)}, f32[8,512]{1,0:T(8,128)S(1)}, u32[]{:S(2)}, u32[]{:S(2)}) collective-permute-start(f32[8,512]{1,0:T(8,128)S(1)} %get-tuple-element.18), channel_id=1, source_target_pairs={{0,16},{16,32},{32,48},{48,64},{64,80},{80,96},{96,112},{1,17},{17... | collective-permute-start | bytes 49160 | tf_op jit(solution)/shard_map/ppermute | solution.py:92
  49.9 6.0 %collective-permute-start.3 = (f32[8,512]{1,0:T(8,128)S(1)}, f32[8,512]{1,0:T(8,128)S(1)}, u32[]{:S(2)}, u32[]{:S(2)}) collective-permute-start(f32[8,512]{1,0:T(8,128)S(1)} %get-tuple-element.19), channel_id=1, source_target_pairs={{16,0},{32,16},{48,32},{64,48},{80,64},{96,80},{112,96},{17,1},{33... | collective-permute-start | bytes 49160 | tf_op jit(solution)/shard_map/ppermute | solution.py:93
  56.9 8.9 %collective-permute-start.4 = (f32[144,64]{1,0:T(8,128)S(1)}, f32[144,64]{1,0:T(8,128)S(1)}, u32[]{:S(2)}, u32[]{:S(2)}) collective-permute-start(f32[144,64]{1,0:T(8,128)S(1)} %get-tuple-element.16), channel_id=1, source_target_pairs={{0,1},{1,2},{2,3},{3,4},{4,5},{5,6},{6,7},{7,8},{8,9},{9,10},{10,1... | collective-permute-start | bytes 110600 | tf_op jit(solution)/shard_map/ppermute | solution.py:95
  63.7 6.6 %collective-permute-start.5 = (f32[144,64]{1,0:T(8,128)S(1)}, f32[144,64]{1,0:T(8,128)S(1)}, u32[]{:S(2)}, u32[]{:S(2)}) collective-permute-start(f32[144,64]{1,0:T(8,128)S(1)} %get-tuple-element.17), channel_id=1, source_target_pairs={{1,0},{2,1},{3,2},{4,3},{5,4},{6,5},{7,6},{8,7},{9,8},{10,9},{11,1... | collective-permute-start | bytes 110600 | tf_op jit(solution)/shard_map/ppermute | solution.py:96

commit v9 on v8

--- a/solution.py
+++ b/solution.py
@@ -147,20 +147,27 @@
     o_ref[...] = field[HALO_Y : HALO_Y + height, HALO_Z : HALO_Z + width]
 
 
-def transpose_kernel(x_ref, o_ref, s_ref):
+def transpose_kernel(x_ref, *refs):
+    o_ref, s_ref = refs[0], refs[-1]
     chunk = 128 * CH
     for j in range(x_ref.shape[1] // chunk):
         s_ref[...] = x_ref[:, pl.ds(chunk * j, chunk)].astype(jnp.float32).T
         for c in range(CH):
             cols = s_ref[pl.ds(c, 128, stride=CH), :]
             o_ref[c, :, pl.ds(128 * j, 128)] = cols.T.astype(o_ref.dtype)
-
-
-def channel_major(x):
+    if len(refs) == 4:
+        rows = x_ref.shape[0]
+        refs[1][...] = o_ref[:, pl.ds(0, REACH), :]
+        refs[2][...] = o_ref[:, pl.ds(rows - REACH, REACH), :]
+
+
+def channel_major(x, with_ends=False):
     rows, lanes = x.shape
+    whole = jax.ShapeDtypeStruct((CH, rows, lanes // CH), x.dtype)
+    ends = jax.ShapeDtypeStruct((CH, REACH, lanes // CH), x.dtype)
     return pl.pallas_call(
         transpose_kernel,
-        out_shape=jax.ShapeDtypeStruct((CH, rows, lanes // CH), x.dtype),
+        out_shape=(whole, ends, ends) if with_ends else whole,
         scratch_shapes=[pltpu.VMEM((128 * CH, rows), jnp.float32)],
     )(x)
 
@@ -264,13 +271,29 @@
 
 
 def softmin_edge_kernel(
-    total_y, n_ref, fe_ref, me_ref, top_ref, bot_ref, pk_ref, dn_ref, nm_ref, _,
-    o_hbm, f_ref, m0_ref, m4_ref, res_ref, sem,
+    total_y, n_ref, fc_hbm, mc_hbm, top_ref, bot_ref, pk_ref, dn_ref, nm_ref, _,
+    o_hbm, f_ref, m0_ref, m4_ref, res_ref, fe_ref, me_ref, sem,
 ):
     height = o_hbm.shape[0]
     lanes_total = fe_ref.shape[2]
     rows = height + 2 * REACH
     span = REACH + 16
+    copies = [
+        pltpu.make_async_copy(
+            fc_hbm.at[:, pl.ds(0, REACH), :], fe_ref.at[:, pl.ds(0, REACH), :], sem.at[2]
+        ),
+        pltpu.make_async_copy(
+            fc_hbm.at[:, pl.ds(height - REACH, REACH), :], fe_ref.at[:, pl.ds(REACH, REACH), :], sem.at[3]
+        ),
+        pltpu.make_async_copy(mc_hbm.at[:, pl.ds(0, 16), :], me_ref.at[:, pl.ds(0, 16), :], sem.at[4]),
+        pltpu.make_async_copy(
+            mc_hbm.at[:, pl.ds(height - 16, 16), :], me_ref.at[:, pl.ds(16, 16), :], sem.at[5]
+        ),
+    ]
+    for cp in copies:
+        cp.start()
+    for cp in copies:
+        cp.wait()
 
     def build(c, carry):
         f_ref[c, pl.ds(0, REACH), :] = fe_ref[c, pl.ds(0, REACH), :].astype(jnp.float32)
@@ -334,13 +357,9 @@
 
     gy_count = lax.axis_size("gy")
     fixed_c = channel_major(fixed_features)
-    moving_c = channel_major(moving_features)
-    top_rows = lax.ppermute(
-        moving_c[:, height - REACH :], "gy", [(i, i + 1) for i in range(gy_count - 1)]
-    )
-    bottom_rows = lax.ppermute(
-        moving_c[:, :REACH], "gy", [(i + 1, i) for i in range(gy_count - 1)]
-    )
+    moving_c, moving_head, moving_tail = channel_major(moving_features, with_ends=True)
+    top_rows = lax.ppermute(moving_tail, "gy", [(i, i + 1) for i in range(gy_count - 1)])
+    bottom_rows = lax.ppermute(moving_head, "gy", [(i + 1, i) for i in range(gy_count - 1)])
 
     rows = height + 2 * REACH
     tiles = height // 8
@@ -354,6 +373,7 @@
     out_shape = jax.ShapeDtypeStruct((height, columns_dev), jnp.float32)
     smem = pl.BlockSpec(memory_space=pltpu.SMEM)
     vmem = pl.BlockSpec(memory_space=pltpu.VMEM)
+    anywhere = pl.BlockSpec(memory_space=pl.ANY)
     edge_shape = jax.ShapeDtypeStruct((2 * REACH, columns_dev), jnp.float32)
     middle, peak_part, den_part, num_part = pl.pallas_call(
         lambda *refs: softmin_middle_kernel(total_y, *refs),
@@ -362,18 +382,21 @@
         scratch_shapes=scratch,
         compiler_params=params,
     )(mult, fixed_c, moving_c)
-    fixed_edge = jnp.concatenate([fixed_c[:, :REACH], fixed_c[:, height - REACH :]], axis=1)
-    moving_edge = jnp.concatenate([moving_c[:, :16], moving_c[:, height - 16 :]], axis=1)
     disp_init = pl.pallas_call(
         lambda *refs: softmin_edge_kernel(total_y, *refs),
         out_shape=out_shape,
-        in_specs=[smem] + [vmem] * 7 + [pl.BlockSpec(memory_space=pl.ANY)],
-        out_specs=pl.BlockSpec(memory_space=pl.ANY),
+        in_specs=[smem, anywhere, anywhere] + [vmem] * 5 + [anywhere],
+        out_specs=anywhere,
         scratch_shapes=scratch
-        + [pltpu.VMEM((2 * REACH, columns_dev), jnp.float32), pltpu.SemaphoreType.DMA((2,))],
+        + [
+            pltpu.VMEM((2 * REACH, columns_dev), jnp.float32),
+            pltpu.VMEM((CH, 2 * REACH, columns_dev), jnp.bfloat16),
+            pltpu.VMEM((CH, 32, columns_dev), jnp.bfloat16),
+            pltpu.SemaphoreType.DMA((6,)),
+        ],
         compiler_params=params,
         input_output_aliases={8: 0},
-    )(mult, fixed_edge, moving_edge, top_rows, bottom_rows, peak_part, den_part, num_part, middle)
+    )(mult, fixed_c, moving_c, top_rows, bottom_rows, peak_part, den_part, num_part, middle)
 
     ext = exchange_halo(disp_init, HALO_Y, HALO_Z, SEND_Y, SEND_Z)
     rows_ext, lanes_ext = ext.shape

time: 79.9 us -> 74.2 us (0.929)
  the two profiles are of different devices: /device:TPU:11 before, /device:TPU:38 now
where the time goes in v9:
time: 74.2 us; the launch traced here: 73.3 us
  Pallas kernels  38.3 us (52%)
  starting transfers between devices  19.9 us (27%)
  waiting for transfers between devices  9.69 us (13%)
  other arithmetic  2.34 us (3%)
  local copies, waits for them, and re-layouts  2.23 us (3%)
  between operations  0.8 us (1%)
    pallas_call x1, Pallas kernels, per_device(): pl.pallas_call(lambda *refs: softmin_middle_kernel(total_y, *refs), out_s...  15.1 us
    pallas_call x2, Pallas kernels, channel_major(): pl.pallas_call(transpose_kernel, out_shape=(whole, ends, ends) if with_en...  10.1 us
    pallas_call x1, Pallas kernels, per_device(): pl.pallas_call(lambda *refs: softmin_edge_kernel(total_y, *refs), out_sha...  6.73 us
    pallas_call x1, Pallas kernels, per_device(): pl.pallas_call(adam_kernel, out_shape=jax.ShapeDtypeStruct((height, colum...  6.44 us
    ppermute x1, waiting for transfers between devices, exchange_halo(): lax.ppermute(cells[-send_y:], 'gy', [(i, i + 1) for i in range(ny - 1)])  5.3 us
    ppermute x1, starting transfers between devices, per_device(): lax.ppermute(moving_tail, 'gy', [(i, i + 1) for i in range(gy_count - 1)])  5.09 us
    ppermute x1, starting transfers between devices, exchange_halo(): lax.ppermute(cells[:send_y], 'gy', [(i + 1, i) for i in range(ny - 1)])  4.63 us
    ppermute x1, waiting for transfers between devices, exchange_halo(): lax.ppermute(cells[:, -send_z:], 'gz', [(i, i + 1) for i in range(nz - 1)])  4.03 us
  transfers between devices with their start and end apart: 6, of which 3 were waited for; matrix products, arithmetic and copies ran while one was open for 1% of the time, Pallas kernels for 27%

profile of v9, /device:TPU:38, one launch (start us, length us, event | category | flops | bytes accessed | tf_op | source)
XLA Modules:
  0.0 73.3 jit_solution(14904523270305103786)
XLA Ops:
  0.6 0.0 copy-start.4
  0.6 0.0 copy-start.3
  0.7 5.2 %shard_map.72 = (bf16[16,128,512]{2,1,0:T(8,128)(2,1)}, bf16[16,32,512]{2,1,0:T(8,128)(2,1)}, bf16[16,32,512]{2,1,0:T(8,128)(2,1)}) custom-call(bf16[128,8192]{1,0:T(8,128)(2,1)} %x_ref.3), custom_call_target="tpu_custom_call" | custom-call | tf_op jit(solution)/shard_map/pallas_call | solution.py:168
  5.9 5.1 %collective-permute-start = (bf16[16,32,512]{2,1,0:T(8,128)(2,1)}, bf16[16,32,512]{2,1,0:T(8,128)(2,1)S(1)}, u32[]{:S(2)}, u32[]{:S(2)}) collective-permute-start(bf16[16,32,512]{2,1,0:T(8,128)(2,1)} %get-tuple-element.10), channel_id=1, source_target_pairs={{0,16},{16,32},{32,48},{48,64},{64,80},{80,96},{96,112},{1,17},{17... | collective-permute-start | bytes 1572872 | tf_op jit(solution)/shard_map/ppermute | solution.py:361
  11.0 3.1 %collective-permute-start.1 = (bf16[16,32,512]{2,1,0:T(8,128)(2,1)}, bf16[16,32,512]{2,1,0:T(8,128)(2,1)S(1)}, u32[]{:S(2)}, u32[]{:S(2)}) collective-permute-start(bf16[16,32,512]{2,1,0:T(8,128)(2,1)} %get-tuple-element.11), channel_id=1, source_target_pairs={{16,0},{32,16},{48,32},{64,48},{80,64},{96,80},{112,96},{17,1},{33... | collective-permute-start | bytes 1572872 | tf_op jit(solution)/shard_map/ppermute | solution.py:362
  14.2 0.0 copy-done.4
  14.2 0.0 copy-done.3
  14.2 0.1 convert_reduce_fusion
  14.3 0.7 copy.10.refs_0_
  15.0 4.9 %shard_map.71.refs_1_ = bf16[16,128,512]{2,1,0:T(8,128)(2,1)} custom-call(bf16[128,8192]{1,0:T(8,128)(2,1)} %x_ref.2), custom_call_target="tpu_custom_call" | custom-call | tf_op jit(solution)/shard_map/pallas_call | solution.py:168
  19.8 15.1 %shard_map.73 = (f32[128,512]{1,0:T(8,128)}, f32[64,512]{1,0:T(8,128)}, f32[64,512]{1,0:T(8,128)}, f32[64,512]{1,0:T(8,128)}) custom-call(f32[32,17]{1,0:T(8,128)} %copy.10.refs_0_, bf16[16,128,512]{2,1,0:T(8,128)(2,1)} %shard_map.71.refs_1_, bf16[16,128,512]{2,1,0:T(8,128)(2,1)} %get-tuple-element.9.refs_2_), custom_call_target="tpu_custom_call" | custom-call | tf_op jit(solution)/shard_map/pallas_call | solution.py:378
  34.9 0.0 collective-permute-done.refs_3_
  34.9 0.0 copy-start.1
  34.9 0.4 collective-permute-done.1.refs_4_
  35.3 0.0 copy-start.2
  35.3 0.4 copy-done.1
  35.7 0.4 copy-done.2
  36.1 0.0 copy-start
  36.1 6.7 %shard_map.74 = f32[128,512]{1,0:T(8,128)} custom-call(f32[32,17]{1,0:T(8,128)} %copy.10.refs_0_, bf16[16,128,512]{2,1,0:T(8,128)(2,1)} %shard_map.71.refs_1_, bf16[16,128,512]{2,1,0:T(8,128)(2,1)} %get-tuple-element.9.refs_2_, bf16[16,32,512]{2,1,0:T(8,128)(2,1)} %copy-done.1, bf16[16,32,512]{2,1,0:T(8,128)(2,1)} %copy-done.2, ...), custom_call_target="tpu_custom_call", output_to_operand_aliasing={{}: (8, {})} | custom-call | tf_op jit(solution)/shard_map/pallas_call | solution.py:385
  42.8 0.7 %fusion.2 = (f32[8,512]{1,0:T(8,128)S(1)}, f32[8,512]{1,0:T(8,128)S(1)}) fusion(f32[128,512]{1,0:T(8,128)} %shard_map.74), kind=kLoop, calls=%fused_computation.12 | loop fusion | bytes 65536 | tf_op jit(solution)/shard_map/slice | solution.py:92
  43.6 4.6 %collective-permute-start.3 = (f32[8,512]{1,0:T(8,128)S(1)}, f32[8,512]{1,0:T(8,128)S(1)}, u32[]{:S(2)}, u32[]{:S(2)}) collective-permute-start(f32[8,512]{1,0:T(8,128)S(1)} %get-tuple-element.19), channel_id=1, source_target_pairs={{16,0},{32,16},{48,32},{64,48},{80,64},{96,80},{112,96},{17,1},{33... | collective-permute-start | bytes 49160 | tf_op jit(solution)/shard_map/ppermute | solution.py:93
  48.2 2.7 %collective-permute-start.2 = (f32[8,512]{1,0:T(8,128)S(1)}, f32[8,512]{1,0:T(8,128)S(1)}, u32[]{:S(2)}, u32[]{:S(2)}) collective-permute-start(f32[8,512]{1,0:T(8,128)S(1)} %get-tuple-element.18), channel_id=1, source_target_pairs={{0,16},{16,32},{32,48},{48,64},{64,80},{80,96},{96,112},{1,17},{17... | collective-permute-start | bytes 49160 | tf_op jit(solution)/shard_map/ppermute | solution.py:92
  50.9 0.0 collective-permute-done.3
  50.9 5.3 %collective-permute-done.2 = f32[8,512]{1,0:T(8,128)S(1)} collective-permute-done((f32[8,512]{1,0:T(8,128)S(1)}, f32[8,512]{1,0:T(8,128)S(1)}, u32[]{:S(2)}, u32[]{:S(2)}) %collective-permute-start.2) | collective-permute-done | bytes 16416 | tf_op jit(solution)/shard_map/ppermute | solution.py:92
  56.2 1.0 %pad_maximum_fusion.3 = (f32[144,64]{1,0:T(8,128)S(1)}, f32[144,64]{1,0:T(8,128)S(1)}) fusion(f32[8,512]{1,0:T(8,128)S(1)} %collective-permute-done.3, f32[128,512]{1,0:T(8,128)} %shard_map.74, f32[8,512]{1,0:T(8,128)S(1)} %collective-permute-done.2), kind=kLoop, calls=%fused_computation.5 | loop fusion | flops 36864 | bytes 368640 | tf_op jit(solution)/shard_map/slice | solution.py:95
  57.2 1.9 %collective-permute-start.5 = (f32[144,64]{1,0:T(8,128)S(1)}, f32[144,64]{1,0:T(8,128)S(1)}, u32[]{:S(2)}, u32[]{:S(2)}) collective-permute-start(f32[144,64]{1,0:T(8,128)S(1)} %get-tuple-element.17), channel_id=1, source_target_pairs={{1,0},{2,1},{3,2},{4,3},{5,4},{6,5},{7,6},{8,7},{9,8},{10,9},{11,1... | collective-permute-start | bytes 110600 | tf_op jit(solution)/shard_map/ppermute | solution.py:96
  59.1 2.4 %collective-permute-start.4 = (f32[144,64]{1,0:T(8,128)S(1)}, f32[144,64]{1,0:T(8,128)S(1)}, u32[]{:S(2)}, u32[]{:S(2)}) collective-permute-start(f32[144,64]{1,0:T(8,128)S(1)} %get-tuple-element.16), channel_id=1, source_target_pairs={{0,1},{1,2},{2,3},{3,4},{4,5},{5,6},{6,7},{7,8},{8,9},{9,10},{10,1... | collective-permute-start | bytes 110600 | tf_op jit(solution)/shard_map/ppermute | solution.py:95
  61.5 0.1 and_convert_fusion.mask_ref
  61.6 0.0 collective-permute-done.5
  61.7 4.0 %collective-permute-done.4 = f32[144,64]{1,0:T(8,128)S(1)} collective-permute-done((f32[144,64]{1,0:T(8,128)S(1)}, f32[144,64]{1,0:T(8,128)S(1)}, u32[]{:S(2)}, u32[]{:S(2)}) %collective-permute-start.4) | collective-permute-done | bytes 36896 | tf_op jit(solution)/shard_map/ppermute | solution.py:95
  65.7 1.1 %pad_maximum_fusion.d_ref = f32[144,640]{1,0:T(8,128)S(1)} fusion(f32[144,64]{1,0:T(8,128)S(1)} %collective-permute-done.5, f32[8,512]{1,0:T(8,128)S(1)} %collective-permute-done.3, f32[128,512]{1,0:T(8,128)} %shard_map.74, f32[8,512]{1,0:T(8,128)S(1)} %collective-permute-done.2, f32[144,64]{1,0:T(8,128)S(1)} %collective-permute-done.4), kind=kLoop, calls=%fused_computation | loop fusion | flops 368640 | bytes 737280 | tf_op jit(solution)/shard_map/concatenate | solution.py:97
  66.8 0.0 copy-done
  66.8 6.4 %shard_map.75 = f32[128,512]{1,0:T(8,128)} custom-call(s32[3]{0:T(128)S(1)} %copy-done, f32[144,640]{1,0:T(8,128)S(1)} %pad_maximum_fusion.d_ref, f32[144,640]{1,0:T(8,128)S(1)} %and_convert_fusion.mask_ref), custom_call_target="tpu_custom_call" | custom-call | tf_op jit(solution)/shard_map/pallas_call | solution.py:416
  (4 shorter events, 0.0 us)
Async XLA Ops:
  0.6 13.5 %copy-start.4 = (s32[32,1]{0,1:T(1,128)S(1)}, s32[32,1]{0,1:T(1,128)}, u32[]{:S(2)}) copy-start(s32[32,1]{0,1:T(1,128)} %param.8) | copy-start | bytes 388
  0.6 13.5 %copy-start.3 = (s32[32,1,16]{0,2,1:T(8,128)S(1)}, s32[32,1,16]{0,2,1:T(8,128)}, u32[]{:S(2)}) copy-start(s32[32,1,16]{0,2,1:T(8,128)} %param.7) | copy-start | bytes 6148
  5.9 29.0 %collective-permute-start = (bf16[16,32,512]{2,1,0:T(8,128)(2,1)}, bf16[16,32,512]{2,1,0:T(8,128)(2,1)S(1)}, u32[]{:S(2)}, u32[]{:S(2)}) collective-permute-start(bf16[16,32,512]{2,1,0:T(8,128)(2,1)} %get-tuple-element.10), channel_id=1, source_target_pairs={{0,16},{16,32},{32,48},{48,64},{64,80},{80,96},{96,112},{1,17},{17... | collective-permute-start | bytes 1572872 | tf_op jit(solution)/shard_map/ppermute | solution.py:361
  11.0 24.3 %collective-permute-start.1 = (bf16[16,32,512]{2,1,0:T(8,128)(2,1)}, bf16[16,32,512]{2,1,0:T(8,128)(2,1)S(1)}, u32[]{:S(2)}, u32[]{:S(2)}) collective-permute-start(bf16[16,32,512]{2,1,0:T(8,128)(2,1)} %get-tuple-element.11), channel_id=1, source_target_pairs={{16,0},{32,16},{48,32},{64,48},{80,64},{96,80},{112,96},{17,1},{33... | collective-permute-start | bytes 1572872 | tf_op jit(solution)/shard_map/ppermute | solution.py:362
  34.9 0.8 %copy-start.1 = (bf16[16,32,512]{2,1,0:T(8,128)(2,1)}, bf16[16,32,512]{2,1,0:T(8,128)(2,1)S(1)}, u32[]{:S(2)}) copy-start(bf16[16,32,512]{2,1,0:T(8,128)(2,1)S(1)} %collective-permute-done.refs_3_) | copy-start | bytes 1572868
  35.3 0.8 %copy-start.2 = (bf16[16,32,512]{2,1,0:T(8,128)(2,1)}, bf16[16,32,512]{2,1,0:T(8,128)(2,1)S(1)}, u32[]{:S(2)}) copy-start(bf16[16,32,512]{2,1,0:T(8,128)(2,1)S(1)} %collective-permute-done.1.refs_4_) | copy-start | bytes 1572868
  36.1 30.8 %copy-start = (s32[3]{0:T(128)S(1)}, s32[3]{0:T(128)}, u32[]{:S(2)}) copy-start(s32[3]{0:T(128)} %radii_ref.1) | copy-start | bytes 40
  43.6 7.4 %collective-permute-start.3 = (f32[8,512]{1,0:T(8,128)S(1)}, f32[8,512]{1,0:T(8,128)S(1)}, u32[]{:S(2)}, u32[]{:S(2)}) collective-permute-start(f32[8,512]{1,0:T(8,128)S(1)} %get-tuple-element.19), channel_id=1, source_target_pairs={{16,0},{32,16},{48,32},{64,48},{80,64},{96,80},{112,96},{17,1},{33... | collective-permute-start | bytes 49160 | tf_op jit(solution)/shard_map/ppermute | solution.py:93
  48.2 8.0 %collective-permute-start.2 = (f32[8,512]{1,0:T(8,128)S(1)}, f32[8,512]{1,0:T(8,128)S(1)}, u32[]{:S(2)}, u32[]{:S(2)}) collective-permute-start(f32[8,512]{1,0:T(8,128)S(1)} %get-tuple-element.18), channel_id=1, source_target_pairs={{0,16},{16,32},{32,48},{48,64},{64,80},{80,96},{96,112},{1,17},{17... | collective-permute-start | bytes 49160 | tf_op jit(solution)/shard_map/ppermute | solution.py:92
  57.2 4.5 %collective-permute-start.5 = (f32[144,64]{1,0:T(8,128)S(1)}, f32[144,64]{1,0:T(8,128)S(1)}, u32[]{:S(2)}, u32[]{:S(2)}) collective-permute-start(f32[144,64]{1,0:T(8,128)S(1)} %get-tuple-element.17), channel_id=1, source_target_pairs={{1,0},{2,1},{3,2},{4,3},{5,4},{6,5},{7,6},{8,7},{9,8},{10,9},{11,1... | collective-permute-start | bytes 110600 | tf_op jit(solution)/shard_map/ppermute | solution.py:96
  59.1 6.6 %collective-permute-start.4 = (f32[144,64]{1,0:T(8,128)S(1)}, f32[144,64]{1,0:T(8,128)S(1)}, u32[]{:S(2)}, u32[]{:S(2)}) collective-permute-start(f32[144,64]{1,0:T(8,128)S(1)} %get-tuple-element.16), channel_id=1, source_target_pairs={{0,1},{1,2},{2,3},{3,4},{4,5},{5,6},{6,7},{7,8},{8,9},{9,10},{10,1... | collective-permute-start | bytes 110600 | tf_op jit(solution)/shard_map/ppermute | solution.py:95

commit v10 on v9

--- a/solution.py
+++ b/solution.py
@@ -124,10 +124,28 @@
     return along_x * scale
 
 
-def adam_kernel(radii_ref, d_ref, mask_ref, o_ref):
-    target = d_ref[...]
-    inside = mask_ref[...] > 0.0
-    lane_x = lax.broadcasted_iota(jnp.int32, target.shape, 1) % XS
+def adam_kernel(radii_ref, pos_ref, d_ref, y_ref, z_ref, o_ref, ext_ref):
+    height, width = d_ref.shape
+    ext_ref[pl.ds(0, height), pl.ds(0, width)] = d_ref[...]
+    ext_ref[pl.ds(height, 2 * HALO_Y), pl.ds(0, width)] = y_ref[...]
+    ext_ref[:, pl.ds(width, 2 * HALO_Z)] = z_ref[...]
+    target = ext_ref[...]
+    rows = lax.broadcasted_iota(jnp.int32, target.shape, 0)
+    lanes = lax.broadcasted_iota(jnp.int32, target.shape, 1)
+    gy = pos_ref[0]
+    gz = pos_ref[1]
+    row_ok = (
+        (rows < height)
+        | ((rows < height + HALO_Y) & (gy < pos_ref[2] - 1))
+        | ((rows >= height + HALO_Y) & (gy > 0))
+    )
+    lane_ok = (
+        (lanes < width)
+        | ((lanes < width + HALO_Z) & (gz < pos_ref[3] - 1))
+        | ((lanes >= width + HALO_Z) & (gz > 0))
+    )
+    inside = row_ok & lane_ok
+    lane_x = lanes % XS
     field = jnp.where(inside, target, 0.0)
     first_moment = jnp.zeros_like(target)
     second_moment = jnp.zeros_like(target)
@@ -142,9 +160,7 @@
             field, target, smoothed, first_moment, second_moment, iteration
         )
         field = jnp.where(inside, field, 0.0)
-    height = o_ref.shape[0]
-    width = o_ref.shape[1]
-    o_ref[...] = field[HALO_Y : HALO_Y + height, HALO_Z : HALO_Z + width]
+    o_ref[...] = field[:height, :width]
 
 
 def transpose_kernel(x_ref, *refs):
@@ -398,31 +414,37 @@
         input_output_aliases={8: 0},
     )(mult, fixed_c, moving_c, top_rows, bottom_rows, peak_part, den_part, num_part, middle)
 
-    ext = exchange_halo(disp_init, HALO_Y, HALO_Z, SEND_Y, SEND_Z)
-    rows_ext, lanes_ext = ext.shape
-    row_global = lax.axis_index("gy") * height - HALO_Y + lax.broadcasted_iota(
-        jnp.int32, (rows_ext, lanes_ext), 0
-    )
-    lane_global = lax.axis_index("gz") * columns_dev - HALO_Z + lax.broadcasted_iota(
-        jnp.int32, (rows_ext, lanes_ext), 1
-    )
-    inside = (
-        (row_global >= 0)
-        & (row_global < total_y)
-        & (lane_global >= 0)
-        & (lane_global < columns_dev * lax.axis_size("gz"))
-    )
-    grid_mask = inside.astype(jnp.float32)
+    gz_count = lax.axis_size("gz")
+    below = lax.ppermute(disp_init[:HALO_Y], "gy", [(i + 1, i) for i in range(gy_count - 1)])
+    above = lax.ppermute(disp_init[-HALO_Y:], "gy", [(i, i + 1) for i in range(gy_count - 1)])
+
+    def ring_columns(lo, hi):
+        return jnp.concatenate([disp_init[:, lo:hi], below[:, lo:hi], above[:, lo:hi]], axis=0)
+
+    left = lax.ppermute(
+        ring_columns(columns_dev - HALO_Z, columns_dev),
+        "gz",
+        [(i, i + 1) for i in range(gz_count - 1)],
+    )
+    right = lax.ppermute(ring_columns(0, HALO_Z), "gz", [(i + 1, i) for i in range(gz_count - 1)])
+    position = jnp.stack(
+        [lax.axis_index("gy"), lax.axis_index("gz"), jnp.int32(gy_count), jnp.int32(gz_count)]
+    ).astype(jnp.int32)
     final_ext = pl.pallas_call(
         adam_kernel,
         out_shape=jax.ShapeDtypeStruct((height, columns_dev), jnp.float32),
-        in_specs=[
-            pl.BlockSpec(memory_space=pltpu.SMEM),
-            pl.BlockSpec(memory_space=pltpu.VMEM),
-            pl.BlockSpec(memory_space=pltpu.VMEM),
+        in_specs=[smem, smem, vmem, vmem, vmem],
+        scratch_shapes=[
+            pltpu.VMEM((height + 2 * HALO_Y, columns_dev + 2 * HALO_Z), jnp.float32)
         ],
         compiler_params=pltpu.CompilerParams(vmem_limit_bytes=32 * 1024 * 1024),
-    )(smooth_radii.astype(jnp.int32), ext, grid_mask)
+    )(
+        smooth_radii.astype(jnp.int32),
+        position,
+        disp_init,
+        jnp.concatenate([below, above], axis=0),
+        jnp.concatenate([right, left], axis=1),
+    )
     return (disp_init, final_ext)
 
 

time: 74.2 us -> 74.8 us (level)
  the two profiles are of different devices: /device:TPU:38 before, /device:TPU:11 now
where the time goes in v10:
time: 74.8 us; the launch traced here: 74.7 us
  Pallas kernels  38.9 us (52%)
  starting transfers between devices  23.7 us (32%)
  waiting for transfers between devices  6.71 us (9%)
  local copies, waits for them, and re-layouts  4.28 us (6%)
  between operations  0.8 us (1%)
    pallas_call x1, Pallas kernels, per_device(): pl.pallas_call(lambda *refs: softmin_middle_kernel(total_y, *refs), out_s...  15.1 us
    pallas_call x2, Pallas kernels, channel_major(): pl.pallas_call(transpose_kernel, out_shape=(whole, ends, ends) if with_en...  10.1 us
    pallas_call x1, Pallas kernels, per_device(): pl.pallas_call(adam_kernel, out_shape=jax.ShapeDtypeStruct((height, colum...  6.92 us
    pallas_call x1, Pallas kernels, per_device(): pl.pallas_call(lambda *refs: softmin_edge_kernel(total_y, *refs), out_sha...  6.73 us
    ppermute x1, starting transfers between devices, per_device(): lax.ppermute(ring_columns(columns_dev - HALO_Z, columns_dev), 'gz', [(i,...  6.49 us
    ppermute x1, starting transfers between devices, per_device(): lax.ppermute(disp_init[:HALO_Y], 'gy', [(i + 1, i) for i in range(gy_coun...  5.51 us
    ppermute x1, waiting for transfers between devices, per_device(): lax.ppermute(ring_columns(0, HALO_Z), 'gz', [(i + 1, i) for i in range(gz...  4.62 us
    ppermute x1, starting transfers between devices, per_device(): lax.ppermute(moving_tail, 'gy', [(i, i + 1) for i in range(gy_count - 1)])  3.91 us
  transfers between devices with their start and end apart: 6, of which 3 were waited for; matrix products, arithmetic and copies ran while one was open for 3% of the time, Pallas kernels for 27%

profile of v10, /device:TPU:11, one launch (start us, length us, event | category | flops | bytes accessed | tf_op | source)
XLA Modules:
  0.0 74.7 jit_solution(1944551060185782269)
XLA Ops:
  0.6 0.0 copy-start.5
  0.6 0.0 copy-start.4
  0.7 5.3 %shard_map.72 = (bf16[16,128,512]{2,1,0:T(8,128)(2,1)}, bf16[16,32,512]{2,1,0:T(8,128)(2,1)}, bf16[16,32,512]{2,1,0:T(8,128)(2,1)}) custom-call(bf16[128,8192]{1,0:T(8,128)(2,1)} %x_ref.3), custom_call_target="tpu_custom_call" | custom-call | tf_op jit(solution)/shard_map/pallas_call | solution.py:184
  5.9 3.9 %collective-permute-start = (bf16[16,32,512]{2,1,0:T(8,128)(2,1)}, bf16[16,32,512]{2,1,0:T(8,128)(2,1)S(1)}, u32[]{:S(2)}, u32[]{:S(2)}) collective-permute-start(bf16[16,32,512]{2,1,0:T(8,128)(2,1)} %get-tuple-element.10), channel_id=1, source_target_pairs={{0,16},{16,32},{32,48},{48,64},{64,80},{80,96},{96,112},{1,17},{17... | collective-permute-start | bytes 1572872 | tf_op jit(solution)/shard_map/ppermute | solution.py:377
  9.8 3.8 %collective-permute-start.1 = (bf16[16,32,512]{2,1,0:T(8,128)(2,1)}, bf16[16,32,512]{2,1,0:T(8,128)(2,1)S(1)}, u32[]{:S(2)}, u32[]{:S(2)}) collective-permute-start(bf16[16,32,512]{2,1,0:T(8,128)(2,1)} %get-tuple-element.11), channel_id=1, source_target_pairs={{16,0},{32,16},{48,32},{64,48},{80,64},{96,80},{112,96},{17,1},{33... | collective-permute-start | bytes 1572872 | tf_op jit(solution)/shard_map/ppermute | solution.py:378
  13.6 0.0 copy-done.5
  13.6 0.0 copy-done.4
  13.7 0.1 convert_reduce_fusion
  13.8 0.7 copy.10.refs_0_
  14.5 4.9 %shard_map.71.refs_1_ = bf16[16,128,512]{2,1,0:T(8,128)(2,1)} custom-call(bf16[128,8192]{1,0:T(8,128)(2,1)} %x_ref.2), custom_call_target="tpu_custom_call" | custom-call | tf_op jit(solution)/shard_map/pallas_call | solution.py:184
  19.3 15.1 %shard_map.73 = (f32[128,512]{1,0:T(8,128)}, f32[64,512]{1,0:T(8,128)}, f32[64,512]{1,0:T(8,128)}, f32[64,512]{1,0:T(8,128)}) custom-call(f32[32,17]{1,0:T(8,128)} %copy.10.refs_0_, bf16[16,128,512]{2,1,0:T(8,128)(2,1)} %shard_map.71.refs_1_, bf16[16,128,512]{2,1,0:T(8,128)(2,1)} %get-tuple-element.9.refs_2_), custom_call_target="tpu_custom_call" | custom-call | tf_op jit(solution)/shard_map/pallas_call | solution.py:394
  34.4 0.1 pad_add_fusion.pos_ref
  34.5 0.0 collective-permute-done.refs_3_
  34.5 0.0 copy-start.2
  34.5 1.0 %collective-permute-done.1.refs_4_ = bf16[16,32,512]{2,1,0:T(8,128)(2,1)S(1)} collective-permute-done((bf16[16,32,512]{2,1,0:T(8,128)(2,1)}, bf16[16,32,512]{2,1,0:T(8,128)(2,1)S(1)}, u32[]{:S(2)}, u32[]{:S(2)}) %collective-permute-start.1) | collective-permute-done | bytes 524320 | tf_op jit(solution)/shard_map/ppermute | solution.py:378
  35.5 0.0 copy-start.3
  35.5 0.0 copy-done.2
  35.5 0.8 %copy-done.3 = bf16[16,32,512]{2,1,0:T(8,128)(2,1)} copy-done((bf16[16,32,512]{2,1,0:T(8,128)(2,1)}, bf16[16,32,512]{2,1,0:T(8,128)(2,1)S(1)}, u32[]{:S(2)}) %copy-start.3) | copy-done | bytes 524312
  36.3 0.0 copy-start.1
  36.3 6.7 %shard_map.74.d_ref = f32[128,512]{1,0:T(8,128)} custom-call(f32[32,17]{1,0:T(8,128)} %copy.10.refs_0_, bf16[16,128,512]{2,1,0:T(8,128)(2,1)} %shard_map.71.refs_1_, bf16[16,128,512]{2,1,0:T(8,128)(2,1)} %get-tuple-element.9.refs_2_, bf16[16,32,512]{2,1,0:T(8,128)(2,1)} %copy-done.2, bf16[16,32,512]{2,1,0:T(8,128)(2,1)} %copy-done.3, ...), custom_call_target="tpu_custom_call", output_to_operand_aliasing={{}: (8, {})} | custom-call | tf_op jit(solution)/shard_map/pallas_call | solution.py:401
  43.0 0.7 fusion.1
  43.8 2.2 %collective-permute-start.3 = (f32[8,512]{1,0:T(8,128)S(1)}, f32[8,512]{1,0:T(8,128)S(1)}, u32[]{:S(2)}, u32[]{:S(2)}) collective-permute-start(f32[8,512]{1,0:T(8,128)S(1)} %get-tuple-element.19), channel_id=1, source_target_pairs={{0,16},{16,32},{32,48},{48,64},{64,80},{80,96},{96,112},{1,17},{17... | collective-permute-start | bytes 49160 | tf_op jit(solution)/shard_map/ppermute | solution.py:419
  45.9 1.0 %fusion = (f32[128,64]{1,0:T(8,128)S(1)}, f32[128,64]{1,0:T(8,128)S(1)}) fusion(f32[128,512]{1,0:T(8,128)} %shard_map.74.d_ref), kind=kLoop, calls=%fused_computation.8 | loop fusion | bytes 131072 | tf_op jit(solution)/shard_map/slice | solution.py:422
  46.9 5.5 %collective-permute-start.2 = (f32[8,512]{1,0:T(8,128)S(1)}, f32[8,512]{1,0:T(8,128)S(1)}, u32[]{:S(2)}, u32[]{:S(2)}) collective-permute-start(f32[8,512]{1,0:T(8,128)S(1)} %get-tuple-element.18), channel_id=1, source_target_pairs={{16,0},{32,16},{48,32},{64,48},{80,64},{96,80},{112,96},{17,1},{33... | collective-permute-start | bytes 49160 | tf_op jit(solution)/shard_map/ppermute | solution.py:418
  52.4 0.0 collective-permute-done.3
  52.4 0.1 fusion.3
  52.5 1.1 %collective-permute-done.2 = f32[8,512]{1,0:T(8,128)S(1)} collective-permute-done((f32[8,512]{1,0:T(8,128)S(1)}, f32[8,512]{1,0:T(8,128)S(1)}, u32[]{:S(2)}, u32[]{:S(2)}) %collective-permute-start.2) | collective-permute-done | bytes 16416 | tf_op jit(solution)/shard_map/ppermute | solution.py:418
  53.6 0.1 fusion.2
  53.6 6.5 %collective-permute-start.5 = (f32[144,64]{1,0:T(8,128)S(1)}, f32[144,64]{1,0:T(8,128)S(1)}, u32[]{:S(2)}, u32[]{:S(2)}) collective-permute-start(f32[144,64]{1,0:T(8,128)S(1)} %pad_maximum_fusion.1), channel_id=1, source_target_pairs={{0,1},{1,2},{2,3},{3,4},{4,5},{5,6},{6,7},{7,8},{8,9},{9,10},{10,1... | collective-permute-start | bytes 110600 | tf_op jit(solution)/shard_map/ppermute | solution.py:424
  60.1 1.9 %collective-permute-start.4 = (f32[144,64]{1,0:T(8,128)S(1)}, f32[144,64]{1,0:T(8,128)S(1)}, u32[]{:S(2)}, u32[]{:S(2)}) collective-permute-start(f32[144,64]{1,0:T(8,128)S(1)} %pad_maximum_fusion), channel_id=1, source_target_pairs={{1,0},{2,1},{3,2},{4,3},{5,4},{6,5},{7,6},{8,7},{9,8},{10,9},{11,1... | collective-permute-start | bytes 110600 | tf_op jit(solution)/shard_map/ppermute | solution.py:429
  62.1 0.0 collective-permute-done.5
  62.1 4.6 %collective-permute-done.4 = f32[144,64]{1,0:T(8,128)S(1)} collective-permute-done((f32[144,64]{1,0:T(8,128)S(1)}, f32[144,64]{1,0:T(8,128)S(1)}, u32[]{:S(2)}, u32[]{:S(2)}) %collective-permute-start.4) | collective-permute-done | bytes 36896 | tf_op jit(solution)/shard_map/ppermute | solution.py:429
  66.7 0.1 pad_maximum_fusion.2.z_ref
  66.8 0.0 copy-done.1
  66.8 0.0 copy-start
  66.8 0.9 %copy-done = f32[128,512]{1,0:T(8,128)S(1)} copy-done((f32[128,512]{1,0:T(8,128)S(1)}, f32[128,512]{1,0:T(8,128)}, u32[]{:S(2)}) %copy-start) | copy-done | bytes 262168
  67.8 6.9 %shard_map.75 = f32[128,512]{1,0:T(8,128)} custom-call(s32[3]{0:T(128)S(1)} %copy-done.1, s32[4]{0:T(128)S(1)} %pad_add_fusion.pos_ref, f32[128,512]{1,0:T(8,128)S(1)} %copy-done, f32[16,512]{1,0:T(8,128)S(1)} %pad_maximum_fusion.3.y_ref, f32[144,128]{1,0:T(8,128)S(1)} %pad_maximum_fusion.2.z_ref), custom_call_target="tpu_custom_call" | custom-call | tf_op jit(solution)/shard_map/pallas_call | solution.py:433
  (5 shorter events, 0.0 us)
Async XLA Ops:
  0.6 13.0 %copy-start.5 = (s32[32,1]{0,1:T(1,128)S(1)}, s32[32,1]{0,1:T(1,128)}, u32[]{:S(2)}) copy-start(s32[32,1]{0,1:T(1,128)} %param.8) | copy-start | bytes 388
  0.6 13.0 %copy-start.4 = (s32[32,1,16]{0,2,1:T(8,128)S(1)}, s32[32,1,16]{0,2,1:T(8,128)}, u32[]{:S(2)}) copy-start(s32[32,1,16]{0,2,1:T(8,128)} %param.7) | copy-start | bytes 6148
  5.9 28.6 %collective-permute-start = (bf16[16,32,512]{2,1,0:T(8,128)(2,1)}, bf16[16,32,512]{2,1,0:T(8,128)(2,1)S(1)}, u32[]{:S(2)}, u32[]{:S(2)}) collective-permute-start(bf16[16,32,512]{2,1,0:T(8,128)(2,1)} %get-tuple-element.10), channel_id=1, source_target_pairs={{0,16},{16,32},{32,48},{48,64},{64,80},{80,96},{96,112},{1,17},{17... | collective-permute-start | bytes 1572872 | tf_op jit(solution)/shard_map/ppermute | solution.py:377
  9.8 25.7 %collective-permute-start.1 = (bf16[16,32,512]{2,1,0:T(8,128)(2,1)}, bf16[16,32,512]{2,1,0:T(8,128)(2,1)S(1)}, u32[]{:S(2)}, u32[]{:S(2)}) collective-permute-start(bf16[16,32,512]{2,1,0:T(8,128)(2,1)} %get-tuple-element.11), channel_id=1, source_target_pairs={{16,0},{32,16},{48,32},{64,48},{80,64},{96,80},{112,96},{17,1},{33... | collective-permute-start | bytes 1572872 | tf_op jit(solution)/shard_map/ppermute | solution.py:378
  34.5 1.0 %copy-start.2 = (bf16[16,32,512]{2,1,0:T(8,128)(2,1)}, bf16[16,32,512]{2,1,0:T(8,128)(2,1)S(1)}, u32[]{:S(2)}) copy-start(bf16[16,32,512]{2,1,0:T(8,128)(2,1)S(1)} %collective-permute-done.refs_3_) | copy-start | bytes 1572868
  35.5 0.8 %copy-start.3 = (bf16[16,32,512]{2,1,0:T(8,128)(2,1)}, bf16[16,32,512]{2,1,0:T(8,128)(2,1)S(1)}, u32[]{:S(2)}) copy-start(bf16[16,32,512]{2,1,0:T(8,128)(2,1)S(1)} %collective-permute-done.1.refs_4_) | copy-start | bytes 1572868
  36.3 30.5 %copy-start.1 = (s32[3]{0:T(128)S(1)}, s32[3]{0:T(128)}, u32[]{:S(2)}) copy-start(s32[3]{0:T(128)} %radii_ref.1) | copy-start | bytes 40
  43.8 8.6 %collective-permute-start.3 = (f32[8,512]{1,0:T(8,128)S(1)}, f32[8,512]{1,0:T(8,128)S(1)}, u32[]{:S(2)}, u32[]{:S(2)}) collective-permute-start(f32[8,512]{1,0:T(8,128)S(1)} %get-tuple-element.19), channel_id=1, source_target_pairs={{0,16},{16,32},{32,48},{48,64},{64,80},{80,96},{96,112},{1,17},{17... | collective-permute-start | bytes 49160 | tf_op jit(solution)/shard_map/ppermute | solution.py:419
  46.9 6.7 %collective-permute-start.2 = (f32[8,512]{1,0:T(8,128)S(1)}, f32[8,512]{1,0:T(8,128)S(1)}, u32[]{:S(2)}, u32[]{:S(2)}) collective-permute-start(f32[8,512]{1,0:T(8,128)S(1)} %get-tuple-element.18), channel_id=1, source_target_pairs={{16,0},{32,16},{48,32},{64,48},{80,64},{96,80},{112,96},{17,1},{33... | collective-permute-start | bytes 49160 | tf_op jit(solution)/shard_map/ppermute | solution.py:418
  53.6 8.5 %collective-permute-start.5 = (f32[144,64]{1,0:T(8,128)S(1)}, f32[144,64]{1,0:T(8,128)S(1)}, u32[]{:S(2)}, u32[]{:S(2)}) collective-permute-start(f32[144,64]{1,0:T(8,128)S(1)} %pad_maximum_fusion.1), channel_id=1, source_target_pairs={{0,1},{1,2},{2,3},{3,4},{4,5},{5,6},{6,7},{7,8},{8,9},{9,10},{10,1... | collective-permute-start | bytes 110600 | tf_op jit(solution)/shard_map/ppermute | solution.py:424
  60.1 6.6 %collective-permute-start.4 = (f32[144,64]{1,0:T(8,128)S(1)}, f32[144,64]{1,0:T(8,128)S(1)}, u32[]{:S(2)}, u32[]{:S(2)}) collective-permute-start(f32[144,64]{1,0:T(8,128)S(1)} %pad_maximum_fusion), channel_id=1, source_target_pairs={{1,0},{2,1},{3,2},{4,3},{5,4},{6,5},{7,6},{8,7},{9,8},{10,9},{11,1... | collective-permute-start | bytes 110600 | tf_op jit(solution)/shard_map/ppermute | solution.py:429
  66.8 1.0 %copy-start = (f32[128,512]{1,0:T(8,128)S(1)}, f32[128,512]{1,0:T(8,128)}, u32[]{:S(2)}) copy-start(f32[128,512]{1,0:T(8,128)} %shard_map.74.d_ref) | copy-start | bytes 786436

commit v11 on v10

--- a/solution.py
+++ b/solution.py
@@ -250,13 +250,29 @@
     return [o for o in range(NOFF) if 8 * t + 4 * o < REACH or 8 * t + 4 * o + 8 > height + REACH]
 
 
-def softmin_middle_kernel(total_y, n_ref, ft_ref, mt_ref, o_ref, pk_ref, dn_ref, nm_ref, f_ref, m0_ref, m4_ref):
-    height = ft_ref.shape[1]
-    lanes_total = ft_ref.shape[2]
+def to_channel_major(x_ref, s_ref, store):
+    chunk = 128 * CH
+    for j in range(x_ref.shape[1] // chunk):
+        s_ref[...] = x_ref[:, pl.ds(chunk * j, chunk)].astype(jnp.float32).T
+        for c in range(CH):
+            store(c, j, s_ref[pl.ds(c, 128, stride=CH), :].T)
+
+
+def softmin_middle_kernel(
+    total_y, n_ref, fx_ref, mt_ref, o_ref, pk_ref, dn_ref, nm_ref, fe_ref, f_ref, m0_ref, m4_ref, s_ref
+):
+    height = fx_ref.shape[0]
+    lanes_total = mt_ref.shape[2]
     rows = height + 2 * REACH
 
+    def store_fixed(c, j, block):
+        f_ref[c, :, pl.ds(128 * j, 128)] = block
+
+    to_channel_major(fx_ref, s_ref, store_fixed)
+    fe_ref[:, pl.ds(0, REACH), :] = f_ref[:, pl.ds(0, REACH), :].astype(fe_ref.dtype)
+    fe_ref[:, pl.ds(REACH, REACH), :] = f_ref[:, pl.ds(height - REACH, REACH), :].astype(fe_ref.dtype)
+
     def build(c, carry):
-        f_ref[c] = ft_ref[c].astype(jnp.float32)
         m0_ref[c, pl.ds(REACH, height), :] = mt_ref[c].astype(jnp.float32)
         m0_ref[c, pl.ds(0, REACH), :] = jnp.zeros((REACH, lanes_total), jnp.float32)
         m0_ref[c, pl.ds(REACH + height, REACH), :] = jnp.zeros((REACH, lanes_total), jnp.float32)
@@ -287,20 +303,14 @@
 
 
 def softmin_edge_kernel(
-    total_y, n_ref, fc_hbm, mc_hbm, top_ref, bot_ref, pk_ref, dn_ref, nm_ref, _,
-    o_hbm, f_ref, m0_ref, m4_ref, res_ref, fe_ref, me_ref, sem,
+    total_y, n_ref, fe_ref, mc_hbm, top_ref, bot_ref, pk_ref, dn_ref, nm_ref, _,
+    o_hbm, f_ref, m0_ref, m4_ref, res_ref, me_ref, s_ref, sem,
 ):
     height = o_hbm.shape[0]
     lanes_total = fe_ref.shape[2]
     rows = height + 2 * REACH
     span = REACH + 16
     copies = [
-        pltpu.make_async_copy(
-            fc_hbm.at[:, pl.ds(0, REACH), :], fe_ref.at[:, pl.ds(0, REACH), :], sem.at[2]
-        ),
-        pltpu.make_async_copy(
-            fc_hbm.at[:, pl.ds(height - REACH, REACH), :], fe_ref.at[:, pl.ds(REACH, REACH), :], sem.at[3]
-        ),
         pltpu.make_async_copy(mc_hbm.at[:, pl.ds(0, 16), :], me_ref.at[:, pl.ds(0, 16), :], sem.at[4]),
         pltpu.make_async_copy(
             mc_hbm.at[:, pl.ds(height - 16, 16), :], me_ref.at[:, pl.ds(16, 16), :], sem.at[5]
@@ -308,6 +318,15 @@
     ]
     for cp in copies:
         cp.start()
+
+    def store_top(c, j, block):
+        m0_ref[c, pl.ds(0, REACH), pl.ds(128 * j, 128)] = block
+
+    def store_bottom(c, j, block):
+        m0_ref[c, pl.ds(rows - REACH, REACH), pl.ds(128 * j, 128)] = block
+
+    to_channel_major(top_ref, s_ref, store_top)
+    to_channel_major(bot_ref, s_ref, store_bottom)
     for cp in copies:
         cp.wait()
 
@@ -316,10 +335,8 @@
         f_ref[c, pl.ds(height - REACH, REACH), :] = fe_ref[c, pl.ds(REACH, REACH), :].astype(
             jnp.float32
         )
-        m0_ref[c, pl.ds(0, REACH), :] = top_ref[c].astype(jnp.float32)
         m0_ref[c, pl.ds(REACH, 16), :] = me_ref[c, pl.ds(0, 16), :].astype(jnp.float32)
         m0_ref[c, pl.ds(rows - span, 16), :] = me_ref[c, pl.ds(16, 16), :].astype(jnp.float32)
-        m0_ref[c, pl.ds(rows - REACH, REACH), :] = bot_ref[c].astype(jnp.float32)
         m4_ref[c, pl.ds(0, span - 8), :] = m0_ref[c, pl.ds(4, span - 8), :]
         m4_ref[c, pl.ds(rows - span, span - 8), :] = m0_ref[c, pl.ds(rows - span + 4, span - 8), :]
         m4_ref[c, pl.ds(rows - 8, 8), :] = jnp.zeros((8, lanes_total), jnp.float32)
@@ -372,10 +389,13 @@
     mult = jnp.sum(hits.astype(jnp.float32), axis=1)
 
     gy_count = lax.axis_size("gy")
-    fixed_c = channel_major(fixed_features)
-    moving_c, moving_head, moving_tail = channel_major(moving_features, with_ends=True)
-    top_rows = lax.ppermute(moving_tail, "gy", [(i, i + 1) for i in range(gy_count - 1)])
-    bottom_rows = lax.ppermute(moving_head, "gy", [(i + 1, i) for i in range(gy_count - 1)])
+    top_rows = lax.ppermute(
+        moving_features[height - REACH :], "gy", [(i, i + 1) for i in range(gy_count - 1)]
+    )
+    bottom_rows = lax.ppermute(
+        moving_features[:REACH], "gy", [(i + 1, i) for i in range(gy_count - 1)]
+    )
+    moving_c = channel_major(moving_features)
 
     rows = height + 2 * REACH
     tiles = height // 8
@@ -391,28 +411,29 @@
     vmem = pl.BlockSpec(memory_space=pltpu.VMEM)
     anywhere = pl.BlockSpec(memory_space=pl.ANY)
     edge_shape = jax.ShapeDtypeStruct((2 * REACH, columns_dev), jnp.float32)
-    middle, peak_part, den_part, num_part = pl.pallas_call(
+    fixed_edge_shape = jax.ShapeDtypeStruct((CH, 2 * REACH, columns_dev), fixed_features.dtype)
+    middle, peak_part, den_part, num_part, fixed_edge = pl.pallas_call(
         lambda *refs: softmin_middle_kernel(total_y, *refs),
-        out_shape=(out_shape, edge_shape, edge_shape, edge_shape),
+        out_shape=(out_shape, edge_shape, edge_shape, edge_shape, fixed_edge_shape),
         in_specs=[smem, vmem, vmem],
-        scratch_shapes=scratch,
+        scratch_shapes=scratch + [pltpu.VMEM((128 * CH, height), jnp.float32)],
         compiler_params=params,
-    )(mult, fixed_c, moving_c)
+    )(mult, fixed_features, moving_c)
     disp_init = pl.pallas_call(
         lambda *refs: softmin_edge_kernel(total_y, *refs),
         out_shape=out_shape,
-        in_specs=[smem, anywhere, anywhere] + [vmem] * 5 + [anywhere],
+        in_specs=[smem, vmem, anywhere] + [vmem] * 5 + [anywhere],
         out_specs=anywhere,
         scratch_shapes=scratch
         + [
             pltpu.VMEM((2 * REACH, columns_dev), jnp.float32),
-            pltpu.VMEM((CH, 2 * REACH, columns_dev), jnp.bfloat16),
             pltpu.VMEM((CH, 32, columns_dev), jnp.bfloat16),
+            pltpu.VMEM((128 * CH, REACH), jnp.float32),
             pltpu.SemaphoreType.DMA((6,)),
         ],
         compiler_params=params,
         input_output_aliases={8: 0},
-    )(mult, fixed_c, moving_c, top_rows, bottom_rows, peak_part, den_part, num_part, middle)
+    )(mult, fixed_edge, moving_c, top_rows, bottom_rows, peak_part, den_part, num_part, middle)
 
     gz_count = lax.axis_size("gz")
     below = lax.ppermute(disp_init[:HALO_Y], "gy", [(i + 1, i) for i in range(gy_count - 1)])

time: 74.8 us -> 78.4 us (1.048); the launches traced: 74.7 us -> 77 us
  waiting for transfers between devices: 6.71 us -> 9.43 us
  local copies, waits for them, and re-layouts: 4.28 us -> 5.76 us
  starting transfers between devices: 23.7 us -> 22.4 us
    pallas_call x2 -> x1, Pallas kernels: 10.1 us -> 4.87 us  [channel_major(): pl.pallas_call(transpose_kernel, out_shape=(whole, ends, ends) if with_en...]
    ppermute x1, waiting for transfers between devices: 0.01 us -> 4.8 us  [per_device(): lax.ppermute(disp_init[-HALO_Y:], 'gy', [(i, i + 1) for i in range(gy_cou...]
    pallas_call x1, Pallas kernels: 6.73 us -> 9.55 us  [per_device(): pl.pallas_call(lambda *refs: softmin_edge_kernel(total_y, *refs), out_sha...]
    pallas_call x1, Pallas kernels: 15.1 us -> 17.2 us  [per_device(): pl.pallas_call(lambda *refs: softmin_middle_kernel(total_y, *refs), out_s...]
    slice x0 -> x1, local copies, waits for them, and re-layouts: none -> 1.27 us  [per_device(): moving_features[:REACH]]
    ppermute x1, waiting for transfers between devices: 1.06 us -> 0.01 us  [per_device(): lax.ppermute(disp_init[:HALO_Y], 'gy', [(i + 1, i) for i in range(gy_coun...]
    ppermute x2, waiting for transfers between devices: 1.02 us -> 0.01 us  [the longest x1 0.01 us: per_device(): lax.ppermute(moving_features[:REACH], 'gy', [(i + 1, i) for i in range(gy...]
    ppermute x2, starting transfers between devices: 7.67 us -> 6.79 us  [the longest x1 3.9 us: per_device(): lax.ppermute(moving_features[:REACH], 'gy', [(i + 1, i) for i in range(gy...]
  transfers between devices with their start and end apart: 6 -> 6, of which waited for: 3 -> 2; matrix products, arithmetic and copies ran while one was open for 3% -> 3% of each run, Pallas kernels for 27% -> 29%
where the time goes in v11:
time: 78.4 us; the launch traced here: 77 us
  Pallas kernels  38.3 us (49%)
  starting transfers between devices  22.4 us (29%)
  waiting for transfers between devices  9.43 us (12%)
  local copies, waits for them, and re-layouts  5.76 us (7%)
  between operations  0.8 us (1%)
    pallas_call x1, Pallas kernels, per_device(): pl.pallas_call(lambda *refs: softmin_middle_kernel(total_y, *refs), out_s...  17.2 us
    pallas_call x1, Pallas kernels, per_device(): pl.pallas_call(lambda *refs: softmin_edge_kernel(total_y, *refs), out_sha...  9.55 us
    ppermute x1, starting transfers between devices, per_device(): lax.ppermute(ring_columns(columns_dev - HALO_Z, columns_dev), 'gz', [(i,...  6.88 us
    pallas_call x1, Pallas kernels, per_device(): pl.pallas_call(adam_kernel, out_shape=jax.ShapeDtypeStruct((height, colum...  6.72 us
    pallas_call x1, Pallas kernels, channel_major(): pl.pallas_call(transpose_kernel, out_shape=(whole, ends, ends) if with_en...  4.87 us
    ppermute x1, waiting for transfers between devices, per_device(): lax.ppermute(disp_init[-HALO_Y:], 'gy', [(i, i + 1) for i in range(gy_cou...  4.8 us
    ppermute x1, starting transfers between devices, per_device(): lax.ppermute(disp_init[:HALO_Y], 'gy', [(i + 1, i) for i in range(gy_coun...  4.78 us
    ppermute x1, waiting for transfers between devices, per_device(): lax.ppermute(ring_columns(0, HALO_Z), 'gz', [(i + 1, i) for i in range(gz...  4.62 us
  transfers between devices with their start and end apart: 6, of which 2 were waited for; matrix products, arithmetic and copies ran while one was open for 3% of the time, Pallas kernels for 29%

profile of v11, /device:TPU:11, one launch (start us, length us, event | category | flops | bytes accessed | tf_op | source)
XLA Modules:
  0.0 77.0 jit_solution(10648682729900949184)
XLA Ops:
  0.6 1.3 %fusion = (bf16[32,8192]{1,0:T(8,128)(2,1)S(1)}, bf16[32,8192]{1,0:T(8,128)(2,1)S(1)}) fusion(bf16[128,8192]{1,0:T(8,128)(2,1)} %x_ref.1), kind=kLoop, calls=%fused_computation.8 | loop fusion | bytes 2097152 | tf_op jit(solution)/shard_map/slice | solution.py:396
  1.9 3.9 %collective-permute-start.1 = (bf16[32,8192]{1,0:T(8,128)(2,1)S(1)}, bf16[32,8192]{1,0:T(8,128)(2,1)S(1)}, u32[]{:S(2)}, u32[]{:S(2)}) collective-permute-start(bf16[32,8192]{1,0:T(8,128)(2,1)S(1)} %get-tuple-element.12), channel_id=1, source_target_pairs={{16,0},{32,16},{48,32},{64,48},{80,64},{96,80},{112,96},{17,1},{33... | collective-permute-start | bytes 1572872 | tf_op jit(solution)/shard_map/ppermute | solution.py:395
  5.8 2.9 %collective-permute-start = (bf16[32,8192]{1,0:T(8,128)(2,1)S(1)}, bf16[32,8192]{1,0:T(8,128)(2,1)S(1)}, u32[]{:S(2)}, u32[]{:S(2)}) collective-permute-start(bf16[32,8192]{1,0:T(8,128)(2,1)S(1)} %get-tuple-element.13), channel_id=1, source_target_pairs={{0,16},{16,32},{32,48},{48,64},{64,80},{80,96},{96,112},{1,17},{17... | collective-permute-start | bytes 1572872 | tf_op jit(solution)/shard_map/ppermute | solution.py:392
  8.7 0.0 copy-start.5
  8.7 0.0 copy-start.4
  8.7 4.9 %shard_map.71.refs_2_ = bf16[16,128,512]{2,1,0:T(8,128)(2,1)} custom-call(bf16[128,8192]{1,0:T(8,128)(2,1)} %x_ref.1), custom_call_target="tpu_custom_call" | custom-call | tf_op jit(solution)/shard_map/pallas_call | solution.py:184
  13.6 0.0 copy-done.5
  13.6 0.0 copy-done.4
  13.6 0.1 convert_reduce_fusion
  13.8 0.7 copy.10.refs_0_
  14.4 17.2 %shard_map.72 = (f32[128,512]{1,0:T(8,128)}, f32[64,512]{1,0:T(8,128)}, f32[64,512]{1,0:T(8,128)}, f32[64,512]{1,0:T(8,128)}, bf16[16,64,512]{2,1,0:T(8,128)(2,1)}) custom-call(f32[32,17]{1,0:T(8,128)} %copy.10.refs_0_, bf16[128,8192]{1,0:T(8,128)(2,1)} %refs_1_.1, bf16[16,128,512]{2,1,0:T(8,128)(2,1)} %shard_map.71.refs_2_), custom_call_target="tpu_custom_call" | custom-call | tf_op jit(solution)/shard_map/pallas_call | solution.py:415
  31.6 0.1 pad_add_fusion.pos_ref
  31.7 0.0 collective-permute-done.1.refs_4_
  31.7 0.0 copy-start.2
  31.7 0.0 collective-permute-done.refs_3_
  31.7 0.0 copy-start.3
  31.7 0.8 %copy-done.2 = bf16[32,8192]{1,0:T(8,128)(2,1)} copy-done((bf16[32,8192]{1,0:T(8,128)(2,1)}, bf16[32,8192]{1,0:T(8,128)(2,1)S(1)}, u32[]{:S(2)}) %copy-start.2) | copy-done | bytes 524312
  32.5 0.2 copy-done.3
  32.7 0.0 copy-start.1
  32.7 9.6 %shard_map.73.d_ref = f32[128,512]{1,0:T(8,128)} custom-call(f32[32,17]{1,0:T(8,128)} %copy.10.refs_0_, bf16[16,64,512]{2,1,0:T(8,128)(2,1)} %get-tuple-element.7.refs_1_, bf16[16,128,512]{2,1,0:T(8,128)(2,1)} %shard_map.71.refs_2_, bf16[32,8192]{1,0:T(8,128)(2,1)} %copy-done.3, bf16[32,8192]{1,0:T(8,128)(2,1)} %copy-done.2, ...), custom_call_target="tpu_custom_call", output_to_operand_aliasing={{}: (8, {})} | custom-call | tf_op jit(solution)/shard_map/pallas_call | solution.py:422
  42.3 0.7 fusion.2
  43.0 4.8 %collective-permute-start.2 = (f32[8,512]{1,0:T(8,128)S(1)}, f32[8,512]{1,0:T(8,128)S(1)}, u32[]{:S(2)}, u32[]{:S(2)}) collective-permute-start(f32[8,512]{1,0:T(8,128)S(1)} %get-tuple-element.16), channel_id=1, source_target_pairs={{16,0},{32,16},{48,32},{64,48},{80,64},{96,80},{112,96},{17,1},{33... | collective-permute-start | bytes 49160 | tf_op jit(solution)/shard_map/ppermute | solution.py:439
  47.8 1.0 %fusion.1 = (f32[128,64]{1,0:T(8,128)S(1)}, f32[128,64]{1,0:T(8,128)S(1)}) fusion(f32[128,512]{1,0:T(8,128)} %shard_map.73.d_ref), kind=kLoop, calls=%fused_computation.9 | loop fusion | bytes 131072 | tf_op jit(solution)/shard_map/slice | solution.py:443
  48.8 2.0 %collective-permute-start.3 = (f32[8,512]{1,0:T(8,128)S(1)}, f32[8,512]{1,0:T(8,128)S(1)}, u32[]{:S(2)}, u32[]{:S(2)}) collective-permute-start(f32[8,512]{1,0:T(8,128)S(1)} %get-tuple-element.17), channel_id=1, source_target_pairs={{0,16},{16,32},{32,48},{48,64},{64,80},{80,96},{96,112},{1,17},{17... | collective-permute-start | bytes 49160 | tf_op jit(solution)/shard_map/ppermute | solution.py:440
  50.8 0.0 collective-permute-done.2
  50.8 0.1 fusion.3
  50.9 4.8 %collective-permute-done.3 = f32[8,512]{1,0:T(8,128)S(1)} collective-permute-done((f32[8,512]{1,0:T(8,128)S(1)}, f32[8,512]{1,0:T(8,128)S(1)}, u32[]{:S(2)}, u32[]{:S(2)}) %collective-permute-start.3) | collective-permute-done | bytes 16416 | tf_op jit(solution)/shard_map/ppermute | solution.py:440
  55.7 0.1 fusion.4
  55.7 6.9 %collective-permute-start.5 = (f32[144,64]{1,0:T(8,128)S(1)}, f32[144,64]{1,0:T(8,128)S(1)}, u32[]{:S(2)}, u32[]{:S(2)}) collective-permute-start(f32[144,64]{1,0:T(8,128)S(1)} %pad_maximum_fusion.1), channel_id=1, source_target_pairs={{0,1},{1,2},{2,3},{3,4},{4,5},{5,6},{6,7},{7,8},{8,9},{9,10},{10,1... | collective-permute-start | bytes 110600 | tf_op jit(solution)/shard_map/ppermute | solution.py:445
  62.7 1.9 %collective-permute-start.4 = (f32[144,64]{1,0:T(8,128)S(1)}, f32[144,64]{1,0:T(8,128)S(1)}, u32[]{:S(2)}, u32[]{:S(2)}) collective-permute-start(f32[144,64]{1,0:T(8,128)S(1)} %pad_maximum_fusion), channel_id=1, source_target_pairs={{1,0},{2,1},{3,2},{4,3},{5,4},{6,5},{7,6},{8,7},{9,8},{10,9},{11,1... | collective-permute-start | bytes 110600 | tf_op jit(solution)/shard_map/ppermute | solution.py:450
  64.6 0.0 collective-permute-done.5
  64.6 4.6 %collective-permute-done.4 = f32[144,64]{1,0:T(8,128)S(1)} collective-permute-done((f32[144,64]{1,0:T(8,128)S(1)}, f32[144,64]{1,0:T(8,128)S(1)}, u32[]{:S(2)}, u32[]{:S(2)}) %collective-permute-start.4) | collective-permute-done | bytes 36896 | tf_op jit(solution)/shard_map/ppermute | solution.py:450
  69.2 0.1 pad_maximum_fusion.2.z_ref
  69.3 0.0 copy-done.1
  69.3 0.0 copy-start
  69.3 0.9 %copy-done = f32[128,512]{1,0:T(8,128)S(1)} copy-done((f32[128,512]{1,0:T(8,128)S(1)}, f32[128,512]{1,0:T(8,128)}, u32[]{:S(2)}) %copy-start) | copy-done | bytes 262168
  70.3 6.7 %shard_map.74 = f32[128,512]{1,0:T(8,128)} custom-call(s32[3]{0:T(128)S(1)} %copy-done.1, s32[4]{0:T(128)S(1)} %pad_add_fusion.pos_ref, f32[128,512]{1,0:T(8,128)S(1)} %copy-done, f32[16,512]{1,0:T(8,128)S(1)} %pad_maximum_fusion.3.y_ref, f32[144,128]{1,0:T(8,128)S(1)} %pad_maximum_fusion.2.z_ref), custom_call_target="tpu_custom_call" | custom-call | tf_op jit(solution)/shard_map/pallas_call | solution.py:454
  (5 shorter events, 0.0 us)
Async XLA Ops:
  1.9 29.8 %collective-permute-start.1 = (bf16[32,8192]{1,0:T(8,128)(2,1)S(1)}, bf16[32,8192]{1,0:T(8,128)(2,1)S(1)}, u32[]{:S(2)}, u32[]{:S(2)}) collective-permute-start(bf16[32,8192]{1,0:T(8,128)(2,1)S(1)} %get-tuple-element.12), channel_id=1, source_target_pairs={{16,0},{32,16},{48,32},{64,48},{80,64},{96,80},{112,96},{17,1},{33... | collective-permute-start | bytes 1572872 | tf_op jit(solution)/shard_map/ppermute | solution.py:395
  5.8 25.9 %collective-permute-start = (bf16[32,8192]{1,0:T(8,128)(2,1)S(1)}, bf16[32,8192]{1,0:T(8,128)(2,1)S(1)}, u32[]{:S(2)}, u32[]{:S(2)}) collective-permute-start(bf16[32,8192]{1,0:T(8,128)(2,1)S(1)} %get-tuple-element.13), channel_id=1, source_target_pairs={{0,16},{16,32},{32,48},{48,64},{64,80},{80,96},{96,112},{1,17},{17... | collective-permute-start | bytes 1572872 | tf_op jit(solution)/shard_map/ppermute | solution.py:392
  8.7 4.9 %copy-start.5 = (s32[32,1]{0,1:T(1,128)S(1)}, s32[32,1]{0,1:T(1,128)}, u32[]{:S(2)}) copy-start(s32[32,1]{0,1:T(1,128)} %param.8) | copy-start | bytes 388
  8.7 4.9 %copy-start.4 = (s32[32,1,16]{0,2,1:T(8,128)S(1)}, s32[32,1,16]{0,2,1:T(8,128)}, u32[]{:S(2)}) copy-start(s32[32,1,16]{0,2,1:T(8,128)} %param.7) | copy-start | bytes 6148
  31.7 0.8 %copy-start.2 = (bf16[32,8192]{1,0:T(8,128)(2,1)}, bf16[32,8192]{1,0:T(8,128)(2,1)S(1)}, u32[]{:S(2)}) copy-start(bf16[32,8192]{1,0:T(8,128)(2,1)S(1)} %collective-permute-done.1.refs_4_) | copy-start | bytes 1572868
  31.7 1.0 %copy-start.3 = (bf16[32,8192]{1,0:T(8,128)(2,1)}, bf16[32,8192]{1,0:T(8,128)(2,1)S(1)}, u32[]{:S(2)}) copy-start(bf16[32,8192]{1,0:T(8,128)(2,1)S(1)} %collective-permute-done.refs_3_) | copy-start | bytes 1572868
  32.7 36.6 %copy-start.1 = (s32[3]{0:T(128)S(1)}, s32[3]{0:T(128)}, u32[]{:S(2)}) copy-start(s32[3]{0:T(128)} %radii_ref.1) | copy-start | bytes 40
  43.0 7.7 %collective-permute-start.2 = (f32[8,512]{1,0:T(8,128)S(1)}, f32[8,512]{1,0:T(8,128)S(1)}, u32[]{:S(2)}, u32[]{:S(2)}) collective-permute-start(f32[8,512]{1,0:T(8,128)S(1)} %get-tuple-element.16), channel_id=1, source_target_pairs={{16,0},{32,16},{48,32},{64,48},{80,64},{96,80},{112,96},{17,1},{33... | collective-permute-start | bytes 49160 | tf_op jit(solution)/shard_map/ppermute | solution.py:439
  48.8 6.9 %collective-permute-start.3 = (f32[8,512]{1,0:T(8,128)S(1)}, f32[8,512]{1,0:T(8,128)S(1)}, u32[]{:S(2)}, u32[]{:S(2)}) collective-permute-start(f32[8,512]{1,0:T(8,128)S(1)} %get-tuple-element.17), channel_id=1, source_target_pairs={{0,16},{16,32},{32,48},{48,64},{64,80},{80,96},{96,112},{1,17},{17... | collective-permute-start | bytes 49160 | tf_op jit(solution)/shard_map/ppermute | solution.py:440
  55.7 8.8 %collective-permute-start.5 = (f32[144,64]{1,0:T(8,128)S(1)}, f32[144,64]{1,0:T(8,128)S(1)}, u32[]{:S(2)}, u32[]{:S(2)}) collective-permute-start(f32[144,64]{1,0:T(8,128)S(1)} %pad_maximum_fusion.1), channel_id=1, source_target_pairs={{0,1},{1,2},{2,3},{3,4},{4,5},{5,6},{6,7},{7,8},{8,9},{9,10},{10,1... | collective-permute-start | bytes 110600 | tf_op jit(solution)/shard_map/ppermute | solution.py:445
  62.7 6.6 %collective-permute-start.4 = (f32[144,64]{1,0:T(8,128)S(1)}, f32[144,64]{1,0:T(8,128)S(1)}, u32[]{:S(2)}, u32[]{:S(2)}) collective-permute-start(f32[144,64]{1,0:T(8,128)S(1)} %pad_maximum_fusion), channel_id=1, source_target_pairs={{1,0},{2,1},{3,2},{4,3},{5,4},{6,5},{7,6},{8,7},{9,8},{10,9},{11,1... | collective-permute-start | bytes 110600 | tf_op jit(solution)/shard_map/ppermute | solution.py:450
  69.3 1.0 %copy-start = (f32[128,512]{1,0:T(8,128)S(1)}, f32[128,512]{1,0:T(8,128)}, u32[]{:S(2)}) copy-start(f32[128,512]{1,0:T(8,128)} %shard_map.73.d_ref) | copy-start | bytes 786436

commit v12 on v11

--- a/solution.py
+++ b/solution.py
@@ -304,7 +304,7 @@
 
 def softmin_edge_kernel(
     total_y, n_ref, fe_ref, mc_hbm, top_ref, bot_ref, pk_ref, dn_ref, nm_ref, _,
-    o_hbm, f_ref, m0_ref, m4_ref, res_ref, me_ref, s_ref, sem,
+    o_hbm, f_ref, m0_ref, m4_ref, res_ref, me_ref, sem,
 ):
     height = o_hbm.shape[0]
     lanes_total = fe_ref.shape[2]
@@ -319,14 +319,6 @@
     for cp in copies:
         cp.start()
 
-    def store_top(c, j, block):
-        m0_ref[c, pl.ds(0, REACH), pl.ds(128 * j, 128)] = block
-
-    def store_bottom(c, j, block):
-        m0_ref[c, pl.ds(rows - REACH, REACH), pl.ds(128 * j, 128)] = block
-
-    to_channel_major(top_ref, s_ref, store_top)
-    to_channel_major(bot_ref, s_ref, store_bottom)
     for cp in copies:
         cp.wait()
 
@@ -335,6 +327,8 @@
         f_ref[c, pl.ds(height - REACH, REACH), :] = fe_ref[c, pl.ds(REACH, REACH), :].astype(
             jnp.float32
         )
+        m0_ref[c, pl.ds(0, REACH), :] = top_ref[c].astype(jnp.float32)
+        m0_ref[c, pl.ds(rows - REACH, REACH), :] = bot_ref[c].astype(jnp.float32)
         m0_ref[c, pl.ds(REACH, 16), :] = me_ref[c, pl.ds(0, 16), :].astype(jnp.float32)
         m0_ref[c, pl.ds(rows - span, 16), :] = me_ref[c, pl.ds(16, 16), :].astype(jnp.float32)
         m4_ref[c, pl.ds(0, span - 8), :] = m0_ref[c, pl.ds(4, span - 8), :]
@@ -389,13 +383,9 @@
     mult = jnp.sum(hits.astype(jnp.float32), axis=1)
 
     gy_count = lax.axis_size("gy")
-    top_rows = lax.ppermute(
-        moving_features[height - REACH :], "gy", [(i, i + 1) for i in range(gy_count - 1)]
-    )
-    bottom_rows = lax.ppermute(
-        moving_features[:REACH], "gy", [(i + 1, i) for i in range(gy_count - 1)]
-    )
-    moving_c = channel_major(moving_features)
+    moving_c, moving_head, moving_tail = channel_major(moving_features, with_ends=True)
+    top_rows = lax.ppermute(moving_tail, "gy", [(i, i + 1) for i in range(gy_count - 1)])
+    bottom_rows = lax.ppermute(moving_head, "gy", [(i + 1, i) for i in range(gy_count - 1)])
 
     rows = height + 2 * REACH
     tiles = height // 8
@@ -428,7 +418,6 @@
         + [
             pltpu.VMEM((2 * REACH, columns_dev), jnp.float32),
             pltpu.VMEM((CH, 32, columns_dev), jnp.bfloat16),
-            pltpu.VMEM((128 * CH, REACH), jnp.float32),
             pltpu.SemaphoreType.DMA((6,)),
         ],
         compiler_params=params,

time: 78.4 us -> 75.7 us (0.966)
  Pallas kernels: 38.3 us -> 35.3 us
  local copies, waits for them, and re-layouts: 5.76 us -> 4.28 us
  starting transfers between devices: 22.4 us -> 23.6 us
  waiting for transfers between devices: 9.43 us -> 10.5 us
    ppermute x2, waiting for transfers between devices: 0.01 us -> 3.76 us  [the longest x1 3.53 us: per_device(): lax.ppermute(moving_head, 'gy', [(i + 1, i) for i in range(gy_count - 1)])]
    pallas_call x1, Pallas kernels: 9.55 us -> 6.72 us  [per_device(): pl.pallas_call(lambda *refs: softmin_edge_kernel(total_y, *refs), out_sha...]
    ppermute x1, starting transfers between devices: 1.99 us -> 4.63 us  [per_device(): lax.ppermute(disp_init[-HALO_Y:], 'gy', [(i, i + 1) for i in range(gy_cou...]
    ppermute x1, waiting for transfers between devices: 4.8 us -> 2.16 us  [per_device(): lax.ppermute(disp_init[-HALO_Y:], 'gy', [(i, i + 1) for i in range(gy_cou...]
    ppermute x1, starting transfers between devices: 4.78 us -> 2.14 us  [per_device(): lax.ppermute(disp_init[:HALO_Y], 'gy', [(i + 1, i) for i in range(gy_coun...]
    slice x1 -> x0, local copies, waits for them, and re-layouts: 1.27 us -> none  [per_device(): moving_features[:REACH]]
    ppermute x2, starting transfers between devices: 6.79 us -> 7.67 us  [the longest x1 3.91 us: per_device(): lax.ppermute(moving_tail, 'gy', [(i, i + 1) for i in range(gy_count - 1)])]
  transfers between devices with their start and end apart: 6 -> 6, of which waited for: 2 -> 4; matrix products, arithmetic and copies ran while one was open for 3% -> 3% of each run, Pallas kernels for 29% -> 23%
where the time goes in v12:
time: 75.7 us; the launch traced here: 74.8 us
  Pallas kernels  35.3 us (47%)
  starting transfers between devices  23.6 us (31%)
  waiting for transfers between devices  10.5 us (14%)
  local copies, waits for them, and re-layouts  4.28 us (6%)
  between operations  0.81 us (1%)
    pallas_call x1, Pallas kernels, per_device(): pl.pallas_call(lambda *refs: softmin_middle_kernel(total_y, *refs), out_s...  17.2 us
    ppermute x1, starting transfers between devices, per_device(): lax.ppermute(ring_columns(columns_dev - HALO_Z, columns_dev), 'gz', [(i,...  7.19 us
    pallas_call x1, Pallas kernels, per_device(): pl.pallas_call(lambda *refs: softmin_edge_kernel(total_y, *refs), out_sha...  6.72 us
    pallas_call x1, Pallas kernels, per_device(): pl.pallas_call(adam_kernel, out_shape=jax.ShapeDtypeStruct((height, colum...  6.11 us
    pallas_call x1, Pallas kernels, channel_major(): pl.pallas_call(transpose_kernel, out_shape=(whole, ends, ends) if with_en...  5.27 us
    ppermute x1, starting transfers between devices, per_device(): lax.ppermute(disp_init[-HALO_Y:], 'gy', [(i, i + 1) for i in range(gy_cou...  4.63 us
    ppermute x1, waiting for transfers between devices, per_device(): lax.ppermute(ring_columns(0, HALO_Z), 'gz', [(i + 1, i) for i in range(gz...  4.62 us
    ppermute x1, starting transfers between devices, per_device(): lax.ppermute(moving_tail, 'gy', [(i, i + 1) for i in range(gy_count - 1)])  3.91 us
  transfers between devices with their start and end apart: 6, of which 4 were waited for; matrix products, arithmetic and copies ran while one was open for 3% of the time, Pallas kernels for 23%

profile of v12, /device:TPU:11, one launch (start us, length us, event | category | flops | bytes accessed | tf_op | source)
XLA Modules:
  0.0 74.8 jit_solution(7209073057766845423)
XLA Ops:
  0.6 0.0 copy-start.5
  0.6 0.0 copy-start.4
  0.7 5.3 %shard_map.71 = (bf16[16,128,512]{2,1,0:T(8,128)(2,1)}, bf16[16,32,512]{2,1,0:T(8,128)(2,1)}, bf16[16,32,512]{2,1,0:T(8,128)(2,1)}) custom-call(bf16[128,8192]{1,0:T(8,128)(2,1)} %x_ref.1), custom_call_target="tpu_custom_call" | custom-call | tf_op jit(solution)/shard_map/pallas_call | solution.py:184
  5.9 3.9 %collective-permute-start = (bf16[16,32,512]{2,1,0:T(8,128)(2,1)}, bf16[16,32,512]{2,1,0:T(8,128)(2,1)S(1)}, u32[]{:S(2)}, u32[]{:S(2)}) collective-permute-start(bf16[16,32,512]{2,1,0:T(8,128)(2,1)} %get-tuple-element.12), channel_id=1, source_target_pairs={{0,16},{16,32},{32,48},{48,64},{64,80},{80,96},{96,112},{1,17},{17... | collective-permute-start | bytes 1572872 | tf_op jit(solution)/shard_map/ppermute | solution.py:387
  9.8 3.8 %collective-permute-start.1 = (bf16[16,32,512]{2,1,0:T(8,128)(2,1)}, bf16[16,32,512]{2,1,0:T(8,128)(2,1)S(1)}, u32[]{:S(2)}, u32[]{:S(2)}) collective-permute-start(bf16[16,32,512]{2,1,0:T(8,128)(2,1)} %get-tuple-element.13), channel_id=1, source_target_pairs={{16,0},{32,16},{48,32},{64,48},{80,64},{96,80},{112,96},{17,1},{33... | collective-permute-start | bytes 1572872 | tf_op jit(solution)/shard_map/ppermute | solution.py:388
  13.6 0.0 copy-done.5
  13.6 0.0 copy-done.4
  13.7 0.1 convert_reduce_fusion
  13.8 0.7 copy.10.refs_0_
  14.5 17.2 %shard_map.72 = (f32[128,512]{1,0:T(8,128)}, f32[64,512]{1,0:T(8,128)}, f32[64,512]{1,0:T(8,128)}, f32[64,512]{1,0:T(8,128)}, bf16[16,64,512]{2,1,0:T(8,128)(2,1)}) custom-call(f32[32,17]{1,0:T(8,128)} %copy.10.refs_0_, bf16[128,8192]{1,0:T(8,128)(2,1)} %refs_1_.1, bf16[16,128,512]{2,1,0:T(8,128)(2,1)} %get-tuple-element.10.refs_2_), custom_call_target="tpu_custom_call" | custom-call | tf_op jit(solution)/shard_map/pallas_call | solution.py:405
  31.7 0.1 pad_add_fusion.pos_ref
  31.7 0.2 collective-permute-done.refs_3_
  32.0 0.0 copy-start.2
  32.0 3.5 %collective-permute-done.1.refs_4_ = bf16[16,32,512]{2,1,0:T(8,128)(2,1)S(1)} collective-permute-done((bf16[16,32,512]{2,1,0:T(8,128)(2,1)}, bf16[16,32,512]{2,1,0:T(8,128)(2,1)S(1)}, u32[]{:S(2)}, u32[]{:S(2)}) %collective-permute-start.1) | collective-permute-done | bytes 524320 | tf_op jit(solution)/shard_map/ppermute | solution.py:388
  35.5 0.0 copy-start.3
  35.5 0.0 copy-done.2
  35.5 0.8 %copy-done.3 = bf16[16,32,512]{2,1,0:T(8,128)(2,1)} copy-done((bf16[16,32,512]{2,1,0:T(8,128)(2,1)}, bf16[16,32,512]{2,1,0:T(8,128)(2,1)S(1)}, u32[]{:S(2)}) %copy-start.3) | copy-done | bytes 524312
  36.3 0.0 copy-start.1
  36.3 6.7 %shard_map.73.d_ref = f32[128,512]{1,0:T(8,128)} custom-call(f32[32,17]{1,0:T(8,128)} %copy.10.refs_0_, bf16[16,64,512]{2,1,0:T(8,128)(2,1)} %get-tuple-element.11.refs_1_, bf16[16,128,512]{2,1,0:T(8,128)(2,1)} %get-tuple-element.10.refs_2_, bf16[16,32,512]{2,1,0:T(8,128)(2,1)} %copy-done.2, ...), custom_call_target="tpu_custom_call", output_to_operand_aliasing={{}: (8, {})} | custom-call | tf_op jit(solution)/shard_map/pallas_call | solution.py:412
  43.0 0.7 fusion.1
  43.8 2.1 %collective-permute-start.2 = (f32[8,512]{1,0:T(8,128)S(1)}, f32[8,512]{1,0:T(8,128)S(1)}, u32[]{:S(2)}, u32[]{:S(2)}) collective-permute-start(f32[8,512]{1,0:T(8,128)S(1)} %get-tuple-element.20), channel_id=1, source_target_pairs={{16,0},{32,16},{48,32},{64,48},{80,64},{96,80},{112,96},{17,1},{33... | collective-permute-start | bytes 49160 | tf_op jit(solution)/shard_map/ppermute | solution.py:428
  45.9 1.0 %fusion = (f32[128,64]{1,0:T(8,128)S(1)}, f32[128,64]{1,0:T(8,128)S(1)}) fusion(f32[128,512]{1,0:T(8,128)} %shard_map.73.d_ref), kind=kLoop, calls=%fused_computation.8 | loop fusion | bytes 131072 | tf_op jit(solution)/shard_map/slice | solution.py:432
  46.9 4.6 %collective-permute-start.3 = (f32[8,512]{1,0:T(8,128)S(1)}, f32[8,512]{1,0:T(8,128)S(1)}, u32[]{:S(2)}, u32[]{:S(2)}) collective-permute-start(f32[8,512]{1,0:T(8,128)S(1)} %get-tuple-element.21), channel_id=1, source_target_pairs={{0,16},{16,32},{32,48},{48,64},{64,80},{80,96},{96,112},{1,17},{17... | collective-permute-start | bytes 49160 | tf_op jit(solution)/shard_map/ppermute | solution.py:429
  51.5 0.0 collective-permute-done.2
  51.5 0.1 fusion.2
  51.6 2.2 %collective-permute-done.3 = f32[8,512]{1,0:T(8,128)S(1)} collective-permute-done((f32[8,512]{1,0:T(8,128)S(1)}, f32[8,512]{1,0:T(8,128)S(1)}, u32[]{:S(2)}, u32[]{:S(2)}) %collective-permute-start.3) | collective-permute-done | bytes 16416 | tf_op jit(solution)/shard_map/ppermute | solution.py:429
  53.8 0.1 fusion.3
  53.8 7.2 %collective-permute-start.5 = (f32[144,64]{1,0:T(8,128)S(1)}, f32[144,64]{1,0:T(8,128)S(1)}, u32[]{:S(2)}, u32[]{:S(2)}) collective-permute-start(f32[144,64]{1,0:T(8,128)S(1)} %pad_maximum_fusion.1), channel_id=1, source_target_pairs={{0,1},{1,2},{2,3},{3,4},{4,5},{5,6},{6,7},{7,8},{8,9},{9,10},{10,1... | collective-permute-start | bytes 110600 | tf_op jit(solution)/shard_map/ppermute | solution.py:434
  61.1 1.9 %collective-permute-start.4 = (f32[144,64]{1,0:T(8,128)S(1)}, f32[144,64]{1,0:T(8,128)S(1)}, u32[]{:S(2)}, u32[]{:S(2)}) collective-permute-start(f32[144,64]{1,0:T(8,128)S(1)} %pad_maximum_fusion), channel_id=1, source_target_pairs={{1,0},{2,1},{3,2},{4,3},{5,4},{6,5},{7,6},{8,7},{9,8},{10,9},{11,1... | collective-permute-start | bytes 110600 | tf_op jit(solution)/shard_map/ppermute | solution.py:439
  63.0 0.0 collective-permute-done.5
  63.0 4.6 %collective-permute-done.4 = f32[144,64]{1,0:T(8,128)S(1)} collective-permute-done((f32[144,64]{1,0:T(8,128)S(1)}, f32[144,64]{1,0:T(8,128)S(1)}, u32[]{:S(2)}, u32[]{:S(2)}) %collective-permute-start.4) | collective-permute-done | bytes 36896 | tf_op jit(solution)/shard_map/ppermute | solution.py:439
  67.6 0.1 pad_maximum_fusion.2.z_ref
  67.7 0.0 copy-done.1
  67.7 0.0 copy-start
  67.7 0.9 %copy-done = f32[128,512]{1,0:T(8,128)S(1)} copy-done((f32[128,512]{1,0:T(8,128)S(1)}, f32[128,512]{1,0:T(8,128)}, u32[]{:S(2)}) %copy-start) | copy-done | bytes 262168
  68.7 6.1 %shard_map.74 = f32[128,512]{1,0:T(8,128)} custom-call(s32[3]{0:T(128)S(1)} %copy-done.1, s32[4]{0:T(128)S(1)} %pad_add_fusion.pos_ref, f32[128,512]{1,0:T(8,128)S(1)} %copy-done, f32[16,512]{1,0:T(8,128)S(1)} %pad_maximum_fusion.3.y_ref, f32[144,128]{1,0:T(8,128)S(1)} %pad_maximum_fusion.2.z_ref), custom_call_target="tpu_custom_call" | custom-call | tf_op jit(solution)/shard_map/pallas_call | solution.py:443
  (5 shorter events, 0.0 us)
Async XLA Ops:
  0.6 13.0 %copy-start.5 = (s32[32,1]{0,1:T(1,128)S(1)}, s32[32,1]{0,1:T(1,128)}, u32[]{:S(2)}) copy-start(s32[32,1]{0,1:T(1,128)} %param.8) | copy-start | bytes 388
  0.6 13.0 %copy-start.4 = (s32[32,1,16]{0,2,1:T(8,128)S(1)}, s32[32,1,16]{0,2,1:T(8,128)}, u32[]{:S(2)}) copy-start(s32[32,1,16]{0,2,1:T(8,128)} %param.7) | copy-start | bytes 6148
  5.9 26.0 %collective-permute-start = (bf16[16,32,512]{2,1,0:T(8,128)(2,1)}, bf16[16,32,512]{2,1,0:T(8,128)(2,1)S(1)}, u32[]{:S(2)}, u32[]{:S(2)}) collective-permute-start(bf16[16,32,512]{2,1,0:T(8,128)(2,1)} %get-tuple-element.12), channel_id=1, source_target_pairs={{0,16},{16,32},{32,48},{48,64},{64,80},{80,96},{96,112},{1,17},{17... | collective-permute-start | bytes 1572872 | tf_op jit(solution)/shard_map/ppermute | solution.py:387
  9.8 25.7 %collective-permute-start.1 = (bf16[16,32,512]{2,1,0:T(8,128)(2,1)}, bf16[16,32,512]{2,1,0:T(8,128)(2,1)S(1)}, u32[]{:S(2)}, u32[]{:S(2)}) collective-permute-start(bf16[16,32,512]{2,1,0:T(8,128)(2,1)} %get-tuple-element.13), channel_id=1, source_target_pairs={{16,0},{32,16},{48,32},{64,48},{80,64},{96,80},{112,96},{17,1},{33... | collective-permute-start | bytes 1572872 | tf_op jit(solution)/shard_map/ppermute | solution.py:388
  32.0 3.5 %copy-start.2 = (bf16[16,32,512]{2,1,0:T(8,128)(2,1)}, bf16[16,32,512]{2,1,0:T(8,128)(2,1)S(1)}, u32[]{:S(2)}) copy-start(bf16[16,32,512]{2,1,0:T(8,128)(2,1)S(1)} %collective-permute-done.refs_3_) | copy-start | bytes 1572868
  35.5 0.8 %copy-start.3 = (bf16[16,32,512]{2,1,0:T(8,128)(2,1)}, bf16[16,32,512]{2,1,0:T(8,128)(2,1)S(1)}, u32[]{:S(2)}) copy-start(bf16[16,32,512]{2,1,0:T(8,128)(2,1)S(1)} %collective-permute-done.1.refs_4_) | copy-start | bytes 1572868
  36.3 31.4 %copy-start.1 = (s32[3]{0:T(128)S(1)}, s32[3]{0:T(128)}, u32[]{:S(2)}) copy-start(s32[3]{0:T(128)} %radii_ref.1) | copy-start | bytes 40
  43.8 7.7 %collective-permute-start.2 = (f32[8,512]{1,0:T(8,128)S(1)}, f32[8,512]{1,0:T(8,128)S(1)}, u32[]{:S(2)}, u32[]{:S(2)}) collective-permute-start(f32[8,512]{1,0:T(8,128)S(1)} %get-tuple-element.20), channel_id=1, source_target_pairs={{16,0},{32,16},{48,32},{64,48},{80,64},{96,80},{112,96},{17,1},{33... | collective-permute-start | bytes 49160 | tf_op jit(solution)/shard_map/ppermute | solution.py:428
  46.9 6.9 %collective-permute-start.3 = (f32[8,512]{1,0:T(8,128)S(1)}, f32[8,512]{1,0:T(8,128)S(1)}, u32[]{:S(2)}, u32[]{:S(2)}) collective-permute-start(f32[8,512]{1,0:T(8,128)S(1)} %get-tuple-element.21), channel_id=1, source_target_pairs={{0,16},{16,32},{32,48},{48,64},{64,80},{80,96},{96,112},{1,17},{17... | collective-permute-start | bytes 49160 | tf_op jit(solution)/shard_map/ppermute | solution.py:429
  53.8 9.2 %collective-permute-start.5 = (f32[144,64]{1,0:T(8,128)S(1)}, f32[144,64]{1,0:T(8,128)S(1)}, u32[]{:S(2)}, u32[]{:S(2)}) collective-permute-start(f32[144,64]{1,0:T(8,128)S(1)} %pad_maximum_fusion.1), channel_id=1, source_target_pairs={{0,1},{1,2},{2,3},{3,4},{4,5},{5,6},{6,7},{7,8},{8,9},{9,10},{10,1... | collective-permute-start | bytes 110600 | tf_op jit(solution)/shard_map/ppermute | solution.py:434
  61.1 6.6 %collective-permute-start.4 = (f32[144,64]{1,0:T(8,128)S(1)}, f32[144,64]{1,0:T(8,128)S(1)}, u32[]{:S(2)}, u32[]{:S(2)}) collective-permute-start(f32[144,64]{1,0:T(8,128)S(1)} %pad_maximum_fusion), channel_id=1, source_target_pairs={{1,0},{2,1},{3,2},{4,3},{5,4},{6,5},{7,6},{8,7},{9,8},{10,9},{11,1... | collective-permute-start | bytes 110600 | tf_op jit(solution)/shard_map/ppermute | solution.py:439
  67.7 1.0 %copy-start = (f32[128,512]{1,0:T(8,128)S(1)}, f32[128,512]{1,0:T(8,128)}, u32[]{:S(2)}) copy-start(f32[128,512]{1,0:T(8,128)} %shard_map.73.d_ref) | copy-start | bytes 786436

commit v13 on v9

--- a/solution.py
+++ b/solution.py
@@ -234,13 +234,49 @@
     return [o for o in range(NOFF) if 8 * t + 4 * o < REACH or 8 * t + 4 * o + 8 > height + REACH]
 
 
-def softmin_middle_kernel(total_y, n_ref, ft_ref, mt_ref, o_ref, pk_ref, dn_ref, nm_ref, f_ref, m0_ref, m4_ref):
-    height = ft_ref.shape[1]
-    lanes_total = ft_ref.shape[2]
+def to_channel_major(x_ref, s_ref, store):
+    chunk = 128 * CH
+    for j in range(x_ref.shape[1] // chunk):
+        s_ref[...] = x_ref[:, pl.ds(chunk * j, chunk)].astype(jnp.float32).T
+        for c in range(CH):
+            store(c, j, s_ref[pl.ds(c, 128, stride=CH), :].T)
+
+
+def halo_rows_kernel(x_hbm, head_ref, tail_ref, slab_ref, s_ref, sem):
+    rows = x_hbm.shape[0]
+    copies = [
+        pltpu.make_async_copy(x_hbm.at[pl.ds(0, REACH)], slab_ref.at[pl.ds(0, REACH)], sem.at[0]),
+        pltpu.make_async_copy(
+            x_hbm.at[pl.ds(rows - REACH, REACH)], slab_ref.at[pl.ds(REACH, REACH)], sem.at[1]
+        ),
+    ]
+    for cp in copies:
+        cp.start()
+    for cp in copies:
+        cp.wait()
+
+    def store(c, j, block):
+        head_ref[c, :, pl.ds(128 * j, 128)] = block[:REACH].astype(head_ref.dtype)
+        tail_ref[c, :, pl.ds(128 * j, 128)] = block[REACH:].astype(tail_ref.dtype)
+
+    to_channel_major(slab_ref, s_ref, store)
+
+
+def softmin_middle_kernel(
+    total_y, n_ref, fx_ref, mt_ref, o_ref, pk_ref, dn_ref, nm_ref, fe_ref, f_ref, m0_ref, m4_ref, s_ref
+):
+    height = fx_ref.shape[0]
+    lanes_total = mt_ref.shape[2]
     rows = height + 2 * REACH
 
+    def store_fixed(c, j, block):
+        f_ref[c, :, pl.ds(128 * j, 128)] = block
+
+    to_channel_major(fx_ref, s_ref, store_fixed)
+    fe_ref[:, pl.ds(0, REACH), :] = f_ref[:, pl.ds(0, REACH), :].astype(fe_ref.dtype)
+    fe_ref[:, pl.ds(REACH, REACH), :] = f_ref[:, pl.ds(height - REACH, REACH), :].astype(fe_ref.dtype)
+
     def build(c, carry):
-        f_ref[c] = ft_ref[c].astype(jnp.float32)
         m0_ref[c, pl.ds(REACH, height), :] = mt_ref[c].astype(jnp.float32)
         m0_ref[c, pl.ds(0, REACH), :] = jnp.zeros((REACH, lanes_total), jnp.float32)
         m0_ref[c, pl.ds(REACH + height, REACH), :] = jnp.zeros((REACH, lanes_total), jnp.float32)
@@ -271,20 +307,14 @@
 
 
 def softmin_edge_kernel(
-    total_y, n_ref, fc_hbm, mc_hbm, top_ref, bot_ref, pk_ref, dn_ref, nm_ref, _,
-    o_hbm, f_ref, m0_ref, m4_ref, res_ref, fe_ref, me_ref, sem,
+    total_y, n_ref, fe_ref, mc_hbm, top_ref, bot_ref, pk_ref, dn_ref, nm_ref, _,
+    o_hbm, f_ref, m0_ref, m4_ref, res_ref, me_ref, sem,
 ):
     height = o_hbm.shape[0]
     lanes_total = fe_ref.shape[2]
     rows = height + 2 * REACH
     span = REACH + 16
     copies = [
-        pltpu.make_async_copy(
-            fc_hbm.at[:, pl.ds(0, REACH), :], fe_ref.at[:, pl.ds(0, REACH), :], sem.at[2]
-        ),
-        pltpu.make_async_copy(
-            fc_hbm.at[:, pl.ds(height - REACH, REACH), :], fe_ref.at[:, pl.ds(REACH, REACH), :], sem.at[3]
-        ),
         pltpu.make_async_copy(mc_hbm.at[:, pl.ds(0, 16), :], me_ref.at[:, pl.ds(0, 16), :], sem.at[4]),
         pltpu.make_async_copy(
             mc_hbm.at[:, pl.ds(height - 16, 16), :], me_ref.at[:, pl.ds(16, 16), :], sem.at[5]
@@ -292,6 +322,7 @@
     ]
     for cp in copies:
         cp.start()
+
     for cp in copies:
         cp.wait()
 
@@ -301,9 +332,9 @@
             jnp.float32
         )
         m0_ref[c, pl.ds(0, REACH), :] = top_ref[c].astype(jnp.float32)
+        m0_ref[c, pl.ds(rows - REACH, REACH), :] = bot_ref[c].astype(jnp.float32)
         m0_ref[c, pl.ds(REACH, 16), :] = me_ref[c, pl.ds(0, 16), :].astype(jnp.float32)
         m0_ref[c, pl.ds(rows - span, 16), :] = me_ref[c, pl.ds(16, 16), :].astype(jnp.float32)
-        m0_ref[c, pl.ds(rows - REACH, REACH), :] = bot_ref[c].astype(jnp.float32)
         m4_ref[c, pl.ds(0, span - 8), :] = m0_ref[c, pl.ds(4, span - 8), :]
         m4_ref[c, pl.ds(rows - span, span - 8), :] = m0_ref[c, pl.ds(rows - span + 4, span - 8), :]
         m4_ref[c, pl.ds(rows - 8, 8), :] = jnp.zeros((8, lanes_total), jnp.float32)
@@ -356,10 +387,21 @@
     mult = jnp.sum(hits.astype(jnp.float32), axis=1)
 
     gy_count = lax.axis_size("gy")
-    fixed_c = channel_major(fixed_features)
-    moving_c, moving_head, moving_tail = channel_major(moving_features, with_ends=True)
+    columns_all = moving_features.shape[1]
+    ends = jax.ShapeDtypeStruct((CH, REACH, columns_all // CH), moving_features.dtype)
+    moving_head, moving_tail = pl.pallas_call(
+        halo_rows_kernel,
+        out_shape=(ends, ends),
+        in_specs=[pl.BlockSpec(memory_space=pl.ANY)],
+        scratch_shapes=[
+            pltpu.VMEM((2 * REACH, columns_all), moving_features.dtype),
+            pltpu.VMEM((128 * CH, 2 * REACH), jnp.float32),
+            pltpu.SemaphoreType.DMA((2,)),
+        ],
+    )(moving_features)
     top_rows = lax.ppermute(moving_tail, "gy", [(i, i + 1) for i in range(gy_count - 1)])
     bottom_rows = lax.ppermute(moving_head, "gy", [(i + 1, i) for i in range(gy_count - 1)])
+    moving_c = channel_major(moving_features)
 
     rows = height + 2 * REACH
     tiles = height // 8
@@ -375,28 +417,28 @@
     vmem = pl.BlockSpec(memory_space=pltpu.VMEM)
     anywhere = pl.BlockSpec(memory_space=pl.ANY)
     edge_shape = jax.ShapeDtypeStruct((2 * REACH, columns_dev), jnp.float32)
-    middle, peak_part, den_part, num_part = pl.pallas_call(
+    fixed_edge_shape = jax.ShapeDtypeStruct((CH, 2 * REACH, columns_dev), fixed_features.dtype)
+    middle, peak_part, den_part, num_part, fixed_edge = pl.pallas_call(
         lambda *refs: softmin_middle_kernel(total_y, *refs),
-        out_shape=(out_shape, edge_shape, edge_shape, edge_shape),
+        out_shape=(out_shape, edge_shape, edge_shape, edge_shape, fixed_edge_shape),
         in_specs=[smem, vmem, vmem],
-        scratch_shapes=scratch,
+        scratch_shapes=scratch + [pltpu.VMEM((128 * CH, height), jnp.float32)],
         compiler_params=params,
-    )(mult, fixed_c, moving_c)
+    )(mult, fixed_features, moving_c)
     disp_init = pl.pallas_call(
         lambda *refs: softmin_edge_kernel(total_y, *refs),
         out_shape=out_shape,
-        in_specs=[smem, anywhere, anywhere] + [vmem] * 5 + [anywhere],
+        in_specs=[smem, vmem, anywhere] + [vmem] * 5 + [anywhere],
         out_specs=anywhere,
         scratch_shapes=scratch
         + [
             pltpu.VMEM((2 * REACH, columns_dev), jnp.float32),
-            pltpu.VMEM((CH, 2 * REACH, columns_dev), jnp.bfloat16),
             pltpu.VMEM((CH, 32, columns_dev), jnp.bfloat16),
             pltpu.SemaphoreType.DMA((6,)),
         ],
         compiler_params=params,
         input_output_aliases={8: 0},
-    )(mult, fixed_c, moving_c, top_rows, bottom_rows, peak_part, den_part, num_part, middle)
+    )(mult, fixed_edge, moving_c, top_rows, bottom_rows, peak_part, den_part, num_part, middle)
 
     ext = exchange_halo(disp_init, HALO_Y, HALO_Z, SEND_Y, SEND_Z)
     rows_ext, lanes_ext = ext.shape

time: 74.2 us -> 76 us (1.024)
  the two profiles are of different devices: /device:TPU:38 before, /device:TPU:11 now
where the time goes in v13:
time: 76 us; the launch traced here: 75.7 us
  Pallas kernels  40.1 us (53%)
  starting transfers between devices  24.2 us (32%)
  waiting for transfers between devices  5.82 us (8%)
  local copies, waits for them, and re-layouts  2.43 us (3%)
  other arithmetic  2.33 us (3%)
  between operations  0.8 us (1%)
    pallas_call x1, Pallas kernels, per_device(): pl.pallas_call(lambda *refs: softmin_middle_kernel(total_y, *refs), out_s...  17.2 us
    pallas_call x1, Pallas kernels, per_device(): pl.pallas_call(adam_kernel, out_shape=jax.ShapeDtypeStruct((height, colum...  7.22 us
    ppermute x1, starting transfers between devices, exchange_halo(): lax.ppermute(cells[:, -send_z:], 'gz', [(i, i + 1) for i in range(nz - 1)])  6.88 us
    pallas_call x1, Pallas kernels, per_device(): pl.pallas_call(lambda *refs: softmin_edge_kernel(total_y, *refs), out_sha...  6.72 us
    pallas_call x1, Pallas kernels, channel_major(): pl.pallas_call(transpose_kernel, out_shape=(whole, ends, ends) if with_en...  4.86 us
    ppermute x1, starting transfers between devices, exchange_halo(): lax.ppermute(cells[:send_y], 'gy', [(i + 1, i) for i in range(ny - 1)])  4.66 us
    ppermute x1, waiting for transfers between devices, exchange_halo(): lax.ppermute(cells[:, :send_z], 'gz', [(i + 1, i) for i in range(nz - 1)])  4.51 us
    pallas_call x1, Pallas kernels, per_device(): pl.pallas_call(halo_rows_kernel, out_shape=(ends, ends), in_specs=[pl.Blo...  4.15 us
  transfers between devices with their start and end apart: 6, of which 2 were waited for; matrix products, arithmetic and copies ran while one was open for 1% of the time, Pallas kernels for 29%

profile of v13, /device:TPU:11, one launch (start us, length us, event | category | flops | bytes accessed | tf_op | source)
XLA Modules:
  0.0 75.7 jit_solution(9104585883433276083)
XLA Ops:
  0.6 4.1 %shard_map.73 = (bf16[16,32,512]{2,1,0:T(8,128)(2,1)}, bf16[16,32,512]{2,1,0:T(8,128)(2,1)}) custom-call(bf16[128,8192]{1,0:T(8,128)(2,1)} %x_hbm.1), custom_call_target="tpu_custom_call" | custom-call | tf_op jit(solution)/shard_map/pallas_call | solution.py:392
  4.8 3.9 %collective-permute-start = (bf16[16,32,512]{2,1,0:T(8,128)(2,1)}, bf16[16,32,512]{2,1,0:T(8,128)(2,1)S(1)}, u32[]{:S(2)}, u32[]{:S(2)}) collective-permute-start(bf16[16,32,512]{2,1,0:T(8,128)(2,1)} %get-tuple-element.10), channel_id=1, source_target_pairs={{0,16},{16,32},{32,48},{48,64},{64,80},{80,96},{96,112},{1,17},{17... | collective-permute-start | bytes 1572872 | tf_op jit(solution)/shard_map/ppermute | solution.py:402
  8.7 0.0 copy-start.4
  8.7 0.0 copy-start.3
  8.7 3.8 %collective-permute-start.1 = (bf16[16,32,512]{2,1,0:T(8,128)(2,1)}, bf16[16,32,512]{2,1,0:T(8,128)(2,1)S(1)}, u32[]{:S(2)}, u32[]{:S(2)}) collective-permute-start(bf16[16,32,512]{2,1,0:T(8,128)(2,1)} %get-tuple-element.11), channel_id=1, source_target_pairs={{16,0},{32,16},{48,32},{64,48},{80,64},{96,80},{112,96},{17,1},{33... | collective-permute-start | bytes 1572872 | tf_op jit(solution)/shard_map/ppermute | solution.py:403
  12.5 4.9 %shard_map.71.refs_2_ = bf16[16,128,512]{2,1,0:T(8,128)(2,1)} custom-call(bf16[128,8192]{1,0:T(8,128)(2,1)} %x_hbm.1), custom_call_target="tpu_custom_call" | custom-call | tf_op jit(solution)/shard_map/pallas_call | solution.py:168
  17.4 0.0 copy-done.4
  17.4 0.0 copy-done.3
  17.4 0.1 convert_reduce_fusion
  17.5 0.7 copy.10.refs_0_
  18.2 17.2 %shard_map.72 = (f32[128,512]{1,0:T(8,128)}, f32[64,512]{1,0:T(8,128)}, f32[64,512]{1,0:T(8,128)}, f32[64,512]{1,0:T(8,128)}, bf16[16,64,512]{2,1,0:T(8,128)(2,1)}) custom-call(f32[32,17]{1,0:T(8,128)} %copy.10.refs_0_, bf16[128,8192]{1,0:T(8,128)(2,1)} %refs_1_.1, bf16[16,128,512]{2,1,0:T(8,128)(2,1)} %shard_map.71.refs_2_), custom_call_target="tpu_custom_call" | custom-call | tf_op jit(solution)/shard_map/pallas_call | solution.py:421
  35.4 0.0 collective-permute-done.refs_3_
  35.4 0.0 copy-start.1
  35.4 0.0 collective-permute-done.1.refs_4_
  35.4 0.0 copy-start.2
  35.4 0.8 %copy-done.1 = bf16[16,32,512]{2,1,0:T(8,128)(2,1)} copy-done((bf16[16,32,512]{2,1,0:T(8,128)(2,1)}, bf16[16,32,512]{2,1,0:T(8,128)(2,1)S(1)}, u32[]{:S(2)}) %copy-start.1) | copy-done | bytes 524312
  36.2 0.2 copy-done.2
  36.4 0.0 copy-start
  36.4 6.7 %shard_map.74 = f32[128,512]{1,0:T(8,128)} custom-call(f32[32,17]{1,0:T(8,128)} %copy.10.refs_0_, bf16[16,64,512]{2,1,0:T(8,128)(2,1)} %get-tuple-element.9.refs_1_, bf16[16,128,512]{2,1,0:T(8,128)(2,1)} %shard_map.71.refs_2_, bf16[16,32,512]{2,1,0:T(8,128)(2,1)} %copy-done.1, bf16[16,32,512]{2,1,0:T(8,128)(2,1)} %copy-done.2, ...), custom_call_target="tpu_custom_call", output_to_operand_aliasing={{}: (8, {})} | custom-call | tf_op jit(solution)/shard_map/pallas_call | solution.py:428
  43.1 0.7 fusion.2
  43.9 3.0 %collective-permute-start.2 = (f32[8,512]{1,0:T(8,128)S(1)}, f32[8,512]{1,0:T(8,128)S(1)}, u32[]{:S(2)}, u32[]{:S(2)}) collective-permute-start(f32[8,512]{1,0:T(8,128)S(1)} %get-tuple-element.18), channel_id=1, source_target_pairs={{0,16},{16,32},{32,48},{48,64},{64,80},{80,96},{96,112},{1,17},{17... | collective-permute-start | bytes 49160 | tf_op jit(solution)/shard_map/ppermute | solution.py:92
  46.9 4.7 %collective-permute-start.3 = (f32[8,512]{1,0:T(8,128)S(1)}, f32[8,512]{1,0:T(8,128)S(1)}, u32[]{:S(2)}, u32[]{:S(2)}) collective-permute-start(f32[8,512]{1,0:T(8,128)S(1)} %get-tuple-element.19), channel_id=1, source_target_pairs={{16,0},{32,16},{48,32},{64,48},{80,64},{96,80},{112,96},{17,1},{33... | collective-permute-start | bytes 49160 | tf_op jit(solution)/shard_map/ppermute | solution.py:93
  51.6 0.0 collective-permute-done.2
  51.6 1.3 %collective-permute-done.3 = f32[8,512]{1,0:T(8,128)S(1)} collective-permute-done((f32[8,512]{1,0:T(8,128)S(1)}, f32[8,512]{1,0:T(8,128)S(1)}, u32[]{:S(2)}, u32[]{:S(2)}) %collective-permute-start.3) | collective-permute-done | bytes 16416 | tf_op jit(solution)/shard_map/ppermute | solution.py:93
  52.9 1.0 %pad_maximum_fusion.3 = (f32[144,64]{1,0:T(8,128)S(1)}, f32[144,64]{1,0:T(8,128)S(1)}) fusion(f32[8,512]{1,0:T(8,128)S(1)} %collective-permute-done.3, f32[128,512]{1,0:T(8,128)} %shard_map.74, f32[8,512]{1,0:T(8,128)S(1)} %collective-permute-done.2), kind=kLoop, calls=%fused_computation.5 | loop fusion | flops 36864 | bytes 368640 | tf_op jit(solution)/shard_map/slice | solution.py:95
  53.9 6.9 %collective-permute-start.4 = (f32[144,64]{1,0:T(8,128)S(1)}, f32[144,64]{1,0:T(8,128)S(1)}, u32[]{:S(2)}, u32[]{:S(2)}) collective-permute-start(f32[144,64]{1,0:T(8,128)S(1)} %get-tuple-element.16), channel_id=1, source_target_pairs={{0,1},{1,2},{2,3},{3,4},{4,5},{5,6},{6,7},{7,8},{8,9},{9,10},{10,1... | collective-permute-start | bytes 110600 | tf_op jit(solution)/shard_map/ppermute | solution.py:95
  60.7 1.9 %collective-permute-start.5 = (f32[144,64]{1,0:T(8,128)S(1)}, f32[144,64]{1,0:T(8,128)S(1)}, u32[]{:S(2)}, u32[]{:S(2)}) collective-permute-start(f32[144,64]{1,0:T(8,128)S(1)} %get-tuple-element.17), channel_id=1, source_target_pairs={{1,0},{2,1},{3,2},{4,3},{5,4},{6,5},{7,6},{8,7},{9,8},{10,9},{11,1... | collective-permute-start | bytes 110600 | tf_op jit(solution)/shard_map/ppermute | solution.py:96
  62.7 0.1 and_convert_fusion.mask_ref
  62.8 0.0 collective-permute-done.4
  62.8 4.5 %collective-permute-done.5 = f32[144,64]{1,0:T(8,128)S(1)} collective-permute-done((f32[144,64]{1,0:T(8,128)S(1)}, f32[144,64]{1,0:T(8,128)S(1)}, u32[]{:S(2)}, u32[]{:S(2)}) %collective-permute-start.5) | collective-permute-done | bytes 36896 | tf_op jit(solution)/shard_map/ppermute | solution.py:96
  67.3 1.1 %pad_maximum_fusion.d_ref = f32[144,640]{1,0:T(8,128)S(1)} fusion(f32[144,64]{1,0:T(8,128)S(1)} %collective-permute-done.5, f32[8,512]{1,0:T(8,128)S(1)} %collective-permute-done.3, f32[128,512]{1,0:T(8,128)} %shard_map.74, f32[8,512]{1,0:T(8,128)S(1)} %collective-permute-done.2, f32[144,64]{1,0:T(8,128)S(1)} %collective-permute-done.4), kind=kLoop, calls=%fused_computation | loop fusion | flops 368640 | bytes 737280 | tf_op jit(solution)/shard_map/concatenate | solution.py:97
  68.4 0.0 copy-done
  68.5 7.2 %shard_map.75 = f32[128,512]{1,0:T(8,128)} custom-call(s32[3]{0:T(128)S(1)} %copy-done, f32[144,640]{1,0:T(8,128)S(1)} %pad_maximum_fusion.d_ref, f32[144,640]{1,0:T(8,128)S(1)} %and_convert_fusion.mask_ref), custom_call_target="tpu_custom_call" | custom-call | tf_op jit(solution)/shard_map/pallas_call | solution.py:458
  (4 shorter events, 0.0 us)
Async XLA Ops:
  4.8 30.6 %collective-permute-start = (bf16[16,32,512]{2,1,0:T(8,128)(2,1)}, bf16[16,32,512]{2,1,0:T(8,128)(2,1)S(1)}, u32[]{:S(2)}, u32[]{:S(2)}) collective-permute-start(bf16[16,32,512]{2,1,0:T(8,128)(2,1)} %get-tuple-element.10), channel_id=1, source_target_pairs={{0,16},{16,32},{32,48},{48,64},{64,80},{80,96},{96,112},{1,17},{17... | collective-permute-start | bytes 1572872 | tf_op jit(solution)/shard_map/ppermute | solution.py:402
  8.7 8.7 %copy-start.4 = (s32[32,1]{0,1:T(1,128)S(1)}, s32[32,1]{0,1:T(1,128)}, u32[]{:S(2)}) copy-start(s32[32,1]{0,1:T(1,128)} %param.8) | copy-start | bytes 388
  8.7 8.7 %copy-start.3 = (s32[32,1,16]{0,2,1:T(8,128)S(1)}, s32[32,1,16]{0,2,1:T(8,128)}, u32[]{:S(2)}) copy-start(s32[32,1,16]{0,2,1:T(8,128)} %param.7) | copy-start | bytes 6148
  8.7 26.7 %collective-permute-start.1 = (bf16[16,32,512]{2,1,0:T(8,128)(2,1)}, bf16[16,32,512]{2,1,0:T(8,128)(2,1)S(1)}, u32[]{:S(2)}, u32[]{:S(2)}) collective-permute-start(bf16[16,32,512]{2,1,0:T(8,128)(2,1)} %get-tuple-element.11), channel_id=1, source_target_pairs={{16,0},{32,16},{48,32},{64,48},{80,64},{96,80},{112,96},{17,1},{33... | collective-permute-start | bytes 1572872 | tf_op jit(solution)/shard_map/ppermute | solution.py:403
  35.4 0.8 %copy-start.1 = (bf16[16,32,512]{2,1,0:T(8,128)(2,1)}, bf16[16,32,512]{2,1,0:T(8,128)(2,1)S(1)}, u32[]{:S(2)}) copy-start(bf16[16,32,512]{2,1,0:T(8,128)(2,1)S(1)} %collective-permute-done.refs_3_) | copy-start | bytes 1572868
  35.4 1.0 %copy-start.2 = (bf16[16,32,512]{2,1,0:T(8,128)(2,1)}, bf16[16,32,512]{2,1,0:T(8,128)(2,1)S(1)}, u32[]{:S(2)}) copy-start(bf16[16,32,512]{2,1,0:T(8,128)(2,1)S(1)} %collective-permute-done.1.refs_4_) | copy-start | bytes 1572868
  36.4 32.0 %copy-start = (s32[3]{0:T(128)S(1)}, s32[3]{0:T(128)}, u32[]{:S(2)}) copy-start(s32[3]{0:T(128)} %radii_ref.1) | copy-start | bytes 40
  43.9 7.7 %collective-permute-start.2 = (f32[8,512]{1,0:T(8,128)S(1)}, f32[8,512]{1,0:T(8,128)S(1)}, u32[]{:S(2)}, u32[]{:S(2)}) collective-permute-start(f32[8,512]{1,0:T(8,128)S(1)} %get-tuple-element.18), channel_id=1, source_target_pairs={{0,16},{16,32},{32,48},{48,64},{64,80},{80,96},{96,112},{1,17},{17... | collective-permute-start | bytes 49160 | tf_op jit(solution)/shard_map/ppermute | solution.py:92
  46.9 6.0 %collective-permute-start.3 = (f32[8,512]{1,0:T(8,128)S(1)}, f32[8,512]{1,0:T(8,128)S(1)}, u32[]{:S(2)}, u32[]{:S(2)}) collective-permute-start(f32[8,512]{1,0:T(8,128)S(1)} %get-tuple-element.19), channel_id=1, source_target_pairs={{16,0},{32,16},{48,32},{64,48},{80,64},{96,80},{112,96},{17,1},{33... | collective-permute-start | bytes 49160 | tf_op jit(solution)/shard_map/ppermute | solution.py:93
  53.9 8.9 %collective-permute-start.4 = (f32[144,64]{1,0:T(8,128)S(1)}, f32[144,64]{1,0:T(8,128)S(1)}, u32[]{:S(2)}, u32[]{:S(2)}) collective-permute-start(f32[144,64]{1,0:T(8,128)S(1)} %get-tuple-element.16), channel_id=1, source_target_pairs={{0,1},{1,2},{2,3},{3,4},{4,5},{5,6},{6,7},{7,8},{8,9},{9,10},{10,1... | collective-permute-start | bytes 110600 | tf_op jit(solution)/shard_map/ppermute | solution.py:95
  60.7 6.6 %collective-permute-start.5 = (f32[144,64]{1,0:T(8,128)S(1)}, f32[144,64]{1,0:T(8,128)S(1)}, u32[]{:S(2)}, u32[]{:S(2)}) collective-permute-start(f32[144,64]{1,0:T(8,128)S(1)} %get-tuple-element.17), channel_id=1, source_target_pairs={{1,0},{2,1},{3,2},{4,3},{5,4},{6,5},{7,6},{8,7},{9,8},{10,9},{11,1... | collective-permute-start | bytes 110600 | tf_op jit(solution)/shard_map/ppermute | solution.py:96

commit v14 on v9

--- a/solution.py
+++ b/solution.py
@@ -271,39 +271,59 @@
 
 
 def softmin_edge_kernel(
-    total_y, n_ref, fc_hbm, mc_hbm, top_ref, bot_ref, pk_ref, dn_ref, nm_ref, _,
-    o_hbm, f_ref, m0_ref, m4_ref, res_ref, fe_ref, me_ref, sem,
+    total_y, n_ref, fc_hbm, mc_hbm, top_hbm, bot_hbm, pk_ref, dn_ref, nm_ref, _,
+    o_hbm, f_ref, m0_ref, m4_ref, res_ref, fe_ref, me_ref, top_ref, bot_ref, sem,
 ):
     height = o_hbm.shape[0]
     lanes_total = fe_ref.shape[2]
     rows = height + 2 * REACH
     span = REACH + 16
-    copies = [
+    halo_copies = [
+        pltpu.make_async_copy(top_hbm, top_ref, sem.at[6]),
+        pltpu.make_async_copy(bot_hbm, bot_ref, sem.at[7]),
+    ]
+    fixed_copies = [
         pltpu.make_async_copy(
             fc_hbm.at[:, pl.ds(0, REACH), :], fe_ref.at[:, pl.ds(0, REACH), :], sem.at[2]
         ),
         pltpu.make_async_copy(
             fc_hbm.at[:, pl.ds(height - REACH, REACH), :], fe_ref.at[:, pl.ds(REACH, REACH), :], sem.at[3]
         ),
+    ]
+    moving_copies = [
         pltpu.make_async_copy(mc_hbm.at[:, pl.ds(0, 16), :], me_ref.at[:, pl.ds(0, 16), :], sem.at[4]),
         pltpu.make_async_copy(
             mc_hbm.at[:, pl.ds(height - 16, 16), :], me_ref.at[:, pl.ds(16, 16), :], sem.at[5]
         ),
     ]
-    for cp in copies:
+    for cp in halo_copies + fixed_copies + moving_copies:
         cp.start()
-    for cp in copies:
+    for cp in halo_copies:
         cp.wait()
 
-    def build(c, carry):
+    def build_halo(c, carry):
+        m0_ref[c, pl.ds(0, REACH), :] = top_ref[c].astype(jnp.float32)
+        m0_ref[c, pl.ds(rows - REACH, REACH), :] = bot_ref[c].astype(jnp.float32)
+        return carry
+
+    lax.fori_loop(0, CH, build_halo, 0)
+    for cp in fixed_copies:
+        cp.wait()
+
+    def build_fixed(c, carry):
         f_ref[c, pl.ds(0, REACH), :] = fe_ref[c, pl.ds(0, REACH), :].astype(jnp.float32)
         f_ref[c, pl.ds(height - REACH, REACH), :] = fe_ref[c, pl.ds(REACH, REACH), :].astype(
             jnp.float32
         )
-        m0_ref[c, pl.ds(0, REACH), :] = top_ref[c].astype(jnp.float32)
+        return carry
+
+    lax.fori_loop(0, CH, build_fixed, 0)
+    for cp in moving_copies:
+        cp.wait()
+
+    def build(c, carry):
         m0_ref[c, pl.ds(REACH, 16), :] = me_ref[c, pl.ds(0, 16), :].astype(jnp.float32)
         m0_ref[c, pl.ds(rows - span, 16), :] = me_ref[c, pl.ds(16, 16), :].astype(jnp.float32)
-        m0_ref[c, pl.ds(rows - REACH, REACH), :] = bot_ref[c].astype(jnp.float32)
         m4_ref[c, pl.ds(0, span - 8), :] = m0_ref[c, pl.ds(4, span - 8), :]
         m4_ref[c, pl.ds(rows - span, span - 8), :] = m0_ref[c, pl.ds(rows - span + 4, span - 8), :]
         m4_ref[c, pl.ds(rows - 8, 8), :] = jnp.zeros((8, lanes_total), jnp.float32)
@@ -385,14 +405,16 @@
     disp_init = pl.pallas_call(
         lambda *refs: softmin_edge_kernel(total_y, *refs),
         out_shape=out_shape,
-        in_specs=[smem, anywhere, anywhere] + [vmem] * 5 + [anywhere],
+        in_specs=[smem] + [anywhere] * 4 + [vmem] * 3 + [anywhere],
         out_specs=anywhere,
         scratch_shapes=scratch
         + [
             pltpu.VMEM((2 * REACH, columns_dev), jnp.float32),
             pltpu.VMEM((CH, 2 * REACH, columns_dev), jnp.bfloat16),
             pltpu.VMEM((CH, 32, columns_dev), jnp.bfloat16),
-            pltpu.SemaphoreType.DMA((6,)),
+            pltpu.VMEM((CH, REACH, columns_dev), jnp.bfloat16),
+            pltpu.VMEM((CH, REACH, columns_dev), jnp.bfloat16),
+            pltpu.SemaphoreType.DMA((8,)),
         ],
         compiler_params=params,
         input_output_aliases={8: 0},

time: 74.2 us -> 74 us (level)
  no operation moved by 1% of the time
where the time goes in v14:
time: 74 us; the launch traced here: 73.2 us
  Pallas kernels  38.3 us (52%)
  starting transfers between devices  19.9 us (27%)
  waiting for transfers between devices  9.69 us (13%)
  other arithmetic  2.34 us (3%)
  local copies, waits for them, and re-layouts  2.23 us (3%)
  between operations  0.8 us (1%)
    pallas_call x1, Pallas kernels, per_device(): pl.pallas_call(lambda *refs: softmin_middle_kernel(total_y, *refs), out_s...  15.1 us
    pallas_call x2, Pallas kernels, channel_major(): pl.pallas_call(transpose_kernel, out_shape=(whole, ends, ends) if with_en...  10.1 us
    pallas_call x1, Pallas kernels, per_device(): pl.pallas_call(adam_kernel, out_shape=jax.ShapeDtypeStruct((height, colum...  6.57 us
    pallas_call x1, Pallas kernels, per_device(): pl.pallas_call(lambda *refs: softmin_edge_kernel(total_y, *refs), out_sha...  6.52 us
    ppermute x1, waiting for transfers between devices, exchange_halo(): lax.ppermute(cells[-send_y:], 'gy', [(i, i + 1) for i in range(ny - 1)])  5.3 us
    ppermute x1, starting transfers between devices, per_device(): lax.ppermute(moving_tail, 'gy', [(i, i + 1) for i in range(gy_count - 1)])  5.09 us
    ppermute x1, starting transfers between devices, exchange_halo(): lax.ppermute(cells[:send_y], 'gy', [(i + 1, i) for i in range(ny - 1)])  4.63 us
    ppermute x1, waiting for transfers between devices, exchange_halo(): lax.ppermute(cells[:, -send_z:], 'gz', [(i, i + 1) for i in range(nz - 1)])  4.03 us
  transfers between devices with their start and end apart: 6, of which 3 were waited for; matrix products, arithmetic and copies ran while one was open for 1% of the time, Pallas kernels for 27%

profile of v14, /device:TPU:38, one launch (start us, length us, event | category | flops | bytes accessed | tf_op | source)
XLA Modules:
  0.0 73.2 jit_solution(2703248599239268263)
XLA Ops:
  0.6 0.0 copy-start.4
  0.6 0.0 copy-start.3
  0.7 5.2 %shard_map.72 = (bf16[16,128,512]{2,1,0:T(8,128)(2,1)}, bf16[16,32,512]{2,1,0:T(8,128)(2,1)}, bf16[16,32,512]{2,1,0:T(8,128)(2,1)}) custom-call(bf16[128,8192]{1,0:T(8,128)(2,1)} %x_ref.3), custom_call_target="tpu_custom_call" | custom-call | tf_op jit(solution)/shard_map/pallas_call | solution.py:168
  5.9 5.1 %collective-permute-start = (bf16[16,32,512]{2,1,0:T(8,128)(2,1)}, bf16[16,32,512]{2,1,0:T(8,128)(2,1)S(1)}, u32[]{:S(2)}, u32[]{:S(2)}) collective-permute-start(bf16[16,32,512]{2,1,0:T(8,128)(2,1)} %get-tuple-element.10), channel_id=1, source_target_pairs={{0,16},{16,32},{32,48},{48,64},{64,80},{80,96},{96,112},{1,17},{17... | collective-permute-start | bytes 1572872 | tf_op jit(solution)/shard_map/ppermute | solution.py:381
  11.0 3.1 %collective-permute-start.1 = (bf16[16,32,512]{2,1,0:T(8,128)(2,1)}, bf16[16,32,512]{2,1,0:T(8,128)(2,1)S(1)}, u32[]{:S(2)}, u32[]{:S(2)}) collective-permute-start(bf16[16,32,512]{2,1,0:T(8,128)(2,1)} %get-tuple-element.11), channel_id=1, source_target_pairs={{16,0},{32,16},{48,32},{64,48},{80,64},{96,80},{112,96},{17,1},{33... | collective-permute-start | bytes 1572872 | tf_op jit(solution)/shard_map/ppermute | solution.py:382
  14.2 0.0 copy-done.4
  14.2 0.0 copy-done.3
  14.2 0.1 convert_reduce_fusion
  14.3 0.7 copy.10.refs_0_
  15.0 4.9 %shard_map.71.refs_1_ = bf16[16,128,512]{2,1,0:T(8,128)(2,1)} custom-call(bf16[128,8192]{1,0:T(8,128)(2,1)} %x_ref.2), custom_call_target="tpu_custom_call" | custom-call | tf_op jit(solution)/shard_map/pallas_call | solution.py:168
  19.8 15.1 %shard_map.73 = (f32[128,512]{1,0:T(8,128)}, f32[64,512]{1,0:T(8,128)}, f32[64,512]{1,0:T(8,128)}, f32[64,512]{1,0:T(8,128)}) custom-call(f32[32,17]{1,0:T(8,128)} %copy.10.refs_0_, bf16[16,128,512]{2,1,0:T(8,128)(2,1)} %shard_map.71.refs_1_, bf16[16,128,512]{2,1,0:T(8,128)(2,1)} %get-tuple-element.9.refs_2_), custom_call_target="tpu_custom_call" | custom-call | tf_op jit(solution)/shard_map/pallas_call | solution.py:398
  34.9 0.0 collective-permute-done.refs_3_
  34.9 0.0 copy-start.1
  34.9 0.4 collective-permute-done.1.refs_4_
  35.3 0.0 copy-start.2
  35.3 0.4 copy-done.1
  35.7 0.4 copy-done.2
  36.1 0.0 copy-start
  36.1 6.5 %shard_map.74 = f32[128,512]{1,0:T(8,128)} custom-call(f32[32,17]{1,0:T(8,128)} %copy.10.refs_0_, bf16[16,128,512]{2,1,0:T(8,128)(2,1)} %shard_map.71.refs_1_, bf16[16,128,512]{2,1,0:T(8,128)(2,1)} %get-tuple-element.9.refs_2_, bf16[16,32,512]{2,1,0:T(8,128)(2,1)} %copy-done.1, bf16[16,32,512]{2,1,0:T(8,128)(2,1)} %copy-done.2, ...), custom_call_target="tpu_custom_call", output_to_operand_aliasing={{}: (8, {})} | custom-call | tf_op jit(solution)/shard_map/pallas_call | solution.py:405
  42.6 0.7 %fusion.2 = (f32[8,512]{1,0:T(8,128)S(1)}, f32[8,512]{1,0:T(8,128)S(1)}) fusion(f32[128,512]{1,0:T(8,128)} %shard_map.74), kind=kLoop, calls=%fused_computation.12 | loop fusion | bytes 65536 | tf_op jit(solution)/shard_map/slice | solution.py:92
  43.3 4.6 %collective-permute-start.3 = (f32[8,512]{1,0:T(8,128)S(1)}, f32[8,512]{1,0:T(8,128)S(1)}, u32[]{:S(2)}, u32[]{:S(2)}) collective-permute-start(f32[8,512]{1,0:T(8,128)S(1)} %get-tuple-element.19), channel_id=1, source_target_pairs={{16,0},{32,16},{48,32},{64,48},{80,64},{96,80},{112,96},{17,1},{33... | collective-permute-start | bytes 49160 | tf_op jit(solution)/shard_map/ppermute | solution.py:93
  48.0 2.7 %collective-permute-start.2 = (f32[8,512]{1,0:T(8,128)S(1)}, f32[8,512]{1,0:T(8,128)S(1)}, u32[]{:S(2)}, u32[]{:S(2)}) collective-permute-start(f32[8,512]{1,0:T(8,128)S(1)} %get-tuple-element.18), channel_id=1, source_target_pairs={{0,16},{16,32},{32,48},{48,64},{64,80},{80,96},{96,112},{1,17},{17... | collective-permute-start | bytes 49160 | tf_op jit(solution)/shard_map/ppermute | solution.py:92
  50.7 0.0 collective-permute-done.3
  50.7 5.3 %collective-permute-done.2 = f32[8,512]{1,0:T(8,128)S(1)} collective-permute-done((f32[8,512]{1,0:T(8,128)S(1)}, f32[8,512]{1,0:T(8,128)S(1)}, u32[]{:S(2)}, u32[]{:S(2)}) %collective-permute-start.2) | collective-permute-done | bytes 16416 | tf_op jit(solution)/shard_map/ppermute | solution.py:92
  56.0 1.0 %pad_maximum_fusion.3 = (f32[144,64]{1,0:T(8,128)S(1)}, f32[144,64]{1,0:T(8,128)S(1)}) fusion(f32[8,512]{1,0:T(8,128)S(1)} %collective-permute-done.3, f32[128,512]{1,0:T(8,128)} %shard_map.74, f32[8,512]{1,0:T(8,128)S(1)} %collective-permute-done.2), kind=kLoop, calls=%fused_computation.5 | loop fusion | flops 36864 | bytes 368640 | tf_op jit(solution)/shard_map/slice | solution.py:95
  57.0 1.9 %collective-permute-start.5 = (f32[144,64]{1,0:T(8,128)S(1)}, f32[144,64]{1,0:T(8,128)S(1)}, u32[]{:S(2)}, u32[]{:S(2)}) collective-permute-start(f32[144,64]{1,0:T(8,128)S(1)} %get-tuple-element.17), channel_id=1, source_target_pairs={{1,0},{2,1},{3,2},{4,3},{5,4},{6,5},{7,6},{8,7},{9,8},{10,9},{11,1... | collective-permute-start | bytes 110600 | tf_op jit(solution)/shard_map/ppermute | solution.py:96
  58.9 2.4 %collective-permute-start.4 = (f32[144,64]{1,0:T(8,128)S(1)}, f32[144,64]{1,0:T(8,128)S(1)}, u32[]{:S(2)}, u32[]{:S(2)}) collective-permute-start(f32[144,64]{1,0:T(8,128)S(1)} %get-tuple-element.16), channel_id=1, source_target_pairs={{0,1},{1,2},{2,3},{3,4},{4,5},{5,6},{6,7},{7,8},{8,9},{9,10},{10,1... | collective-permute-start | bytes 110600 | tf_op jit(solution)/shard_map/ppermute | solution.py:95
  61.3 0.1 and_convert_fusion.mask_ref
  61.4 0.0 collective-permute-done.5
  61.4 4.0 %collective-permute-done.4 = f32[144,64]{1,0:T(8,128)S(1)} collective-permute-done((f32[144,64]{1,0:T(8,128)S(1)}, f32[144,64]{1,0:T(8,128)S(1)}, u32[]{:S(2)}, u32[]{:S(2)}) %collective-permute-start.4) | collective-permute-done | bytes 36896 | tf_op jit(solution)/shard_map/ppermute | solution.py:95
  65.5 1.1 %pad_maximum_fusion.d_ref = f32[144,640]{1,0:T(8,128)S(1)} fusion(f32[144,64]{1,0:T(8,128)S(1)} %collective-permute-done.5, f32[8,512]{1,0:T(8,128)S(1)} %collective-permute-done.3, f32[128,512]{1,0:T(8,128)} %shard_map.74, f32[8,512]{1,0:T(8,128)S(1)} %collective-permute-done.2, f32[144,64]{1,0:T(8,128)S(1)} %collective-permute-done.4), kind=kLoop, calls=%fused_computation | loop fusion | flops 368640 | bytes 737280 | tf_op jit(solution)/shard_map/concatenate | solution.py:97
  66.6 0.0 copy-done
  66.6 6.6 %shard_map.75 = f32[128,512]{1,0:T(8,128)} custom-call(s32[3]{0:T(128)S(1)} %copy-done, f32[144,640]{1,0:T(8,128)S(1)} %pad_maximum_fusion.d_ref, f32[144,640]{1,0:T(8,128)S(1)} %and_convert_fusion.mask_ref), custom_call_target="tpu_custom_call" | custom-call | tf_op jit(solution)/shard_map/pallas_call | solution.py:438
  (4 shorter events, 0.0 us)
Async XLA Ops:
  0.6 13.5 %copy-start.4 = (s32[32,1]{0,1:T(1,128)S(1)}, s32[32,1]{0,1:T(1,128)}, u32[]{:S(2)}) copy-start(s32[32,1]{0,1:T(1,128)} %param.8) | copy-start | bytes 388
  0.6 13.5 %copy-start.3 = (s32[32,1,16]{0,2,1:T(8,128)S(1)}, s32[32,1,16]{0,2,1:T(8,128)}, u32[]{:S(2)}) copy-start(s32[32,1,16]{0,2,1:T(8,128)} %param.7) | copy-start | bytes 6148
  5.9 29.0 %collective-permute-start = (bf16[16,32,512]{2,1,0:T(8,128)(2,1)}, bf16[16,32,512]{2,1,0:T(8,128)(2,1)S(1)}, u32[]{:S(2)}, u32[]{:S(2)}) collective-permute-start(bf16[16,32,512]{2,1,0:T(8,128)(2,1)} %get-tuple-element.10), channel_id=1, source_target_pairs={{0,16},{16,32},{32,48},{48,64},{64,80},{80,96},{96,112},{1,17},{17... | collective-permute-start | bytes 1572872 | tf_op jit(solution)/shard_map/ppermute | solution.py:381
  11.0 24.3 %collective-permute-start.1 = (bf16[16,32,512]{2,1,0:T(8,128)(2,1)}, bf16[16,32,512]{2,1,0:T(8,128)(2,1)S(1)}, u32[]{:S(2)}, u32[]{:S(2)}) collective-permute-start(bf16[16,32,512]{2,1,0:T(8,128)(2,1)} %get-tuple-element.11), channel_id=1, source_target_pairs={{16,0},{32,16},{48,32},{64,48},{80,64},{96,80},{112,96},{17,1},{33... | collective-permute-start | bytes 1572872 | tf_op jit(solution)/shard_map/ppermute | solution.py:382
  34.9 0.8 %copy-start.1 = (bf16[16,32,512]{2,1,0:T(8,128)(2,1)}, bf16[16,32,512]{2,1,0:T(8,128)(2,1)S(1)}, u32[]{:S(2)}) copy-start(bf16[16,32,512]{2,1,0:T(8,128)(2,1)S(1)} %collective-permute-done.refs_3_) | copy-start | bytes 1572868
  35.3 0.8 %copy-start.2 = (bf16[16,32,512]{2,1,0:T(8,128)(2,1)}, bf16[16,32,512]{2,1,0:T(8,128)(2,1)S(1)}, u32[]{:S(2)}) copy-start(bf16[16,32,512]{2,1,0:T(8,128)(2,1)S(1)} %collective-permute-done.1.refs_4_) | copy-start | bytes 1572868
  36.1 30.5 %copy-start = (s32[3]{0:T(128)S(1)}, s32[3]{0:T(128)}, u32[]{:S(2)}) copy-start(s32[3]{0:T(128)} %radii_ref.1) | copy-start | bytes 40
  43.3 7.4 %collective-permute-start.3 = (f32[8,512]{1,0:T(8,128)S(1)}, f32[8,512]{1,0:T(8,128)S(1)}, u32[]{:S(2)}, u32[]{:S(2)}) collective-permute-start(f32[8,512]{1,0:T(8,128)S(1)} %get-tuple-element.19), channel_id=1, source_target_pairs={{16,0},{32,16},{48,32},{64,48},{80,64},{96,80},{112,96},{17,1},{33... | collective-permute-start | bytes 49160 | tf_op jit(solution)/shard_map/ppermute | solution.py:93
  48.0 8.0 %collective-permute-start.2 = (f32[8,512]{1,0:T(8,128)S(1)}, f32[8,512]{1,0:T(8,128)S(1)}, u32[]{:S(2)}, u32[]{:S(2)}) collective-permute-start(f32[8,512]{1,0:T(8,128)S(1)} %get-tuple-element.18), channel_id=1, source_target_pairs={{0,16},{16,32},{32,48},{48,64},{64,80},{80,96},{96,112},{1,17},{17... | collective-permute-start | bytes 49160 | tf_op jit(solution)/shard_map/ppermute | solution.py:92
  57.0 4.5 %collective-permute-start.5 = (f32[144,64]{1,0:T(8,128)S(1)}, f32[144,64]{1,0:T(8,128)S(1)}, u32[]{:S(2)}, u32[]{:S(2)}) collective-permute-start(f32[144,64]{1,0:T(8,128)S(1)} %get-tuple-element.17), channel_id=1, source_target_pairs={{1,0},{2,1},{3,2},{4,3},{5,4},{6,5},{7,6},{8,7},{9,8},{10,9},{11,1... | collective-permute-start | bytes 110600 | tf_op jit(solution)/shard_map/ppermute | solution.py:96
  58.9 6.6 %collective-permute-start.4 = (f32[144,64]{1,0:T(8,128)S(1)}, f32[144,64]{1,0:T(8,128)S(1)}, u32[]{:S(2)}, u32[]{:S(2)}) collective-permute-start(f32[144,64]{1,0:T(8,128)S(1)} %get-tuple-element.16), channel_id=1, source_target_pairs={{0,1},{1,2},{2,3},{3,4},{4,5},{5,6},{6,7},{7,8},{8,9},{9,10},{10,1... | collective-permute-start | bytes 110600 | tf_op jit(solution)/shard_map/ppermute | solution.py:95

commit v15 on v14

--- a/solution.py
+++ b/solution.py
@@ -86,11 +86,11 @@
 SEND_Z = 8 * XS
 
 
-def exchange_halo(cells, wy, wz, send_y, send_z):
+def exchange_halo(cells, head, tail, wy, wz, send_y, send_z):
     ny = lax.axis_size("gy")
     nz = lax.axis_size("gz")
-    top = lax.ppermute(cells[-send_y:], "gy", [(i, i + 1) for i in range(ny - 1)])
-    bottom = lax.ppermute(cells[:send_y], "gy", [(i + 1, i) for i in range(ny - 1)])
+    top = lax.ppermute(tail, "gy", [(i, i + 1) for i in range(ny - 1)])
+    bottom = lax.ppermute(head, "gy", [(i + 1, i) for i in range(ny - 1)])
     cells = jnp.concatenate([top, cells, bottom], axis=0)
     left = lax.ppermute(cells[:, -send_z:], "gz", [(i, i + 1) for i in range(nz - 1)])
     right = lax.ppermute(cells[:, :send_z], "gz", [(i + 1, i) for i in range(nz - 1)])
@@ -272,7 +272,7 @@
 
 def softmin_edge_kernel(
     total_y, n_ref, fc_hbm, mc_hbm, top_hbm, bot_hbm, pk_ref, dn_ref, nm_ref, _,
-    o_hbm, f_ref, m0_ref, m4_ref, res_ref, fe_ref, me_ref, top_ref, bot_ref, sem,
+    o_hbm, head_ref, tail_ref, f_ref, m0_ref, m4_ref, res_ref, fe_ref, me_ref, top_ref, bot_ref, sem,
 ):
     height = o_hbm.shape[0]
     lanes_total = fe_ref.shape[2]
@@ -359,6 +359,8 @@
     )
     head.start()
     tail.start()
+    head_ref[...] = res_ref[pl.ds(0, head_ref.shape[0]), :]
+    tail_ref[...] = res_ref[pl.ds(2 * REACH - tail_ref.shape[0], tail_ref.shape[0]), :]
     head.wait()
     tail.wait()
 
@@ -402,11 +404,12 @@
         scratch_shapes=scratch,
         compiler_params=params,
     )(mult, fixed_c, moving_c)
-    disp_init = pl.pallas_call(
+    face_shape = jax.ShapeDtypeStruct((SEND_Y, columns_dev), jnp.float32)
+    disp_init, disp_head, disp_tail = pl.pallas_call(
         lambda *refs: softmin_edge_kernel(total_y, *refs),
-        out_shape=out_shape,
+        out_shape=(out_shape, face_shape, face_shape),
         in_specs=[smem] + [anywhere] * 4 + [vmem] * 3 + [anywhere],
-        out_specs=anywhere,
+        out_specs=(anywhere, vmem, vmem),
         scratch_shapes=scratch
         + [
             pltpu.VMEM((2 * REACH, columns_dev), jnp.float32),
@@ -420,7 +423,7 @@
         input_output_aliases={8: 0},
     )(mult, fixed_c, moving_c, top_rows, bottom_rows, peak_part, den_part, num_part, middle)
 
-    ext = exchange_halo(disp_init, HALO_Y, HALO_Z, SEND_Y, SEND_Z)
+    ext = exchange_halo(disp_init, disp_head, disp_tail, HALO_Y, HALO_Z, SEND_Y, SEND_Z)
     rows_ext, lanes_ext = ext.shape
     row_global = lax.axis_index("gy") * height - HALO_Y + lax.broadcasted_iota(
         jnp.int32, (rows_ext, lanes_ext), 0

time: 74 us -> 70.9 us (0.958)
  the two profiles are of different devices: /device:TPU:38 before, /device:TPU:11 now
where the time goes in v15:
time: 70.9 us; the launch traced here: 69.8 us
  Pallas kernels  39.5 us (56%)
  starting transfers between devices  23.8 us (34%)
  waiting for transfers between devices  2.72 us (4%)
  local copies, waits for them, and re-layouts  2.55 us (4%)
  between operations  0.81 us (1%)
    pallas_call x1, Pallas kernels, per_device(): pl.pallas_call(lambda *refs: softmin_middle_kernel(total_y, *refs), out_s...  15.1 us
    pallas_call x2, Pallas kernels, channel_major(): pl.pallas_call(transpose_kernel, out_shape=(whole, ends, ends) if with_en...  10.1 us
    pallas_call x1, Pallas kernels, per_device(): pl.pallas_call(adam_kernel, out_shape=jax.ShapeDtypeStruct((height, colum...  7.22 us
    pallas_call x1, Pallas kernels, per_device(): pl.pallas_call(lambda *refs: softmin_edge_kernel(total_y, *refs), out_sha...  7.13 us
    ppermute x1, starting transfers between devices, exchange_halo(): bottom = lax.ppermute(head, 'gy', [(i + 1, i) for i in range(ny - 1)])  5.55 us
    ppermute x1, starting transfers between devices, exchange_halo(): lax.ppermute(cells[:, -send_z:], 'gz', [(i, i + 1) for i in range(nz - 1)])  4.23 us
    ppermute x1, starting transfers between devices, exchange_halo(): lax.ppermute(cells[:, :send_z], 'gz', [(i + 1, i) for i in range(nz - 1)])  4.17 us
    ppermute x1, starting transfers between devices, per_device(): lax.ppermute(moving_tail, 'gy', [(i, i + 1) for i in range(gy_count - 1)])  3.91 us
  transfers between devices with their start and end apart: 6, of which 3 were waited for; matrix products, arithmetic and copies ran while one was open for 3% of the time, Pallas kernels for 29%

profile of v15, /device:TPU:11, one launch (start us, length us, event | category | flops | bytes accessed | tf_op | source)
XLA Modules:
  0.0 69.8 jit_solution(17528712449856337109)
XLA Ops:
  0.6 0.0 copy-start.4
  0.6 0.0 copy-start.3
  0.7 5.2 %shard_map.72 = (bf16[16,128,512]{2,1,0:T(8,128)(2,1)}, bf16[16,32,512]{2,1,0:T(8,128)(2,1)}, bf16[16,32,512]{2,1,0:T(8,128)(2,1)}) custom-call(bf16[128,8192]{1,0:T(8,128)(2,1)} %x_ref.3), custom_call_target="tpu_custom_call" | custom-call | tf_op jit(solution)/shard_map/pallas_call | solution.py:168
  5.9 3.9 %collective-permute-start = (bf16[16,32,512]{2,1,0:T(8,128)(2,1)}, bf16[16,32,512]{2,1,0:T(8,128)(2,1)S(1)}, u32[]{:S(2)}, u32[]{:S(2)}) collective-permute-start(bf16[16,32,512]{2,1,0:T(8,128)(2,1)} %get-tuple-element.13), channel_id=1, source_target_pairs={{0,16},{16,32},{32,48},{48,64},{64,80},{80,96},{96,112},{1,17},{17... | collective-permute-start | bytes 1572872 | tf_op jit(solution)/shard_map/ppermute | solution.py:383
  9.8 3.8 %collective-permute-start.1 = (bf16[16,32,512]{2,1,0:T(8,128)(2,1)}, bf16[16,32,512]{2,1,0:T(8,128)(2,1)S(1)}, u32[]{:S(2)}, u32[]{:S(2)}) collective-permute-start(bf16[16,32,512]{2,1,0:T(8,128)(2,1)} %get-tuple-element.14), channel_id=1, source_target_pairs={{16,0},{32,16},{48,32},{64,48},{80,64},{96,80},{112,96},{17,1},{33... | collective-permute-start | bytes 1572872 | tf_op jit(solution)/shard_map/ppermute | solution.py:384
  13.6 0.0 copy-done.4
  13.6 0.0 copy-done.3
  13.6 0.1 convert_reduce_fusion
  13.7 0.7 copy.10.refs_0_
  14.4 4.9 %shard_map.71.refs_1_ = bf16[16,128,512]{2,1,0:T(8,128)(2,1)} custom-call(bf16[128,8192]{1,0:T(8,128)(2,1)} %x_ref.2), custom_call_target="tpu_custom_call" | custom-call | tf_op jit(solution)/shard_map/pallas_call | solution.py:168
  19.3 15.1 %shard_map.73 = (f32[128,512]{1,0:T(8,128)}, f32[64,512]{1,0:T(8,128)}, f32[64,512]{1,0:T(8,128)}, f32[64,512]{1,0:T(8,128)}) custom-call(f32[32,17]{1,0:T(8,128)} %copy.10.refs_0_, bf16[16,128,512]{2,1,0:T(8,128)(2,1)} %shard_map.71.refs_1_, bf16[16,128,512]{2,1,0:T(8,128)(2,1)} %get-tuple-element.12.refs_2_), custom_call_target="tpu_custom_call" | custom-call | tf_op jit(solution)/shard_map/pallas_call | solution.py:400
  34.3 0.0 collective-permute-done.refs_3_
  34.3 0.0 copy-start.1
  34.4 1.1 %collective-permute-done.1.refs_4_ = bf16[16,32,512]{2,1,0:T(8,128)(2,1)S(1)} collective-permute-done((bf16[16,32,512]{2,1,0:T(8,128)(2,1)}, bf16[16,32,512]{2,1,0:T(8,128)(2,1)S(1)}, u32[]{:S(2)}, u32[]{:S(2)}) %collective-permute-start.1) | collective-permute-done | bytes 524320 | tf_op jit(solution)/shard_map/ppermute | solution.py:384
  35.4 0.0 copy-start.2
  35.5 0.0 copy-done.1
  35.5 0.8 %copy-done.2 = bf16[16,32,512]{2,1,0:T(8,128)(2,1)} copy-done((bf16[16,32,512]{2,1,0:T(8,128)(2,1)}, bf16[16,32,512]{2,1,0:T(8,128)(2,1)S(1)}, u32[]{:S(2)}) %copy-start.2) | copy-done | bytes 524312
  36.2 0.0 copy-start
  36.2 7.1 %shard_map.74 = (f32[128,512]{1,0:T(8,128)}, f32[8,512]{1,0:T(8,128)}, f32[8,512]{1,0:T(8,128)}) custom-call(f32[32,17]{1,0:T(8,128)} %copy.10.refs_0_, bf16[16,128,512]{2,1,0:T(8,128)(2,1)} %shard_map.71.refs_1_, bf16[16,128,512]{2,1,0:T(8,128)(2,1)} %get-tuple-element.12.refs_2_, bf16[16,32,512]{2,1,0:T(8,128)(2,1)} %copy-done.1, ...), custom_call_target="tpu_custom_call", output_to_operand_aliasing={{0}: (8, {})} | custom-call | tf_op jit(solution)/shard_map/pallas_call | solution.py:408
  43.4 2.1 %collective-permute-start.2 = (f32[8,512]{1,0:T(8,128)}, f32[8,512]{1,0:T(8,128)S(1)}, u32[]{:S(2)}, u32[]{:S(2)}) collective-permute-start(f32[8,512]{1,0:T(8,128)} %get-tuple-element.20), channel_id=1, source_target_pairs={{0,16},{16,32},{32,48},{48,64},{64,80},{80,96},{96,112},{1,17},{17... | collective-permute-start | bytes 49160 | tf_op jit(solution)/shard_map/ppermute | solution.py:92
  45.5 5.5 %collective-permute-start.3 = (f32[8,512]{1,0:T(8,128)}, f32[8,512]{1,0:T(8,128)S(1)}, u32[]{:S(2)}, u32[]{:S(2)}) collective-permute-start(f32[8,512]{1,0:T(8,128)} %get-tuple-element.21), channel_id=1, source_target_pairs={{16,0},{32,16},{48,32},{64,48},{80,64},{96,80},{112,96},{17,1},{33... | collective-permute-start | bytes 49160 | tf_op jit(solution)/shard_map/ppermute | solution.py:93
  51.1 0.0 collective-permute-done.2
  51.1 1.0 %constant_dynamic-update-slice_fusion.1 = f32[144,512]{1,0:T(8,128)S(1)} fusion(f32[144,512]{1,0:T(8,128)S(1)} %constant_dynamic-update-slice_fusion.2, f32[128,512]{1,0:T(8,128)} %get-tuple-element.10), kind=kLoop, calls=%fused_computation.4 | loop fusion | bytes 524288
  52.1 0.4 collective-permute-done.3
  52.5 0.1 fusion.2
  52.5 4.2 %collective-permute-start.5 = (f32[144,64]{1,0:T(8,128)S(1)}, f32[144,64]{1,0:T(8,128)S(1)}, u32[]{:S(2)}, u32[]{:S(2)}) collective-permute-start(f32[144,64]{1,0:T(8,128)S(1)} %get-tuple-element.23), channel_id=1, source_target_pairs={{1,0},{2,1},{3,2},{4,3},{5,4},{6,5},{7,6},{8,7},{9,8},{10,9},{11,1... | collective-permute-start | bytes 110600 | tf_op jit(solution)/shard_map/ppermute | solution.py:96
  56.7 4.2 %collective-permute-start.4 = (f32[144,64]{1,0:T(8,128)S(1)}, f32[144,64]{1,0:T(8,128)S(1)}, u32[]{:S(2)}, u32[]{:S(2)}) collective-permute-start(f32[144,64]{1,0:T(8,128)S(1)} %get-tuple-element.22), channel_id=1, source_target_pairs={{0,1},{1,2},{2,3},{3,4},{4,5},{5,6},{6,7},{7,8},{8,9},{9,10},{10,1... | collective-permute-start | bytes 110600 | tf_op jit(solution)/shard_map/ppermute | solution.py:95
  61.0 0.1 and_convert_fusion.mask_ref
  61.1 0.0 collective-permute-done.5
  61.1 1.3 %collective-permute-done.4 = f32[144,64]{1,0:T(8,128)S(1)} collective-permute-done((f32[144,64]{1,0:T(8,128)S(1)}, f32[144,64]{1,0:T(8,128)S(1)}, u32[]{:S(2)}, u32[]{:S(2)}) %collective-permute-start.4) | collective-permute-done | bytes 36896 | tf_op jit(solution)/shard_map/ppermute | solution.py:95
  62.3 0.2 pad_maximum_fusion.d_ref
  62.5 0.0 copy-done
  62.5 7.2 %shard_map.75 = f32[128,512]{1,0:T(8,128)} custom-call(s32[3]{0:T(128)S(1)} %copy-done, f32[144,640]{1,0:T(8,128)S(1)} %pad_maximum_fusion.d_ref, f32[144,640]{1,0:T(8,128)S(1)} %and_convert_fusion.mask_ref), custom_call_target="tpu_custom_call" | custom-call | tf_op jit(solution)/shard_map/pallas_call | solution.py:441
  (6 shorter events, 0.0 us)
Async XLA Ops:
  0.6 12.9 %copy-start.4 = (s32[32,1]{0,1:T(1,128)S(1)}, s32[32,1]{0,1:T(1,128)}, u32[]{:S(2)}) copy-start(s32[32,1]{0,1:T(1,128)} %param.8) | copy-start | bytes 388
  0.6 13.0 %copy-start.3 = (s32[32,1,16]{0,2,1:T(8,128)S(1)}, s32[32,1,16]{0,2,1:T(8,128)}, u32[]{:S(2)}) copy-start(s32[32,1,16]{0,2,1:T(8,128)} %param.7) | copy-start | bytes 6148
  5.9 28.5 %collective-permute-start = (bf16[16,32,512]{2,1,0:T(8,128)(2,1)}, bf16[16,32,512]{2,1,0:T(8,128)(2,1)S(1)}, u32[]{:S(2)}, u32[]{:S(2)}) collective-permute-start(bf16[16,32,512]{2,1,0:T(8,128)(2,1)} %get-tuple-element.13), channel_id=1, source_target_pairs={{0,16},{16,32},{32,48},{48,64},{64,80},{80,96},{96,112},{1,17},{17... | collective-permute-start | bytes 1572872 | tf_op jit(solution)/shard_map/ppermute | solution.py:383
  9.8 25.7 %collective-permute-start.1 = (bf16[16,32,512]{2,1,0:T(8,128)(2,1)}, bf16[16,32,512]{2,1,0:T(8,128)(2,1)S(1)}, u32[]{:S(2)}, u32[]{:S(2)}) collective-permute-start(bf16[16,32,512]{2,1,0:T(8,128)(2,1)} %get-tuple-element.14), channel_id=1, source_target_pairs={{16,0},{32,16},{48,32},{64,48},{80,64},{96,80},{112,96},{17,1},{33... | collective-permute-start | bytes 1572872 | tf_op jit(solution)/shard_map/ppermute | solution.py:384
  34.3 1.1 %copy-start.1 = (bf16[16,32,512]{2,1,0:T(8,128)(2,1)}, bf16[16,32,512]{2,1,0:T(8,128)(2,1)S(1)}, u32[]{:S(2)}) copy-start(bf16[16,32,512]{2,1,0:T(8,128)(2,1)S(1)} %collective-permute-done.refs_3_) | copy-start | bytes 1572868
  35.4 0.8 %copy-start.2 = (bf16[16,32,512]{2,1,0:T(8,128)(2,1)}, bf16[16,32,512]{2,1,0:T(8,128)(2,1)S(1)}, u32[]{:S(2)}) copy-start(bf16[16,32,512]{2,1,0:T(8,128)(2,1)S(1)} %collective-permute-done.1.refs_4_) | copy-start | bytes 1572868
  36.2 26.3 %copy-start = (s32[3]{0:T(128)S(1)}, s32[3]{0:T(128)}, u32[]{:S(2)}) copy-start(s32[3]{0:T(128)} %radii_ref.1) | copy-start | bytes 40
  43.4 7.7 %collective-permute-start.2 = (f32[8,512]{1,0:T(8,128)}, f32[8,512]{1,0:T(8,128)S(1)}, u32[]{:S(2)}, u32[]{:S(2)}) collective-permute-start(f32[8,512]{1,0:T(8,128)} %get-tuple-element.20), channel_id=1, source_target_pairs={{0,16},{16,32},{32,48},{48,64},{64,80},{80,96},{96,112},{1,17},{17... | collective-permute-start | bytes 49160 | tf_op jit(solution)/shard_map/ppermute | solution.py:92
  45.5 6.9 %collective-permute-start.3 = (f32[8,512]{1,0:T(8,128)}, f32[8,512]{1,0:T(8,128)S(1)}, u32[]{:S(2)}, u32[]{:S(2)}) collective-permute-start(f32[8,512]{1,0:T(8,128)} %get-tuple-element.21), channel_id=1, source_target_pairs={{16,0},{32,16},{48,32},{64,48},{80,64},{96,80},{112,96},{17,1},{33... | collective-permute-start | bytes 49160 | tf_op jit(solution)/shard_map/ppermute | solution.py:93
  52.5 8.5 %collective-permute-start.5 = (f32[144,64]{1,0:T(8,128)S(1)}, f32[144,64]{1,0:T(8,128)S(1)}, u32[]{:S(2)}, u32[]{:S(2)}) collective-permute-start(f32[144,64]{1,0:T(8,128)S(1)} %get-tuple-element.23), channel_id=1, source_target_pairs={{1,0},{2,1},{3,2},{4,3},{5,4},{6,5},{7,6},{8,7},{9,8},{10,9},{11,1... | collective-permute-start | bytes 110600 | tf_op jit(solution)/shard_map/ppermute | solution.py:96
  56.7 5.6 %collective-permute-start.4 = (f32[144,64]{1,0:T(8,128)S(1)}, f32[144,64]{1,0:T(8,128)S(1)}, u32[]{:S(2)}, u32[]{:S(2)}) collective-permute-start(f32[144,64]{1,0:T(8,128)S(1)} %get-tuple-element.22), channel_id=1, source_target_pairs={{0,1},{1,2},{2,3},{3,4},{4,5},{5,6},{6,7},{7,8},{8,9},{9,10},{10,1... | collective-permute-start | bytes 110600 | tf_op jit(solution)/shard_map/ppermute | solution.py:95

commit v16 on v15

--- a/solution.py
+++ b/solution.py
@@ -104,16 +104,26 @@
     return pltpu.roll(a, (-offset) % a.shape[axis], axis)
 
 
+def window_sum(u, radius, axis, step):
+    if radius == 1:
+        return u + shifted(u, -step, axis) + shifted(u, step, axis)
+    pairs = u + shifted(u, step, axis)
+    quads = pairs + shifted(pairs, 2 * step, axis)
+    if radius == 2:
+        return shifted(quads, -2 * step, axis) + shifted(u, 2 * step, axis)
+    if radius == 3:
+        return (
+            shifted(quads, -3 * step, axis)
+            + shifted(pairs, step, axis)
+            + shifted(u, 3 * step, axis)
+        )
+    return shifted(quads, -4 * step, axis) + quads + shifted(u, 4 * step, axis)
+
+
 def box_smooth(u, radius, lane_x):
     scale = 1.0 / float(2 * radius + 1)
-    along_y = u
-    for o in range(1, radius + 1):
-        along_y = along_y + shifted(u, -o, 0) + shifted(u, o, 0)
-    along_y = along_y * scale
-    along_z = along_y
-    for o in range(1, radius + 1):
-        along_z = along_z + shifted(along_y, -XS * o, 1) + shifted(along_y, XS * o, 1)
-    along_z = along_z * scale
+    along_y = window_sum(u, radius, 0, 1) * scale
+    along_z = window_sum(along_y, radius, 1, XS) * scale
     along_x = along_z
     for o in range(1, radius + 1):
         along_x = (

time: 70.9 us -> 70.1 us (0.989)
  the two profiles are of different devices: /device:TPU:11 before, /device:TPU:34 now
where the time goes in v16:
time: 70.1 us; the launch traced here: 69.6 us
  Pallas kernels  38.2 us (54%)
  starting transfers between devices  20.8 us (30%)
  waiting for transfers between devices  6.86 us (10%)
  local copies, waits for them, and re-layouts  2.55 us (4%)
  between operations  0.81 us (1%)
    pallas_call x1, Pallas kernels, per_device(): pl.pallas_call(lambda *refs: softmin_middle_kernel(total_y, *refs), out_s...  15.1 us
    pallas_call x2, Pallas kernels, channel_major(): pl.pallas_call(transpose_kernel, out_shape=(whole, ends, ends) if with_en...  10.1 us
    pallas_call x1, Pallas kernels, per_device(): pl.pallas_call(lambda *refs: softmin_edge_kernel(total_y, *refs), out_sha...  7.13 us
    pallas_call x1, Pallas kernels, per_device(): pl.pallas_call(adam_kernel, out_shape=jax.ShapeDtypeStruct((height, colum...  5.93 us
    ppermute x1, starting transfers between devices, per_device(): lax.ppermute(moving_tail, 'gy', [(i, i + 1) for i in range(gy_count - 1)])  5.09 us
    ppermute x1, starting transfers between devices, exchange_halo(): top = lax.ppermute(tail, 'gy', [(i, i + 1) for i in range(ny - 1)])  4.37 us
    ppermute x1, waiting for transfers between devices, exchange_halo(): lax.ppermute(cells[:, -send_z:], 'gz', [(i, i + 1) for i in range(nz - 1)])  4.03 us
    ppermute x1, starting transfers between devices, exchange_halo(): bottom = lax.ppermute(head, 'gy', [(i + 1, i) for i in range(ny - 1)])  3.87 us
  transfers between devices with their start and end apart: 6, of which 3 were waited for; matrix products, arithmetic and copies ran while one was open for 3% of the time, Pallas kernels for 29%

profile of v16, /device:TPU:34, one launch (start us, length us, event | category | flops | bytes accessed | tf_op | source)
XLA Modules:
  0.0 69.6 jit_solution(16795484358829130572)
XLA Ops:
  0.6 0.0 copy-start.4
  0.6 0.0 copy-start.3
  0.7 5.2 %shard_map.72 = (bf16[16,128,512]{2,1,0:T(8,128)(2,1)}, bf16[16,32,512]{2,1,0:T(8,128)(2,1)}, bf16[16,32,512]{2,1,0:T(8,128)(2,1)}) custom-call(bf16[128,8192]{1,0:T(8,128)(2,1)} %x_ref.3), custom_call_target="tpu_custom_call" | custom-call | tf_op jit(solution)/shard_map/pallas_call | solution.py:178
  5.9 5.1 %collective-permute-start = (bf16[16,32,512]{2,1,0:T(8,128)(2,1)}, bf16[16,32,512]{2,1,0:T(8,128)(2,1)S(1)}, u32[]{:S(2)}, u32[]{:S(2)}) collective-permute-start(bf16[16,32,512]{2,1,0:T(8,128)(2,1)} %get-tuple-element.13), channel_id=1, source_target_pairs={{0,16},{16,32},{32,48},{48,64},{64,80},{80,96},{96,112},{1,17},{17... | collective-permute-start | bytes 1572872 | tf_op jit(solution)/shard_map/ppermute | solution.py:393
  11.0 3.1 %collective-permute-start.1 = (bf16[16,32,512]{2,1,0:T(8,128)(2,1)}, bf16[16,32,512]{2,1,0:T(8,128)(2,1)S(1)}, u32[]{:S(2)}, u32[]{:S(2)}) collective-permute-start(bf16[16,32,512]{2,1,0:T(8,128)(2,1)} %get-tuple-element.14), channel_id=1, source_target_pairs={{16,0},{32,16},{48,32},{64,48},{80,64},{96,80},{112,96},{17,1},{33... | collective-permute-start | bytes 1572872 | tf_op jit(solution)/shard_map/ppermute | solution.py:394
  14.1 0.0 copy-done.4
  14.2 0.0 copy-done.3
  14.2 0.1 convert_reduce_fusion
  14.3 0.7 copy.10.refs_0_
  15.0 4.9 %shard_map.71.refs_1_ = bf16[16,128,512]{2,1,0:T(8,128)(2,1)} custom-call(bf16[128,8192]{1,0:T(8,128)(2,1)} %x_ref.2), custom_call_target="tpu_custom_call" | custom-call | tf_op jit(solution)/shard_map/pallas_call | solution.py:178
  19.8 15.1 %shard_map.73 = (f32[128,512]{1,0:T(8,128)}, f32[64,512]{1,0:T(8,128)}, f32[64,512]{1,0:T(8,128)}, f32[64,512]{1,0:T(8,128)}) custom-call(f32[32,17]{1,0:T(8,128)} %copy.10.refs_0_, bf16[16,128,512]{2,1,0:T(8,128)(2,1)} %shard_map.71.refs_1_, bf16[16,128,512]{2,1,0:T(8,128)(2,1)} %get-tuple-element.12.refs_2_), custom_call_target="tpu_custom_call" | custom-call | tf_op jit(solution)/shard_map/pallas_call | solution.py:410
  34.9 0.0 collective-permute-done.refs_3_
  34.9 0.0 copy-start.1
  34.9 0.4 collective-permute-done.1.refs_4_
  35.3 0.0 copy-start.2
  35.3 0.4 copy-done.1
  35.7 0.4 copy-done.2
  36.1 0.0 copy-start
  36.1 7.1 %shard_map.74 = (f32[128,512]{1,0:T(8,128)}, f32[8,512]{1,0:T(8,128)}, f32[8,512]{1,0:T(8,128)}) custom-call(f32[32,17]{1,0:T(8,128)} %copy.10.refs_0_, bf16[16,128,512]{2,1,0:T(8,128)(2,1)} %shard_map.71.refs_1_, bf16[16,128,512]{2,1,0:T(8,128)(2,1)} %get-tuple-element.12.refs_2_, bf16[16,32,512]{2,1,0:T(8,128)(2,1)} %copy-done.1, ...), custom_call_target="tpu_custom_call", output_to_operand_aliasing={{0}: (8, {})} | custom-call | tf_op jit(solution)/shard_map/pallas_call | solution.py:418
  43.2 4.4 %collective-permute-start.2 = (f32[8,512]{1,0:T(8,128)}, f32[8,512]{1,0:T(8,128)S(1)}, u32[]{:S(2)}, u32[]{:S(2)}) collective-permute-start(f32[8,512]{1,0:T(8,128)} %get-tuple-element.20), channel_id=1, source_target_pairs={{0,16},{16,32},{32,48},{48,64},{64,80},{80,96},{96,112},{1,17},{17... | collective-permute-start | bytes 49160 | tf_op jit(solution)/shard_map/ppermute | solution.py:92
  47.6 3.9 %collective-permute-start.3 = (f32[8,512]{1,0:T(8,128)}, f32[8,512]{1,0:T(8,128)S(1)}, u32[]{:S(2)}, u32[]{:S(2)}) collective-permute-start(f32[8,512]{1,0:T(8,128)} %get-tuple-element.21), channel_id=1, source_target_pairs={{16,0},{32,16},{48,32},{64,48},{80,64},{96,80},{112,96},{17,1},{33... | collective-permute-start | bytes 49160 | tf_op jit(solution)/shard_map/ppermute | solution.py:93
  51.5 0.0 collective-permute-done.2
  51.5 1.0 %constant_dynamic-update-slice_fusion.1 = f32[144,512]{1,0:T(8,128)S(1)} fusion(f32[144,512]{1,0:T(8,128)S(1)} %constant_dynamic-update-slice_fusion.2, f32[128,512]{1,0:T(8,128)} %get-tuple-element.10), kind=kLoop, calls=%fused_computation.4 | loop fusion | bytes 524288
  52.5 2.5 %collective-permute-done.3 = f32[8,512]{1,0:T(8,128)S(1)} collective-permute-done((f32[8,512]{1,0:T(8,128)}, f32[8,512]{1,0:T(8,128)S(1)}, u32[]{:S(2)}, u32[]{:S(2)}) %collective-permute-start.3) | collective-permute-done | bytes 16416 | tf_op jit(solution)/shard_map/ppermute | solution.py:93
  54.9 0.1 fusion.2
  55.0 1.9 %collective-permute-start.5 = (f32[144,64]{1,0:T(8,128)S(1)}, f32[144,64]{1,0:T(8,128)S(1)}, u32[]{:S(2)}, u32[]{:S(2)}) collective-permute-start(f32[144,64]{1,0:T(8,128)S(1)} %get-tuple-element.23), channel_id=1, source_target_pairs={{1,0},{2,1},{3,2},{4,3},{5,4},{6,5},{7,6},{8,7},{9,8},{10,9},{11,1... | collective-permute-start | bytes 110600 | tf_op jit(solution)/shard_map/ppermute | solution.py:96
  57.0 2.4 %collective-permute-start.4 = (f32[144,64]{1,0:T(8,128)S(1)}, f32[144,64]{1,0:T(8,128)S(1)}, u32[]{:S(2)}, u32[]{:S(2)}) collective-permute-start(f32[144,64]{1,0:T(8,128)S(1)} %get-tuple-element.22), channel_id=1, source_target_pairs={{0,1},{1,2},{2,3},{3,4},{4,5},{5,6},{6,7},{7,8},{8,9},{9,10},{10,1... | collective-permute-start | bytes 110600 | tf_op jit(solution)/shard_map/ppermute | solution.py:95
  59.4 0.1 and_convert_fusion.mask_ref
  59.5 0.0 collective-permute-done.5
  59.5 4.0 %collective-permute-done.4 = f32[144,64]{1,0:T(8,128)S(1)} collective-permute-done((f32[144,64]{1,0:T(8,128)S(1)}, f32[144,64]{1,0:T(8,128)S(1)}, u32[]{:S(2)}, u32[]{:S(2)}) %collective-permute-start.4) | collective-permute-done | bytes 36896 | tf_op jit(solution)/shard_map/ppermute | solution.py:95
  63.5 0.2 pad_maximum_fusion.d_ref
  63.7 0.0 copy-done
  63.7 5.9 %shard_map.75 = f32[128,512]{1,0:T(8,128)} custom-call(s32[3]{0:T(128)S(1)} %copy-done, f32[144,640]{1,0:T(8,128)S(1)} %pad_maximum_fusion.d_ref, f32[144,640]{1,0:T(8,128)S(1)} %and_convert_fusion.mask_ref), custom_call_target="tpu_custom_call" | custom-call | tf_op jit(solution)/shard_map/pallas_call | solution.py:451
  (6 shorter events, 0.0 us)
Async XLA Ops:
  0.6 13.5 %copy-start.4 = (s32[32,1]{0,1:T(1,128)S(1)}, s32[32,1]{0,1:T(1,128)}, u32[]{:S(2)}) copy-start(s32[32,1]{0,1:T(1,128)} %param.8) | copy-start | bytes 388
  0.6 13.5 %copy-start.3 = (s32[32,1,16]{0,2,1:T(8,128)S(1)}, s32[32,1,16]{0,2,1:T(8,128)}, u32[]{:S(2)}) copy-start(s32[32,1,16]{0,2,1:T(8,128)} %param.7) | copy-start | bytes 6148
  5.9 29.0 %collective-permute-start = (bf16[16,32,512]{2,1,0:T(8,128)(2,1)}, bf16[16,32,512]{2,1,0:T(8,128)(2,1)S(1)}, u32[]{:S(2)}, u32[]{:S(2)}) collective-permute-start(bf16[16,32,512]{2,1,0:T(8,128)(2,1)} %get-tuple-element.13), channel_id=1, source_target_pairs={{0,16},{16,32},{32,48},{48,64},{64,80},{80,96},{96,112},{1,17},{17... | collective-permute-start | bytes 1572872 | tf_op jit(solution)/shard_map/ppermute | solution.py:393
  11.0 24.3 %collective-permute-start.1 = (bf16[16,32,512]{2,1,0:T(8,128)(2,1)}, bf16[16,32,512]{2,1,0:T(8,128)(2,1)S(1)}, u32[]{:S(2)}, u32[]{:S(2)}) collective-permute-start(bf16[16,32,512]{2,1,0:T(8,128)(2,1)} %get-tuple-element.14), channel_id=1, source_target_pairs={{16,0},{32,16},{48,32},{64,48},{80,64},{96,80},{112,96},{17,1},{33... | collective-permute-start | bytes 1572872 | tf_op jit(solution)/shard_map/ppermute | solution.py:394
  34.9 0.8 %copy-start.1 = (bf16[16,32,512]{2,1,0:T(8,128)(2,1)}, bf16[16,32,512]{2,1,0:T(8,128)(2,1)S(1)}, u32[]{:S(2)}) copy-start(bf16[16,32,512]{2,1,0:T(8,128)(2,1)S(1)} %collective-permute-done.refs_3_) | copy-start | bytes 1572868
  35.3 0.8 %copy-start.2 = (bf16[16,32,512]{2,1,0:T(8,128)(2,1)}, bf16[16,32,512]{2,1,0:T(8,128)(2,1)S(1)}, u32[]{:S(2)}) copy-start(bf16[16,32,512]{2,1,0:T(8,128)(2,1)S(1)} %collective-permute-done.1.refs_4_) | copy-start | bytes 1572868
  36.1 27.6 %copy-start = (s32[3]{0:T(128)S(1)}, s32[3]{0:T(128)}, u32[]{:S(2)}) copy-start(s32[3]{0:T(128)} %radii_ref.1) | copy-start | bytes 40
  43.2 8.3 %collective-permute-start.2 = (f32[8,512]{1,0:T(8,128)}, f32[8,512]{1,0:T(8,128)S(1)}, u32[]{:S(2)}, u32[]{:S(2)}) collective-permute-start(f32[8,512]{1,0:T(8,128)} %get-tuple-element.20), channel_id=1, source_target_pairs={{0,16},{16,32},{32,48},{48,64},{64,80},{80,96},{96,112},{1,17},{17... | collective-permute-start | bytes 49160 | tf_op jit(solution)/shard_map/ppermute | solution.py:92
  47.6 7.3 %collective-permute-start.3 = (f32[8,512]{1,0:T(8,128)}, f32[8,512]{1,0:T(8,128)S(1)}, u32[]{:S(2)}, u32[]{:S(2)}) collective-permute-start(f32[8,512]{1,0:T(8,128)} %get-tuple-element.21), channel_id=1, source_target_pairs={{16,0},{32,16},{48,32},{64,48},{80,64},{96,80},{112,96},{17,1},{33... | collective-permute-start | bytes 49160 | tf_op jit(solution)/shard_map/ppermute | solution.py:93
  55.0 4.5 %collective-permute-start.5 = (f32[144,64]{1,0:T(8,128)S(1)}, f32[144,64]{1,0:T(8,128)S(1)}, u32[]{:S(2)}, u32[]{:S(2)}) collective-permute-start(f32[144,64]{1,0:T(8,128)S(1)} %get-tuple-element.23), channel_id=1, source_target_pairs={{1,0},{2,1},{3,2},{4,3},{5,4},{6,5},{7,6},{8,7},{9,8},{10,9},{11,1... | collective-permute-start | bytes 110600 | tf_op jit(solution)/shard_map/ppermute | solution.py:96
  57.0 6.6 %collective-permute-start.4 = (f32[144,64]{1,0:T(8,128)S(1)}, f32[144,64]{1,0:T(8,128)S(1)}, u32[]{:S(2)}, u32[]{:S(2)}) collective-permute-start(f32[144,64]{1,0:T(8,128)S(1)} %get-tuple-element.22), channel_id=1, source_target_pairs={{0,1},{1,2},{2,3},{3,4},{4,5},{5,6},{6,7},{7,8},{8,9},{9,10},{10,1... | collective-permute-start | bytes 110600 | tf_op jit(solution)/shard_map/ppermute | solution.py:95
